TPU v7x, 256 devices: a whole 4x4x8 slice. The times are simulated.
256 devices in a mesh: seq: 32 (over z, x), head: 8 (over y, core).
Axes of the slice: x: 4, y: 4, z: 8, core: 2. Of those that a mesh axis runs over, the one named last changes fastest.
Arguments:
- queries: bfloat16 [16384, 4096], P('seq', 'head'), may hold values from -6 to 6
- key_rows: bfloat16 [16384, 4096], P('seq', 'head'), may hold values from -6 to 6
- value_rows: bfloat16 [16384, 4096], P('seq', 'head'), may hold values from -18 to 18
- out_grad: bfloat16 [16384, 4096], P('seq', 'head'), may hold values from -6 to 6
- log_decay: float32 [32, 16384], P('head', 'seq'), may hold values from -0.6 to 0
Outputs:
- query_gradient: bfloat16 [16384, 4096], P('seq', 'head')
- key_grad: bfloat16 [16384, 4096], P('seq', 'head')
- value_grad: bfloat16 [16384, 4096], P('seq', 'head')
All inputs are finite; a program needn't handle non-finite values.
Results may differ from a plain program's by a relative error of at most 0.006.
Values sent between devices are 32-bit elements; how exact they have to be, the bound alone decides.
No kernel may reach another device: no remote copies, remote signals or barrier semaphores. Data moves between devices by JAX's collectives and lax.ppermute only.
A program may use at most 64 MiB of HBM per device.

v0:
```python
import jax
import jax.numpy as jnp
from jax import lax
from jax.sharding import PartitionSpec as P

HEAD_COUNT = 32
DH = 128
BLOCK = 128


epsilon = 1e-06
highest = lax.Precision.HIGHEST


def shards(queries, key_rows, value_rows, out_grad, log_decay):
    tok_rows, row_width = queries.shape
    heads_dev = log_decay.shape[0]
    head_size = row_width // heads_dev
    blocks = tok_rows // BLOCK
    total_width = HEAD_COUNT * DH
    block_shape = (blocks, BLOCK, heads_dev, head_size)
    query_block_rows = queries.reshape(block_shape)
    key_blocks = key_rows.reshape(block_shape)
    value_block_rows = value_rows.reshape(block_shape)
    grad_blocks = out_grad.reshape(block_shape)
    decay_blocks = jnp.transpose(log_decay.reshape(heads_dev, blocks, BLOCK), (1, 2, 0))
    inside_block_mask = jnp.cumsum(decay_blocks, axis=1)
    totals = inside_block_mask[:, -1, :]
    before = jnp.cumsum(totals, axis=0) - totals
    shard_total = jnp.sum(totals, axis=0)
    token_positions = jnp.arange(BLOCK)
    causal = (token_positions[:, None] >= token_positions[None, :]).astype(jnp.float32)
    within_heads = jnp.transpose(inside_block_mask, (0, 2, 1))
    exponent = within_heads[:, :, :, None] - within_heads[:, :, None, :]
    decay_mask = jnp.exp(jnp.minimum(exponent, 0.0)) * causal
    scores = jnp.einsum(
        "nihd,njhd->nhij", query_block_rows, key_blocks, preferred_element_type=jnp.float32
    )
    attention_weights = (scores * decay_mask).astype(jnp.bfloat16)
    intra_out = jnp.einsum(
        "nhij,njhd->nihd", attention_weights, value_block_rows, preferred_element_type=jnp.float32
    )
    to_end = jnp.exp(totals[:, None, :] - inside_block_mask)
    keys_scaled = (to_end[..., None] * key_blocks).astype(jnp.bfloat16)
    block_terms = jnp.einsum(
        "njhd,njhe->nhde", keys_scaled, value_block_rows, preferred_element_type=jnp.float32
    )
    block_ids = jnp.arange(blocks)
    earlier_blocks = (block_ids[:, None] > block_ids[None, :]).astype(jnp.float32)
    forward_exp = before[:, None, :] - before[None, :, :] - totals[None, :, :]
    forward_mix = jnp.exp(jnp.minimum(forward_exp, 0.0)) * earlier_blocks[:, :, None]
    local_states = jnp.einsum("nmh,mhde->nhde", forward_mix, block_terms, precision=highest)
    shard_state = jnp.einsum(
        "mh,mhde->hde",
        jnp.exp(shard_total[None, :] - before - totals),
        block_terms,
        precision=highest,
    )
    all_totals, all_states = (
        lax.all_gather(shard_total[None], "seq", axis=0, tiled=True),
        lax.all_gather(shard_state[None], "seq", axis=0, tiled=True),
    )
    seq_ranks = lax.axis_size("seq")
    my_rank = lax.axis_index("seq")
    starts = jnp.cumsum(all_totals, axis=0) - all_totals
    my_start = lax.dynamic_index_in_dim(starts, my_rank, 0, keepdims=False)
    rank_ids = jnp.arange(seq_ranks)
    reach_log = my_start[None, :] - starts - all_totals
    mixing = jnp.exp(jnp.minimum(reach_log, 0.0)) * (rank_ids < my_rank)[:, None].astype(
        jnp.float32
    )
    incoming = jnp.einsum("rh,rhde->hde", mixing, all_states, precision=highest)
    states = local_states + jnp.exp(before)[:, :, None, None] * incoming[None]
    backward_state = states.astype(jnp.bfloat16)
    inter_out = jnp.einsum(
        "nihd,nhde->nihe", query_block_rows, backward_state, preferred_element_type=jnp.float32
    )
    attention_output = intra_out + jnp.exp(inside_block_mask)[..., None] * inter_out
    square = jnp.sum(attention_output * attention_output, axis=(2, 3))
    square_total = lax.psum(square, "head")
    inv_rms = lax.rsqrt(square_total / total_width + epsilon)
    normed = attention_output * inv_rms[:, :, None, None]
    cross_local = jnp.sum(grad_blocks.astype(jnp.float32) * normed, axis=(2, 3))
    cross_total = lax.psum(cross_local, "head")
    mean_cross = cross_total / total_width
    attention_gradient = (
        inv_rms[:, :, None, None]
        * (grad_blocks.astype(jnp.float32) - normed * mean_cross[:, :, None, None])
    ).astype(jnp.bfloat16)
    score_gradient = jnp.einsum(
        "nihe,njhe->nhij", attention_gradient, value_block_rows, preferred_element_type=jnp.float32
    )
    grad_probs = (score_gradient * decay_mask).astype(jnp.bfloat16)
    query_gradient = jnp.einsum(
        "nhij,njhd->nihd", grad_probs, key_blocks, preferred_element_type=jnp.float32
    )
    query_gradient = query_gradient + jnp.exp(inside_block_mask)[..., None] * jnp.einsum(
        "nihe,nhde->nihd", attention_gradient, backward_state, preferred_element_type=jnp.float32
    )
    key_intra = jnp.einsum(
        "nhij,nihd->njhd", grad_probs, query_block_rows, preferred_element_type=jnp.float32
    )
    value_within_block = jnp.einsum(
        "nhij,nihe->njhe", attention_weights, attention_gradient, preferred_element_type=jnp.float32
    )
    scaled_query_rows = (jnp.exp(inside_block_mask)[..., None] * query_block_rows).astype(
        jnp.bfloat16
    )
    backward_terms = jnp.einsum(
        "nihd,nihe->nhde", scaled_query_rows, attention_gradient, preferred_element_type=jnp.float32
    )
    later_blocks = (block_ids[:, None] < block_ids[None, :]).astype(jnp.float32)
    backward_exp = before[None, :, :] - before[:, None, :] - totals[:, None, :]
    backward_mix = jnp.exp(jnp.minimum(backward_exp, 0.0)) * later_blocks[:, :, None]
    local_back = jnp.einsum("nmh,mhde->nhde", backward_mix, backward_terms, precision=highest)
    shard_back = jnp.einsum("mh,mhde->hde", jnp.exp(before), backward_terms, precision=highest)
    shard_piece = lax.all_gather(shard_back[None], "seq", axis=0, tiled=True)
    piece_rows = shard_piece.shape[0]
    piece_ranks = jnp.arange(piece_rows)
    reach_log = starts - my_start[None, :] - shard_total[None, :]
    mixing = jnp.exp(jnp.minimum(reach_log, 0.0)) * (piece_ranks > my_rank)[:, None].astype(
        jnp.float32
    )
    later_state = jnp.einsum("rh,rhde->hde", mixing, shard_piece, precision=highest)
    back_states = (
        local_back
        + jnp.exp(shard_total[None, :] - before - totals)[:, :, None, None] * later_state[None]
    )
    back_b = back_states.astype(jnp.bfloat16)
    key_grad = key_intra + to_end[..., None] * jnp.einsum(
        "njhe,nhde->njhd", value_block_rows, back_b, preferred_element_type=jnp.float32
    )
    value_grad = value_within_block + to_end[..., None] * jnp.einsum(
        "njhd,nhde->njhe", key_blocks, back_b, preferred_element_type=jnp.float32
    )
    return (
        query_gradient.reshape(tok_rows, row_width).astype(jnp.bfloat16),
        key_grad.reshape(tok_rows, row_width).astype(jnp.bfloat16),
        value_grad.reshape(tok_rows, row_width).astype(jnp.bfloat16),
    )


def solution(mesh):
    return jax.shard_map(
        shards,
        mesh=mesh,
        in_specs=(
            P("seq", "head"),
            P("seq", "head"),
            P("seq", "head"),
            P("seq", "head"),
            P("head", "seq"),
        ),
        out_specs=(P("seq", "head"), P("seq", "head"), P("seq", "head")),
        check_vma=False,
    )
```

profile of v0, /device:TPU:32, one launch (start us, length us, event | category | flops | bytes accessed | tf_op | source)
XLA Modules:
  0.0 285.0 jit_solution(773826581241886380)
XLA Ops:
  13.2 3.1 %fusion.24 = f32[4,1,128,128]{3,1,2,0:T(1,128)} fusion(f32[4,4,1,1]{0,2,3,1:T(1,128)S(1)} %copy.132, f32[4,4,128,128]{3,2,1,0:T(8,128)S(1)} %fusion.27), kind=kOutput, calls=%fused_computation.42 | convolution fusion | flops 3145728 | bytes 1310784 | tf_op jit(solution)/shard_map/mh,mhde->hde/dot_general | solution.py:53
  18.7 72.5 %all-reduce = f32[128]{0:T(128)S(1)} all-reduce(f32[128]{0:T(128)S(1)} %dynamic-update-slice), channel_id=2, replica_groups=mesh['seq'=32,'head'=8] {'seq'}, use_global_device_ids=true, to_apply=%add | all-reduce | flops 128 | bytes 1024
  92.4 1.3 reshape.133
  93.7 1.6 copy.106
  96.9 1.5 convolution_bitcast_fusion.9
  98.4 17.1 %all-gather.6.cloned.1.call-done = f32[128,128,128]{2,1,0:T(8,128)} async-done(((f32[4,128,128]{2,1,0:T(8,128)}), f32[128,128,128]{2,1,0:T(8,128)}) %all-gather.6.cloned.1.call-update) | async-done | bytes 8388624 | tf_op jit(solution)/shard_map/all_gather | solution.py:61
  115.5 12.2 %fusion.2 = f32[4,1,128,128]{3,1,2,0:T(1,128)S(1)} fusion(f32[32,4,1,1]{0,2,3,1:T(1,128)S(1)} %copy.134, f32[32,4,128,128]{3,2,1,0:T(8,128)} %bitcast.121), kind=kOutput, calls=%fused_computation.2 | convolution fusion | flops 25165824 | bytes 8651264 | tf_op jit(solution)/shard_map/rh,rhde->hde/dot_general | solution.py:72
  127.7 2.7 fusion.18
  130.4 1.6 multiply_reduce_fusion.1
  132.0 14.0 %psum.14 = f32[4,128]{1,0:T(4,128)S(1)} all-reduce(f32[4,128]{1,0:T(4,128)S(1)} %get-tuple-element.13), channel_id=1, replica_groups=mesh['seq'=32,'head'=8] {'head'}, use_global_device_ids=true, to_apply=%region_5.6 | all-reduce | flops 512 | bytes 4096 | tf_op jit(solution)/shard_map/psum | solution.py:80
  146.2 12.6 %psum.15 = f32[4,128]{1,0:T(4,128)S(1)} all-reduce(f32[4,128]{1,0:T(4,128)S(1)} %multiply_reduce_fusion), channel_id=1, replica_groups=mesh['seq'=32,'head'=8] {'head'}, use_global_device_ids=true, to_apply=%region_7.8 | all-reduce | flops 512 | bytes 4096 | tf_op jit(solution)/shard_map/psum | solution.py:84
  159.8 1.6 fusion.28
  161.4 3.1 %fusion.21 = f32[4,1,128,128]{3,1,2,0:T(1,128)} fusion(f32[4,4,1,1]{0,2,3,1:T(1,128)S(1)} %copy.143, f32[4,4,128,128]{3,2,1,0:T(8,128)S(1)} %fusion.28), kind=kOutput, calls=%fused_computation.39 | convolution fusion | flops 3145728 | bytes 1310784 | tf_op jit(solution)/shard_map/mh,mhde->hde/dot_general | solution.py:116
  164.7 1.6 fusion.19
  167.7 2.3 fusion.14
  170.0 2.2 copy.113
  172.2 1.9 copy.196
  174.2 2.6 convolution_bitcast_fusion.2
  176.8 2.5 convolution_bitcast_fusion.4
  179.3 77.6 %all-gather.8.cloned.1.call-done = f32[128,128,128]{2,1,0:T(8,128)} async-done(((f32[4,128,128]{2,1,0:T(8,128)}), f32[128,128,128]{2,1,0:T(8,128)}) %all-gather.8.cloned.1.call-update) | async-done | bytes 8388624 | tf_op jit(solution)/shard_map/all_gather | solution.py:117
  256.9 12.3 %fusion = f32[4,1,128,128]{3,1,2,0:T(1,128)S(1)} fusion(f32[32,4,1,1]{0,2,3,1:T(1,128)S(1)} %copy.145, f32[32,4,128,128]{3,2,1,0:T(8,128)} %bitcast.122), kind=kOutput, calls=%fused_computation | convolution fusion | flops 25165824 | bytes 8651264 | tf_op jit(solution)/shard_map/rh,rhde->hde/dot_general | solution.py:124
  269.2 2.6 fusion.20
  272.2 1.7 fusion.15
  275.2 1.6 fusion.16
  (76 shorter events, 16.0 us)
Async XLA Ops:
  7.2 84.7 %copy-start.11 = (bf16[512,512]{1,0:T(8,128)(2,1)S(1)}, bf16[512,512]{1,0:T(8,128)(2,1)}, u32[]{:S(2)}) copy-start(bf16[512,512]{1,0:T(8,128)(2,1)} %param.5) | copy-start | bytes 1572868
  7.2 85.3 %copy-start.10 = (bf16[512,512]{1,0:T(8,128)(2,1)S(1)}, bf16[512,512]{1,0:T(8,128)(2,1)}, u32[]{:S(2)}) copy-start(bf16[512,512]{1,0:T(8,128)(2,1)} %param.8) | copy-start | bytes 1572868
  7.2 108.3 %all-gather.6.cloned.1.call-start = ((), (), s32[]{:S(2)}) async-start(), calls=%async_computation | async-start | bytes 8650752 | tf_op jit(solution)/shard_map/all_gather | solution.py:61
  12.1 1.1 copy-start.4
  16.3 240.7 %all-gather.8.cloned.1.call-start = ((), (), s32[]{:S(2)}) async-start(), calls=%async_computation.1 | async-start | bytes 8650752 | tf_op jit(solution)/shard_map/all_gather | solution.py:117
  92.3 35.4 %copy-start.2 = (bf16[4,128,4,128]{1,3,2,0:T(8,128)(2,1)}, bf16[4,128,4,128]{1,3,2,0:T(8,128)(2,1)S(1)}, u32[]{:S(2)}) copy-start(bf16[4,128,4,128]{1,3,2,0:T(8,128)(2,1)S(1)} %copy.116) | copy-start | bytes 1572868
  96.1 0.8 copy-start.8
  115.5 12.2 %copy-start.5 = (f32[4,4,128,128]{3,2,1,0:T(8,128)S(1)}, f32[4,4,128,128]{3,2,1,0:T(8,128)}, u32[]{:S(2)}) copy-start(f32[4,4,128,128]{3,2,1,0:T(8,128)} %copy-done.4) | copy-start | bytes 3145732
  115.5 14.9 %copy-start.6 = (f32[4,128,4,128]{1,3,2,0:T(8,128)S(1)}, f32[4,128,4,128]{1,3,2,0:T(8,128)}, u32[]{:S(2)}) copy-start(f32[4,128,4,128]{1,3,2,0:T(8,128)} %convolution_bitcast_fusion.9) | copy-start | bytes 3145732
  130.4 1.7 copy-start.7
  159.0 0.8 copy-start
  159.8 16.9 %copy-start.3 = (bf16[4,128,4,128]{1,3,2,0:T(8,128)(2,1)S(1)}, bf16[4,128,4,128]{1,3,2,0:T(8,128)(2,1)}, u32[]{:S(2)}) copy-start(bf16[4,128,4,128]{1,3,2,0:T(8,128)(2,1)} %copy-done.2) | copy-start | bytes 1572868
  161.4 12.7 %copy-start.1 = (bf16[4,128,4,128]{1,3,2,0:T(8,128)(2,1)S(1)}, bf16[4,128,4,128]{1,3,2,0:T(8,128)(2,1)}, u32[]{:S(2)}) copy-start(bf16[4,128,4,128]{1,3,2,0:T(8,128)(2,1)} %copy-done) | copy-start | bytes 1572868
  166.4 0.8 copy-start.9
Sparse Core Ops, SparseCore 0:
  16.4 99.0 all-gather.5
  164.7 92.2 all-gather.7
where the time goes:
time: 288 us; the launch traced here: 285 us
  blocking collectives  99.1 us (34%)
  waiting for transfers between devices  94.7 us (33%)
  matrix products  55.1 us (19%)
  local copies, waits for them, and re-layouts  19.9 us (7%)
  between operations  15 us (5%)
    all_gather x1, waiting for transfers between devices, shards(): shard_piece = lax.all_gather(shard_back[None], 'seq', axis=0, tiled=True)  77.6 us
    unnamed x1, blocking collectives  72.5 us
    all_gather x1, waiting for transfers between devices, shards(): lax.all_gather(shard_state[None], 'seq', axis=0, tiled=True)  17.1 us
    psum x1, blocking collectives, shards(): square_total = lax.psum(square, 'head')  14 us
    psum x1, blocking collectives, shards(): cross_total = lax.psum(cross_local, 'head')  12.6 us
    dot_general x1, matrix products, shards(): jnp.einsum('rh,rhde->hde', mixing, shard_piece, precision=highest)  12.3 us
    dot_general x1, matrix products, shards(): incoming = jnp.einsum('rh,rhde->hde', mixing, all_states, precision=highest)  12.2 us
    unnamed x30, local copies, waits for them, and re-layouts  8.69 us
  transfers between devices with their start and end apart: 2, of which 2 were waited for; matrix products, arithmetic and copies ran while one was open for 8% of the time, Pallas kernels for 0%

commit v1 on v0

--- a/solution.py
+++ b/solution.py
@@ -12,7 +12,49 @@
 highest = lax.Precision.HIGHEST
 
 
-def shards(queries, key_rows, value_rows, out_grad, log_decay):
+def pack(total, state):
+    row = jnp.broadcast_to(total[:, None, None], (state.shape[0], 1, state.shape[2]))
+    return jnp.concatenate([state, row], axis=1)
+
+
+def unpack(payload):
+    rows = payload.shape[1] - 1
+    return payload[:, rows, 0], payload[:, :rows, :]
+
+
+def forward_scan(total, state, ranks):
+    win_a, win_b = total, state
+    excl_a, excl_b = jnp.zeros_like(total), jnp.zeros_like(state)
+    shift = 1
+    while shift < ranks:
+        pairs = [(i, i + shift) for i in range(ranks - shift)]
+        got_a, got_b = unpack(lax.ppermute(pack(win_a, win_b), "seq", pairs))
+        excl_b = jnp.exp(excl_a)[:, None, None] * got_b + excl_b
+        excl_a = excl_a + got_a
+        if 2 * shift < ranks:
+            win_b = jnp.exp(win_a)[:, None, None] * got_b + win_b
+            win_a = win_a + got_a
+        shift *= 2
+    return excl_b
+
+
+def backward_scan(total, state, ranks):
+    win_a, win_c = total, state
+    excl_a, excl_c = jnp.zeros_like(total), jnp.zeros_like(state)
+    shift = 1
+    while shift < ranks:
+        pairs = [(i + shift, i) for i in range(ranks - shift)]
+        got_a, got_c = unpack(lax.ppermute(pack(win_a, win_c), "seq", pairs))
+        excl_c = excl_c + jnp.exp(excl_a)[:, None, None] * got_c
+        excl_a = excl_a + got_a
+        if 2 * shift < ranks:
+            win_c = win_c + jnp.exp(win_a)[:, None, None] * got_c
+            win_a = win_a + got_a
+        shift *= 2
+    return excl_c
+
+
+def shards(queries, key_rows, value_rows, out_grad, log_decay, seq_ranks):
     tok_rows, row_width = queries.shape
     heads_dev = log_decay.shape[0]
     head_size = row_width // heads_dev
@@ -56,36 +98,23 @@
         block_terms,
         precision=highest,
     )
-    all_totals, all_states = (
-        lax.all_gather(shard_total[None], "seq", axis=0, tiled=True),
-        lax.all_gather(shard_state[None], "seq", axis=0, tiled=True),
-    )
-    seq_ranks = lax.axis_size("seq")
-    my_rank = lax.axis_index("seq")
-    starts = jnp.cumsum(all_totals, axis=0) - all_totals
-    my_start = lax.dynamic_index_in_dim(starts, my_rank, 0, keepdims=False)
-    rank_ids = jnp.arange(seq_ranks)
-    reach_log = my_start[None, :] - starts - all_totals
-    mixing = jnp.exp(jnp.minimum(reach_log, 0.0)) * (rank_ids < my_rank)[:, None].astype(
-        jnp.float32
-    )
-    incoming = jnp.einsum("rh,rhde->hde", mixing, all_states, precision=highest)
+    incoming = forward_scan(shard_total, shard_state, seq_ranks)
     states = local_states + jnp.exp(before)[:, :, None, None] * incoming[None]
     backward_state = states.astype(jnp.bfloat16)
     inter_out = jnp.einsum(
         "nihd,nhde->nihe", query_block_rows, backward_state, preferred_element_type=jnp.float32
     )
     attention_output = intra_out + jnp.exp(inside_block_mask)[..., None] * inter_out
+    grad_f32 = grad_blocks.astype(jnp.float32)
     square = jnp.sum(attention_output * attention_output, axis=(2, 3))
-    square_total = lax.psum(square, "head")
-    inv_rms = lax.rsqrt(square_total / total_width + epsilon)
+    cross_raw = jnp.sum(grad_f32 * attention_output, axis=(2, 3))
+    stats = lax.psum(jnp.stack([square, cross_raw]), "head")
+    inv_rms = lax.rsqrt(stats[0] / total_width + epsilon)
+    mean_cross = inv_rms * stats[1] / total_width
     normed = attention_output * inv_rms[:, :, None, None]
-    cross_local = jnp.sum(grad_blocks.astype(jnp.float32) * normed, axis=(2, 3))
-    cross_total = lax.psum(cross_local, "head")
-    mean_cross = cross_total / total_width
     attention_gradient = (
         inv_rms[:, :, None, None]
-        * (grad_blocks.astype(jnp.float32) - normed * mean_cross[:, :, None, None])
+        * (grad_f32 - normed * mean_cross[:, :, None, None])
     ).astype(jnp.bfloat16)
     score_gradient = jnp.einsum(
         "nihe,njhe->nhij", attention_gradient, value_block_rows, preferred_element_type=jnp.float32
@@ -114,14 +143,7 @@
     backward_mix = jnp.exp(jnp.minimum(backward_exp, 0.0)) * later_blocks[:, :, None]
     local_back = jnp.einsum("nmh,mhde->nhde", backward_mix, backward_terms, precision=highest)
     shard_back = jnp.einsum("mh,mhde->hde", jnp.exp(before), backward_terms, precision=highest)
-    shard_piece = lax.all_gather(shard_back[None], "seq", axis=0, tiled=True)
-    piece_rows = shard_piece.shape[0]
-    piece_ranks = jnp.arange(piece_rows)
-    reach_log = starts - my_start[None, :] - shard_total[None, :]
-    mixing = jnp.exp(jnp.minimum(reach_log, 0.0)) * (piece_ranks > my_rank)[:, None].astype(
-        jnp.float32
-    )
-    later_state = jnp.einsum("rh,rhde->hde", mixing, shard_piece, precision=highest)
+    later_state = backward_scan(shard_total, shard_back, seq_ranks)
     back_states = (
         local_back
         + jnp.exp(shard_total[None, :] - before - totals)[:, :, None, None] * later_state[None]
@@ -141,8 +163,13 @@
 
 
 def solution(mesh):
+    seq_ranks = mesh.shape["seq"]
+
+    def body(queries, key_rows, value_rows, out_grad, log_decay):
+        return shards(queries, key_rows, value_rows, out_grad, log_decay, seq_ranks)
+
     return jax.shard_map(
-        shards,
+        body,
         mesh=mesh,
         in_specs=(
             P("seq", "head"),

time: 288 us -> 188 us (0.65)
  the two profiles are of different devices: /device:TPU:32 before, /device:TPU:39 now
where the time goes in v1:
time: 188 us; the launch traced here: 187 us
  waiting for transfers between devices  74.4 us (40%)
  starting transfers between devices  34.3 us (18%)
  local copies, waits for them, and re-layouts  25.2 us (13%)
  matrix products  23.7 us (13%)
  other arithmetic  14.3 us (8%)
  blocking collectives  13.3 us (7%)
    ppermute x5, waiting for transfers between devices, backward_scan(): got_a, got_c = unpack(lax.ppermute(pack(win_a, win_c), 'seq', pairs))  45.8 us
    ppermute x5, waiting for transfers between devices, forward_scan(): got_a, got_b = unpack(lax.ppermute(pack(win_a, win_b), 'seq', pairs))  28.6 us
    ppermute x5, starting transfers between devices, forward_scan(): got_a, got_b = unpack(lax.ppermute(pack(win_a, win_b), 'seq', pairs))  23.7 us
    psum x1, blocking collectives, shards(): stats = lax.psum(jnp.stack([square, cross_raw]), 'head')  13.3 us
    unnamed x79, local copies, waits for them, and re-layouts  13.2 us
    ppermute x5, starting transfers between devices, backward_scan(): got_a, got_c = unpack(lax.ppermute(pack(win_a, win_c), 'seq', pairs))  10.7 us
    add x4, other arithmetic, backward_scan(): win_c = win_c + jnp.exp(win_a)[:, None, None] * got_c  4.74 us
  transfers between devices with their start and end apart: 10, of which 8 were waited for; matrix products, arithmetic and copies ran while one was open for 10% of the time, Pallas kernels for 0%

profile of v1, /device:TPU:39, one launch (start us, length us, event | category | flops | bytes accessed | tf_op | source)
XLA Modules:
  0.0 186.5 jit_solution(16064281633360679951)
XLA Ops:
  4.9 2.4 %fusion.20 = f32[4,1,128,128]{3,1,2,0:T(1,128)S(1)} fusion(f32[4,4,1,1]{0,2,3,1:T(1,128)S(1)} %copy.146, f32[4,4,128,128]{3,2,1,0:T(8,128)S(1)} %fusion.23), kind=kOutput, calls=%fused_computation.38 | convolution fusion | flops 3145728 | bytes 1310784 | tf_op jit(solution)/shard_map/mh,mhde->hde/dot_general | solution.py:95
  7.7 3.5 %collective-permute-start = (f32[4,129,128]{2,0,1:T(4,128)S(1)}, f32[4,129,128]{2,0,1:T(4,128)S(1)}, u32[]{:S(2)}, u32[]{:S(2)}) collective-permute-start(f32[4,129,128]{2,0,1:T(4,128)S(1)} %pad_maximum_fusion.1), channel_id=1, source_target_pairs={{0,8},{8,16},{16,24},{24,32},{32,40},{40,48},{48,56},{56,64},{64,7... | collective-permute-start | bytes 792584 | tf_op jit(solution)/shard_map/ppermute | solution.py:31
  11.1 5.6 %collective-permute-done = f32[4,129,128]{2,0,1:T(4,128)S(1)} collective-permute-done((f32[4,129,128]{2,0,1:T(4,128)S(1)}, f32[4,129,128]{2,0,1:T(4,128)S(1)}, u32[]{:S(2)}, u32[]{:S(2)}) %collective-permute-start) | collective-permute-done | bytes 264224 | tf_op jit(solution)/shard_map/ppermute | solution.py:31
  17.2 4.4 %collective-permute-start.1 = (f32[4,129,128]{2,0,1:T(4,128)S(1)}, f32[4,129,128]{2,0,1:T(4,128)S(1)}, u32[]{:S(2)}, u32[]{:S(2)}) collective-permute-start(f32[4,129,128]{2,0,1:T(4,128)S(1)} %pad_maximum_fusion.2), channel_id=1, source_target_pairs={{0,16},{8,24},{16,32},{24,40},{32,48},{40,56},{48,64},{56,72},{64,... | collective-permute-start | bytes 792584 | tf_op jit(solution)/shard_map/ppermute | solution.py:31
  21.6 5.4 %collective-permute-done.1 = f32[4,129,128]{2,0,1:T(4,128)S(1)} collective-permute-done((f32[4,129,128]{2,0,1:T(4,128)S(1)}, f32[4,129,128]{2,0,1:T(4,128)S(1)}, u32[]{:S(2)}, u32[]{:S(2)}) %collective-permute-start.1) | collective-permute-done | bytes 264224 | tf_op jit(solution)/shard_map/ppermute | solution.py:31
  28.6 3.5 %collective-permute-start.2 = (f32[4,129,128]{2,0,1:T(4,128)}, f32[4,129,128]{2,0,1:T(4,128)}, u32[]{:S(2)}, u32[]{:S(2)}) collective-permute-start(f32[4,129,128]{2,0,1:T(4,128)} %pad_maximum_fusion.3), channel_id=1, source_target_pairs={{0,32},{8,40},{16,48},{24,56},{32,64},{40,72},{48,80},{56,88},{64,... | collective-permute-start | bytes 792584 | tf_op jit(solution)/shard_map/ppermute | solution.py:31
  41.2 6.1 %collective-permute-start.3 = (f32[4,129,128]{2,0,1:T(4,128)S(1)}, f32[4,129,128]{2,0,1:T(4,128)S(1)}, u32[]{:S(2)}, u32[]{:S(2)}) collective-permute-start(f32[4,129,128]{2,0,1:T(4,128)S(1)} %pad_maximum_fusion.4), channel_id=1, source_target_pairs={{0,64},{8,72},{16,80},{24,88},{32,96},{40,104},{48,112},{56,120},{... | collective-permute-start | bytes 792584 | tf_op jit(solution)/shard_map/ppermute | solution.py:31
  48.7 9.1 %collective-permute-done.3 = f32[4,129,128]{2,0,1:T(4,128)S(1)} collective-permute-done((f32[4,129,128]{2,0,1:T(4,128)S(1)}, f32[4,129,128]{2,0,1:T(4,128)S(1)}, u32[]{:S(2)}, u32[]{:S(2)}) %collective-permute-start.3) | collective-permute-done | bytes 264224 | tf_op jit(solution)/shard_map/ppermute | solution.py:31
  60.5 6.1 %collective-permute-start.4 = (f32[4,129,128]{2,0,1:T(4,128)S(1)}, f32[4,129,128]{2,0,1:T(4,128)S(1)}, u32[]{:S(2)}, u32[]{:S(2)}) collective-permute-start(f32[4,129,128]{2,0,1:T(4,128)S(1)} %pad_maximum_fusion.5), channel_id=1, source_target_pairs={{0,128},{8,136},{16,144},{24,152},{32,160},{40,168},{48,176},{56,1... | collective-permute-start | bytes 792584 | tf_op jit(solution)/shard_map/ppermute | solution.py:31
  67.2 8.6 %collective-permute-done.4 = f32[4,129,128]{2,0,1:T(4,128)S(1)} collective-permute-done((f32[4,129,128]{2,0,1:T(4,128)S(1)}, f32[4,129,128]{2,0,1:T(4,128)S(1)}, u32[]{:S(2)}, u32[]{:S(2)}) %collective-permute-start.4) | collective-permute-done | bytes 264224 | tf_op jit(solution)/shard_map/ppermute | solution.py:31
  77.7 2.7 %fusion.14 = bf16[4,4,128,128]{3,0,2,1:T(4,128)(2,1)S(1)} fusion(f32[4,4,128,128]{3,2,1,0:T(8,128)S(1)} %copy-done.1, f32[4,128,128]{2,1,0:T(8,128)S(1)} %copy.111, f32[4,4]{0,1:T(4,128)S(1)} %copy-done.30, f32[4,4]{1,0:T(4,128)S(1)} %copy-done.29, f32[4,4]{0,1:T(4,128)S(1)} %copy.104, f32[4,4]{0,1:T(4,128)S(1)} %copy.103, f32[4,4]{0,1:T(4,128)S(1)} %copy.102), kind=kOutput, calls=%fused_computation.26 | convolution fusion | flops 13369600 | bytes 1835328 | tf_op jit(solution)/shard_map/nmh,mhde->nhde/dot_general | solution.py:94
  81.9 13.3 %psum.7 = f32[2,4,128]{2,1,0:T(4,128)S(1)} all-reduce(f32[2,4,128]{2,1,0:T(4,128)S(1)} %pad_maximum_fusion.10), channel_id=1, replica_groups=mesh['seq'=32,'head'=8] {'head'}, use_global_device_ids=true, to_apply=%region_5.6 | all-reduce | flops 1024 | bytes 8192 | tf_op jit(solution)/shard_map/psum | solution.py:111
  97.1 2.4 %fusion.17 = f32[4,1,128,128]{3,1,2,0:T(1,128)S(1)} fusion(f32[4,4,1,1]{0,2,3,1:T(1,128)S(1)} %copy.154, f32[4,4,128,128]{3,2,1,0:T(8,128)S(1)} %fusion.24), kind=kOutput, calls=%fused_computation.35 | convolution fusion | flops 3145728 | bytes 1310784 | tf_op jit(solution)/shard_map/mh,mhde->hde/dot_general | solution.py:145
  99.8 4.1 %collective-permute-start.5 = (f32[4,129,128]{2,0,1:T(4,128)S(1)}, f32[4,129,128]{2,0,1:T(4,128)S(1)}, u32[]{:S(2)}, u32[]{:S(2)}) collective-permute-start(f32[4,129,128]{2,0,1:T(4,128)S(1)} %pad_maximum_fusion), channel_id=1, source_target_pairs={{8,0},{16,8},{24,16},{32,24},{40,32},{48,40},{56,48},{64,56},{72,6... | collective-permute-start | bytes 792584 | tf_op jit(solution)/shard_map/ppermute | solution.py:47
  105.3 9.2 %collective-permute-done.5 = f32[4,129,128]{2,0,1:T(4,128)S(1)} collective-permute-done((f32[4,129,128]{2,0,1:T(4,128)S(1)}, f32[4,129,128]{2,0,1:T(4,128)S(1)}, u32[]{:S(2)}, u32[]{:S(2)}) %collective-permute-start.5) | collective-permute-done | bytes 264224 | tf_op jit(solution)/shard_map/ppermute | solution.py:47
  117.8 1.9 %collective-permute-start.6 = (f32[4,129,128]{2,0,1:T(4,128)S(1)}, f32[4,129,128]{2,0,1:T(4,128)S(1)}, u32[]{:S(2)}, u32[]{:S(2)}) collective-permute-start(f32[4,129,128]{2,0,1:T(4,128)S(1)} %pad_maximum_fusion.6), channel_id=1, source_target_pairs={{16,0},{24,8},{32,16},{40,24},{48,32},{56,40},{64,48},{72,56},{80,... | collective-permute-start | bytes 792584 | tf_op jit(solution)/shard_map/ppermute | solution.py:47
  121.3 7.7 %collective-permute-done.6 = f32[4,129,128]{2,0,1:T(4,128)S(1)} collective-permute-done((f32[4,129,128]{2,0,1:T(4,128)S(1)}, f32[4,129,128]{2,0,1:T(4,128)S(1)}, u32[]{:S(2)}, u32[]{:S(2)}) %collective-permute-start.6) | collective-permute-done | bytes 264224 | tf_op jit(solution)/shard_map/ppermute | solution.py:47
  131.8 1.9 %collective-permute-start.7 = (f32[4,129,128]{2,0,1:T(4,128)}, f32[4,129,128]{2,0,1:T(4,128)S(1)}, u32[]{:S(2)}, u32[]{:S(2)}) collective-permute-start(f32[4,129,128]{2,0,1:T(4,128)} %pad_maximum_fusion.7), channel_id=1, source_target_pairs={{32,0},{40,8},{48,16},{56,24},{64,32},{72,40},{80,48},{88,56},{96,... | collective-permute-start | bytes 792584 | tf_op jit(solution)/shard_map/ppermute | solution.py:47
  133.7 2.1 %fusion.10 = bf16[4,128,4,128]{1,3,2,0:T(8,128)(2,1)} fusion(f32[4,128,4,128]{1,3,2,0:T(8,128)S(1)} %copy-done.4, bf16[4,128,4,128]{1,3,2,0:T(8,128)(2,1)S(1)} %multiply_convert_fusion.1, f32[4,128,4]{1,2,0:T(4,128)S(1)} %copy.96, bf16[4,4,128,128]{3,0,2,1:T(4,128)(2,1)} %copy-done.8), kind=kOutput, calls=%fused_computation.22 | convolution fusion | flops 67895296 | bytes 2629632 | tf_op jit(solution)/shard_map/nihe,nhde->nihd/dot_general | solution.py:126
  135.9 2.1 %copy.122 = bf16[4,128,4,128]{3,2,1,0:T(4,128)(2,1)} copy(bf16[4,128,4,128]{1,3,2,0:T(8,128)(2,1)} %fusion.10) | data formatting | bytes 1048576 | tf_op jit(solution)/shard_map/convert_element_type | solution.py:159
  138.0 1.9 %copy.212 = bf16[64,8,4,128]{3,1,2,0:T(8,128)(2,1)} copy(bf16[64,8,4,128]{3,2,1,0:T(4,128)(2,1)} %bitcast.180) | data formatting | bytes 1048576
  144.8 12.1 %collective-permute-done.8 = f32[4,129,128]{2,0,1:T(4,128)S(1)} collective-permute-done((f32[4,129,128]{2,0,1:T(4,128)S(1)}, f32[4,129,128]{2,0,1:T(4,128)S(1)}, u32[]{:S(2)}, u32[]{:S(2)}) %collective-permute-start.8) | collective-permute-done | bytes 264224 | tf_op jit(solution)/shard_map/ppermute | solution.py:47
  161.9 16.8 %collective-permute-done.9 = f32[4,129,128]{2,0,1:T(4,128)S(1)} collective-permute-done((f32[4,129,128]{2,0,1:T(4,128)S(1)}, f32[4,129,128]{2,0,1:T(4,128)S(1)}, u32[]{:S(2)}, u32[]{:S(2)}) %collective-permute-start.9) | collective-permute-done | bytes 264224 | tf_op jit(solution)/shard_map/ppermute | solution.py:47
  179.0 2.6 %fusion.16 = bf16[4,4,128,128]{3,0,2,1:T(4,128)(2,1)S(1)} fusion(f32[4,4,128,128]{3,2,1,0:T(8,128)S(1)} %fusion.24, f32[4,128,128]{2,1,0:T(8,128)S(1)} %copy.134, f32[4,4]{0,1:T(4,128)S(1)} %copy.129, f32[4,4]{1,0:T(4,128)S(1)} %fusion.68, f32[4,4]{0,1:T(4,128)S(1)} %copy.104, f32[4,4]{0,1:T(4,128)S(1)} %copy.103, f32[4,4]{0,1:T(4,128)S(1)} %copy.102), kind=kOutput, calls=%fused_computation.28 | convolution fusion | flops 13369600 | bytes 1835328 | tf_op jit(solution)/shard_map/nmh,mhde->nhde/dot_general | solution.py:144
  (178 shorter events, 49.7 us)
Async XLA Ops:
  4.9 2.7 %copy-start = (f32[4,4,128,128]{3,2,1,0:T(8,128)}, f32[4,4,128,128]{3,2,1,0:T(8,128)S(1)}, u32[]{:S(2)}) copy-start(f32[4,4,128,128]{3,2,1,0:T(8,128)S(1)} %fusion.23) | copy-start | bytes 3145732
  7.7 9.1 %collective-permute-start = (f32[4,129,128]{2,0,1:T(4,128)S(1)}, f32[4,129,128]{2,0,1:T(4,128)S(1)}, u32[]{:S(2)}, u32[]{:S(2)}) collective-permute-start(f32[4,129,128]{2,0,1:T(4,128)S(1)} %pad_maximum_fusion.1), channel_id=1, source_target_pairs={{0,8},{8,16},{16,24},{24,32},{32,40},{40,48},{48,56},{56,64},{64,7... | collective-permute-start | bytes 792584 | tf_op jit(solution)/shard_map/ppermute | solution.py:31
  11.1 5.8 %copy-start.33 = (f32[4]{0:T(128)}, f32[4]{0:T(128)S(1)}, u32[]{:S(2)}) copy-start(f32[4]{0:T(128)S(1)} %exp.111) | copy-start | bytes 52
  17.2 9.8 %collective-permute-start.1 = (f32[4,129,128]{2,0,1:T(4,128)S(1)}, f32[4,129,128]{2,0,1:T(4,128)S(1)}, u32[]{:S(2)}, u32[]{:S(2)}) collective-permute-start(f32[4,129,128]{2,0,1:T(4,128)S(1)} %pad_maximum_fusion.2), channel_id=1, source_target_pairs={{0,16},{8,24},{16,32},{24,40},{32,48},{40,56},{48,64},{56,72},{64,... | collective-permute-start | bytes 792584 | tf_op jit(solution)/shard_map/ppermute | solution.py:31
  27.8 6.1 %copy-start.28 = (bf16[512,512]{1,0:T(8,128)(2,1)S(1)}, bf16[512,512]{1,0:T(8,128)(2,1)}, u32[]{:S(2)}) copy-start(bf16[512,512]{1,0:T(8,128)(2,1)} %param.5) | copy-start | bytes 1572868
  28.6 9.4 %collective-permute-start.2 = (f32[4,129,128]{2,0,1:T(4,128)}, f32[4,129,128]{2,0,1:T(4,128)}, u32[]{:S(2)}, u32[]{:S(2)}) collective-permute-start(f32[4,129,128]{2,0,1:T(4,128)} %pad_maximum_fusion.3), channel_id=1, source_target_pairs={{0,32},{8,40},{16,48},{24,56},{32,64},{40,72},{48,80},{56,88},{64,... | collective-permute-start | bytes 792584 | tf_op jit(solution)/shard_map/ppermute | solution.py:31
  41.2 16.6 %collective-permute-start.3 = (f32[4,129,128]{2,0,1:T(4,128)S(1)}, f32[4,129,128]{2,0,1:T(4,128)S(1)}, u32[]{:S(2)}, u32[]{:S(2)}) collective-permute-start(f32[4,129,128]{2,0,1:T(4,128)S(1)} %pad_maximum_fusion.4), channel_id=1, source_target_pairs={{0,64},{8,72},{16,80},{24,88},{32,96},{40,104},{48,112},{56,120},{... | collective-permute-start | bytes 792584 | tf_op jit(solution)/shard_map/ppermute | solution.py:31
  59.2 7.5 %copy-start.9 = (bf16[4,4,128,128]{3,2,1,0:T(8,128)(2,1)S(1)}, bf16[4,4,128,128]{3,2,1,0:T(8,128)(2,1)}, u32[]{:S(2)}) copy-start(bf16[4,4,128,128]{3,2,1,0:T(8,128)(2,1)} %fusion.13) | copy-start | bytes 1572868
  60.5 15.3 %copy-start.16 = (f32[4,129,128]{2,0,1:T(4,128)S(1)}, f32[4,129,128]{2,0,1:T(4,128)}, u32[]{:S(2)}) copy-start(f32[4,129,128]{2,0,1:T(4,128)} %copy-done.15) | copy-start | bytes 792580
  60.5 15.3 %copy-start.24 = (f32[4,129,128]{2,0,1:T(4,128)S(1)}, f32[4,129,128]{2,0,1:T(4,128)}, u32[]{:S(2)}) copy-start(f32[4,129,128]{2,0,1:T(4,128)} %copy-done.23) | copy-start | bytes 792580
  60.5 15.2 %collective-permute-start.4 = (f32[4,129,128]{2,0,1:T(4,128)S(1)}, f32[4,129,128]{2,0,1:T(4,128)S(1)}, u32[]{:S(2)}, u32[]{:S(2)}) collective-permute-start(f32[4,129,128]{2,0,1:T(4,128)S(1)} %pad_maximum_fusion.5), channel_id=1, source_target_pairs={{0,128},{8,136},{16,144},{24,152},{32,160},{40,168},{48,176},{56,1... | collective-permute-start | bytes 792584 | tf_op jit(solution)/shard_map/ppermute | solution.py:31
  99.8 14.7 %collective-permute-start.5 = (f32[4,129,128]{2,0,1:T(4,128)S(1)}, f32[4,129,128]{2,0,1:T(4,128)S(1)}, u32[]{:S(2)}, u32[]{:S(2)}) collective-permute-start(f32[4,129,128]{2,0,1:T(4,128)S(1)} %pad_maximum_fusion), channel_id=1, source_target_pairs={{8,0},{16,8},{24,16},{32,24},{40,32},{48,40},{56,48},{64,56},{72,6... | collective-permute-start | bytes 792584 | tf_op jit(solution)/shard_map/ppermute | solution.py:47
  115.9 3.8 %copy-start.11 = (bf16[4,4,128,128]{3,2,1,0:T(8,128)(2,1)S(1)}, bf16[4,4,128,128]{3,2,1,0:T(8,128)(2,1)}, u32[]{:S(2)}) copy-start(bf16[4,4,128,128]{3,2,1,0:T(8,128)(2,1)} %fusion.15) | copy-start | bytes 1572868
  117.8 11.1 %collective-permute-start.6 = (f32[4,129,128]{2,0,1:T(4,128)S(1)}, f32[4,129,128]{2,0,1:T(4,128)S(1)}, u32[]{:S(2)}, u32[]{:S(2)}) collective-permute-start(f32[4,129,128]{2,0,1:T(4,128)S(1)} %pad_maximum_fusion.6), channel_id=1, source_target_pairs={{16,0},{24,8},{32,16},{40,24},{48,32},{56,40},{64,48},{72,56},{80,... | collective-permute-start | bytes 792584 | tf_op jit(solution)/shard_map/ppermute | solution.py:47
  119.8 10.0 %copy-start.7 = (f32[4,128,128]{2,0,1:T(4,128)S(1)}, f32[4,128,128]{2,0,1:T(4,128)}, u32[]{:S(2)}) copy-start(f32[4,128,128]{2,0,1:T(4,128)} %copy-done.6) | copy-start | bytes 786436
  129.8 3.9 %copy-start.4 = (f32[4,128,4,128]{1,3,2,0:T(8,128)S(1)}, f32[4,128,4,128]{1,3,2,0:T(8,128)}, u32[]{:S(2)}) copy-start(f32[4,128,4,128]{1,3,2,0:T(8,128)} %convolution_bitcast_fusion.6) | copy-start | bytes 3145732
  131.8 8.1 %collective-permute-start.7 = (f32[4,129,128]{2,0,1:T(4,128)}, f32[4,129,128]{2,0,1:T(4,128)S(1)}, u32[]{:S(2)}, u32[]{:S(2)}) collective-permute-start(f32[4,129,128]{2,0,1:T(4,128)} %pad_maximum_fusion.7), channel_id=1, source_target_pairs={{32,0},{40,8},{48,16},{56,24},{64,32},{72,40},{80,48},{88,56},{96,... | collective-permute-start | bytes 792584 | tf_op jit(solution)/shard_map/ppermute | solution.py:47
  142.0 14.9 %collective-permute-start.8 = (f32[4,129,128]{2,0,1:T(4,128)S(1)}, f32[4,129,128]{2,0,1:T(4,128)S(1)}, u32[]{:S(2)}, u32[]{:S(2)}) collective-permute-start(f32[4,129,128]{2,0,1:T(4,128)S(1)} %pad_maximum_fusion.8), channel_id=1, source_target_pairs={{64,0},{72,8},{80,16},{88,24},{96,32},{104,40},{112,48},{120,56},{... | collective-permute-start | bytes 792584 | tf_op jit(solution)/shard_map/ppermute | solution.py:47
  157.7 2.8 %copy-start.10 = (bf16[4,4,128,128]{3,2,1,0:T(8,128)(2,1)S(1)}, bf16[4,4,128,128]{3,2,1,0:T(8,128)(2,1)}, u32[]{:S(2)}) copy-start(bf16[4,4,128,128]{3,2,1,0:T(8,128)(2,1)} %fusion.13) | copy-start | bytes 1572868
  158.9 19.8 %copy-start.14 = (f32[4,129,128]{2,0,1:T(4,128)S(1)}, f32[4,129,128]{2,0,1:T(4,128)}, u32[]{:S(2)}) copy-start(f32[4,129,128]{2,0,1:T(4,128)} %copy-done.13) | copy-start | bytes 792580
  159.0 19.8 %copy-start.18 = (f32[4,129,128]{2,0,1:T(4,128)S(1)}, f32[4,129,128]{2,0,1:T(4,128)}, u32[]{:S(2)}) copy-start(f32[4,129,128]{2,0,1:T(4,128)} %copy-done.17) | copy-start | bytes 792580
  159.0 19.8 %copy-start.20 = (f32[4,129,128]{2,0,1:T(4,128)S(1)}, f32[4,129,128]{2,0,1:T(4,128)}, u32[]{:S(2)}) copy-start(f32[4,129,128]{2,0,1:T(4,128)} %copy-done.19) | copy-start | bytes 792580
  159.0 19.8 %copy-start.22 = (f32[4,129,128]{2,0,1:T(4,128)S(1)}, f32[4,129,128]{2,0,1:T(4,128)}, u32[]{:S(2)}) copy-start(f32[4,129,128]{2,0,1:T(4,128)} %copy-done.21) | copy-start | bytes 792580
  159.0 19.8 %collective-permute-start.9 = (f32[4,129,128]{2,0,1:T(4,128)S(1)}, f32[4,129,128]{2,0,1:T(4,128)S(1)}, u32[]{:S(2)}, u32[]{:S(2)}) collective-permute-start(f32[4,129,128]{2,0,1:T(4,128)S(1)} %pad_maximum_fusion.9), channel_id=1, source_target_pairs={{128,0},{136,8},{144,16},{152,24},{160,32},{168,40},{176,48},{184,... | collective-permute-start | bytes 792584 | tf_op jit(solution)/shard_map/ppermute | solution.py:47
  (21 other events, 20.1 us)

commit v2 on v1

--- a/solution.py
+++ b/solution.py
@@ -1,11 +1,12 @@
 import jax
 import jax.numpy as jnp
 from jax import lax
-from jax.sharding import PartitionSpec as P
+from jax.sharding import Mesh, PartitionSpec as P
 
 HEAD_COUNT = 32
 DH = 128
 BLOCK = 128
+ROW = 4
 
 
 epsilon = 1e-06
@@ -22,13 +23,13 @@
     return payload[:, rows, 0], payload[:, :rows, :]
 
 
-def forward_scan(total, state, ranks):
+def forward_scan(total, state, axis, ranks):
     win_a, win_b = total, state
     excl_a, excl_b = jnp.zeros_like(total), jnp.zeros_like(state)
     shift = 1
     while shift < ranks:
         pairs = [(i, i + shift) for i in range(ranks - shift)]
-        got_a, got_b = unpack(lax.ppermute(pack(win_a, win_b), "seq", pairs))
+        got_a, got_b = unpack(lax.ppermute(pack(win_a, win_b), axis, pairs))
         excl_b = jnp.exp(excl_a)[:, None, None] * got_b + excl_b
         excl_a = excl_a + got_a
         if 2 * shift < ranks:
@@ -38,13 +39,13 @@
     return excl_b
 
 
-def backward_scan(total, state, ranks):
+def backward_scan(total, state, axis, ranks):
     win_a, win_c = total, state
     excl_a, excl_c = jnp.zeros_like(total), jnp.zeros_like(state)
     shift = 1
     while shift < ranks:
         pairs = [(i + shift, i) for i in range(ranks - shift)]
-        got_a, got_c = unpack(lax.ppermute(pack(win_a, win_c), "seq", pairs))
+        got_a, got_c = unpack(lax.ppermute(pack(win_a, win_c), axis, pairs))
         excl_c = excl_c + jnp.exp(excl_a)[:, None, None] * got_c
         excl_a = excl_a + got_a
         if 2 * shift < ranks:
@@ -54,7 +55,60 @@
     return excl_c
 
 
-def shards(queries, key_rows, value_rows, out_grad, log_decay, seq_ranks):
+def exchange(payload, axis, ranks):
+    me = lax.axis_index(axis)
+    got = [lax.dynamic_index_in_dim(payload, me, 0, keepdims=False)]
+    for shift in range(1, ranks):
+        send = lax.dynamic_index_in_dim(payload, (me + shift) % ranks, 0, keepdims=False)
+        pairs = [(i, (i + shift) % ranks) for i in range(ranks)]
+        got.append(lax.ppermute(send, axis, pairs))
+    stacked = jnp.stack(got)
+    order = (me - jnp.arange(ranks)) % ranks
+    return jnp.take(stacked, order, axis=0)
+
+
+def incoming_states(shard_total, shard_state, row_ranks, col_ranks):
+    parts = exchange(pack(shard_total, shard_state), "sx", row_ranks)
+    part_a, part_b = parts[:, -1, 0], parts[:, :-1, :]
+    run_a = jnp.zeros((), jnp.float32)
+    run_b = jnp.zeros_like(part_b[0])
+    row_a, row_b = [], []
+    for pos in range(row_ranks):
+        row_a.append(run_a)
+        row_b.append(run_b)
+        run_b = jnp.exp(part_a[pos]) * run_b + part_b[pos]
+        run_a = run_a + part_a[pos]
+    before_row = forward_scan(run_a[None], run_b[None], "sz", col_ranks)[0]
+    result = jnp.stack(
+        [jnp.exp(row_a[pos]) * before_row + row_b[pos] for pos in range(row_ranks)]
+    )
+    return exchange(result, "sx", row_ranks)
+
+
+def outgoing_states(shard_total, shard_back, row_ranks, col_ranks):
+    parts = exchange(pack(shard_total, shard_back), "sx", row_ranks)
+    part_a, part_c = parts[:, -1, 0], parts[:, :-1, :]
+    run_a = jnp.zeros((), jnp.float32)
+    run_c = jnp.zeros_like(part_c[0])
+    row_a, row_c = [None] * row_ranks, [None] * row_ranks
+    for pos in reversed(range(row_ranks)):
+        row_a[pos] = run_a
+        row_c[pos] = run_c
+        run_c = part_c[pos] + jnp.exp(part_a[pos]) * run_c
+        run_a = run_a + part_a[pos]
+    after_row = backward_scan(run_a[None], run_c[None], "sz", col_ranks)[0]
+    result = jnp.stack(
+        [row_c[pos] + jnp.exp(row_a[pos]) * after_row for pos in range(row_ranks)]
+    )
+    return exchange(result, "sx", row_ranks)
+
+
+def head_sum(values, ranks):
+    gathered = exchange(jnp.broadcast_to(values[None], (ranks,) + values.shape), "head", ranks)
+    return jnp.sum(gathered, axis=0)
+
+
+def shards(queries, key_rows, value_rows, out_grad, log_decay, row_ranks, col_ranks, head_ranks):
     tok_rows, row_width = queries.shape
     heads_dev = log_decay.shape[0]
     head_size = row_width // heads_dev
@@ -98,7 +152,7 @@
         block_terms,
         precision=highest,
     )
-    incoming = forward_scan(shard_total, shard_state, seq_ranks)
+    incoming = incoming_states(shard_total, shard_state, row_ranks, col_ranks)
     states = local_states + jnp.exp(before)[:, :, None, None] * incoming[None]
     backward_state = states.astype(jnp.bfloat16)
     inter_out = jnp.einsum(
@@ -108,7 +162,7 @@
     grad_f32 = grad_blocks.astype(jnp.float32)
     square = jnp.sum(attention_output * attention_output, axis=(2, 3))
     cross_raw = jnp.sum(grad_f32 * attention_output, axis=(2, 3))
-    stats = lax.psum(jnp.stack([square, cross_raw]), "head")
+    stats = head_sum(jnp.stack([square, cross_raw]), head_ranks)
     inv_rms = lax.rsqrt(stats[0] / total_width + epsilon)
     mean_cross = inv_rms * stats[1] / total_width
     normed = attention_output * inv_rms[:, :, None, None]
@@ -143,7 +197,7 @@
     backward_mix = jnp.exp(jnp.minimum(backward_exp, 0.0)) * later_blocks[:, :, None]
     local_back = jnp.einsum("nmh,mhde->nhde", backward_mix, backward_terms, precision=highest)
     shard_back = jnp.einsum("mh,mhde->hde", jnp.exp(before), backward_terms, precision=highest)
-    later_state = backward_scan(shard_total, shard_back, seq_ranks)
+    later_state = outgoing_states(shard_total, shard_back, row_ranks, col_ranks)
     back_states = (
         local_back
         + jnp.exp(shard_total[None, :] - before - totals)[:, :, None, None] * later_state[None]
@@ -164,20 +218,21 @@
 
 def solution(mesh):
     seq_ranks = mesh.shape["seq"]
+    head_ranks = mesh.shape["head"]
+    row_ranks = ROW if seq_ranks % ROW == 0 else 1
+    col_ranks = seq_ranks // row_ranks
+    grid = Mesh(mesh.devices.reshape(col_ranks, row_ranks, head_ranks), ("sz", "sx", "head"))
 
     def body(queries, key_rows, value_rows, out_grad, log_decay):
-        return shards(queries, key_rows, value_rows, out_grad, log_decay, seq_ranks)
-
+        return shards(
+            queries, key_rows, value_rows, out_grad, log_decay, row_ranks, col_ranks, head_ranks
+        )
+
+    rows = P(("sz", "sx"), "head")
     return jax.shard_map(
         body,
-        mesh=mesh,
-        in_specs=(
-            P("seq", "head"),
-            P("seq", "head"),
-            P("seq", "head"),
-            P("seq", "head"),
-            P("head", "seq"),
-        ),
-        out_specs=(P("seq", "head"), P("seq", "head"), P("seq", "head")),
+        mesh=grid,
+        in_specs=(rows, rows, rows, rows, P("head", ("sz", "sx"))),
+        out_specs=(rows, rows, rows),
         check_vma=False,
     )

time: 188 us -> 148 us (0.79)
  the two profiles are of different devices: /device:TPU:39 before, /device:TPU:32 now
where the time goes in v2:
time: 148 us; the launch traced here: 147 us
  starting transfers between devices  50.9 us (34%)
  waiting for transfers between devices  29.3 us (20%)
  matrix products  23.1 us (16%)
  local copies, waits for them, and re-layouts  20.2 us (14%)
  between operations  18.4 us (12%)
  other arithmetic  4.59 us (3%)
    ppermute x19, starting transfers between devices, exchange(): got.append(lax.ppermute(send, axis, pairs))  26.1 us
    ppermute x3, starting transfers between devices, forward_scan(): got_a, got_b = unpack(lax.ppermute(pack(win_a, win_b), axis, pairs))  18.4 us
    ppermute x3, waiting for transfers between devices, backward_scan(): got_a, got_c = unpack(lax.ppermute(pack(win_a, win_c), axis, pairs))  14.5 us
    ppermute x19, waiting for transfers between devices, exchange(): got.append(lax.ppermute(send, axis, pairs))  10.2 us
    ppermute x3, starting transfers between devices, backward_scan(): got_a, got_c = unpack(lax.ppermute(pack(win_a, win_c), axis, pairs))  6.41 us
    unnamed x37, local copies, waits for them, and re-layouts  5.87 us
    ppermute x3, waiting for transfers between devices, forward_scan(): got_a, got_b = unpack(lax.ppermute(pack(win_a, win_b), axis, pairs))  4.64 us
    dot_general x1, matrix products, shards(): jnp.einsum('nmh,mhde->nhde', forward_mix, block_terms, precision=highest)  4.02 us
  transfers between devices with their start and end apart: 25, of which 15 were waited for; matrix products, arithmetic and copies ran while one was open for 9% of the time, Pallas kernels for 0%

profile of v2, /device:TPU:32, one launch (start us, length us, event | category | flops | bytes accessed | tf_op | source)
XLA Modules:
  0.0 146.5 jit_solution(12126061870762597974)
XLA Ops:
  6.0 2.4 %fusion.20 = f32[4,1,128,128]{3,1,2,0:T(1,128)S(1)} fusion(f32[4,4,1,1]{0,2,3,1:T(1,128)S(1)} %copy.177, f32[4,4,128,128]{3,2,1,0:T(8,128)S(1)} %fusion.23), kind=kOutput, calls=%fused_computation.43 | convolution fusion | flops 3145728 | bytes 1310784 | tf_op jit(solution)/shard_map/mh,mhde->hde/dot_general | solution.py:149
  10.0 2.7 %collective-permute-start.1 = (f32[129,128]{1,0:T(8,128)S(1)}, f32[129,128]{1,0:T(8,128)S(1)}, u32[]{:S(2)}, u32[]{:S(2)}) collective-permute-start(f32[129,128]{1,0:T(8,128)S(1)} %get-tuple-element.30), channel_id=1, source_target_pairs={{0,16},{8,24},{16,0},{24,8},{1,17},{9,25},{17,1},{25,9},{2,18},{10... | collective-permute-start | bytes 198152 | tf_op jit(solution)/shard_map/ppermute | solution.py:64
  27.1 3.8 %collective-permute-start.3 = (f32[1,129,128]{2,1,0:T(8,128)S(1)}, f32[1,129,128]{2,1,0:T(8,128)S(1)}, u32[]{:S(2)}, u32[]{:S(2)}) collective-permute-start(f32[1,129,128]{2,1,0:T(8,128)S(1)} %concatenate.25), channel_id=1, source_target_pairs={{0,32},{32,64},{64,96},{96,128},{128,160},{160,192},{192,224},{1,3... | collective-permute-start | bytes 198152 | tf_op jit(solution)/shard_map/ppermute | solution.py:32
  31.0 2.3 %collective-permute-done.3 = f32[1,129,128]{2,1,0:T(8,128)S(1)} collective-permute-done((f32[1,129,128]{2,1,0:T(8,128)S(1)}, f32[1,129,128]{2,1,0:T(8,128)S(1)}, u32[]{:S(2)}, u32[]{:S(2)}) %collective-permute-start.3) | collective-permute-done | bytes 66080 | tf_op jit(solution)/shard_map/ppermute | solution.py:32
  34.7 5.9 %collective-permute-start.4 = (f32[1,129,128]{2,1,0:T(8,128)S(1)}, f32[1,129,128]{2,1,0:T(8,128)S(1)}, u32[]{:S(2)}, u32[]{:S(2)}) collective-permute-start(f32[1,129,128]{2,1,0:T(8,128)S(1)} %concatenate.26), channel_id=1, source_target_pairs={{0,64},{32,96},{64,128},{96,160},{128,192},{160,224},{1,65},{33,97... | collective-permute-start | bytes 198152 | tf_op jit(solution)/shard_map/ppermute | solution.py:32
  40.7 1.9 %collective-permute-done.4 = f32[1,129,128]{2,1,0:T(8,128)S(1)} collective-permute-done((f32[1,129,128]{2,1,0:T(8,128)S(1)}, f32[1,129,128]{2,1,0:T(8,128)S(1)}, u32[]{:S(2)}, u32[]{:S(2)}) %collective-permute-start.4) | collective-permute-done | bytes 66080 | tf_op jit(solution)/shard_map/ppermute | solution.py:32
  43.7 8.6 %collective-permute-start.5 = (f32[1,129,128]{2,1,0:T(8,128)S(1)}, f32[1,129,128]{2,1,0:T(8,128)S(1)}, u32[]{:S(2)}, u32[]{:S(2)}) collective-permute-start(f32[1,129,128]{2,1,0:T(8,128)S(1)} %concatenate.27), channel_id=1, source_target_pairs={{0,128},{32,160},{64,192},{96,224},{1,129},{33,161},{65,193},{97,2... | collective-permute-start | bytes 198152 | tf_op jit(solution)/shard_map/ppermute | solution.py:32
  56.6 1.9 %collective-permute-start.8 = (f32[128,128]{1,0:T(8,128)S(1)}, f32[128,128]{1,0:T(8,128)S(1)}, u32[]{:S(2)}, u32[]{:S(2)}) collective-permute-start(f32[128,128]{1,0:T(8,128)S(1)} %get-tuple-element.40), channel_id=1, source_target_pairs={{0,24},{8,0},{16,8},{24,16},{1,25},{9,1},{17,9},{25,17},{2,26},{10... | collective-permute-start | bytes 196616 | tf_op jit(solution)/shard_map/ppermute | solution.py:64
  58.5 2.1 %collective-permute-done.6 = f32[128,128]{1,0:T(8,128)S(1)} collective-permute-done((f32[128,128]{1,0:T(8,128)S(1)}, f32[128,128]{1,0:T(8,128)S(1)}, u32[]{:S(2)}, u32[]{:S(2)}) %collective-permute-start.6) | collective-permute-done | bytes 65568 | tf_op jit(solution)/shard_map/ppermute | solution.py:64
  62.8 4.0 %fusion.14 = bf16[4,4,128,128]{3,0,2,1:T(4,128)(2,1)S(1)} fusion(f32[4,4,128,128]{3,2,1,0:T(8,128)} %copy-done.1, f32[4,128,128]{2,1,0:T(8,128)S(1)} %broadcast_select_fusion.3, f32[4,4]{0,1:T(4,128)S(1)} %copy.146, f32[4,4]{1,0:T(4,128)S(1)} %fusion.81, f32[4,4]{0,1:T(4,128)S(1)} %copy.144, f32[4,4]{0,1:T(4,128)S(1)} %copy.143, f32[4,4]{0,1:T(4,128)S(1)} %copy.142), kind=kOutput, calls=%fused_computation.31 | convolution fusion | flops 13369600 | bytes 1835328 | tf_op jit(solution)/shard_map/nmh,mhde->nhde/dot_general | solution.py:148
  68.4 1.7 %collective-permute-start.10 = (f32[2,4,128]{2,1,0:T(4,128)S(1)}, f32[2,4,128]{2,1,0:T(4,128)S(1)}, u32[]{:S(2)}, u32[]{:S(2)}) collective-permute-start(f32[2,4,128]{2,1,0:T(4,128)S(1)} %pad_maximum_fusion.6), channel_id=1, source_target_pairs={{0,2},{1,3},{2,4},{3,5},{4,6},{5,7},{6,0},{7,1},{8,10},{9,11},{10,... | collective-permute-start | bytes 12296 | tf_op jit(solution)/shard_map/ppermute | solution.py:64
  70.0 2.2 %collective-permute-start.11 = (f32[2,4,128]{2,1,0:T(4,128)S(1)}, f32[2,4,128]{2,1,0:T(4,128)S(1)}, u32[]{:S(2)}, u32[]{:S(2)}) collective-permute-start(f32[2,4,128]{2,1,0:T(4,128)S(1)} %pad_maximum_fusion.6), channel_id=1, source_target_pairs={{0,3},{1,4},{2,5},{3,6},{4,7},{5,0},{6,1},{7,2},{8,11},{9,12},{10,... | collective-permute-start | bytes 12296 | tf_op jit(solution)/shard_map/ppermute | solution.py:64
  72.2 1.8 %collective-permute-start.12 = (f32[2,4,128]{2,1,0:T(4,128)S(1)}, f32[2,4,128]{2,1,0:T(4,128)S(1)}, u32[]{:S(2)}, u32[]{:S(2)}) collective-permute-start(f32[2,4,128]{2,1,0:T(4,128)S(1)} %pad_maximum_fusion.6), channel_id=1, source_target_pairs={{0,4},{1,5},{2,6},{3,7},{4,0},{5,1},{6,2},{7,3},{8,12},{9,13},{10,... | collective-permute-start | bytes 12296 | tf_op jit(solution)/shard_map/ppermute | solution.py:64
  74.1 1.8 %collective-permute-start.13 = (f32[2,4,128]{2,1,0:T(4,128)S(1)}, f32[2,4,128]{2,1,0:T(4,128)S(1)}, u32[]{:S(2)}, u32[]{:S(2)}) collective-permute-start(f32[2,4,128]{2,1,0:T(4,128)S(1)} %pad_maximum_fusion.6), channel_id=1, source_target_pairs={{0,5},{1,6},{2,7},{3,0},{4,1},{5,2},{6,3},{7,4},{8,13},{9,14},{10,... | collective-permute-start | bytes 12296 | tf_op jit(solution)/shard_map/ppermute | solution.py:64
  77.3 2.2 %collective-permute-done.14 = f32[2,4,128]{2,1,0:T(4,128)S(1)} collective-permute-done((f32[2,4,128]{2,1,0:T(4,128)S(1)}, f32[2,4,128]{2,1,0:T(4,128)S(1)}, u32[]{:S(2)}, u32[]{:S(2)}) %collective-permute-start.14) | collective-permute-done | bytes 4128 | tf_op jit(solution)/shard_map/ppermute | solution.py:64
  82.1 2.4 %fusion.17 = f32[4,1,128,128]{3,1,2,0:T(1,128)S(1)} fusion(f32[4,4,1,1]{0,2,3,1:T(1,128)S(1)} %copy.185, f32[4,4,128,128]{3,2,1,0:T(8,128)S(1)} %fusion.24), kind=kOutput, calls=%fused_computation.40 | convolution fusion | flops 3145728 | bytes 1310784 | tf_op jit(solution)/shard_map/mh,mhde->hde/dot_general | solution.py:199
  85.9 2.6 %collective-permute-start.17 = (f32[129,128]{1,0:T(8,128)S(1)}, f32[129,128]{1,0:T(8,128)S(1)}, u32[]{:S(2)}, u32[]{:S(2)}) collective-permute-start(f32[129,128]{1,0:T(8,128)S(1)} %get-tuple-element.27), channel_id=1, source_target_pairs={{0,16},{8,24},{16,0},{24,8},{1,17},{9,25},{17,1},{25,9},{2,18},{10... | collective-permute-start | bytes 198152 | tf_op jit(solution)/shard_map/ppermute | solution.py:64
  90.4 1.9 %collective-permute-done.17 = f32[129,128]{1,0:T(8,128)S(1)} collective-permute-done((f32[129,128]{1,0:T(8,128)S(1)}, f32[129,128]{1,0:T(8,128)S(1)}, u32[]{:S(2)}, u32[]{:S(2)}) %collective-permute-start.17) | collective-permute-done | bytes 66080 | tf_op jit(solution)/shard_map/ppermute | solution.py:64
  100.9 3.8 %collective-permute-start.19 = (f32[1,129,128]{2,1,0:T(8,128)S(1)}, f32[1,129,128]{2,1,0:T(8,128)S(1)}, u32[]{:S(2)}, u32[]{:S(2)}) collective-permute-start(f32[1,129,128]{2,1,0:T(8,128)S(1)} %concatenate.29), channel_id=1, source_target_pairs={{32,0},{64,32},{96,64},{128,96},{160,128},{192,160},{224,192},{33,... | collective-permute-start | bytes 198152 | tf_op jit(solution)/shard_map/ppermute | solution.py:48
  105.4 1.9 %collective-permute-done.19 = f32[1,129,128]{2,1,0:T(8,128)S(1)} collective-permute-done((f32[1,129,128]{2,1,0:T(8,128)S(1)}, f32[1,129,128]{2,1,0:T(8,128)S(1)}, u32[]{:S(2)}, u32[]{:S(2)}) %collective-permute-start.19) | collective-permute-done | bytes 66080 | tf_op jit(solution)/shard_map/ppermute | solution.py:48
  110.8 6.7 %collective-permute-done.20 = f32[1,129,128]{2,1,0:T(8,128)S(1)} collective-permute-done((f32[1,129,128]{2,1,0:T(8,128)S(1)}, f32[1,129,128]{2,1,0:T(8,128)S(1)}, u32[]{:S(2)}, u32[]{:S(2)}) %collective-permute-start.20) | collective-permute-done | bytes 66080 | tf_op jit(solution)/shard_map/ppermute | solution.py:48
  123.3 5.9 %collective-permute-done.21 = f32[1,129,128]{2,1,0:T(8,128)S(1)} collective-permute-done((f32[1,129,128]{2,1,0:T(8,128)S(1)}, f32[1,129,128]{2,1,0:T(8,128)S(1)}, u32[]{:S(2)}, u32[]{:S(2)}) %collective-permute-start.21) | collective-permute-done | bytes 66080 | tf_op jit(solution)/shard_map/ppermute | solution.py:48
  130.1 3.0 %collective-permute-start.23 = (f32[128,128]{1,0:T(8,128)S(1)}, f32[128,128]{1,0:T(8,128)}, u32[]{:S(2)}, u32[]{:S(2)}) collective-permute-start(f32[128,128]{1,0:T(8,128)S(1)} %get-tuple-element.35), channel_id=1, source_target_pairs={{0,16},{8,24},{16,0},{24,8},{1,17},{9,25},{17,1},{25,9},{2,18},{10... | collective-permute-start | bytes 196616 | tf_op jit(solution)/shard_map/ppermute | solution.py:64
  139.0 2.6 %fusion.16 = bf16[4,4,128,128]{3,0,2,1:T(4,128)(2,1)S(1)} fusion(f32[4,4,128,128]{3,2,1,0:T(8,128)S(1)} %fusion.24, f32[4,128,128]{2,1,0:T(8,128)S(1)} %broadcast_select_fusion.2, f32[4,4]{0,1:T(4,128)S(1)} %copy.165, f32[4,4]{1,0:T(4,128)S(1)} %fusion.82, f32[4,4]{0,1:T(4,128)S(1)} %copy.144, f32[4,4]{0,1:T(4,128)S(1)} %copy.143, f32[4,4]{0,1:T(4,128)S(1)} %copy.142), kind=kOutput, calls=%fused_computation.33 | convolution fusion | flops 13369600 | bytes 1835328 | tf_op jit(solution)/shard_map/nmh,mhde->nhde/dot_general | solution.py:198
  (166 shorter events, 52.0 us)
Async XLA Ops:
  8.5 12.0 %collective-permute-start = (f32[129,128]{1,0:T(8,128)S(1)}, f32[129,128]{1,0:T(8,128)S(1)}, u32[]{:S(2)}, u32[]{:S(2)}) collective-permute-start(f32[129,128]{1,0:T(8,128)S(1)} %get-tuple-element.31), channel_id=1, source_target_pairs={{0,8},{8,16},{16,24},{24,0},{1,9},{9,17},{17,25},{25,1},{2,10},{10... | collective-permute-start | bytes 198152 | tf_op jit(solution)/shard_map/ppermute | solution.py:64
  10.0 10.5 %collective-permute-start.1 = (f32[129,128]{1,0:T(8,128)S(1)}, f32[129,128]{1,0:T(8,128)S(1)}, u32[]{:S(2)}, u32[]{:S(2)}) collective-permute-start(f32[129,128]{1,0:T(8,128)S(1)} %get-tuple-element.30), channel_id=1, source_target_pairs={{0,16},{8,24},{16,0},{24,8},{1,17},{9,25},{17,1},{25,9},{2,18},{10... | collective-permute-start | bytes 198152 | tf_op jit(solution)/shard_map/ppermute | solution.py:64
  12.8 7.7 %collective-permute-start.2 = (f32[129,128]{1,0:T(8,128)S(1)}, f32[129,128]{1,0:T(8,128)S(1)}, u32[]{:S(2)}, u32[]{:S(2)}) collective-permute-start(f32[129,128]{1,0:T(8,128)S(1)} %get-tuple-element.32), channel_id=1, source_target_pairs={{0,24},{8,0},{16,8},{24,16},{1,25},{9,1},{17,9},{25,17},{2,26},{10... | collective-permute-start | bytes 198152 | tf_op jit(solution)/shard_map/ppermute | solution.py:64
  27.1 6.2 %collective-permute-start.3 = (f32[1,129,128]{2,1,0:T(8,128)S(1)}, f32[1,129,128]{2,1,0:T(8,128)S(1)}, u32[]{:S(2)}, u32[]{:S(2)}) collective-permute-start(f32[1,129,128]{2,1,0:T(8,128)S(1)} %concatenate.25), channel_id=1, source_target_pairs={{0,32},{32,64},{64,96},{96,128},{128,160},{160,192},{192,224},{1,3... | collective-permute-start | bytes 198152 | tf_op jit(solution)/shard_map/ppermute | solution.py:32
  34.7 7.9 %collective-permute-start.4 = (f32[1,129,128]{2,1,0:T(8,128)S(1)}, f32[1,129,128]{2,1,0:T(8,128)S(1)}, u32[]{:S(2)}, u32[]{:S(2)}) collective-permute-start(f32[1,129,128]{2,1,0:T(8,128)S(1)} %concatenate.26), channel_id=1, source_target_pairs={{0,64},{32,96},{64,128},{96,160},{128,192},{160,224},{1,65},{33,97... | collective-permute-start | bytes 198152 | tf_op jit(solution)/shard_map/ppermute | solution.py:32
  43.7 11.2 %collective-permute-start.5 = (f32[1,129,128]{2,1,0:T(8,128)S(1)}, f32[1,129,128]{2,1,0:T(8,128)S(1)}, u32[]{:S(2)}, u32[]{:S(2)}) collective-permute-start(f32[1,129,128]{2,1,0:T(8,128)S(1)} %concatenate.27), channel_id=1, source_target_pairs={{0,128},{32,160},{64,192},{96,224},{1,129},{33,161},{65,193},{97,2... | collective-permute-start | bytes 198152 | tf_op jit(solution)/shard_map/ppermute | solution.py:32
  55.0 5.6 %collective-permute-start.6 = (f32[128,128]{1,0:T(8,128)S(1)}, f32[128,128]{1,0:T(8,128)S(1)}, u32[]{:S(2)}, u32[]{:S(2)}) collective-permute-start(f32[128,128]{1,0:T(8,128)S(1)} %get-tuple-element.42), channel_id=1, source_target_pairs={{0,8},{8,16},{16,24},{24,0},{1,9},{9,17},{17,25},{25,1},{2,10},{10... | collective-permute-start | bytes 196616 | tf_op jit(solution)/shard_map/ppermute | solution.py:64
  55.7 5.8 %collective-permute-start.7 = (f32[128,128]{1,0:T(8,128)S(1)}, f32[128,128]{1,0:T(8,128)S(1)}, u32[]{:S(2)}, u32[]{:S(2)}) collective-permute-start(f32[128,128]{1,0:T(8,128)S(1)} %get-tuple-element.41), channel_id=1, source_target_pairs={{0,16},{8,24},{16,0},{24,8},{1,17},{9,25},{17,1},{25,9},{2,18},{10... | collective-permute-start | bytes 196616 | tf_op jit(solution)/shard_map/ppermute | solution.py:64
  56.6 5.6 %collective-permute-start.8 = (f32[128,128]{1,0:T(8,128)S(1)}, f32[128,128]{1,0:T(8,128)S(1)}, u32[]{:S(2)}, u32[]{:S(2)}) collective-permute-start(f32[128,128]{1,0:T(8,128)S(1)} %get-tuple-element.40), channel_id=1, source_target_pairs={{0,24},{8,0},{16,8},{24,16},{1,25},{9,1},{17,9},{25,17},{2,26},{10... | collective-permute-start | bytes 196616 | tf_op jit(solution)/shard_map/ppermute | solution.py:64
  68.3 7.6 %collective-permute-start.9 = (f32[2,4,128]{2,1,0:T(4,128)S(1)}, f32[2,4,128]{2,1,0:T(4,128)S(1)}, u32[]{:S(2)}, u32[]{:S(2)}) collective-permute-start(f32[2,4,128]{2,1,0:T(4,128)S(1)} %pad_maximum_fusion.6), channel_id=1, source_target_pairs={{0,1},{1,2},{2,3},{3,4},{4,5},{5,6},{6,7},{7,0},{8,9},{9,10},{10,1... | collective-permute-start | bytes 12296 | tf_op jit(solution)/shard_map/ppermute | solution.py:64
  68.4 8.9 %collective-permute-start.10 = (f32[2,4,128]{2,1,0:T(4,128)S(1)}, f32[2,4,128]{2,1,0:T(4,128)S(1)}, u32[]{:S(2)}, u32[]{:S(2)}) collective-permute-start(f32[2,4,128]{2,1,0:T(4,128)S(1)} %pad_maximum_fusion.6), channel_id=1, source_target_pairs={{0,2},{1,3},{2,4},{3,5},{4,6},{5,7},{6,0},{7,1},{8,10},{9,11},{10,... | collective-permute-start | bytes 12296 | tf_op jit(solution)/shard_map/ppermute | solution.py:64
  70.0 7.2 %collective-permute-start.11 = (f32[2,4,128]{2,1,0:T(4,128)S(1)}, f32[2,4,128]{2,1,0:T(4,128)S(1)}, u32[]{:S(2)}, u32[]{:S(2)}) collective-permute-start(f32[2,4,128]{2,1,0:T(4,128)S(1)} %pad_maximum_fusion.6), channel_id=1, source_target_pairs={{0,3},{1,4},{2,5},{3,6},{4,7},{5,0},{6,1},{7,2},{8,11},{9,12},{10,... | collective-permute-start | bytes 12296 | tf_op jit(solution)/shard_map/ppermute | solution.py:64
  72.2 5.1 %collective-permute-start.12 = (f32[2,4,128]{2,1,0:T(4,128)S(1)}, f32[2,4,128]{2,1,0:T(4,128)S(1)}, u32[]{:S(2)}, u32[]{:S(2)}) collective-permute-start(f32[2,4,128]{2,1,0:T(4,128)S(1)} %pad_maximum_fusion.6), channel_id=1, source_target_pairs={{0,4},{1,5},{2,6},{3,7},{4,0},{5,1},{6,2},{7,3},{8,12},{9,13},{10,... | collective-permute-start | bytes 12296 | tf_op jit(solution)/shard_map/ppermute | solution.py:64
  74.1 3.3 %collective-permute-start.13 = (f32[2,4,128]{2,1,0:T(4,128)S(1)}, f32[2,4,128]{2,1,0:T(4,128)S(1)}, u32[]{:S(2)}, u32[]{:S(2)}) collective-permute-start(f32[2,4,128]{2,1,0:T(4,128)S(1)} %pad_maximum_fusion.6), channel_id=1, source_target_pairs={{0,5},{1,6},{2,7},{3,0},{4,1},{5,2},{6,3},{7,4},{8,13},{9,14},{10,... | collective-permute-start | bytes 12296 | tf_op jit(solution)/shard_map/ppermute | solution.py:64
  75.9 3.6 %collective-permute-start.14 = (f32[2,4,128]{2,1,0:T(4,128)S(1)}, f32[2,4,128]{2,1,0:T(4,128)S(1)}, u32[]{:S(2)}, u32[]{:S(2)}) collective-permute-start(f32[2,4,128]{2,1,0:T(4,128)S(1)} %pad_maximum_fusion.6), channel_id=1, source_target_pairs={{0,6},{1,7},{2,0},{3,1},{4,2},{5,3},{6,4},{7,5},{8,14},{9,15},{10,... | collective-permute-start | bytes 12296 | tf_op jit(solution)/shard_map/ppermute | solution.py:64
  84.5 5.8 %collective-permute-start.16 = (f32[129,128]{1,0:T(8,128)S(1)}, f32[129,128]{1,0:T(8,128)S(1)}, u32[]{:S(2)}, u32[]{:S(2)}) collective-permute-start(f32[129,128]{1,0:T(8,128)S(1)} %get-tuple-element.26), channel_id=1, source_target_pairs={{0,8},{8,16},{16,24},{24,0},{1,9},{9,17},{17,25},{25,1},{2,10},{10... | collective-permute-start | bytes 198152 | tf_op jit(solution)/shard_map/ppermute | solution.py:64
  85.9 6.3 %collective-permute-start.17 = (f32[129,128]{1,0:T(8,128)S(1)}, f32[129,128]{1,0:T(8,128)S(1)}, u32[]{:S(2)}, u32[]{:S(2)}) collective-permute-start(f32[129,128]{1,0:T(8,128)S(1)} %get-tuple-element.27), channel_id=1, source_target_pairs={{0,16},{8,24},{16,0},{24,8},{1,17},{9,25},{17,1},{25,9},{2,18},{10... | collective-permute-start | bytes 198152 | tf_op jit(solution)/shard_map/ppermute | solution.py:64
  88.6 4.3 %collective-permute-start.18 = (f32[129,128]{1,0:T(8,128)S(1)}, f32[129,128]{1,0:T(8,128)S(1)}, u32[]{:S(2)}, u32[]{:S(2)}) collective-permute-start(f32[129,128]{1,0:T(8,128)S(1)} %get-tuple-element.28), channel_id=1, source_target_pairs={{0,24},{8,0},{16,8},{24,16},{1,25},{9,1},{17,9},{25,17},{2,26},{10... | collective-permute-start | bytes 198152 | tf_op jit(solution)/shard_map/ppermute | solution.py:64
  100.9 6.3 %collective-permute-start.19 = (f32[1,129,128]{2,1,0:T(8,128)S(1)}, f32[1,129,128]{2,1,0:T(8,128)S(1)}, u32[]{:S(2)}, u32[]{:S(2)}) collective-permute-start(f32[1,129,128]{2,1,0:T(8,128)S(1)} %concatenate.29), channel_id=1, source_target_pairs={{32,0},{64,32},{96,64},{128,96},{160,128},{192,160},{224,192},{33,... | collective-permute-start | bytes 198152 | tf_op jit(solution)/shard_map/ppermute | solution.py:48
  108.4 9.1 %collective-permute-start.20 = (f32[1,129,128]{2,1,0:T(8,128)S(1)}, f32[1,129,128]{2,1,0:T(8,128)S(1)}, u32[]{:S(2)}, u32[]{:S(2)}) collective-permute-start(f32[1,129,128]{2,1,0:T(8,128)S(1)} %concatenate.30), channel_id=1, source_target_pairs={{64,0},{96,32},{128,64},{160,96},{192,128},{224,160},{65,1},{97,33... | collective-permute-start | bytes 198152 | tf_op jit(solution)/shard_map/ppermute | solution.py:48
  118.7 10.6 %collective-permute-start.21 = (f32[1,129,128]{2,1,0:T(8,128)S(1)}, f32[1,129,128]{2,1,0:T(8,128)S(1)}, u32[]{:S(2)}, u32[]{:S(2)}) collective-permute-start(f32[1,129,128]{2,1,0:T(8,128)S(1)} %concatenate.31), channel_id=1, source_target_pairs={{128,0},{160,32},{192,64},{224,96},{129,1},{161,33},{193,65},{225,... | collective-permute-start | bytes 198152 | tf_op jit(solution)/shard_map/ppermute | solution.py:48
  129.4 6.5 %collective-permute-start.22 = (f32[128,128]{1,0:T(8,128)S(1)}, f32[128,128]{1,0:T(8,128)S(1)}, u32[]{:S(2)}, u32[]{:S(2)}) collective-permute-start(f32[128,128]{1,0:T(8,128)S(1)} %get-tuple-element.36), channel_id=1, source_target_pairs={{0,8},{8,16},{16,24},{24,0},{1,9},{9,17},{17,25},{25,1},{2,10},{10... | collective-permute-start | bytes 196616 | tf_op jit(solution)/shard_map/ppermute | solution.py:64
  130.1 6.1 %collective-permute-start.23 = (f32[128,128]{1,0:T(8,128)S(1)}, f32[128,128]{1,0:T(8,128)}, u32[]{:S(2)}, u32[]{:S(2)}) collective-permute-start(f32[128,128]{1,0:T(8,128)S(1)} %get-tuple-element.35), channel_id=1, source_target_pairs={{0,16},{8,24},{16,0},{24,8},{1,17},{9,25},{17,1},{25,9},{2,18},{10... | collective-permute-start | bytes 196616 | tf_op jit(solution)/shard_map/ppermute | solution.py:64
  133.1 4.4 %collective-permute-start.24 = (f32[128,128]{1,0:T(8,128)S(1)}, f32[128,128]{1,0:T(8,128)}, u32[]{:S(2)}, u32[]{:S(2)}) collective-permute-start(f32[128,128]{1,0:T(8,128)S(1)} %get-tuple-element.34), channel_id=1, source_target_pairs={{0,24},{8,0},{16,8},{24,16},{1,25},{9,1},{17,9},{25,17},{2,26},{10... | collective-permute-start | bytes 196616 | tf_op jit(solution)/shard_map/ppermute | solution.py:64
  (16 other events, 37.9 us)

commit v3 on v2

--- a/solution.py
+++ b/solution.py
@@ -67,6 +67,34 @@
     return jnp.take(stacked, order, axis=0)
 
 
+def column_forward(total, state, axis, ranks):
+    rows = state.shape[0] // ranks
+    pieces = pack(jnp.broadcast_to(total, (ranks,)), state.reshape(ranks, rows, state.shape[1]))
+    got = lax.all_to_all(pieces, axis, 0, 0, tiled=True)
+    got_a, got_b = unpack(got)
+    run = jnp.zeros_like(got_b[0])
+    outs = []
+    for k in range(ranks):
+        outs.append(run)
+        run = jnp.exp(got_a[k]) * run + got_b[k]
+    back = lax.all_to_all(jnp.stack(outs), axis, 0, 0, tiled=True)
+    return back.reshape(state.shape)
+
+
+def column_backward(total, state, axis, ranks):
+    rows = state.shape[0] // ranks
+    pieces = pack(jnp.broadcast_to(total, (ranks,)), state.reshape(ranks, rows, state.shape[1]))
+    got = lax.all_to_all(pieces, axis, 0, 0, tiled=True)
+    got_a, got_c = unpack(got)
+    run = jnp.zeros_like(got_c[0])
+    outs = [None] * ranks
+    for k in reversed(range(ranks)):
+        outs[k] = run
+        run = got_c[k] + jnp.exp(got_a[k]) * run
+    back = lax.all_to_all(jnp.stack(outs), axis, 0, 0, tiled=True)
+    return back.reshape(state.shape)
+
+
 def incoming_states(shard_total, shard_state, row_ranks, col_ranks):
     parts = exchange(pack(shard_total, shard_state), "sx", row_ranks)
     part_a, part_b = parts[:, -1, 0], parts[:, :-1, :]
@@ -78,7 +106,7 @@
         row_b.append(run_b)
         run_b = jnp.exp(part_a[pos]) * run_b + part_b[pos]
         run_a = run_a + part_a[pos]
-    before_row = forward_scan(run_a[None], run_b[None], "sz", col_ranks)[0]
+    before_row = column_forward(run_a, run_b, "sz", col_ranks)
     result = jnp.stack(
         [jnp.exp(row_a[pos]) * before_row + row_b[pos] for pos in range(row_ranks)]
     )
@@ -96,7 +124,7 @@
         row_c[pos] = run_c
         run_c = part_c[pos] + jnp.exp(part_a[pos]) * run_c
         run_a = run_a + part_a[pos]
-    after_row = backward_scan(run_a[None], run_c[None], "sz", col_ranks)[0]
+    after_row = column_backward(run_a, run_c, "sz", col_ranks)
     result = jnp.stack(
         [row_c[pos] + jnp.exp(row_a[pos]) * after_row for pos in range(row_ranks)]
     )
@@ -104,7 +132,8 @@
 
 
 def head_sum(values, ranks):
-    gathered = exchange(jnp.broadcast_to(values[None], (ranks,) + values.shape), "head", ranks)
+    copies = jnp.broadcast_to(values[None], (ranks,) + values.shape)
+    gathered = lax.all_to_all(copies, "head", 0, 0, tiled=True)
     return jnp.sum(gathered, axis=0)
 
 

time: 148 us -> 167 us (1.13)
  other arithmetic: 4.59 us -> 17.3 us
  local copies, waits for them, and re-layouts: 20.2 us -> 25.8 us
  starting transfers between devices: 50.9 us -> 47.8 us
  matrix products: 23.1 us -> 26 us
  between operations: 18.4 us -> 21.2 us
  waiting for transfers between devices: 29.3 us -> 27.2 us
    all_to_all x0 -> x5, starting transfers between devices: none -> 29.1 us  [the longest x1 8.7 us: column_forward(): got = lax.all_to_all(pieces, axis, 0, 0, tiled=True)]
    ppermute x6 -> x0, starting transfers between devices: 24.8 us -> none  [the longest x3 18.4 us: forward_scan(): got_a, got_b = unpack(lax.ppermute(pack(win_a, win_b), axis, pairs))]
    all_to_all x0 -> x5, waiting for transfers between devices: none -> 19.8 us  [the longest x1 6 us: column_forward(): got = lax.all_to_all(pieces, axis, 0, 0, tiled=True)]
    ppermute x6 -> x0, waiting for transfers between devices: 19.1 us -> none  [the longest x3 14.5 us: backward_scan(): got_a, got_c = unpack(lax.ppermute(pack(win_a, win_c), axis, pairs))]
    ppermute x19 -> x12, starting transfers between devices: 26.1 us -> 18.7 us  [exchange(): got.append(lax.ppermute(send, axis, pairs))]
    unnamed x1 -> x11, other arithmetic: 0.01 us -> 6.64 us
    unnamed x37 -> x80, local copies, waits for them, and re-layouts: 5.87 us -> 8.81 us
    ppermute x19 -> x12, waiting for transfers between devices: 10.2 us -> 7.48 us  [exchange(): got.append(lax.ppermute(send, axis, pairs))]
  transfers between devices with their start and end apart: 25 -> 17, of which waited for: 15 -> 12; matrix products, arithmetic and copies ran while one was open for 9% -> 12% of each run, Pallas kernels for 0% -> 0%
where the time goes in v3:
time: 167 us; the launch traced here: 165 us
  starting transfers between devices  47.8 us (29%)
  waiting for transfers between devices  27.2 us (16%)
  matrix products  26 us (16%)
  local copies, waits for them, and re-layouts  25.8 us (15%)
  between operations  21.2 us (13%)
  other arithmetic  17.3 us (10%)
    ppermute x12, starting transfers between devices, exchange(): got.append(lax.ppermute(send, axis, pairs))  18.7 us
    unnamed x80, local copies, waits for them, and re-layouts  8.81 us
    all_to_all x1, starting transfers between devices, column_forward(): got = lax.all_to_all(pieces, axis, 0, 0, tiled=True)  8.7 us
    ppermute x12, waiting for transfers between devices, exchange(): got.append(lax.ppermute(send, axis, pairs))  7.48 us
    unnamed x11, other arithmetic  6.64 us
    all_to_all x1, starting transfers between devices, column_backward(): got = lax.all_to_all(pieces, axis, 0, 0, tiled=True)  6.51 us
    all_to_all x1, waiting for transfers between devices, column_forward(): got = lax.all_to_all(pieces, axis, 0, 0, tiled=True)  6 us
    all_to_all x1, waiting for transfers between devices, column_backward(): got = lax.all_to_all(pieces, axis, 0, 0, tiled=True)  4.79 us
  transfers between devices with their start and end apart: 17, of which 12 were waited for; matrix products, arithmetic and copies ran while one was open for 12% of the time, Pallas kernels for 0%

profile of v3, /device:TPU:32, one launch (start us, length us, event | category | flops | bytes accessed | tf_op | source)
XLA Modules:
  0.0 165.3 jit_solution(5727678786603484023)
XLA Ops:
  6.5 2.4 %fusion.20 = f32[4,1,128,128]{3,1,2,0:T(1,128)S(1)} fusion(f32[4,4,1,1]{0,2,3,1:T(1,128)S(1)} %copy.177, f32[4,4,128,128]{3,2,1,0:T(8,128)S(1)} %fusion.23), kind=kOutput, calls=%fused_computation.42 | convolution fusion | flops 3145728 | bytes 1310784 | tf_op jit(solution)/shard_map/mh,mhde->hde/dot_general | solution.py:178
  11.2 2.7 %collective-permute-start.1 = (f32[129,128]{1,0:T(8,128)}, f32[129,128]{1,0:T(8,128)}, u32[]{:S(2)}, u32[]{:S(2)}) collective-permute-start(f32[129,128]{1,0:T(8,128)} %get-tuple-element.39), channel_id=1, source_target_pairs={{0,16},{8,24},{16,0},{24,8},{1,17},{9,25},{17,1},{25,9},{2,18},{10... | collective-permute-start | bytes 198152 | tf_op jit(solution)/shard_map/ppermute | solution.py:64
  26.4 8.7 %all-to-all-start = ((f32[8,17,128]{2,1,0:T(8,128)}), f32[8,17,128]{2,1,0:T(8,128)S(1)}, u32[]{:S(2)}, u32[]{:S(2)}) async-start(f32[8,17,128]{2,1,0:T(8,128)} %concatenate.13), calls=%async_computation | async-start | bytes 196608 | tf_op jit(solution)/shard_map/all_to_all | solution.py:73
  36.4 6.0 %all-to-all-done = f32[8,17,128]{2,1,0:T(8,128)S(1)} async-done(((f32[8,17,128]{2,1,0:T(8,128)}), f32[8,17,128]{2,1,0:T(8,128)S(1)}, u32[]{:S(2)}, u32[]{:S(2)}) %all-to-all-start) | async-done | bytes 69664 | tf_op jit(solution)/shard_map/all_to_all | solution.py:73
  52.0 4.7 %all-to-all-start.1 = ((f32[8,16,128]{2,1,0:T(8,128)}), f32[8,16,128]{2,1,0:T(8,128)S(1)}, u32[]{:S(2)}, u32[]{:S(2)}) async-start(f32[8,16,128]{2,1,0:T(8,128)} %constant_dynamic-update-slice_fusion), calls=%async_computation.1 | async-start | bytes 131072 | tf_op jit(solution)/shard_map/all_to_all | solution.py:80
  56.7 1.5 convolution_bitcast_fusion.9
  61.2 1.5 copy.149
  64.4 3.5 %collective-permute-start.4 = (f32[128,128]{1,0:T(8,128)S(1)}, f32[128,128]{1,0:T(8,128)S(1)}, u32[]{:S(2)}, u32[]{:S(2)}) collective-permute-start(f32[128,128]{1,0:T(8,128)S(1)} %get-tuple-element.50), channel_id=1, source_target_pairs={{0,16},{8,24},{16,0},{24,8},{1,17},{9,25},{17,1},{25,9},{2,18},{10... | collective-permute-start | bytes 196616 | tf_op jit(solution)/shard_map/ppermute | solution.py:64
  69.3 1.6 collective-permute-done.4
  73.0 4.0 %fusion.14 = bf16[4,4,128,128]{3,0,2,1:T(4,128)(2,1)S(1)} fusion(f32[4,4,128,128]{3,2,1,0:T(8,128)} %copy-done.1, f32[4,128,128]{2,1,0:T(8,128)S(1)} %broadcast_select_fusion.3, f32[4,4]{0,1:T(4,128)S(1)} %copy.146, f32[4,4]{1,0:T(4,128)S(1)} %fusion.79, f32[4,4]{0,1:T(4,128)S(1)} %copy.144, f32[4,4]{0,1:T(4,128)S(1)} %copy.143, f32[4,4]{0,1:T(4,128)S(1)} %copy.142), kind=kOutput, calls=%fused_computation.30 | convolution fusion | flops 13369600 | bytes 1835328 | tf_op jit(solution)/shard_map/nmh,mhde->nhde/dot_general | solution.py:177
  79.2 4.5 %all-to-all-start.2 = ((f32[8,2,4,128]{3,2,1,0:T(4,128)}), f32[8,2,4,128]{3,2,1,0:T(4,128)S(1)}, u32[]{:S(2)}, u32[]{:S(2)}) async-start(f32[8,2,4,128]{3,2,1,0:T(4,128)} %broadcast_in_dim.17), calls=%async_computation.2 | async-start | bytes 65536 | tf_op jit(solution)/shard_map/all_to_all | solution.py:136
  85.1 4.0 %all-to-all-done.2 = f32[8,2,4,128]{3,2,1,0:T(4,128)S(1)} async-done(((f32[8,2,4,128]{3,2,1,0:T(4,128)}), f32[8,2,4,128]{3,2,1,0:T(4,128)S(1)}, u32[]{:S(2)}, u32[]{:S(2)}) %all-to-all-start.2) | async-done | bytes 32800 | tf_op jit(solution)/shard_map/all_to_all | solution.py:136
  92.0 2.4 %fusion.17 = f32[4,1,128,128]{3,1,2,0:T(1,128)S(1)} fusion(f32[4,4,1,1]{0,2,3,1:T(1,128)S(1)} %copy.185, f32[4,4,128,128]{3,2,1,0:T(8,128)S(1)} %fusion.24), kind=kOutput, calls=%fused_computation.39 | convolution fusion | flops 3145728 | bytes 1310784 | tf_op jit(solution)/shard_map/mh,mhde->hde/dot_general | solution.py:228
  94.5 3.1 %collective-permute-start.7 = (f32[129,128]{1,0:T(8,128)S(1)}, f32[129,128]{1,0:T(8,128)S(1)}, u32[]{:S(2)}, u32[]{:S(2)}) collective-permute-start(f32[129,128]{1,0:T(8,128)S(1)} %get-tuple-element.36), channel_id=1, source_target_pairs={{0,16},{8,24},{16,0},{24,8},{1,17},{9,25},{17,1},{25,9},{2,18},{10... | collective-permute-start | bytes 198152 | tf_op jit(solution)/shard_map/ppermute | solution.py:64
  98.7 1.5 convolution_bitcast_fusion.6
  111.5 6.5 %all-to-all-start.3 = ((f32[8,17,128]{2,1,0:T(8,128)}), f32[8,17,128]{2,1,0:T(8,128)S(1)}, u32[]{:S(2)}, u32[]{:S(2)}) async-start(f32[8,17,128]{2,1,0:T(8,128)} %concatenate.15), calls=%async_computation.3 | async-start | bytes 196608 | tf_op jit(solution)/shard_map/all_to_all | solution.py:87
  118.0 2.5 %fusion.10 = bf16[4,128,4,128]{1,3,2,0:T(8,128)(2,1)} fusion(f32[4,128,4,128]{1,3,2,0:T(8,128)} %convolution_bitcast_fusion.6, bf16[4,128,4,128]{1,3,2,0:T(8,128)(2,1)S(1)} %multiply_convert_fusion.1, f32[4,128,4]{1,2,0:T(4,128)S(1)} %copy.136, bf16[4,4,128,128]{3,0,2,1:T(4,128)(2,1)} %copy-done.4), kind=kOutput, calls=%fused_computation.26 | convolution fusion | flops 67895296 | bytes 2629632 | tf_op jit(solution)/shard_map/nihe,nhde->nihd/dot_general | solution.py:209
  120.5 4.8 %all-to-all-done.3 = f32[8,17,128]{2,1,0:T(8,128)S(1)} async-done(((f32[8,17,128]{2,1,0:T(8,128)}), f32[8,17,128]{2,1,0:T(8,128)S(1)}, u32[]{:S(2)}, u32[]{:S(2)}) %all-to-all-start.3) | async-done | bytes 69664 | tf_op jit(solution)/shard_map/all_to_all | solution.py:87
  135.4 4.7 %all-to-all-start.4 = ((f32[8,16,128]{2,1,0:T(8,128)}), f32[8,16,128]{2,1,0:T(8,128)S(1)}, u32[]{:S(2)}, u32[]{:S(2)}) async-start(f32[8,16,128]{2,1,0:T(8,128)} %constant_dynamic-update-slice_fusion.8), calls=%async_computation.4 | async-start | bytes 131072 | tf_op jit(solution)/shard_map/all_to_all | solution.py:94
  140.1 2.6 %convolution_bitcast_fusion.4 = f32[4,128,4,128]{3,1,2,0:T(8,128)} fusion(bf16[4,4,128,128]{3,2,1,0:T(8,128)(2,1)} %copy-done.8, bf16[4,128,4,128]{1,3,2,0:T(8,128)(2,1)S(1)} %copy.161), kind=kOutput, calls=%fused_computation.13 | convolution fusion | flops 67108864 | bytes 2097152 | tf_op jit(solution)/shard_map/nhij,nihd->njhd/dot_general | solution.py:212
  142.8 4.2 %all-to-all-done.4 = f32[8,16,128]{2,1,0:T(8,128)S(1)} async-done(((f32[8,16,128]{2,1,0:T(8,128)}), f32[8,16,128]{2,1,0:T(8,128)S(1)}, u32[]{:S(2)}, u32[]{:S(2)}) %all-to-all-start.4) | async-done | bytes 65568 | tf_op jit(solution)/shard_map/all_to_all | solution.py:94
  148.2 2.9 %collective-permute-start.10 = (f32[128,128]{1,0:T(8,128)S(1)}, f32[128,128]{1,0:T(8,128)S(1)}, u32[]{:S(2)}, u32[]{:S(2)}) collective-permute-start(f32[128,128]{1,0:T(8,128)S(1)} %get-tuple-element.44), channel_id=1, source_target_pairs={{0,16},{8,24},{16,0},{24,8},{1,17},{9,25},{17,1},{25,9},{2,18},{10... | collective-permute-start | bytes 196616 | tf_op jit(solution)/shard_map/ppermute | solution.py:64
  151.4 1.5 convolution_bitcast_fusion.2
  157.8 2.6 %fusion.16 = bf16[4,4,128,128]{3,0,2,1:T(4,128)(2,1)S(1)} fusion(f32[4,4,128,128]{3,2,1,0:T(8,128)S(1)} %fusion.24, f32[4,128,128]{2,1,0:T(8,128)S(1)} %broadcast_select_fusion.2, f32[4,4]{0,1:T(4,128)S(1)} %copy-done.37, f32[4,4]{1,0:T(4,128)S(1)} %copy-done.36, f32[4,4]{0,1:T(4,128)S(1)} %copy-done.33, f32[4,4]{0,1:T(4,128)S(1)} %copy-done.31, ...), kind=kOutput, calls=%fused_computation.32 | convolution fusion | flops 13369600 | bytes 1835328 | tf_op jit(solution)/shard_map/nmh,mhde->nhde/dot_general | solution.py:227
  (189 shorter events, 59.6 us)
Async XLA Ops:
  6.5 10.8 %copy-start.1 = (f32[4,4,128,128]{3,2,1,0:T(8,128)}, f32[4,4,128,128]{3,2,1,0:T(8,128)S(1)}, u32[]{:S(2)}) copy-start(f32[4,4,128,128]{3,2,1,0:T(8,128)S(1)} %fusion.23) | copy-start | bytes 3145732
  9.7 8.1 %collective-permute-start = (f32[129,128]{1,0:T(8,128)}, f32[129,128]{1,0:T(8,128)}, u32[]{:S(2)}, u32[]{:S(2)}) collective-permute-start(f32[129,128]{1,0:T(8,128)} %get-tuple-element.40), channel_id=1, source_target_pairs={{0,8},{8,16},{16,24},{24,0},{1,9},{9,17},{17,25},{25,1},{2,10},{10... | collective-permute-start | bytes 198152 | tf_op jit(solution)/shard_map/ppermute | solution.py:64
  11.2 6.6 %collective-permute-start.1 = (f32[129,128]{1,0:T(8,128)}, f32[129,128]{1,0:T(8,128)}, u32[]{:S(2)}, u32[]{:S(2)}) collective-permute-start(f32[129,128]{1,0:T(8,128)} %get-tuple-element.39), channel_id=1, source_target_pairs={{0,16},{8,24},{16,0},{24,8},{1,17},{9,25},{17,1},{25,9},{2,18},{10... | collective-permute-start | bytes 198152 | tf_op jit(solution)/shard_map/ppermute | solution.py:64
  13.9 4.4 %collective-permute-start.2 = (f32[129,128]{1,0:T(8,128)S(1)}, f32[129,128]{1,0:T(8,128)}, u32[]{:S(2)}, u32[]{:S(2)}) collective-permute-start(f32[129,128]{1,0:T(8,128)S(1)} %get-tuple-element.41), channel_id=1, source_target_pairs={{0,24},{8,0},{16,8},{24,16},{1,25},{9,1},{17,9},{25,17},{2,26},{10... | collective-permute-start | bytes 198152 | tf_op jit(solution)/shard_map/ppermute | solution.py:64
  26.4 8.7 %copy-start.16 = (f32[128,128]{1,0:T(8,128)S(1)}, f32[128,128]{1,0:T(8,128)}, u32[]{:S(2)}) copy-start(f32[128,128]{1,0:T(8,128)} %fusion.51) | copy-start | bytes 196612
  26.4 8.7 %copy-start.26 = (f32[4,4,128]{2,1,0:T(4,128)S(1)}, f32[4,4,128]{2,1,0:T(4,128)}, u32[]{:S(2)}) copy-start(f32[4,4,128]{2,1,0:T(4,128)} %copy.133) | copy-start | bytes 24580
  26.4 16.0 %all-to-all-start = ((f32[8,17,128]{2,1,0:T(8,128)}), f32[8,17,128]{2,1,0:T(8,128)S(1)}, u32[]{:S(2)}, u32[]{:S(2)}) async-start(f32[8,17,128]{2,1,0:T(8,128)} %concatenate.13), calls=%async_computation | async-start | bytes 196608 | tf_op jit(solution)/shard_map/all_to_all | solution.py:73
  35.8 22.4 %copy-start.6 = (bf16[4,4,128,128]{3,2,1,0:T(8,128)(2,1)}, bf16[4,4,128,128]{3,2,1,0:T(8,128)(2,1)S(1)}, u32[]{:S(2)}) copy-start(bf16[4,4,128,128]{3,2,1,0:T(8,128)(2,1)S(1)} %fusion.13) | copy-start | bytes 1572868
  52.0 11.7 %all-to-all-start.1 = ((f32[8,16,128]{2,1,0:T(8,128)}), f32[8,16,128]{2,1,0:T(8,128)S(1)}, u32[]{:S(2)}, u32[]{:S(2)}) async-start(f32[8,16,128]{2,1,0:T(8,128)} %constant_dynamic-update-slice_fusion), calls=%async_computation.1 | async-start | bytes 131072 | tf_op jit(solution)/shard_map/all_to_all | solution.py:80
  58.3 14.7 %copy-start.30 = (f32[4,4]{0,1:T(4,128)}, f32[4,4]{0,1:T(4,128)S(1)}, u32[]{:S(2)}) copy-start(f32[4,4]{0,1:T(4,128)S(1)} %copy.143) | copy-start | bytes 196
  58.4 14.6 %copy-start.32 = (f32[4,4]{0,1:T(4,128)}, f32[4,4]{0,1:T(4,128)S(1)}, u32[]{:S(2)}) copy-start(f32[4,4]{0,1:T(4,128)S(1)} %copy.144) | copy-start | bytes 196
  59.8 13.2 %copy-start.34 = (f32[4,4]{0,1:T(4,128)}, f32[4,4]{0,1:T(4,128)S(1)}, u32[]{:S(2)}) copy-start(f32[4,4]{0,1:T(4,128)S(1)} %copy.142) | copy-start | bytes 196
  63.7 5.6 %collective-permute-start.3 = (f32[128,128]{1,0:T(8,128)S(1)}, f32[128,128]{1,0:T(8,128)S(1)}, u32[]{:S(2)}, u32[]{:S(2)}) collective-permute-start(f32[128,128]{1,0:T(8,128)S(1)} %get-tuple-element.51), channel_id=1, source_target_pairs={{0,8},{8,16},{16,24},{24,0},{1,9},{9,17},{17,25},{25,1},{2,10},{10... | collective-permute-start | bytes 196616 | tf_op jit(solution)/shard_map/ppermute | solution.py:64
  64.4 6.4 %collective-permute-start.4 = (f32[128,128]{1,0:T(8,128)S(1)}, f32[128,128]{1,0:T(8,128)S(1)}, u32[]{:S(2)}, u32[]{:S(2)}) collective-permute-start(f32[128,128]{1,0:T(8,128)S(1)} %get-tuple-element.50), channel_id=1, source_target_pairs={{0,16},{8,24},{16,0},{24,8},{1,17},{9,25},{17,1},{25,9},{2,18},{10... | collective-permute-start | bytes 196616 | tf_op jit(solution)/shard_map/ppermute | solution.py:64
  67.9 4.3 %collective-permute-start.5 = (f32[128,128]{1,0:T(8,128)S(1)}, f32[128,128]{1,0:T(8,128)S(1)}, u32[]{:S(2)}, u32[]{:S(2)}) collective-permute-start(f32[128,128]{1,0:T(8,128)S(1)} %get-tuple-element.49), channel_id=1, source_target_pairs={{0,24},{8,0},{16,8},{24,16},{1,25},{9,1},{17,9},{25,17},{2,26},{10... | collective-permute-start | bytes 196616 | tf_op jit(solution)/shard_map/ppermute | solution.py:64
  79.2 9.9 %all-to-all-start.2 = ((f32[8,2,4,128]{3,2,1,0:T(4,128)}), f32[8,2,4,128]{3,2,1,0:T(4,128)S(1)}, u32[]{:S(2)}, u32[]{:S(2)}) async-start(f32[8,2,4,128]{3,2,1,0:T(4,128)} %broadcast_in_dim.17), calls=%async_computation.2 | async-start | bytes 65536 | tf_op jit(solution)/shard_map/all_to_all | solution.py:136
  94.5 6.6 %collective-permute-start.6 = (f32[129,128]{1,0:T(8,128)S(1)}, f32[129,128]{1,0:T(8,128)S(1)}, u32[]{:S(2)}, u32[]{:S(2)}) collective-permute-start(f32[129,128]{1,0:T(8,128)S(1)} %get-tuple-element.35), channel_id=1, source_target_pairs={{0,8},{8,16},{16,24},{24,0},{1,9},{9,17},{17,25},{25,1},{2,10},{10... | collective-permute-start | bytes 198152 | tf_op jit(solution)/shard_map/ppermute | solution.py:64
  94.5 6.6 %collective-permute-start.7 = (f32[129,128]{1,0:T(8,128)S(1)}, f32[129,128]{1,0:T(8,128)S(1)}, u32[]{:S(2)}, u32[]{:S(2)}) collective-permute-start(f32[129,128]{1,0:T(8,128)S(1)} %get-tuple-element.36), channel_id=1, source_target_pairs={{0,16},{8,24},{16,0},{24,8},{1,17},{9,25},{17,1},{25,9},{2,18},{10... | collective-permute-start | bytes 198152 | tf_op jit(solution)/shard_map/ppermute | solution.py:64
  97.6 4.3 %collective-permute-start.8 = (f32[129,128]{1,0:T(8,128)S(1)}, f32[129,128]{1,0:T(8,128)S(1)}, u32[]{:S(2)}, u32[]{:S(2)}) collective-permute-start(f32[129,128]{1,0:T(8,128)S(1)} %get-tuple-element.37), channel_id=1, source_target_pairs={{0,24},{8,0},{16,8},{24,16},{1,25},{9,1},{17,9},{25,17},{2,26},{10... | collective-permute-start | bytes 198152 | tf_op jit(solution)/shard_map/ppermute | solution.py:64
  111.5 13.8 %all-to-all-start.3 = ((f32[8,17,128]{2,1,0:T(8,128)}), f32[8,17,128]{2,1,0:T(8,128)S(1)}, u32[]{:S(2)}, u32[]{:S(2)}) async-start(f32[8,17,128]{2,1,0:T(8,128)} %concatenate.15), calls=%async_computation.3 | async-start | bytes 196608 | tf_op jit(solution)/shard_map/all_to_all | solution.py:87
  135.4 11.7 %all-to-all-start.4 = ((f32[8,16,128]{2,1,0:T(8,128)}), f32[8,16,128]{2,1,0:T(8,128)S(1)}, u32[]{:S(2)}, u32[]{:S(2)}) async-start(f32[8,16,128]{2,1,0:T(8,128)} %constant_dynamic-update-slice_fusion.8), calls=%async_computation.4 | async-start | bytes 131072 | tf_op jit(solution)/shard_map/all_to_all | solution.py:94
  147.2 6.9 %collective-permute-start.9 = (f32[128,128]{1,0:T(8,128)S(1)}, f32[128,128]{1,0:T(8,128)S(1)}, u32[]{:S(2)}, u32[]{:S(2)}) collective-permute-start(f32[128,128]{1,0:T(8,128)S(1)} %get-tuple-element.45), channel_id=1, source_target_pairs={{0,8},{8,16},{16,24},{24,0},{1,9},{9,17},{17,25},{25,1},{2,10},{10... | collective-permute-start | bytes 196616 | tf_op jit(solution)/shard_map/ppermute | solution.py:64
  148.2 5.9 %collective-permute-start.10 = (f32[128,128]{1,0:T(8,128)S(1)}, f32[128,128]{1,0:T(8,128)S(1)}, u32[]{:S(2)}, u32[]{:S(2)}) collective-permute-start(f32[128,128]{1,0:T(8,128)S(1)} %get-tuple-element.44), channel_id=1, source_target_pairs={{0,16},{8,24},{16,0},{24,8},{1,17},{9,25},{17,1},{25,9},{2,18},{10... | collective-permute-start | bytes 196616 | tf_op jit(solution)/shard_map/ppermute | solution.py:64
  151.1 4.4 %collective-permute-start.11 = (f32[128,128]{1,0:T(8,128)S(1)}, f32[128,128]{1,0:T(8,128)}, u32[]{:S(2)}, u32[]{:S(2)}) collective-permute-start(f32[128,128]{1,0:T(8,128)S(1)} %get-tuple-element.43), channel_id=1, source_target_pairs={{0,24},{8,0},{16,8},{24,16},{1,25},{9,1},{17,9},{25,17},{2,26},{10... | collective-permute-start | bytes 196616 | tf_op jit(solution)/shard_map/ppermute | solution.py:64
  (31 other events, 61.0 us)

commit v4 on v2

--- a/solution.py
+++ b/solution.py
@@ -13,14 +13,12 @@
 highest = lax.Precision.HIGHEST
 
 
-def pack(total, state):
-    row = jnp.broadcast_to(total[:, None, None], (state.shape[0], 1, state.shape[2]))
-    return jnp.concatenate([state, row], axis=1)
+def pack(total_row, state):
+    return jnp.concatenate([state, total_row], axis=1)
 
 
 def unpack(payload):
-    rows = payload.shape[1] - 1
-    return payload[:, rows, 0], payload[:, :rows, :]
+    return payload[:, -1:, :], payload[:, :-1, :]
 
 
 def forward_scan(total, state, axis, ranks):
@@ -30,10 +28,10 @@
     while shift < ranks:
         pairs = [(i, i + shift) for i in range(ranks - shift)]
         got_a, got_b = unpack(lax.ppermute(pack(win_a, win_b), axis, pairs))
-        excl_b = jnp.exp(excl_a)[:, None, None] * got_b + excl_b
+        excl_b = jnp.exp(excl_a) * got_b + excl_b
         excl_a = excl_a + got_a
         if 2 * shift < ranks:
-            win_b = jnp.exp(win_a)[:, None, None] * got_b + win_b
+            win_b = jnp.exp(win_a) * got_b + win_b
             win_a = win_a + got_a
         shift *= 2
     return excl_b
@@ -46,10 +44,10 @@
     while shift < ranks:
         pairs = [(i + shift, i) for i in range(ranks - shift)]
         got_a, got_c = unpack(lax.ppermute(pack(win_a, win_c), axis, pairs))
-        excl_c = excl_c + jnp.exp(excl_a)[:, None, None] * got_c
+        excl_c = excl_c + jnp.exp(excl_a) * got_c
         excl_a = excl_a + got_a
         if 2 * shift < ranks:
-            win_c = win_c + jnp.exp(win_a)[:, None, None] * got_c
+            win_c = win_c + jnp.exp(win_a) * got_c
             win_a = win_a + got_a
         shift *= 2
     return excl_c
@@ -67,10 +65,14 @@
     return jnp.take(stacked, order, axis=0)
 
 
+def lane_rows(shard_total, width):
+    return jnp.broadcast_to(shard_total[:, None, None], (shard_total.shape[0], 1, width))
+
+
 def incoming_states(shard_total, shard_state, row_ranks, col_ranks):
-    parts = exchange(pack(shard_total, shard_state), "sx", row_ranks)
-    part_a, part_b = parts[:, -1, 0], parts[:, :-1, :]
-    run_a = jnp.zeros((), jnp.float32)
+    parts = exchange(pack(lane_rows(shard_total, shard_state.shape[2]), shard_state), "sx", row_ranks)
+    part_a, part_b = unpack(parts)
+    run_a = jnp.zeros_like(part_a[0])
     run_b = jnp.zeros_like(part_b[0])
     row_a, row_b = [], []
     for pos in range(row_ranks):
@@ -86,9 +88,9 @@
 
 
 def outgoing_states(shard_total, shard_back, row_ranks, col_ranks):
-    parts = exchange(pack(shard_total, shard_back), "sx", row_ranks)
-    part_a, part_c = parts[:, -1, 0], parts[:, :-1, :]
-    run_a = jnp.zeros((), jnp.float32)
+    parts = exchange(pack(lane_rows(shard_total, shard_back.shape[2]), shard_back), "sx", row_ranks)
+    part_a, part_c = unpack(parts)
+    run_a = jnp.zeros_like(part_a[0])
     run_c = jnp.zeros_like(part_c[0])
     row_a, row_c = [None] * row_ranks, [None] * row_ranks
     for pos in reversed(range(row_ranks)):
@@ -104,7 +106,8 @@
 
 
 def head_sum(values, ranks):
-    gathered = exchange(jnp.broadcast_to(values[None], (ranks,) + values.shape), "head", ranks)
+    copies = jnp.broadcast_to(values[None], (ranks,) + values.shape)
+    gathered = lax.all_to_all(copies, "head", 0, 0, tiled=True)
     return jnp.sum(gathered, axis=0)
 
 

time: 148 us -> 128 us (0.86)
  between operations: 18.4 us -> 1.33 us
  local copies, waits for them, and re-layouts: 20.2 us -> 17.1 us
  waiting for transfers between devices: 29.3 us -> 32.1 us
  starting transfers between devices: 50.9 us -> 48.1 us
    ppermute x19 -> x12, starting transfers between devices: 26.1 us -> 18.6 us  [exchange(): got.append(lax.ppermute(send, axis, pairs))]
    all_to_all x0 -> x1, waiting for transfers between devices: none -> 5.25 us  [head_sum(): gathered = lax.all_to_all(copies, 'head', 0, 0, tiled=True)]
    all_to_all x0 -> x1, starting transfers between devices: none -> 4.47 us  [head_sum(): gathered = lax.all_to_all(copies, 'head', 0, 0, tiled=True)]
    slice x6 -> x0, local copies, waits for them, and re-layouts: 3.32 us -> none  [the longest x4 2.14 us: unpack(): return (payload[:, rows, 0], payload[:, :rows, :])]
    ppermute x19 -> x12, waiting for transfers between devices: 10.2 us -> 9.6 us  [exchange(): got.append(lax.ppermute(send, axis, pairs))]
    gather x5 -> x4, local copies, waits for them, and re-layouts: 3.55 us -> 3.22 us  [exchange(): return jnp.take(stacked, order, axis=0)]
    unnamed x37 -> x31, local copies, waits for them, and re-layouts: 5.87 us -> 5.83 us
  transfers between devices with their start and end apart: 25 -> 19, of which waited for: 15 -> 15; matrix products, arithmetic and copies ran while one was open for 9% -> 11% of each run, Pallas kernels for 0% -> 0%
where the time goes in v4:
time: 128 us; the launch traced here: 126 us
  starting transfers between devices  48.1 us (38%)
  waiting for transfers between devices  32.1 us (25%)
  matrix products  23.2 us (18%)
  local copies, waits for them, and re-layouts  17.1 us (13%)
  other arithmetic  4.35 us (3%)
  between operations  1.33 us (1%)
    ppermute x12, starting transfers between devices, exchange(): got.append(lax.ppermute(send, axis, pairs))  18.6 us
    ppermute x3, starting transfers between devices, forward_scan(): got_a, got_b = unpack(lax.ppermute(pack(win_a, win_b), axis, pairs))  18.4 us
    ppermute x3, waiting for transfers between devices, backward_scan(): got_a, got_c = unpack(lax.ppermute(pack(win_a, win_c), axis, pairs))  13.5 us
    ppermute x12, waiting for transfers between devices, exchange(): got.append(lax.ppermute(send, axis, pairs))  9.6 us
    ppermute x3, starting transfers between devices, backward_scan(): got_a, got_c = unpack(lax.ppermute(pack(win_a, win_c), axis, pairs))  6.71 us
    unnamed x31, local copies, waits for them, and re-layouts  5.83 us
    all_to_all x1, waiting for transfers between devices, head_sum(): gathered = lax.all_to_all(copies, 'head', 0, 0, tiled=True)  5.25 us
    all_to_all x1, starting transfers between devices, head_sum(): gathered = lax.all_to_all(copies, 'head', 0, 0, tiled=True)  4.47 us
  transfers between devices with their start and end apart: 19, of which 15 were waited for; matrix products, arithmetic and copies ran while one was open for 11% of the time, Pallas kernels for 0%

profile of v4, /device:TPU:32, one launch (start us, length us, event | category | flops | bytes accessed | tf_op | source)
XLA Modules:
  0.0 126.2 jit_solution(16786728163119174098)
XLA Ops:
  6.0 2.4 %fusion.20 = f32[4,1,128,128]{3,1,2,0:T(1,128)S(1)} fusion(f32[4,4,1,1]{0,2,3,1:T(1,128)S(1)} %copy.177, f32[4,4,128,128]{3,2,1,0:T(8,128)S(1)} %fusion.23), kind=kOutput, calls=%fused_computation.42 | convolution fusion | flops 3145728 | bytes 1310784 | tf_op jit(solution)/shard_map/mh,mhde->hde/dot_general | solution.py:152
  8.5 1.6 %collective-permute-start = (f32[129,128]{1,0:T(8,128)S(1)}, f32[129,128]{1,0:T(8,128)S(1)}, u32[]{:S(2)}, u32[]{:S(2)}) collective-permute-start(f32[129,128]{1,0:T(8,128)S(1)} %get-tuple-element.45), channel_id=1, source_target_pairs={{0,8},{8,16},{16,24},{24,0},{1,9},{9,17},{17,25},{25,1},{2,10},{10... | collective-permute-start | bytes 198152 | tf_op jit(solution)/shard_map/ppermute | solution.py:62
  10.0 2.7 %collective-permute-start.1 = (f32[129,128]{1,0:T(8,128)S(1)}, f32[129,128]{1,0:T(8,128)S(1)}, u32[]{:S(2)}, u32[]{:S(2)}) collective-permute-start(f32[129,128]{1,0:T(8,128)S(1)} %get-tuple-element.44), channel_id=1, source_target_pairs={{0,16},{8,24},{16,0},{24,8},{1,17},{9,25},{17,1},{25,9},{2,18},{10... | collective-permute-start | bytes 198152 | tf_op jit(solution)/shard_map/ppermute | solution.py:62
  17.8 3.8 %collective-permute-start.3 = (f32[1,129,128]{2,1,0:T(8,128)S(1)}, f32[1,129,128]{2,1,0:T(8,128)S(1)}, u32[]{:S(2)}, u32[]{:S(2)}) collective-permute-start(f32[1,129,128]{2,1,0:T(8,128)S(1)} %pad_maximum_fusion.6), channel_id=1, source_target_pairs={{0,32},{32,64},{64,96},{96,128},{128,160},{160,192},{192,224},{1,3... | collective-permute-start | bytes 198152 | tf_op jit(solution)/shard_map/ppermute | solution.py:30
  21.7 2.4 %collective-permute-done.3 = f32[1,129,128]{2,1,0:T(8,128)S(1)} collective-permute-done((f32[1,129,128]{2,1,0:T(8,128)S(1)}, f32[1,129,128]{2,1,0:T(8,128)S(1)}, u32[]{:S(2)}, u32[]{:S(2)}) %collective-permute-start.3) | collective-permute-done | bytes 66080 | tf_op jit(solution)/shard_map/ppermute | solution.py:30
  24.1 5.9 %collective-permute-start.4 = (f32[1,129,128]{2,1,0:T(8,128)S(1)}, f32[1,129,128]{2,1,0:T(8,128)S(1)}, u32[]{:S(2)}, u32[]{:S(2)}) collective-permute-start(f32[1,129,128]{2,1,0:T(8,128)S(1)} %pad_maximum_fusion.7), channel_id=1, source_target_pairs={{0,64},{32,96},{64,128},{96,160},{128,192},{160,224},{1,65},{33,97... | collective-permute-start | bytes 198152 | tf_op jit(solution)/shard_map/ppermute | solution.py:30
  32.0 8.6 %collective-permute-start.5 = (f32[1,129,128]{2,1,0:T(8,128)S(1)}, f32[1,129,128]{2,1,0:T(8,128)S(1)}, u32[]{:S(2)}, u32[]{:S(2)}) collective-permute-start(f32[1,129,128]{2,1,0:T(8,128)S(1)} %pad_maximum_fusion.8), channel_id=1, source_target_pairs={{0,128},{32,160},{64,192},{96,224},{1,129},{33,161},{65,193},{97,2... | collective-permute-start | bytes 198152 | tf_op jit(solution)/shard_map/ppermute | solution.py:30
  40.7 1.5 %convolution_bitcast_fusion.9 = f32[4,128,4,128]{1,3,2,0:T(8,128)} fusion(bf16[4,4,128,128]{3,2,1,0:T(8,128)(2,1)S(1)} %fusion.13, bf16[4,128,4,128]{3,2,1,0:T(4,128)(2,1)S(1)} %reshape.471), kind=kOutput, calls=%fused_computation.24 | convolution fusion | flops 67108864 | bytes 2097152 | tf_op jit(solution)/shard_map/nhij,njhd->nihd/dot_general | solution.py:139
  44.0 1.5 %copy.149 = f32[4,128,4,128]{1,3,2,0:T(8,128)S(1)} copy(f32[4,128,4,128]{3,2,1,0:T(4,128)} %reshape.472) | data formatting | bytes 2097152 | tf_op jit(solution)/shard_map/convert_element_type | solution.py:165
  46.4 3.5 %collective-permute-start.7 = (f32[128,128]{1,0:T(8,128)S(1)}, f32[128,128]{1,0:T(8,128)S(1)}, u32[]{:S(2)}, u32[]{:S(2)}) collective-permute-start(f32[128,128]{1,0:T(8,128)S(1)} %get-tuple-element.55), channel_id=1, source_target_pairs={{0,16},{8,24},{16,0},{24,8},{1,17},{9,25},{17,1},{25,9},{2,18},{10... | collective-permute-start | bytes 196616 | tf_op jit(solution)/shard_map/ppermute | solution.py:62
  51.2 1.6 %collective-permute-done.7 = f32[128,128]{1,0:T(8,128)S(1)} collective-permute-done((f32[128,128]{1,0:T(8,128)S(1)}, f32[128,128]{1,0:T(8,128)S(1)}, u32[]{:S(2)}, u32[]{:S(2)}) %collective-permute-start.7) | collective-permute-done | bytes 65568 | tf_op jit(solution)/shard_map/ppermute | solution.py:62
  54.8 4.0 %fusion.14 = bf16[4,4,128,128]{3,0,2,1:T(4,128)(2,1)S(1)} fusion(f32[4,4,128,128]{3,2,1,0:T(8,128)} %copy-done.1, f32[4,128,128]{2,1,0:T(8,128)S(1)} %broadcast_select_fusion.3, f32[4,4]{0,1:T(4,128)S(1)} %copy.146, f32[4,4]{1,0:T(4,128)S(1)} %fusion.81, f32[4,4]{0,1:T(4,128)S(1)} %copy.144, f32[4,4]{0,1:T(4,128)S(1)} %copy.143, f32[4,4]{0,1:T(4,128)S(1)} %copy.142), kind=kOutput, calls=%fused_computation.30 | convolution fusion | flops 13369600 | bytes 1835328 | tf_op jit(solution)/shard_map/nmh,mhde->nhde/dot_general | solution.py:151
  60.9 4.5 %all-to-all-start = ((f32[8,2,4,128]{3,2,1,0:T(4,128)}), f32[8,2,4,128]{3,2,1,0:T(4,128)S(1)}, u32[]{:S(2)}, u32[]{:S(2)}) async-start(f32[8,2,4,128]{3,2,1,0:T(4,128)} %broadcast_in_dim.17), calls=%async_computation | async-start | bytes 65536 | tf_op jit(solution)/shard_map/all_to_all | solution.py:110
  65.6 5.3 %all-to-all-done = f32[8,2,4,128]{3,2,1,0:T(4,128)S(1)} async-done(((f32[8,2,4,128]{3,2,1,0:T(4,128)}), f32[8,2,4,128]{3,2,1,0:T(4,128)S(1)}, u32[]{:S(2)}, u32[]{:S(2)}) %all-to-all-start) | async-done | bytes 32800 | tf_op jit(solution)/shard_map/all_to_all | solution.py:110
  72.8 2.4 %fusion.17 = f32[4,1,128,128]{3,1,2,0:T(1,128)S(1)} fusion(f32[4,4,1,1]{0,2,3,1:T(1,128)S(1)} %copy.185, f32[4,4,128,128]{3,2,1,0:T(8,128)S(1)} %fusion.24), kind=kOutput, calls=%fused_computation.39 | convolution fusion | flops 3145728 | bytes 1310784 | tf_op jit(solution)/shard_map/mh,mhde->hde/dot_general | solution.py:202
  75.3 2.9 %collective-permute-start.10 = (f32[129,128]{1,0:T(8,128)S(1)}, f32[129,128]{1,0:T(8,128)S(1)}, u32[]{:S(2)}, u32[]{:S(2)}) collective-permute-start(f32[129,128]{1,0:T(8,128)S(1)} %get-tuple-element.41), channel_id=1, source_target_pairs={{0,16},{8,24},{16,0},{24,8},{1,17},{9,25},{17,1},{25,9},{2,18},{10... | collective-permute-start | bytes 198152 | tf_op jit(solution)/shard_map/ppermute | solution.py:62
  83.2 1.5 %gather_fusion.2 = f32[4,129,128]{2,1,0:T(8,128)S(1)} fusion(f32[4,129,128]{2,1,0:T(8,128)} %pad_maximum_fusion.1, s32[1024]{0:T(1024)S(1)} %pad_clamp_fusion), kind=kCustom, calls=%fused_computation.2.clone | custom fusion | bytes 528400 | tf_op jit(solution)/shard_map/jit(_take)/gather | solution.py:65
  84.9 4.1 %collective-permute-start.12 = (f32[1,129,128]{2,1,0:T(8,128)S(1)}, f32[1,129,128]{2,1,0:T(8,128)S(1)}, u32[]{:S(2)}, u32[]{:S(2)}) collective-permute-start(f32[1,129,128]{2,1,0:T(8,128)S(1)} %pad_maximum_fusion.9), channel_id=1, source_target_pairs={{32,0},{64,32},{96,64},{128,96},{160,128},{192,160},{224,192},{33,... | collective-permute-start | bytes 198152 | tf_op jit(solution)/shard_map/ppermute | solution.py:46
  89.6 1.5 %collective-permute-done.12 = f32[1,129,128]{2,1,0:T(8,128)S(1)} collective-permute-done((f32[1,129,128]{2,1,0:T(8,128)S(1)}, f32[1,129,128]{2,1,0:T(8,128)S(1)}, u32[]{:S(2)}, u32[]{:S(2)}) %collective-permute-start.12) | collective-permute-done | bytes 66080 | tf_op jit(solution)/shard_map/ppermute | solution.py:46
  93.6 4.7 %collective-permute-done.13 = f32[1,129,128]{2,1,0:T(8,128)S(1)} collective-permute-done((f32[1,129,128]{2,1,0:T(8,128)S(1)}, f32[1,129,128]{2,1,0:T(8,128)S(1)}, u32[]{:S(2)}, u32[]{:S(2)}) %collective-permute-start.13) | collective-permute-done | bytes 66080 | tf_op jit(solution)/shard_map/ppermute | solution.py:46
  99.6 1.5 %convolution_bitcast_fusion.4 = f32[4,128,4,128]{3,1,2,0:T(8,128)} fusion(bf16[4,4,128,128]{3,2,1,0:T(8,128)(2,1)S(1)} %copy-done.9, bf16[4,128,4,128]{1,3,2,0:T(8,128)(2,1)S(1)} %copy.161), kind=kOutput, calls=%fused_computation.13 | convolution fusion | flops 67108864 | bytes 2097152 | tf_op jit(solution)/shard_map/nhij,nihd->njhd/dot_general | solution.py:186
  101.1 7.3 %collective-permute-done.14 = f32[1,129,128]{2,1,0:T(8,128)S(1)} collective-permute-done((f32[1,129,128]{2,1,0:T(8,128)S(1)}, f32[1,129,128]{2,1,0:T(8,128)S(1)}, u32[]{:S(2)}, u32[]{:S(2)}) %collective-permute-start.14) | collective-permute-done | bytes 66080 | tf_op jit(solution)/shard_map/ppermute | solution.py:46
  109.8 2.9 %collective-permute-start.16 = (f32[128,128]{1,0:T(8,128)S(1)}, f32[128,128]{1,0:T(8,128)}, u32[]{:S(2)}, u32[]{:S(2)}) collective-permute-start(f32[128,128]{1,0:T(8,128)S(1)} %get-tuple-element.49), channel_id=1, source_target_pairs={{0,16},{8,24},{16,0},{24,8},{1,17},{9,25},{17,1},{25,9},{2,18},{10... | collective-permute-start | bytes 196616 | tf_op jit(solution)/shard_map/ppermute | solution.py:62
  118.7 2.6 %fusion.16 = bf16[4,4,128,128]{3,0,2,1:T(4,128)(2,1)S(1)} fusion(f32[4,4,128,128]{3,2,1,0:T(8,128)S(1)} %fusion.24, f32[4,128,128]{2,1,0:T(8,128)S(1)} %broadcast_select_fusion.2, f32[4,4]{0,1:T(4,128)S(1)} %copy.165, f32[4,4]{1,0:T(4,128)S(1)} %fusion.82, f32[4,4]{0,1:T(4,128)S(1)} %copy.144, f32[4,4]{0,1:T(4,128)S(1)} %copy.143, f32[4,4]{0,1:T(4,128)S(1)} %copy.142), kind=kOutput, calls=%fused_computation.32 | convolution fusion | flops 13369600 | bytes 1835328 | tf_op jit(solution)/shard_map/nmh,mhde->nhde/dot_general | solution.py:201
  (145 shorter events, 44.1 us)
Async XLA Ops:
  8.3 6.0 %copy-start.13 = (bf16[512,512]{1,0:T(8,128)(2,1)S(1)}, bf16[512,512]{1,0:T(8,128)(2,1)}, u32[]{:S(2)}) copy-start(bf16[512,512]{1,0:T(8,128)(2,1)} %param.9) | copy-start | bytes 1572868
  8.5 6.3 %collective-permute-start = (f32[129,128]{1,0:T(8,128)S(1)}, f32[129,128]{1,0:T(8,128)S(1)}, u32[]{:S(2)}, u32[]{:S(2)}) collective-permute-start(f32[129,128]{1,0:T(8,128)S(1)} %get-tuple-element.45), channel_id=1, source_target_pairs={{0,8},{8,16},{16,24},{24,0},{1,9},{9,17},{17,25},{25,1},{2,10},{10... | collective-permute-start | bytes 198152 | tf_op jit(solution)/shard_map/ppermute | solution.py:62
  10.0 6.1 %collective-permute-start.1 = (f32[129,128]{1,0:T(8,128)S(1)}, f32[129,128]{1,0:T(8,128)S(1)}, u32[]{:S(2)}, u32[]{:S(2)}) collective-permute-start(f32[129,128]{1,0:T(8,128)S(1)} %get-tuple-element.44), channel_id=1, source_target_pairs={{0,16},{8,24},{16,0},{24,8},{1,17},{9,25},{17,1},{25,9},{2,18},{10... | collective-permute-start | bytes 198152 | tf_op jit(solution)/shard_map/ppermute | solution.py:62
  12.8 4.3 %collective-permute-start.2 = (f32[129,128]{1,0:T(8,128)S(1)}, f32[129,128]{1,0:T(8,128)S(1)}, u32[]{:S(2)}, u32[]{:S(2)}) collective-permute-start(f32[129,128]{1,0:T(8,128)S(1)} %get-tuple-element.46), channel_id=1, source_target_pairs={{0,24},{8,0},{16,8},{24,16},{1,25},{9,1},{17,9},{25,17},{2,26},{10... | collective-permute-start | bytes 198152 | tf_op jit(solution)/shard_map/ppermute | solution.py:62
  17.8 6.2 %collective-permute-start.3 = (f32[1,129,128]{2,1,0:T(8,128)S(1)}, f32[1,129,128]{2,1,0:T(8,128)S(1)}, u32[]{:S(2)}, u32[]{:S(2)}) collective-permute-start(f32[1,129,128]{2,1,0:T(8,128)S(1)} %pad_maximum_fusion.6), channel_id=1, source_target_pairs={{0,32},{32,64},{64,96},{96,128},{128,160},{160,192},{192,224},{1,3... | collective-permute-start | bytes 198152 | tf_op jit(solution)/shard_map/ppermute | solution.py:30
  24.1 7.9 %collective-permute-start.4 = (f32[1,129,128]{2,1,0:T(8,128)S(1)}, f32[1,129,128]{2,1,0:T(8,128)S(1)}, u32[]{:S(2)}, u32[]{:S(2)}) collective-permute-start(f32[1,129,128]{2,1,0:T(8,128)S(1)} %pad_maximum_fusion.7), channel_id=1, source_target_pairs={{0,64},{32,96},{64,128},{96,160},{128,192},{160,224},{1,65},{33,97... | collective-permute-start | bytes 198152 | tf_op jit(solution)/shard_map/ppermute | solution.py:30
  30.6 10.0 %copy-start.7 = (bf16[4,4,128,128]{3,2,1,0:T(8,128)(2,1)}, bf16[4,4,128,128]{3,2,1,0:T(8,128)(2,1)S(1)}, u32[]{:S(2)}) copy-start(bf16[4,4,128,128]{3,2,1,0:T(8,128)(2,1)S(1)} %fusion.13) | copy-start | bytes 1572868
  32.0 13.5 %collective-permute-start.5 = (f32[1,129,128]{2,1,0:T(8,128)S(1)}, f32[1,129,128]{2,1,0:T(8,128)S(1)}, u32[]{:S(2)}, u32[]{:S(2)}) collective-permute-start(f32[1,129,128]{2,1,0:T(8,128)S(1)} %pad_maximum_fusion.8), channel_id=1, source_target_pairs={{0,128},{32,160},{64,192},{96,224},{1,129},{33,161},{65,193},{97,2... | collective-permute-start | bytes 198152 | tf_op jit(solution)/shard_map/ppermute | solution.py:30
  45.7 5.6 %collective-permute-start.6 = (f32[128,128]{1,0:T(8,128)S(1)}, f32[128,128]{1,0:T(8,128)S(1)}, u32[]{:S(2)}, u32[]{:S(2)}) collective-permute-start(f32[128,128]{1,0:T(8,128)S(1)} %get-tuple-element.56), channel_id=1, source_target_pairs={{0,8},{8,16},{16,24},{24,0},{1,9},{9,17},{17,25},{25,1},{2,10},{10... | collective-permute-start | bytes 196616 | tf_op jit(solution)/shard_map/ppermute | solution.py:62
  46.4 6.4 %collective-permute-start.7 = (f32[128,128]{1,0:T(8,128)S(1)}, f32[128,128]{1,0:T(8,128)S(1)}, u32[]{:S(2)}, u32[]{:S(2)}) collective-permute-start(f32[128,128]{1,0:T(8,128)S(1)} %get-tuple-element.55), channel_id=1, source_target_pairs={{0,16},{8,24},{16,0},{24,8},{1,17},{9,25},{17,1},{25,9},{2,18},{10... | collective-permute-start | bytes 196616 | tf_op jit(solution)/shard_map/ppermute | solution.py:62
  49.9 4.3 %collective-permute-start.8 = (f32[128,128]{1,0:T(8,128)S(1)}, f32[128,128]{1,0:T(8,128)S(1)}, u32[]{:S(2)}, u32[]{:S(2)}) collective-permute-start(f32[128,128]{1,0:T(8,128)S(1)} %get-tuple-element.54), channel_id=1, source_target_pairs={{0,24},{8,0},{16,8},{24,16},{1,25},{9,1},{17,9},{25,17},{2,26},{10... | collective-permute-start | bytes 196616 | tf_op jit(solution)/shard_map/ppermute | solution.py:62
  54.8 4.0 %copy-start = (f32[4,128,4,128]{1,3,2,0:T(8,128)S(1)}, f32[4,128,4,128]{1,3,2,0:T(8,128)}, u32[]{:S(2)}) copy-start(f32[4,128,4,128]{1,3,2,0:T(8,128)} %convolution_bitcast_fusion.9) | copy-start | bytes 3145732
  60.9 9.9 %all-to-all-start = ((f32[8,2,4,128]{3,2,1,0:T(4,128)}), f32[8,2,4,128]{3,2,1,0:T(4,128)S(1)}, u32[]{:S(2)}, u32[]{:S(2)}) async-start(f32[8,2,4,128]{3,2,1,0:T(4,128)} %broadcast_in_dim.17), calls=%async_computation | async-start | bytes 65536 | tf_op jit(solution)/shard_map/all_to_all | solution.py:110
  75.2 6.6 %collective-permute-start.9 = (f32[129,128]{1,0:T(8,128)S(1)}, f32[129,128]{1,0:T(8,128)S(1)}, u32[]{:S(2)}, u32[]{:S(2)}) collective-permute-start(f32[129,128]{1,0:T(8,128)S(1)} %get-tuple-element.40), channel_id=1, source_target_pairs={{0,8},{8,16},{16,24},{24,0},{1,9},{9,17},{17,25},{25,1},{2,10},{10... | collective-permute-start | bytes 198152 | tf_op jit(solution)/shard_map/ppermute | solution.py:62
  75.3 6.6 %collective-permute-start.10 = (f32[129,128]{1,0:T(8,128)S(1)}, f32[129,128]{1,0:T(8,128)S(1)}, u32[]{:S(2)}, u32[]{:S(2)}) collective-permute-start(f32[129,128]{1,0:T(8,128)S(1)} %get-tuple-element.41), channel_id=1, source_target_pairs={{0,16},{8,24},{16,0},{24,8},{1,17},{9,25},{17,1},{25,9},{2,18},{10... | collective-permute-start | bytes 198152 | tf_op jit(solution)/shard_map/ppermute | solution.py:62
  78.2 4.3 %collective-permute-start.11 = (f32[129,128]{1,0:T(8,128)S(1)}, f32[129,128]{1,0:T(8,128)S(1)}, u32[]{:S(2)}, u32[]{:S(2)}) collective-permute-start(f32[129,128]{1,0:T(8,128)S(1)} %get-tuple-element.42), channel_id=1, source_target_pairs={{0,24},{8,0},{16,8},{24,16},{1,25},{9,1},{17,9},{25,17},{2,26},{10... | collective-permute-start | bytes 198152 | tf_op jit(solution)/shard_map/ppermute | solution.py:62
  84.7 4.3 %copy-start.9 = (bf16[4,4,128,128]{3,2,1,0:T(8,128)(2,1)S(1)}, bf16[4,4,128,128]{3,2,1,0:T(8,128)(2,1)}, u32[]{:S(2)}) copy-start(bf16[4,4,128,128]{3,2,1,0:T(8,128)(2,1)} %fusion.15) | copy-start | bytes 1572868
  84.9 6.2 %collective-permute-start.12 = (f32[1,129,128]{2,1,0:T(8,128)S(1)}, f32[1,129,128]{2,1,0:T(8,128)S(1)}, u32[]{:S(2)}, u32[]{:S(2)}) collective-permute-start(f32[1,129,128]{2,1,0:T(8,128)S(1)} %pad_maximum_fusion.9), channel_id=1, source_target_pairs={{32,0},{64,32},{96,64},{128,96},{160,128},{192,160},{224,192},{33,... | collective-permute-start | bytes 198152 | tf_op jit(solution)/shard_map/ppermute | solution.py:46
  91.2 7.1 %collective-permute-start.13 = (f32[1,129,128]{2,1,0:T(8,128)S(1)}, f32[1,129,128]{2,1,0:T(8,128)S(1)}, u32[]{:S(2)}, u32[]{:S(2)}) collective-permute-start(f32[1,129,128]{2,1,0:T(8,128)S(1)} %pad_maximum_fusion.10), channel_id=1, source_target_pairs={{64,0},{96,32},{128,64},{160,96},{192,128},{224,160},{65,1},{97,33... | collective-permute-start | bytes 198152 | tf_op jit(solution)/shard_map/ppermute | solution.py:46
  98.3 10.1 %collective-permute-start.14 = (f32[1,129,128]{2,1,0:T(8,128)S(1)}, f32[1,129,128]{2,1,0:T(8,128)S(1)}, u32[]{:S(2)}, u32[]{:S(2)}) collective-permute-start(f32[1,129,128]{2,1,0:T(8,128)S(1)} %pad_maximum_fusion.11), channel_id=1, source_target_pairs={{128,0},{160,32},{192,64},{224,96},{129,1},{161,33},{193,65},{225,... | collective-permute-start | bytes 198152 | tf_op jit(solution)/shard_map/ppermute | solution.py:46
  108.5 4.3 %copy-start.8 = (bf16[4,4,128,128]{3,2,1,0:T(8,128)(2,1)S(1)}, bf16[4,4,128,128]{3,2,1,0:T(8,128)(2,1)}, u32[]{:S(2)}) copy-start(bf16[4,4,128,128]{3,2,1,0:T(8,128)(2,1)} %copy-done.7) | copy-start | bytes 1572868
  108.6 6.9 %collective-permute-start.15 = (f32[128,128]{1,0:T(8,128)S(1)}, f32[128,128]{1,0:T(8,128)S(1)}, u32[]{:S(2)}, u32[]{:S(2)}) collective-permute-start(f32[128,128]{1,0:T(8,128)S(1)} %get-tuple-element.50), channel_id=1, source_target_pairs={{0,8},{8,16},{16,24},{24,0},{1,9},{9,17},{17,25},{25,1},{2,10},{10... | collective-permute-start | bytes 196616 | tf_op jit(solution)/shard_map/ppermute | solution.py:62
  109.8 5.9 %collective-permute-start.16 = (f32[128,128]{1,0:T(8,128)S(1)}, f32[128,128]{1,0:T(8,128)}, u32[]{:S(2)}, u32[]{:S(2)}) collective-permute-start(f32[128,128]{1,0:T(8,128)S(1)} %get-tuple-element.49), channel_id=1, source_target_pairs={{0,16},{8,24},{16,0},{24,8},{1,17},{9,25},{17,1},{25,9},{2,18},{10... | collective-permute-start | bytes 196616 | tf_op jit(solution)/shard_map/ppermute | solution.py:62
  112.7 4.4 %collective-permute-start.17 = (f32[128,128]{1,0:T(8,128)S(1)}, f32[128,128]{1,0:T(8,128)}, u32[]{:S(2)}, u32[]{:S(2)}) collective-permute-start(f32[128,128]{1,0:T(8,128)S(1)} %get-tuple-element.48), channel_id=1, source_target_pairs={{0,24},{8,0},{16,8},{24,16},{1,25},{9,1},{17,9},{25,17},{2,26},{10... | collective-permute-start | bytes 196616 | tf_op jit(solution)/shard_map/ppermute | solution.py:62
  (10 other events, 14.6 us)

commit v5 on v4

--- a/solution.py
+++ b/solution.py
@@ -21,35 +21,51 @@
     return payload[:, -1:, :], payload[:, :-1, :]
 
 
+def radix_shifts(ranks):
+    rounds, width = [], 1
+    while width < ranks:
+        rounds.append([s for s in (width, 2 * width) if s < ranks])
+        width *= 3
+    return rounds
+
+
 def forward_scan(total, state, axis, ranks):
     win_a, win_b = total, state
     excl_a, excl_b = jnp.zeros_like(total), jnp.zeros_like(state)
-    shift = 1
-    while shift < ranks:
-        pairs = [(i, i + shift) for i in range(ranks - shift)]
-        got_a, got_b = unpack(lax.ppermute(pack(win_a, win_b), axis, pairs))
-        excl_b = jnp.exp(excl_a) * got_b + excl_b
-        excl_a = excl_a + got_a
-        if 2 * shift < ranks:
-            win_b = jnp.exp(win_a) * got_b + win_b
-            win_a = win_a + got_a
-        shift *= 2
+    rounds = radix_shifts(ranks)
+    for step, shifts in enumerate(rounds):
+        payload = pack(win_a, win_b)
+        got = [
+            unpack(lax.ppermute(payload, axis, [(i, i + s) for i in range(ranks - s)]))
+            for s in shifts
+        ]
+        last = step == len(rounds) - 1
+        for got_a, got_b in got:
+            excl_b = jnp.exp(excl_a) * got_b + excl_b
+            excl_a = excl_a + got_a
+            if not last:
+                win_b = jnp.exp(win_a) * got_b + win_b
+                win_a = win_a + got_a
     return excl_b
 
 
 def backward_scan(total, state, axis, ranks):
     win_a, win_c = total, state
     excl_a, excl_c = jnp.zeros_like(total), jnp.zeros_like(state)
-    shift = 1
-    while shift < ranks:
-        pairs = [(i + shift, i) for i in range(ranks - shift)]
-        got_a, got_c = unpack(lax.ppermute(pack(win_a, win_c), axis, pairs))
-        excl_c = excl_c + jnp.exp(excl_a) * got_c
-        excl_a = excl_a + got_a
-        if 2 * shift < ranks:
-            win_c = win_c + jnp.exp(win_a) * got_c
-            win_a = win_a + got_a
-        shift *= 2
+    rounds = radix_shifts(ranks)
+    for step, shifts in enumerate(rounds):
+        payload = pack(win_a, win_c)
+        got = [
+            unpack(lax.ppermute(payload, axis, [(i + s, i) for i in range(ranks - s)]))
+            for s in shifts
+        ]
+        last = step == len(rounds) - 1
+        for got_a, got_c in got:
+            excl_c = excl_c + jnp.exp(excl_a) * got_c
+            excl_a = excl_a + got_a
+            if not last:
+                win_c = win_c + jnp.exp(win_a) * got_c
+                win_a = win_a + got_a
     return excl_c
 
 

time: 128 us -> 126 us (0.984)
  waiting for transfers between devices: 32.1 us -> 29.4 us
  matrix products: 23.2 us -> 24.5 us
    ppermute x6 -> x8, waiting for transfers between devices: 17.2 us -> 15.3 us  [the longest x4 12.1 us: backward_scan(): lax.ppermute(payload, axis, [(i + s, i) for i in range(ranks - s)])]
    ppermute x6 -> x8, starting transfers between devices: 25.1 us -> 25 us  [the longest x4 19.1 us: forward_scan(): lax.ppermute(payload, axis, [(i, i + s) for i in range(ranks - s)])]
    unnamed x31 -> x35, local copies, waits for them, and re-layouts: 5.83 us -> 5.83 us
  transfers between devices with their start and end apart: 19 -> 21, of which waited for: 15 -> 16; matrix products, arithmetic and copies ran while one was open for 11% -> 12% of each run, Pallas kernels for 0% -> 0%
where the time goes in v5:
time: 126 us; the launch traced here: 125 us
  starting transfers between devices  48 us (38%)
  waiting for transfers between devices  29.4 us (23%)
  matrix products  24.5 us (19%)
  local copies, waits for them, and re-layouts  17.1 us (14%)
  other arithmetic  4.98 us (4%)
  between operations  1.35 us (1%)
    ppermute x4, starting transfers between devices, forward_scan(): lax.ppermute(payload, axis, [(i, i + s) for i in range(ranks - s)])  19.1 us
    ppermute x12, starting transfers between devices, exchange(): got.append(lax.ppermute(send, axis, pairs))  18.5 us
    ppermute x4, waiting for transfers between devices, backward_scan(): lax.ppermute(payload, axis, [(i + s, i) for i in range(ranks - s)])  12.1 us
    ppermute x12, waiting for transfers between devices, exchange(): got.append(lax.ppermute(send, axis, pairs))  8.9 us
    ppermute x4, starting transfers between devices, backward_scan(): lax.ppermute(payload, axis, [(i + s, i) for i in range(ranks - s)])  5.92 us
    unnamed x35, local copies, waits for them, and re-layouts  5.83 us
    all_to_all x1, waiting for transfers between devices, head_sum(): gathered = lax.all_to_all(copies, 'head', 0, 0, tiled=True)  5.25 us
    all_to_all x1, starting transfers between devices, head_sum(): gathered = lax.all_to_all(copies, 'head', 0, 0, tiled=True)  4.47 us
  transfers between devices with their start and end apart: 21, of which 16 were waited for; matrix products, arithmetic and copies ran while one was open for 12% of the time, Pallas kernels for 0%

profile of v5, /device:TPU:32, one launch (start us, length us, event | category | flops | bytes accessed | tf_op | source)
XLA Modules:
  0.0 125.4 jit_solution(2284167692956557366)
XLA Ops:
  6.0 2.4 %fusion.20 = f32[4,1,128,128]{3,1,2,0:T(1,128)S(1)} fusion(f32[4,4,1,1]{0,2,3,1:T(1,128)S(1)} %copy.177, f32[4,4,128,128]{3,2,1,0:T(8,128)S(1)} %fusion.23), kind=kOutput, calls=%fused_computation.42 | convolution fusion | flops 3145728 | bytes 1310784 | tf_op jit(solution)/shard_map/mh,mhde->hde/dot_general | solution.py:168
  8.5 1.6 %collective-permute-start = (f32[129,128]{1,0:T(8,128)S(1)}, f32[129,128]{1,0:T(8,128)S(1)}, u32[]{:S(2)}, u32[]{:S(2)}) collective-permute-start(f32[129,128]{1,0:T(8,128)S(1)} %get-tuple-element.41), channel_id=1, source_target_pairs={{0,8},{8,16},{16,24},{24,0},{1,9},{9,17},{17,25},{25,1},{2,10},{10... | collective-permute-start | bytes 198152 | tf_op jit(solution)/shard_map/ppermute | solution.py:78
  10.0 2.7 %collective-permute-start.1 = (f32[129,128]{1,0:T(8,128)S(1)}, f32[129,128]{1,0:T(8,128)S(1)}, u32[]{:S(2)}, u32[]{:S(2)}) collective-permute-start(f32[129,128]{1,0:T(8,128)S(1)} %get-tuple-element.40), channel_id=1, source_target_pairs={{0,16},{8,24},{16,0},{24,8},{1,17},{9,25},{17,1},{25,9},{2,18},{10... | collective-permute-start | bytes 198152 | tf_op jit(solution)/shard_map/ppermute | solution.py:78
  17.9 3.8 %collective-permute-start.3 = (f32[1,129,128]{2,1,0:T(8,128)S(1)}, f32[1,129,128]{2,1,0:T(8,128)S(1)}, u32[]{:S(2)}, u32[]{:S(2)}) collective-permute-start(f32[1,129,128]{2,1,0:T(8,128)S(1)} %pad_maximum_fusion.6), channel_id=1, source_target_pairs={{0,32},{32,64},{64,96},{96,128},{128,160},{160,192},{192,224},{1,3... | collective-permute-start | bytes 198152 | tf_op jit(solution)/shard_map/ppermute | solution.py:39
  21.7 6.4 %collective-permute-start.4 = (f32[1,129,128]{2,1,0:T(8,128)S(1)}, f32[1,129,128]{2,1,0:T(8,128)S(1)}, u32[]{:S(2)}, u32[]{:S(2)}) collective-permute-start(f32[1,129,128]{2,1,0:T(8,128)S(1)} %pad_maximum_fusion.6), channel_id=1, source_target_pairs={{0,64},{32,96},{64,128},{96,160},{128,192},{160,224},{1,65},{33,97... | collective-permute-start | bytes 198152 | tf_op jit(solution)/shard_map/ppermute | solution.py:39
  30.1 7.6 %collective-permute-start.5 = (f32[1,129,128]{2,1,0:T(8,128)S(1)}, f32[1,129,128]{2,1,0:T(8,128)S(1)}, u32[]{:S(2)}, u32[]{:S(2)}) collective-permute-start(f32[1,129,128]{2,1,0:T(8,128)S(1)} %pad_maximum_fusion.7), channel_id=1, source_target_pairs={{0,96},{32,128},{64,160},{96,192},{128,224},{1,97},{33,129},{65,16... | collective-permute-start | bytes 198152 | tf_op jit(solution)/shard_map/ppermute | solution.py:39
  41.0 1.5 %copy.149 = f32[4,128,4,128]{1,3,2,0:T(8,128)S(1)} copy(f32[4,128,4,128]{3,2,1,0:T(4,128)} %reshape.476) | data formatting | bytes 2097152 | tf_op jit(solution)/shard_map/convert_element_type | solution.py:181
  43.9 1.9 %collective-permute-done.6 = f32[1,129,128]{2,1,0:T(8,128)S(1)} collective-permute-done((f32[1,129,128]{2,1,0:T(8,128)S(1)}, f32[1,129,128]{2,1,0:T(8,128)S(1)}, u32[]{:S(2)}, u32[]{:S(2)}) %collective-permute-start.6) | collective-permute-done | bytes 66080 | tf_op jit(solution)/shard_map/ppermute | solution.py:39
  46.6 3.5 %collective-permute-start.8 = (f32[128,128]{1,0:T(8,128)S(1)}, f32[128,128]{1,0:T(8,128)S(1)}, u32[]{:S(2)}, u32[]{:S(2)}) collective-permute-start(f32[128,128]{1,0:T(8,128)S(1)} %get-tuple-element.51), channel_id=1, source_target_pairs={{0,16},{8,24},{16,0},{24,8},{1,17},{9,25},{17,1},{25,9},{2,18},{10... | collective-permute-start | bytes 196616 | tf_op jit(solution)/shard_map/ppermute | solution.py:78
  51.5 1.6 %collective-permute-done.8 = f32[128,128]{1,0:T(8,128)S(1)} collective-permute-done((f32[128,128]{1,0:T(8,128)S(1)}, f32[128,128]{1,0:T(8,128)S(1)}, u32[]{:S(2)}, u32[]{:S(2)}) %collective-permute-start.8) | collective-permute-done | bytes 65568 | tf_op jit(solution)/shard_map/ppermute | solution.py:78
  55.1 4.0 %fusion.14 = bf16[4,4,128,128]{3,0,2,1:T(4,128)(2,1)S(1)} fusion(f32[4,4,128,128]{3,2,1,0:T(8,128)} %copy-done.1, f32[4,128,128]{2,1,0:T(8,128)S(1)} %broadcast_select_fusion.3, f32[4,4]{0,1:T(4,128)S(1)} %copy.146, f32[4,4]{1,0:T(4,128)S(1)} %fusion.83, f32[4,4]{0,1:T(4,128)S(1)} %copy.144, f32[4,4]{0,1:T(4,128)S(1)} %copy.143, f32[4,4]{0,1:T(4,128)S(1)} %copy.142), kind=kOutput, calls=%fused_computation.30 | convolution fusion | flops 13369600 | bytes 1835328 | tf_op jit(solution)/shard_map/nmh,mhde->nhde/dot_general | solution.py:167
  61.2 4.5 %all-to-all-start = ((f32[8,2,4,128]{3,2,1,0:T(4,128)}), f32[8,2,4,128]{3,2,1,0:T(4,128)S(1)}, u32[]{:S(2)}, u32[]{:S(2)}) async-start(f32[8,2,4,128]{3,2,1,0:T(4,128)} %broadcast_in_dim.17), calls=%async_computation | async-start | bytes 65536 | tf_op jit(solution)/shard_map/all_to_all | solution.py:126
  65.8 5.3 %all-to-all-done = f32[8,2,4,128]{3,2,1,0:T(4,128)S(1)} async-done(((f32[8,2,4,128]{3,2,1,0:T(4,128)}), f32[8,2,4,128]{3,2,1,0:T(4,128)S(1)}, u32[]{:S(2)}, u32[]{:S(2)}) %all-to-all-start) | async-done | bytes 32800 | tf_op jit(solution)/shard_map/all_to_all | solution.py:126
  73.6 2.4 %fusion.17 = f32[4,1,128,128]{3,1,2,0:T(1,128)S(1)} fusion(f32[4,4,1,1]{0,2,3,1:T(1,128)S(1)} %copy.185, f32[4,4,128,128]{3,2,1,0:T(8,128)S(1)} %fusion.24), kind=kOutput, calls=%fused_computation.39 | convolution fusion | flops 3145728 | bytes 1310784 | tf_op jit(solution)/shard_map/mh,mhde->hde/dot_general | solution.py:218
  76.2 2.9 %collective-permute-start.11 = (f32[129,128]{1,0:T(8,128)S(1)}, f32[129,128]{1,0:T(8,128)S(1)}, u32[]{:S(2)}, u32[]{:S(2)}) collective-permute-start(f32[129,128]{1,0:T(8,128)S(1)} %get-tuple-element.37), channel_id=1, source_target_pairs={{0,16},{8,24},{16,0},{24,8},{1,17},{9,25},{17,1},{25,9},{2,18},{10... | collective-permute-start | bytes 198152 | tf_op jit(solution)/shard_map/ppermute | solution.py:78
  84.1 1.5 %gather_fusion.2 = f32[4,129,128]{2,1,0:T(8,128)S(1)} fusion(f32[4,129,128]{2,1,0:T(8,128)} %pad_maximum_fusion.1, s32[1024]{0:T(1024)S(1)} %pad_clamp_fusion), kind=kCustom, calls=%fused_computation.2.clone | custom fusion | bytes 528400 | tf_op jit(solution)/shard_map/jit(_take)/gather | solution.py:81
  85.8 2.1 %collective-permute-start.13 = (f32[1,129,128]{2,1,0:T(8,128)S(1)}, f32[1,129,128]{2,1,0:T(8,128)S(1)}, u32[]{:S(2)}, u32[]{:S(2)}) collective-permute-start(f32[1,129,128]{2,1,0:T(8,128)S(1)} %pad_maximum_fusion.8), channel_id=1, source_target_pairs={{32,0},{64,32},{96,64},{128,96},{160,128},{192,160},{224,192},{33,... | collective-permute-start | bytes 198152 | tf_op jit(solution)/shard_map/ppermute | solution.py:59
  89.2 2.2 %fusion.10 = bf16[4,128,4,128]{1,3,2,0:T(8,128)(2,1)} fusion(f32[4,128,4,128]{1,3,2,0:T(8,128)S(1)} %copy-done.3, bf16[4,128,4,128]{1,3,2,0:T(8,128)(2,1)S(1)} %multiply_convert_fusion.1, f32[4,128,4]{1,2,0:T(4,128)S(1)} %copy.136, bf16[4,4,128,128]{3,0,2,1:T(4,128)(2,1)} %copy-done.5), kind=kOutput, calls=%fused_computation.26 | convolution fusion | flops 67895296 | bytes 2629632 | tf_op jit(solution)/shard_map/nihe,nhde->nihd/dot_general | solution.py:199
  91.4 1.8 %collective-permute-done.13 = f32[1,129,128]{2,1,0:T(8,128)S(1)} collective-permute-done((f32[1,129,128]{2,1,0:T(8,128)S(1)}, f32[1,129,128]{2,1,0:T(8,128)S(1)}, u32[]{:S(2)}, u32[]{:S(2)}) %collective-permute-start.13) | collective-permute-done | bytes 66080 | tf_op jit(solution)/shard_map/ppermute | solution.py:59
  93.2 2.5 %collective-permute-done.14 = f32[1,129,128]{2,1,0:T(8,128)S(1)} collective-permute-done((f32[1,129,128]{2,1,0:T(8,128)S(1)}, f32[1,129,128]{2,1,0:T(8,128)S(1)}, u32[]{:S(2)}, u32[]{:S(2)}) %collective-permute-start.14) | collective-permute-done | bytes 66080 | tf_op jit(solution)/shard_map/ppermute | solution.py:59
  99.8 5.1 %collective-permute-done.15 = f32[1,129,128]{2,1,0:T(8,128)S(1)} collective-permute-done((f32[1,129,128]{2,1,0:T(8,128)S(1)}, f32[1,129,128]{2,1,0:T(8,128)S(1)}, u32[]{:S(2)}, u32[]{:S(2)}) %collective-permute-start.15) | collective-permute-done | bytes 66080 | tf_op jit(solution)/shard_map/ppermute | solution.py:59
  105.0 2.6 %collective-permute-done.16 = f32[1,129,128]{2,1,0:T(8,128)S(1)} collective-permute-done((f32[1,129,128]{2,1,0:T(8,128)S(1)}, f32[1,129,128]{2,1,0:T(8,128)S(1)}, u32[]{:S(2)}, u32[]{:S(2)}) %collective-permute-start.16) | collective-permute-done | bytes 66080 | tf_op jit(solution)/shard_map/ppermute | solution.py:59
  108.8 3.1 %collective-permute-start.18 = (f32[128,128]{1,0:T(8,128)S(1)}, f32[128,128]{1,0:T(8,128)}, u32[]{:S(2)}, u32[]{:S(2)}) collective-permute-start(f32[128,128]{1,0:T(8,128)S(1)} %get-tuple-element.45), channel_id=1, source_target_pairs={{0,16},{8,24},{16,0},{24,8},{1,17},{9,25},{17,1},{25,9},{2,18},{10... | collective-permute-start | bytes 196616 | tf_op jit(solution)/shard_map/ppermute | solution.py:78
  117.8 2.6 %fusion.16 = bf16[4,4,128,128]{3,0,2,1:T(4,128)(2,1)S(1)} fusion(f32[4,4,128,128]{3,2,1,0:T(8,128)S(1)} %fusion.24, f32[4,128,128]{2,1,0:T(8,128)S(1)} %broadcast_select_fusion.2, f32[4,4]{0,1:T(4,128)S(1)} %copy.165, f32[4,4]{1,0:T(4,128)S(1)} %fusion.84, f32[4,4]{0,1:T(4,128)S(1)} %copy.144, f32[4,4]{0,1:T(4,128)S(1)} %copy.143, f32[4,4]{0,1:T(4,128)S(1)} %copy.142), kind=kOutput, calls=%fused_computation.32 | convolution fusion | flops 13369600 | bytes 1835328 | tf_op jit(solution)/shard_map/nmh,mhde->nhde/dot_general | solution.py:217
  (149 shorter events, 48.5 us)
Async XLA Ops:
  8.5 7.0 %collective-permute-start = (f32[129,128]{1,0:T(8,128)S(1)}, f32[129,128]{1,0:T(8,128)S(1)}, u32[]{:S(2)}, u32[]{:S(2)}) collective-permute-start(f32[129,128]{1,0:T(8,128)S(1)} %get-tuple-element.41), channel_id=1, source_target_pairs={{0,8},{8,16},{16,24},{24,0},{1,9},{9,17},{17,25},{25,1},{2,10},{10... | collective-permute-start | bytes 198152 | tf_op jit(solution)/shard_map/ppermute | solution.py:78
  10.0 6.1 %collective-permute-start.1 = (f32[129,128]{1,0:T(8,128)S(1)}, f32[129,128]{1,0:T(8,128)S(1)}, u32[]{:S(2)}, u32[]{:S(2)}) collective-permute-start(f32[129,128]{1,0:T(8,128)S(1)} %get-tuple-element.40), channel_id=1, source_target_pairs={{0,16},{8,24},{16,0},{24,8},{1,17},{9,25},{17,1},{25,9},{2,18},{10... | collective-permute-start | bytes 198152 | tf_op jit(solution)/shard_map/ppermute | solution.py:78
  12.8 4.3 %collective-permute-start.2 = (f32[129,128]{1,0:T(8,128)S(1)}, f32[129,128]{1,0:T(8,128)S(1)}, u32[]{:S(2)}, u32[]{:S(2)}) collective-permute-start(f32[129,128]{1,0:T(8,128)S(1)} %get-tuple-element.42), channel_id=1, source_target_pairs={{0,24},{8,0},{16,8},{24,16},{1,25},{9,1},{17,9},{25,17},{2,26},{10... | collective-permute-start | bytes 198152 | tf_op jit(solution)/shard_map/ppermute | solution.py:78
  17.8 10.3 %copy-start.15 = (f32[128,128]{1,0:T(8,128)S(1)}, f32[128,128]{1,0:T(8,128)}, u32[]{:S(2)}) copy-start(f32[128,128]{1,0:T(8,128)} %fusion.55) | copy-start | bytes 196612
  17.9 10.9 %collective-permute-start.3 = (f32[1,129,128]{2,1,0:T(8,128)S(1)}, f32[1,129,128]{2,1,0:T(8,128)S(1)}, u32[]{:S(2)}, u32[]{:S(2)}) collective-permute-start(f32[1,129,128]{2,1,0:T(8,128)S(1)} %pad_maximum_fusion.6), channel_id=1, source_target_pairs={{0,32},{32,64},{64,96},{96,128},{128,160},{160,192},{192,224},{1,3... | collective-permute-start | bytes 198152 | tf_op jit(solution)/shard_map/ppermute | solution.py:39
  21.7 8.3 %collective-permute-start.4 = (f32[1,129,128]{2,1,0:T(8,128)S(1)}, f32[1,129,128]{2,1,0:T(8,128)S(1)}, u32[]{:S(2)}, u32[]{:S(2)}) collective-permute-start(f32[1,129,128]{2,1,0:T(8,128)S(1)} %pad_maximum_fusion.6), channel_id=1, source_target_pairs={{0,64},{32,96},{64,128},{96,160},{128,192},{160,224},{1,65},{33,97... | collective-permute-start | bytes 198152 | tf_op jit(solution)/shard_map/ppermute | solution.py:39
  28.7 9.0 %copy-start.7 = (bf16[4,4,128,128]{3,2,1,0:T(8,128)(2,1)}, bf16[4,4,128,128]{3,2,1,0:T(8,128)(2,1)S(1)}, u32[]{:S(2)}) copy-start(bf16[4,4,128,128]{3,2,1,0:T(8,128)(2,1)S(1)} %fusion.13) | copy-start | bytes 1572868
  30.1 13.8 %collective-permute-start.5 = (f32[1,129,128]{2,1,0:T(8,128)S(1)}, f32[1,129,128]{2,1,0:T(8,128)S(1)}, u32[]{:S(2)}, u32[]{:S(2)}) collective-permute-start(f32[1,129,128]{2,1,0:T(8,128)S(1)} %pad_maximum_fusion.7), channel_id=1, source_target_pairs={{0,96},{32,128},{64,160},{96,192},{128,224},{1,97},{33,129},{65,16... | collective-permute-start | bytes 198152 | tf_op jit(solution)/shard_map/ppermute | solution.py:39
  42.6 3.2 %collective-permute-start.6 = (f32[1,129,128]{2,1,0:T(8,128)S(1)}, f32[1,129,128]{2,1,0:T(8,128)S(1)}, u32[]{:S(2)}, u32[]{:S(2)}) collective-permute-start(f32[1,129,128]{2,1,0:T(8,128)S(1)} %pad_maximum_fusion.7), channel_id=1, source_target_pairs={{0,192},{32,224},{1,193},{33,225},{2,194},{34,226},{3,195},{35,227... | collective-permute-start | bytes 198152 | tf_op jit(solution)/shard_map/ppermute | solution.py:39
  45.9 5.6 %collective-permute-start.7 = (f32[128,128]{1,0:T(8,128)S(1)}, f32[128,128]{1,0:T(8,128)S(1)}, u32[]{:S(2)}, u32[]{:S(2)}) collective-permute-start(f32[128,128]{1,0:T(8,128)S(1)} %get-tuple-element.52), channel_id=1, source_target_pairs={{0,8},{8,16},{16,24},{24,0},{1,9},{9,17},{17,25},{25,1},{2,10},{10... | collective-permute-start | bytes 196616 | tf_op jit(solution)/shard_map/ppermute | solution.py:78
  46.6 6.4 %collective-permute-start.8 = (f32[128,128]{1,0:T(8,128)S(1)}, f32[128,128]{1,0:T(8,128)S(1)}, u32[]{:S(2)}, u32[]{:S(2)}) collective-permute-start(f32[128,128]{1,0:T(8,128)S(1)} %get-tuple-element.51), channel_id=1, source_target_pairs={{0,16},{8,24},{16,0},{24,8},{1,17},{9,25},{17,1},{25,9},{2,18},{10... | collective-permute-start | bytes 196616 | tf_op jit(solution)/shard_map/ppermute | solution.py:78
  50.1 4.3 %collective-permute-start.9 = (f32[128,128]{1,0:T(8,128)S(1)}, f32[128,128]{1,0:T(8,128)S(1)}, u32[]{:S(2)}, u32[]{:S(2)}) collective-permute-start(f32[128,128]{1,0:T(8,128)S(1)} %get-tuple-element.50), channel_id=1, source_target_pairs={{0,24},{8,0},{16,8},{24,16},{1,25},{9,1},{17,9},{25,17},{2,26},{10... | collective-permute-start | bytes 196616 | tf_op jit(solution)/shard_map/ppermute | solution.py:78
  61.2 9.9 %all-to-all-start = ((f32[8,2,4,128]{3,2,1,0:T(4,128)}), f32[8,2,4,128]{3,2,1,0:T(4,128)S(1)}, u32[]{:S(2)}, u32[]{:S(2)}) async-start(f32[8,2,4,128]{3,2,1,0:T(4,128)} %broadcast_in_dim.17), calls=%async_computation | async-start | bytes 65536 | tf_op jit(solution)/shard_map/all_to_all | solution.py:126
  76.1 6.6 %collective-permute-start.10 = (f32[129,128]{1,0:T(8,128)S(1)}, f32[129,128]{1,0:T(8,128)S(1)}, u32[]{:S(2)}, u32[]{:S(2)}) collective-permute-start(f32[129,128]{1,0:T(8,128)S(1)} %get-tuple-element.36), channel_id=1, source_target_pairs={{0,8},{8,16},{16,24},{24,0},{1,9},{9,17},{17,25},{25,1},{2,10},{10... | collective-permute-start | bytes 198152 | tf_op jit(solution)/shard_map/ppermute | solution.py:78
  76.2 6.6 %collective-permute-start.11 = (f32[129,128]{1,0:T(8,128)S(1)}, f32[129,128]{1,0:T(8,128)S(1)}, u32[]{:S(2)}, u32[]{:S(2)}) collective-permute-start(f32[129,128]{1,0:T(8,128)S(1)} %get-tuple-element.37), channel_id=1, source_target_pairs={{0,16},{8,24},{16,0},{24,8},{1,17},{9,25},{17,1},{25,9},{2,18},{10... | collective-permute-start | bytes 198152 | tf_op jit(solution)/shard_map/ppermute | solution.py:78
  79.0 4.3 %collective-permute-start.12 = (f32[129,128]{1,0:T(8,128)S(1)}, f32[129,128]{1,0:T(8,128)S(1)}, u32[]{:S(2)}, u32[]{:S(2)}) collective-permute-start(f32[129,128]{1,0:T(8,128)S(1)} %get-tuple-element.38), channel_id=1, source_target_pairs={{0,24},{8,0},{16,8},{24,16},{1,25},{9,1},{17,9},{25,17},{2,26},{10... | collective-permute-start | bytes 198152 | tf_op jit(solution)/shard_map/ppermute | solution.py:78
  85.8 7.4 %collective-permute-start.13 = (f32[1,129,128]{2,1,0:T(8,128)S(1)}, f32[1,129,128]{2,1,0:T(8,128)S(1)}, u32[]{:S(2)}, u32[]{:S(2)}) collective-permute-start(f32[1,129,128]{2,1,0:T(8,128)S(1)} %pad_maximum_fusion.8), channel_id=1, source_target_pairs={{32,0},{64,32},{96,64},{128,96},{160,128},{192,160},{224,192},{33,... | collective-permute-start | bytes 198152 | tf_op jit(solution)/shard_map/ppermute | solution.py:59
  87.9 7.8 %collective-permute-start.14 = (f32[1,129,128]{2,1,0:T(8,128)S(1)}, f32[1,129,128]{2,1,0:T(8,128)S(1)}, u32[]{:S(2)}, u32[]{:S(2)}) collective-permute-start(f32[1,129,128]{2,1,0:T(8,128)S(1)} %pad_maximum_fusion.8), channel_id=1, source_target_pairs={{64,0},{96,32},{128,64},{160,96},{192,128},{224,160},{65,1},{97,33... | collective-permute-start | bytes 198152 | tf_op jit(solution)/shard_map/ppermute | solution.py:59
  89.2 7.9 %copy-start.10 = (bf16[4,4,128,128]{3,2,1,0:T(8,128)(2,1)S(1)}, bf16[4,4,128,128]{3,2,1,0:T(8,128)(2,1)}, u32[]{:S(2)}) copy-start(bf16[4,4,128,128]{3,2,1,0:T(8,128)(2,1)} %copy-done.9) | copy-start | bytes 1572868
  95.7 9.2 %collective-permute-start.15 = (f32[1,129,128]{2,1,0:T(8,128)S(1)}, f32[1,129,128]{2,1,0:T(8,128)S(1)}, u32[]{:S(2)}, u32[]{:S(2)}) collective-permute-start(f32[1,129,128]{2,1,0:T(8,128)S(1)} %pad_maximum_fusion.9), channel_id=1, source_target_pairs={{96,0},{128,32},{160,64},{192,96},{224,128},{97,1},{129,33},{161,6... | collective-permute-start | bytes 198152 | tf_op jit(solution)/shard_map/ppermute | solution.py:59
  98.6 9.0 %collective-permute-start.16 = (f32[1,129,128]{2,1,0:T(8,128)S(1)}, f32[1,129,128]{2,1,0:T(8,128)S(1)}, u32[]{:S(2)}, u32[]{:S(2)}) collective-permute-start(f32[1,129,128]{2,1,0:T(8,128)S(1)} %pad_maximum_fusion.9), channel_id=1, source_target_pairs={{192,0},{224,32},{193,1},{225,33},{194,2},{226,34},{195,3},{227,35... | collective-permute-start | bytes 198152 | tf_op jit(solution)/shard_map/ppermute | solution.py:59
  107.8 6.9 %collective-permute-start.17 = (f32[128,128]{1,0:T(8,128)S(1)}, f32[128,128]{1,0:T(8,128)S(1)}, u32[]{:S(2)}, u32[]{:S(2)}) collective-permute-start(f32[128,128]{1,0:T(8,128)S(1)} %get-tuple-element.46), channel_id=1, source_target_pairs={{0,8},{8,16},{16,24},{24,0},{1,9},{9,17},{17,25},{25,1},{2,10},{10... | collective-permute-start | bytes 196616 | tf_op jit(solution)/shard_map/ppermute | solution.py:78
  108.8 6.1 %collective-permute-start.18 = (f32[128,128]{1,0:T(8,128)S(1)}, f32[128,128]{1,0:T(8,128)}, u32[]{:S(2)}, u32[]{:S(2)}) collective-permute-start(f32[128,128]{1,0:T(8,128)S(1)} %get-tuple-element.45), channel_id=1, source_target_pairs={{0,16},{8,24},{16,0},{24,8},{1,17},{9,25},{17,1},{25,9},{2,18},{10... | collective-permute-start | bytes 196616 | tf_op jit(solution)/shard_map/ppermute | solution.py:78
  111.9 4.4 %collective-permute-start.19 = (f32[128,128]{1,0:T(8,128)S(1)}, f32[128,128]{1,0:T(8,128)}, u32[]{:S(2)}, u32[]{:S(2)}) collective-permute-start(f32[128,128]{1,0:T(8,128)S(1)} %get-tuple-element.44), channel_id=1, source_target_pairs={{0,24},{8,0},{16,8},{24,16},{1,25},{9,1},{17,9},{25,17},{2,26},{10... | collective-permute-start | bytes 196616 | tf_op jit(solution)/shard_map/ppermute | solution.py:78
  (14 other events, 36.3 us)

commit v6 on v5

--- a/solution.py
+++ b/solution.py
@@ -125,6 +125,14 @@
     copies = jnp.broadcast_to(values[None], (ranks,) + values.shape)
     gathered = lax.all_to_all(copies, "head", 0, 0, tiled=True)
     return jnp.sum(gathered, axis=0)
+
+
+def weigh_blocks(weights, terms):
+    return jnp.sum(weights[:, :, None, None] * terms, axis=0)
+
+
+def mix_blocks(mix, terms):
+    return jnp.stack([weigh_blocks(mix[n], terms) for n in range(mix.shape[0])])
 
 
 def shards(queries, key_rows, value_rows, out_grad, log_decay, row_ranks, col_ranks, head_ranks):
@@ -164,13 +172,8 @@
     earlier_blocks = (block_ids[:, None] > block_ids[None, :]).astype(jnp.float32)
     forward_exp = before[:, None, :] - before[None, :, :] - totals[None, :, :]
     forward_mix = jnp.exp(jnp.minimum(forward_exp, 0.0)) * earlier_blocks[:, :, None]
-    local_states = jnp.einsum("nmh,mhde->nhde", forward_mix, block_terms, precision=highest)
-    shard_state = jnp.einsum(
-        "mh,mhde->hde",
-        jnp.exp(shard_total[None, :] - before - totals),
-        block_terms,
-        precision=highest,
-    )
+    local_states = mix_blocks(forward_mix, block_terms)
+    shard_state = weigh_blocks(jnp.exp(shard_total[None, :] - before - totals), block_terms)
     incoming = incoming_states(shard_total, shard_state, row_ranks, col_ranks)
     states = local_states + jnp.exp(before)[:, :, None, None] * incoming[None]
     backward_state = states.astype(jnp.bfloat16)
@@ -214,8 +217,8 @@
     later_blocks = (block_ids[:, None] < block_ids[None, :]).astype(jnp.float32)
     backward_exp = before[None, :, :] - before[:, None, :] - totals[:, None, :]
     backward_mix = jnp.exp(jnp.minimum(backward_exp, 0.0)) * later_blocks[:, :, None]
-    local_back = jnp.einsum("nmh,mhde->nhde", backward_mix, backward_terms, precision=highest)
-    shard_back = jnp.einsum("mh,mhde->hde", jnp.exp(before), backward_terms, precision=highest)
+    local_back = mix_blocks(backward_mix, backward_terms)
+    shard_back = weigh_blocks(jnp.exp(before), backward_terms)
     later_state = outgoing_states(shard_total, shard_back, row_ranks, col_ranks)
     back_states = (
         local_back

time: 126 us -> 112 us (0.89)
  matrix products: 24.5 us -> 16.5 us
  starting transfers between devices: 48 us -> 42.6 us
  waiting for transfers between devices: 29.4 us -> 33.5 us
  local copies, waits for them, and re-layouts: 17.1 us -> 14.5 us
  other arithmetic: 4.98 us -> 2.45 us
    dot_general x4 -> x0, matrix products: 11.4 us -> none  [the longest x1 4.01 us: shards(): jnp.einsum('nmh,mhde->nhde', forward_mix, block_terms, precision=highest)]
    ppermute x12, starting transfers between devices: 18.5 us -> 13.1 us  [exchange(): got.append(lax.ppermute(send, axis, pairs))]
    ppermute x12, waiting for transfers between devices: 8.9 us -> 12.1 us  [exchange(): got.append(lax.ppermute(send, axis, pairs))]
    convert_element_type x2, local copies, waits for them, and re-layouts: 2.89 us -> 0.66 us  [shards(): grad_f32 = grad_blocks.astype(jnp.float32)]
    unnamed x35 -> x47, local copies, waits for them, and re-layouts: 5.83 us -> 7.87 us
    dot_general x1, matrix products: 0.36 us -> 1.7 us  [shards(): jnp.einsum('njhe,nhde->njhd', value_block_rows, back_b, preferred_element...]
  transfers between devices with their start and end apart: 21 -> 21, of which waited for: 16 -> 16; matrix products, arithmetic and copies ran while one was open for 12% -> 10% of each run, Pallas kernels for 0% -> 0%
where the time goes in v6:
time: 112 us; the launch traced here: 111 us
  starting transfers between devices  42.6 us (38%)
  waiting for transfers between devices  33.5 us (30%)
  matrix products  16.5 us (15%)
  local copies, waits for them, and re-layouts  14.5 us (13%)
  other arithmetic  2.45 us (2%)
  between operations  1.32 us (1%)
    ppermute x4, starting transfers between devices, forward_scan(): lax.ppermute(payload, axis, [(i, i + s) for i in range(ranks - s)])  19.1 us
    ppermute x12, starting transfers between devices, exchange(): got.append(lax.ppermute(send, axis, pairs))  13.1 us
    ppermute x4, waiting for transfers between devices, backward_scan(): lax.ppermute(payload, axis, [(i + s, i) for i in range(ranks - s)])  12.1 us
    ppermute x12, waiting for transfers between devices, exchange(): got.append(lax.ppermute(send, axis, pairs))  12.1 us
    unnamed x47, local copies, waits for them, and re-layouts  7.87 us
    ppermute x4, starting transfers between devices, backward_scan(): lax.ppermute(payload, axis, [(i + s, i) for i in range(ranks - s)])  5.92 us
    all_to_all x1, waiting for transfers between devices, head_sum(): gathered = lax.all_to_all(copies, 'head', 0, 0, tiled=True)  5.44 us
    all_to_all x1, starting transfers between devices, head_sum(): gathered = lax.all_to_all(copies, 'head', 0, 0, tiled=True)  4.47 us
  transfers between devices with their start and end apart: 21, of which 16 were waited for; matrix products, arithmetic and copies ran while one was open for 10% of the time, Pallas kernels for 0%

profile of v6, /device:TPU:32, one launch (start us, length us, event | category | flops | bytes accessed | tf_op | source)
XLA Modules:
  0.0 110.9 jit_solution(8724508248616380655)
XLA Ops:
  4.7 1.9 %multiply_reduce_fusion.7 = (f32[4,128,128]{2,1,0:T(8,128)S(1)}, f32[4,128,128]{2,1,0:T(8,128)}, f32[4,128,128]{2,1,0:T(8,128)}, f32[4,128,128]{2,1,0:T(8,128)}, f32[4,128,128]{2,1,0:T(8,128)}) fusion(f32[4,4]{1,0:T(4,128)S(1)} %subtract_exponential_fusion.1, f32[4,4]{1,0:T(4,128)S(1)} %get-tuple-element.84, f32[4,4]{1,0:T(4,128)S(1)} %get-tuple-element.85, ...), kind=kOutput, calls=%fused_computation.40 | convolution fusion | flops 70189056 | bytes 2367808 | tf_op jit(solution)/shard_map/njhd,njhe->nhde/dot_general | solution.py:168
  6.8 2.8 %collective-permute-start.2 = (f32[129,128]{1,0:T(8,128)S(1)}, f32[129,128]{1,0:T(8,128)S(1)}, u32[]{:S(2)}, u32[]{:S(2)}) collective-permute-start(f32[129,128]{1,0:T(8,128)S(1)} %get-tuple-element.52), channel_id=1, source_target_pairs={{0,24},{8,0},{16,8},{24,16},{1,25},{9,1},{17,9},{25,17},{2,26},{10... | collective-permute-start | bytes 198152 | tf_op jit(solution)/shard_map/ppermute | solution.py:78
  11.9 3.6 %collective-permute-done.1 = f32[129,128]{1,0:T(8,128)S(1)} collective-permute-done((f32[129,128]{1,0:T(8,128)S(1)}, f32[129,128]{1,0:T(8,128)S(1)}, u32[]{:S(2)}, u32[]{:S(2)}) %collective-permute-start.1) | collective-permute-done | bytes 66080 | tf_op jit(solution)/shard_map/ppermute | solution.py:78
  17.0 3.8 %collective-permute-start.3 = (f32[1,129,128]{2,1,0:T(8,128)S(1)}, f32[1,129,128]{2,1,0:T(8,128)S(1)}, u32[]{:S(2)}, u32[]{:S(2)}) collective-permute-start(f32[1,129,128]{2,1,0:T(8,128)S(1)} %pad_maximum_fusion.6), channel_id=1, source_target_pairs={{0,32},{32,64},{64,96},{96,128},{128,160},{160,192},{192,224},{1,3... | collective-permute-start | bytes 198152 | tf_op jit(solution)/shard_map/ppermute | solution.py:39
  20.9 6.4 %collective-permute-start.4 = (f32[1,129,128]{2,1,0:T(8,128)S(1)}, f32[1,129,128]{2,1,0:T(8,128)S(1)}, u32[]{:S(2)}, u32[]{:S(2)}) collective-permute-start(f32[1,129,128]{2,1,0:T(8,128)S(1)} %pad_maximum_fusion.6), channel_id=1, source_target_pairs={{0,64},{32,96},{64,128},{96,160},{128,192},{160,224},{1,65},{33,97... | collective-permute-start | bytes 198152 | tf_op jit(solution)/shard_map/ppermute | solution.py:39
  27.3 1.9 %collective-permute-done.4 = f32[1,129,128]{2,1,0:T(8,128)S(1)} collective-permute-done((f32[1,129,128]{2,1,0:T(8,128)S(1)}, f32[1,129,128]{2,1,0:T(8,128)S(1)}, u32[]{:S(2)}, u32[]{:S(2)}) %collective-permute-start.4) | collective-permute-done | bytes 66080 | tf_op jit(solution)/shard_map/ppermute | solution.py:39
  29.2 7.6 %collective-permute-start.5 = (f32[1,129,128]{2,1,0:T(8,128)S(1)}, f32[1,129,128]{2,1,0:T(8,128)S(1)}, u32[]{:S(2)}, u32[]{:S(2)}) collective-permute-start(f32[1,129,128]{2,1,0:T(8,128)S(1)} %pad_maximum_fusion.7), channel_id=1, source_target_pairs={{0,96},{32,128},{64,160},{96,192},{128,224},{1,97},{33,129},{65,16... | collective-permute-start | bytes 198152 | tf_op jit(solution)/shard_map/ppermute | solution.py:39
  38.8 1.9 %collective-permute-done.6 = f32[1,129,128]{2,1,0:T(8,128)S(1)} collective-permute-done((f32[1,129,128]{2,1,0:T(8,128)S(1)}, f32[1,129,128]{2,1,0:T(8,128)S(1)}, u32[]{:S(2)}, u32[]{:S(2)}) %collective-permute-start.6) | collective-permute-done | bytes 66080 | tf_op jit(solution)/shard_map/ppermute | solution.py:39
  43.5 1.5 %convolution_bitcast_fusion.7 = f32[4,128,4,128]{1,3,2,0:T(8,128)} fusion(bf16[4,4,128,128]{3,2,1,0:T(8,128)(2,1)S(1)} %fusion.11, bf16[4,128,4,128]{3,2,1,0:T(4,128)(2,1)S(1)} %reshape.484), kind=kOutput, calls=%fused_computation.20 | convolution fusion | flops 67108864 | bytes 2097152 | tf_op jit(solution)/shard_map/nhij,njhd->nihd/dot_general | solution.py:163
  49.5 1.9 %multiply_reduce_fusion.6 = (f32[4,128]{1,0:T(4,128)S(1)}, f32[4,128]{1,0:T(4,128)S(1)}, f32[4,128,4,128]{1,3,2,0:T(8,128)S(1)}) fusion(f32[4,128,4,128]{1,3,2,0:T(8,128)S(1)} %copy.114, f32[4,128,4,128]{1,3,2,0:T(8,128)} %convolution_bitcast_fusion.7, bf16[4,128,4,128]{1,3,2,0:T(8,128)(2,1)S(1)} %copy.125, f32[1,4,128,128]{3,2,1,0:T(8,128)S(1)} %bitcast.202, ...), kind=kOutput, calls=%fused_computation.39 | convolution fusion | flops 70253568 | bytes 4993088 | tf_op jit(solution)/shard_map/nihd,nhde->nihe/dot_general | solution.py:180
  52.1 4.5 %all-to-all-start = ((f32[8,2,4,128]{3,2,1,0:T(4,128)}), f32[8,2,4,128]{3,2,1,0:T(4,128)S(1)}, u32[]{:S(2)}, u32[]{:S(2)}) async-start(f32[8,2,4,128]{3,2,1,0:T(4,128)} %broadcast_in_dim.17), calls=%async_computation | async-start | bytes 65536 | tf_op jit(solution)/shard_map/all_to_all | solution.py:126
  56.6 5.4 %all-to-all-done = f32[8,2,4,128]{3,2,1,0:T(4,128)S(1)} async-done(((f32[8,2,4,128]{3,2,1,0:T(4,128)}), f32[8,2,4,128]{3,2,1,0:T(4,128)S(1)}, u32[]{:S(2)}, u32[]{:S(2)}) %all-to-all-start) | async-done | bytes 32800 | tf_op jit(solution)/shard_map/all_to_all | solution.py:126
  63.7 1.7 %multiply_reduce_fusion = (f32[4,128,128]{2,1,0:T(8,128)S(1)}, f32[4,128,128]{2,1,0:T(8,128)}, f32[4,128,128]{2,1,0:T(8,128)}, f32[4,128,128]{2,1,0:T(8,128)}, f32[4,128,128]{2,1,0:T(8,128)}) fusion(f32[4,4]{1,0:T(4,128)S(1)} %get-tuple-element.23, f32[4,4]{1,0:T(4,128)S(1)} %get-tuple-element.80, f32[4,4]{1,0:T(4,128)S(1)} %get-tuple-element.81, ...), kind=kOutput, calls=%fused_computation.31 | convolution fusion | flops 70189056 | bytes 2367808 | tf_op jit(solution)/shard_map/nihd,nihe->nhde/dot_general | solution.py:214
  65.4 2.0 %collective-permute-start.12 = (f32[129,128]{1,0:T(8,128)S(1)}, f32[129,128]{1,0:T(8,128)S(1)}, u32[]{:S(2)}, u32[]{:S(2)}) collective-permute-start(f32[129,128]{1,0:T(8,128)S(1)} %get-tuple-element.48), channel_id=1, source_target_pairs={{0,24},{8,0},{16,8},{24,16},{1,25},{9,1},{17,9},{25,17},{2,26},{10... | collective-permute-start | bytes 198152 | tf_op jit(solution)/shard_map/ppermute | solution.py:78
  68.6 1.5 %convolution_bitcast_fusion.5 = f32[4,128,4,128]{1,3,2,0:T(8,128)} fusion(bf16[4,4,128,128]{3,2,1,0:T(8,128)(2,1)S(1)} %fusion.12, bf16[4,128,4,128]{3,2,1,0:T(4,128)(2,1)S(1)} %copy-done.1), kind=kOutput, calls=%fused_computation.15 | convolution fusion | flops 67108864 | bytes 2097152 | tf_op jit(solution)/shard_map/nhij,njhd->nihd/dot_general | solution.py:199
  70.4 2.9 %collective-permute-done.11 = f32[129,128]{1,0:T(8,128)S(1)} collective-permute-done((f32[129,128]{1,0:T(8,128)S(1)}, f32[129,128]{1,0:T(8,128)S(1)}, u32[]{:S(2)}, u32[]{:S(2)}) %collective-permute-start.11) | collective-permute-done | bytes 66080 | tf_op jit(solution)/shard_map/ppermute | solution.py:78
  74.8 2.1 %collective-permute-start.13 = (f32[1,129,128]{2,1,0:T(8,128)S(1)}, f32[1,129,128]{2,1,0:T(8,128)S(1)}, u32[]{:S(2)}, u32[]{:S(2)}) collective-permute-start(f32[1,129,128]{2,1,0:T(8,128)S(1)} %pad_maximum_fusion.8), channel_id=1, source_target_pairs={{32,0},{64,32},{96,64},{128,96},{160,128},{192,160},{224,192},{33,... | collective-permute-start | bytes 198152 | tf_op jit(solution)/shard_map/ppermute | solution.py:59
  78.1 1.6 %fusion.8 = bf16[4,128,4,128]{1,3,2,0:T(8,128)(2,1)S(1)} fusion(f32[4,128,4,128]{1,3,2,0:T(8,128)S(1)} %copy-done.8, bf16[4,128,4,128]{1,3,2,0:T(8,128)(2,1)S(1)} %multiply_convert_fusion.1, f32[4,128,4]{1,2,0:T(4,128)S(1)} %copy.106, f32[1,4,128,128]{3,2,1,0:T(8,128)} %bitcast.201, f32[1,4,128,128]{3,2,1,0:T(8,128)} %bitcast.203, ...), kind=kOutput, calls=%fused_computation.22 | convolution fusion | flops 69468160 | bytes 3416128 | tf_op jit(solution)/shard_map/nihe,nhde->nihd/dot_general | solution.py:202
  79.7 2.5 %collective-permute-done.13 = f32[1,129,128]{2,1,0:T(8,128)S(1)} collective-permute-done((f32[1,129,128]{2,1,0:T(8,128)S(1)}, f32[1,129,128]{2,1,0:T(8,128)S(1)}, u32[]{:S(2)}, u32[]{:S(2)}) %collective-permute-start.13) | collective-permute-done | bytes 66080 | tf_op jit(solution)/shard_map/ppermute | solution.py:59
  82.2 2.5 %collective-permute-done.14 = f32[1,129,128]{2,1,0:T(8,128)S(1)} collective-permute-done((f32[1,129,128]{2,1,0:T(8,128)S(1)}, f32[1,129,128]{2,1,0:T(8,128)S(1)}, u32[]{:S(2)}, u32[]{:S(2)}) %collective-permute-start.14) | collective-permute-done | bytes 66080 | tf_op jit(solution)/shard_map/ppermute | solution.py:59
  86.0 1.5 %convolution_bitcast_fusion.3 = f32[4,128,4,128]{3,1,2,0:T(8,128)} fusion(bf16[4,4,128,128]{3,2,1,0:T(8,128)(2,1)S(1)} %fusion.12, bf16[4,128,4,128]{1,3,2,0:T(8,128)(2,1)S(1)} %copy.125), kind=kOutput, calls=%fused_computation.11 | convolution fusion | flops 67108864 | bytes 2097152 | tf_op jit(solution)/shard_map/nhij,nihd->njhd/dot_general | solution.py:205
  88.8 5.8 %collective-permute-done.15 = f32[1,129,128]{2,1,0:T(8,128)S(1)} collective-permute-done((f32[1,129,128]{2,1,0:T(8,128)S(1)}, f32[1,129,128]{2,1,0:T(8,128)S(1)}, u32[]{:S(2)}, u32[]{:S(2)}) %collective-permute-start.15) | collective-permute-done | bytes 66080 | tf_op jit(solution)/shard_map/ppermute | solution.py:59
  98.9 1.5 %convolution_bitcast_fusion.1 = f32[4,128,4,128]{3,1,2,0:T(8,128)} fusion(bf16[4,128,4,128]{1,3,2,0:T(8,128)(2,1)S(1)} %multiply_convert_fusion.1, bf16[4,4,128,128]{3,2,1,0:T(8,128)(2,1)S(1)} %copy-done.6), kind=kOutput, calls=%fused_computation.7 | convolution fusion | flops 67108864 | bytes 2097152 | tf_op jit(solution)/shard_map/nhij,nihe->njhe/dot_general | solution.py:208
  105.6 1.7 %fusion.9 = bf16[4,128,4,128]{3,1,2,0:T(8,128)(2,1)S(1)} fusion(f32[4,128,4,128]{3,1,2,0:T(8,128)S(1)} %copy-done.7, f32[4,128,4]{1,2,0:T(4,128)S(1)} %copy.108, bf16[4,128,4,128]{3,2,1,0:T(4,128)(2,1)S(1)} %copy-done.4, f32[1,4,128,128]{3,2,1,0:T(8,128)S(1)} %bitcast.229, f32[1,4,128,128]{3,2,1,0:T(8,128)} %bitcast.231, f32[1,4,128,128]{3,2,1,0:T(8,128)} %bitcast.233, ...), kind=kOutput, calls=%fused_computation.23 | convolution fusion | flops 69468160 | bytes 3416128 | tf_op jit(solution)/shard_map/njhe,nhde->njhd/dot_general | solution.py:228
  (150 shorter events, 39.1 us)
Async XLA Ops:
  3.8 33.0 %copy-start = (bf16[4,128,4,128]{3,2,1,0:T(4,128)(2,1)}, bf16[4,128,4,128]{3,2,1,0:T(4,128)(2,1)S(1)}, u32[]{:S(2)}) copy-start(bf16[4,128,4,128]{3,2,1,0:T(4,128)(2,1)S(1)} %reshape.482) | copy-start | bytes 1572868
  4.0 39.5 %copy-start.2 = (bf16[4,128,4,128]{3,2,1,0:T(4,128)(2,1)}, bf16[4,128,4,128]{3,2,1,0:T(4,128)(2,1)S(1)}, u32[]{:S(2)}) copy-start(bf16[4,128,4,128]{3,2,1,0:T(4,128)(2,1)S(1)} %reshape.484) | copy-start | bytes 1572868
  6.8 5.2 %collective-permute-start.2 = (f32[129,128]{1,0:T(8,128)S(1)}, f32[129,128]{1,0:T(8,128)S(1)}, u32[]{:S(2)}, u32[]{:S(2)}) collective-permute-start(f32[129,128]{1,0:T(8,128)S(1)} %get-tuple-element.52), channel_id=1, source_target_pairs={{0,24},{8,0},{16,8},{24,16},{1,25},{9,1},{17,9},{25,17},{2,26},{10... | collective-permute-start | bytes 198152 | tf_op jit(solution)/shard_map/ppermute | solution.py:78
  9.6 5.9 %collective-permute-start.1 = (f32[129,128]{1,0:T(8,128)S(1)}, f32[129,128]{1,0:T(8,128)S(1)}, u32[]{:S(2)}, u32[]{:S(2)}) collective-permute-start(f32[129,128]{1,0:T(8,128)S(1)} %get-tuple-element.50), channel_id=1, source_target_pairs={{0,16},{8,24},{16,0},{24,8},{1,17},{9,25},{17,1},{25,9},{2,18},{10... | collective-permute-start | bytes 198152 | tf_op jit(solution)/shard_map/ppermute | solution.py:78
  10.4 5.8 %collective-permute-start = (f32[129,128]{1,0:T(8,128)S(1)}, f32[129,128]{1,0:T(8,128)S(1)}, u32[]{:S(2)}, u32[]{:S(2)}) collective-permute-start(f32[129,128]{1,0:T(8,128)S(1)} %get-tuple-element.51), channel_id=1, source_target_pairs={{0,8},{8,16},{16,24},{24,0},{1,9},{9,17},{17,25},{25,1},{2,10},{10... | collective-permute-start | bytes 198152 | tf_op jit(solution)/shard_map/ppermute | solution.py:78
  17.0 10.3 %collective-permute-start.3 = (f32[1,129,128]{2,1,0:T(8,128)S(1)}, f32[1,129,128]{2,1,0:T(8,128)S(1)}, u32[]{:S(2)}, u32[]{:S(2)}) collective-permute-start(f32[1,129,128]{2,1,0:T(8,128)S(1)} %pad_maximum_fusion.6), channel_id=1, source_target_pairs={{0,32},{32,64},{64,96},{96,128},{128,160},{160,192},{192,224},{1,3... | collective-permute-start | bytes 198152 | tf_op jit(solution)/shard_map/ppermute | solution.py:39
  20.9 8.3 %collective-permute-start.4 = (f32[1,129,128]{2,1,0:T(8,128)S(1)}, f32[1,129,128]{2,1,0:T(8,128)S(1)}, u32[]{:S(2)}, u32[]{:S(2)}) collective-permute-start(f32[1,129,128]{2,1,0:T(8,128)S(1)} %pad_maximum_fusion.6), channel_id=1, source_target_pairs={{0,64},{32,96},{64,128},{96,160},{128,192},{160,224},{1,65},{33,97... | collective-permute-start | bytes 198152 | tf_op jit(solution)/shard_map/ppermute | solution.py:39
  29.2 9.5 %collective-permute-start.5 = (f32[1,129,128]{2,1,0:T(8,128)S(1)}, f32[1,129,128]{2,1,0:T(8,128)S(1)}, u32[]{:S(2)}, u32[]{:S(2)}) collective-permute-start(f32[1,129,128]{2,1,0:T(8,128)S(1)} %pad_maximum_fusion.7), channel_id=1, source_target_pairs={{0,96},{32,128},{64,160},{96,192},{128,224},{1,97},{33,129},{65,16... | collective-permute-start | bytes 198152 | tf_op jit(solution)/shard_map/ppermute | solution.py:39
  37.4 6.1 %copy-start.5 = (bf16[4,4,128,128]{3,2,1,0:T(8,128)(2,1)}, bf16[4,4,128,128]{3,2,1,0:T(8,128)(2,1)S(1)}, u32[]{:S(2)}) copy-start(bf16[4,4,128,128]{3,2,1,0:T(8,128)(2,1)S(1)} %fusion.11) | copy-start | bytes 1572868
  37.4 3.2 %collective-permute-start.6 = (f32[1,129,128]{2,1,0:T(8,128)S(1)}, f32[1,129,128]{2,1,0:T(8,128)S(1)}, u32[]{:S(2)}, u32[]{:S(2)}) collective-permute-start(f32[1,129,128]{2,1,0:T(8,128)S(1)} %pad_maximum_fusion.7), channel_id=1, source_target_pairs={{0,192},{32,224},{1,193},{33,225},{2,194},{34,226},{3,195},{35,227... | collective-permute-start | bytes 198152 | tf_op jit(solution)/shard_map/ppermute | solution.py:39
  40.8 5.0 %collective-permute-start.9 = (f32[128,128]{1,0:T(8,128)S(1)}, f32[128,128]{1,0:T(8,128)S(1)}, u32[]{:S(2)}, u32[]{:S(2)}) collective-permute-start(f32[128,128]{1,0:T(8,128)S(1)} %get-tuple-element.58), channel_id=1, source_target_pairs={{0,24},{8,0},{16,8},{24,16},{1,25},{9,1},{17,9},{25,17},{2,26},{10... | collective-permute-start | bytes 196616 | tf_op jit(solution)/shard_map/ppermute | solution.py:78
  41.4 5.8 %collective-permute-start.8 = (f32[128,128]{1,0:T(8,128)S(1)}, f32[128,128]{1,0:T(8,128)S(1)}, u32[]{:S(2)}, u32[]{:S(2)}) collective-permute-start(f32[128,128]{1,0:T(8,128)S(1)} %get-tuple-element.59), channel_id=1, source_target_pairs={{0,16},{8,24},{16,0},{24,8},{1,17},{9,25},{17,1},{25,9},{2,18},{10... | collective-permute-start | bytes 196616 | tf_op jit(solution)/shard_map/ppermute | solution.py:78
  42.3 5.6 %collective-permute-start.7 = (f32[128,128]{1,0:T(8,128)S(1)}, f32[128,128]{1,0:T(8,128)S(1)}, u32[]{:S(2)}, u32[]{:S(2)}) collective-permute-start(f32[128,128]{1,0:T(8,128)S(1)} %get-tuple-element.60), channel_id=1, source_target_pairs={{0,8},{8,16},{16,24},{24,0},{1,9},{9,17},{17,25},{25,1},{2,10},{10... | collective-permute-start | bytes 196616 | tf_op jit(solution)/shard_map/ppermute | solution.py:78
  52.1 9.9 %all-to-all-start = ((f32[8,2,4,128]{3,2,1,0:T(4,128)}), f32[8,2,4,128]{3,2,1,0:T(4,128)S(1)}, u32[]{:S(2)}, u32[]{:S(2)}) async-start(f32[8,2,4,128]{3,2,1,0:T(4,128)} %broadcast_in_dim.17), calls=%async_computation | async-start | bytes 65536 | tf_op jit(solution)/shard_map/all_to_all | solution.py:126
  65.4 5.0 %collective-permute-start.12 = (f32[129,128]{1,0:T(8,128)S(1)}, f32[129,128]{1,0:T(8,128)S(1)}, u32[]{:S(2)}, u32[]{:S(2)}) collective-permute-start(f32[129,128]{1,0:T(8,128)S(1)} %get-tuple-element.48), channel_id=1, source_target_pairs={{0,24},{8,0},{16,8},{24,16},{1,25},{9,1},{17,9},{25,17},{2,26},{10... | collective-permute-start | bytes 198152 | tf_op jit(solution)/shard_map/ppermute | solution.py:78
  67.4 5.8 %collective-permute-start.11 = (f32[129,128]{1,0:T(8,128)S(1)}, f32[129,128]{1,0:T(8,128)S(1)}, u32[]{:S(2)}, u32[]{:S(2)}) collective-permute-start(f32[129,128]{1,0:T(8,128)S(1)} %get-tuple-element.47), channel_id=1, source_target_pairs={{0,16},{8,24},{16,0},{24,8},{1,17},{9,25},{17,1},{25,9},{2,18},{10... | collective-permute-start | bytes 198152 | tf_op jit(solution)/shard_map/ppermute | solution.py:78
  68.3 5.7 %collective-permute-start.10 = (f32[129,128]{1,0:T(8,128)S(1)}, f32[129,128]{1,0:T(8,128)S(1)}, u32[]{:S(2)}, u32[]{:S(2)}) collective-permute-start(f32[129,128]{1,0:T(8,128)S(1)} %get-tuple-element.46), channel_id=1, source_target_pairs={{0,8},{8,16},{16,24},{24,0},{1,9},{9,17},{17,25},{25,1},{2,10},{10... | collective-permute-start | bytes 198152 | tf_op jit(solution)/shard_map/ppermute | solution.py:78
  74.8 7.4 %collective-permute-start.13 = (f32[1,129,128]{2,1,0:T(8,128)S(1)}, f32[1,129,128]{2,1,0:T(8,128)S(1)}, u32[]{:S(2)}, u32[]{:S(2)}) collective-permute-start(f32[1,129,128]{2,1,0:T(8,128)S(1)} %pad_maximum_fusion.8), channel_id=1, source_target_pairs={{32,0},{64,32},{96,64},{128,96},{160,128},{192,160},{224,192},{33,... | collective-permute-start | bytes 198152 | tf_op jit(solution)/shard_map/ppermute | solution.py:59
  76.8 7.8 %collective-permute-start.14 = (f32[1,129,128]{2,1,0:T(8,128)S(1)}, f32[1,129,128]{2,1,0:T(8,128)S(1)}, u32[]{:S(2)}, u32[]{:S(2)}) collective-permute-start(f32[1,129,128]{2,1,0:T(8,128)S(1)} %pad_maximum_fusion.8), channel_id=1, source_target_pairs={{64,0},{96,32},{128,64},{160,96},{192,128},{224,160},{65,1},{97,33... | collective-permute-start | bytes 198152 | tf_op jit(solution)/shard_map/ppermute | solution.py:59
  84.7 9.9 %collective-permute-start.15 = (f32[1,129,128]{2,1,0:T(8,128)S(1)}, f32[1,129,128]{2,1,0:T(8,128)S(1)}, u32[]{:S(2)}, u32[]{:S(2)}) collective-permute-start(f32[1,129,128]{2,1,0:T(8,128)S(1)} %pad_maximum_fusion.9), channel_id=1, source_target_pairs={{96,0},{128,32},{160,64},{192,96},{224,128},{97,1},{129,33},{161,6... | collective-permute-start | bytes 198152 | tf_op jit(solution)/shard_map/ppermute | solution.py:59
  87.5 8.5 %collective-permute-start.16 = (f32[1,129,128]{2,1,0:T(8,128)S(1)}, f32[1,129,128]{2,1,0:T(8,128)S(1)}, u32[]{:S(2)}, u32[]{:S(2)}) collective-permute-start(f32[1,129,128]{2,1,0:T(8,128)S(1)} %pad_maximum_fusion.9), channel_id=1, source_target_pairs={{192,0},{224,32},{193,1},{225,33},{194,2},{226,34},{195,3},{227,35... | collective-permute-start | bytes 198152 | tf_op jit(solution)/shard_map/ppermute | solution.py:59
  96.2 5.5 %collective-permute-start.19 = (f32[128,128]{1,0:T(8,128)S(1)}, f32[128,128]{1,0:T(8,128)S(1)}, u32[]{:S(2)}, u32[]{:S(2)}) collective-permute-start(f32[128,128]{1,0:T(8,128)S(1)} %get-tuple-element.54), channel_id=1, source_target_pairs={{0,24},{8,0},{16,8},{24,16},{1,25},{9,1},{17,9},{25,17},{2,26},{10... | collective-permute-start | bytes 196616 | tf_op jit(solution)/shard_map/ppermute | solution.py:78
  96.8 5.8 %collective-permute-start.18 = (f32[128,128]{1,0:T(8,128)S(1)}, f32[128,128]{1,0:T(8,128)S(1)}, u32[]{:S(2)}, u32[]{:S(2)}) collective-permute-start(f32[128,128]{1,0:T(8,128)S(1)} %get-tuple-element.55), channel_id=1, source_target_pairs={{0,16},{8,24},{16,0},{24,8},{1,17},{9,25},{17,1},{25,9},{2,18},{10... | collective-permute-start | bytes 196616 | tf_op jit(solution)/shard_map/ppermute | solution.py:78
  97.7 5.7 %collective-permute-start.17 = (f32[128,128]{1,0:T(8,128)S(1)}, f32[128,128]{1,0:T(8,128)}, u32[]{:S(2)}, u32[]{:S(2)}) collective-permute-start(f32[128,128]{1,0:T(8,128)S(1)} %get-tuple-element.56), channel_id=1, source_target_pairs={{0,8},{8,16},{16,24},{24,0},{1,9},{9,17},{17,25},{25,1},{2,10},{10... | collective-permute-start | bytes 196616 | tf_op jit(solution)/shard_map/ppermute | solution.py:78
  (19 other events, 36.9 us)

commit v7 on v6

--- a/solution.py
+++ b/solution.py
@@ -22,11 +22,7 @@
 
 
 def radix_shifts(ranks):
-    rounds, width = [], 1
-    while width < ranks:
-        rounds.append([s for s in (width, 2 * width) if s < ranks])
-        width *= 3
-    return rounds
+    return [list(range(1, ranks))]
 
 
 def forward_scan(total, state, axis, ranks):

time: 112 us -> 116 us (1.036)
  starting transfers between devices: 42.6 us -> 47.8 us
  matrix products: 16.5 us -> 15 us
    ppermute x4 -> x7, starting transfers between devices: 5.92 us -> 13.1 us  [backward_scan(): lax.ppermute(payload, axis, [(i + s, i) for i in range(ranks - s)])]
    ppermute x4 -> x7, waiting for transfers between devices: 3.79 us -> 0.93 us  [forward_scan(): lax.ppermute(payload, axis, [(i, i + s) for i in range(ranks - s)])]
    ppermute x4 -> x7, waiting for transfers between devices: 12.1 us -> 13.9 us  [backward_scan(): lax.ppermute(payload, axis, [(i + s, i) for i in range(ranks - s)])]
    ppermute x4 -> x7, starting transfers between devices: 19.1 us -> 17.3 us  [forward_scan(): lax.ppermute(payload, axis, [(i, i + s) for i in range(ranks - s)])]
    unnamed x47 -> x55, local copies, waits for them, and re-layouts: 7.87 us -> 8.37 us
  transfers between devices with their start and end apart: 21 -> 27, of which waited for: 16 -> 14; matrix products, arithmetic and copies ran while one was open for 10% -> 8% of each run, Pallas kernels for 0% -> 0%
where the time goes in v7:
time: 116 us; the launch traced here: 115 us
  starting transfers between devices  47.8 us (41%)
  waiting for transfers between devices  33.5 us (29%)
  local copies, waits for them, and re-layouts  15 us (13%)
  matrix products  15 us (13%)
  other arithmetic  2.45 us (2%)
  between operations  1.4 us (1%)
    ppermute x7, starting transfers between devices, forward_scan(): lax.ppermute(payload, axis, [(i, i + s) for i in range(ranks - s)])  17.3 us
    ppermute x7, waiting for transfers between devices, backward_scan(): lax.ppermute(payload, axis, [(i + s, i) for i in range(ranks - s)])  13.9 us
    ppermute x12, waiting for transfers between devices, exchange(): got.append(lax.ppermute(send, axis, pairs))  13.3 us
    ppermute x7, starting transfers between devices, backward_scan(): lax.ppermute(payload, axis, [(i + s, i) for i in range(ranks - s)])  13.1 us
    ppermute x12, starting transfers between devices, exchange(): got.append(lax.ppermute(send, axis, pairs))  12.9 us
    unnamed x55, local copies, waits for them, and re-layouts  8.37 us
    all_to_all x1, waiting for transfers between devices, head_sum(): gathered = lax.all_to_all(copies, 'head', 0, 0, tiled=True)  5.44 us
    all_to_all x1, starting transfers between devices, head_sum(): gathered = lax.all_to_all(copies, 'head', 0, 0, tiled=True)  4.47 us
  transfers between devices with their start and end apart: 27, of which 14 were waited for; matrix products, arithmetic and copies ran while one was open for 8% of the time, Pallas kernels for 0%

profile of v7, /device:TPU:32, one launch (start us, length us, event | category | flops | bytes accessed | tf_op | source)
XLA Modules:
  0.0 115.2 jit_solution(12843849851177339571)
XLA Ops:
  4.8 2.0 %multiply_reduce_fusion.7 = (f32[4,128,128]{2,1,0:T(8,128)S(1)}, f32[4,128,128]{2,1,0:T(8,128)}, f32[4,128,128]{2,1,0:T(8,128)}, f32[4,128,128]{2,1,0:T(8,128)}, f32[4,128,128]{2,1,0:T(8,128)}) fusion(f32[4,4]{1,0:T(4,128)S(1)} %subtract_exponential_fusion.1, f32[4,4]{1,0:T(4,128)S(1)} %get-tuple-element.82, f32[4,4]{1,0:T(4,128)S(1)} %get-tuple-element.83, ...), kind=kOutput, calls=%fused_computation.40 | convolution fusion | flops 70189056 | bytes 2367808 | tf_op jit(solution)/shard_map/njhd,njhe->nhde/dot_general | solution.py:164
  6.8 2.8 %collective-permute-start.2 = (f32[129,128]{1,0:T(8,128)S(1)}, f32[129,128]{1,0:T(8,128)S(1)}, u32[]{:S(2)}, u32[]{:S(2)}) collective-permute-start(f32[129,128]{1,0:T(8,128)S(1)} %get-tuple-element.52), channel_id=1, source_target_pairs={{0,24},{8,0},{16,8},{24,16},{1,25},{9,1},{17,9},{25,17},{2,26},{10... | collective-permute-start | bytes 198152 | tf_op jit(solution)/shard_map/ppermute | solution.py:74
  12.0 3.6 %collective-permute-done.1 = f32[129,128]{1,0:T(8,128)S(1)} collective-permute-done((f32[129,128]{1,0:T(8,128)S(1)}, f32[129,128]{1,0:T(8,128)S(1)}, u32[]{:S(2)}, u32[]{:S(2)}) %collective-permute-start.1) | collective-permute-done | bytes 66080 | tf_op jit(solution)/shard_map/ppermute | solution.py:74
  17.1 3.8 %collective-permute-start.3 = (f32[1,129,128]{2,1,0:T(8,128)S(1)}, f32[1,129,128]{2,1,0:T(8,128)S(1)}, u32[]{:S(2)}, u32[]{:S(2)}) collective-permute-start(f32[1,129,128]{2,1,0:T(8,128)S(1)} %pad_maximum_fusion.6), channel_id=1, source_target_pairs={{0,32},{32,64},{64,96},{96,128},{128,160},{160,192},{192,224},{1,3... | collective-permute-start | bytes 198152 | tf_op jit(solution)/shard_map/ppermute | solution.py:35
  20.9 6.4 %collective-permute-start.4 = (f32[1,129,128]{2,1,0:T(8,128)S(1)}, f32[1,129,128]{2,1,0:T(8,128)S(1)}, u32[]{:S(2)}, u32[]{:S(2)}) collective-permute-start(f32[1,129,128]{2,1,0:T(8,128)S(1)} %pad_maximum_fusion.6), channel_id=1, source_target_pairs={{0,64},{32,96},{64,128},{96,160},{128,192},{160,224},{1,65},{33,97... | collective-permute-start | bytes 198152 | tf_op jit(solution)/shard_map/ppermute | solution.py:35
  28.6 1.8 %collective-permute-start.7 = (f32[1,129,128]{2,1,0:T(8,128)S(1)}, f32[1,129,128]{2,1,0:T(8,128)S(1)}, u32[]{:S(2)}, u32[]{:S(2)}) collective-permute-start(f32[1,129,128]{2,1,0:T(8,128)S(1)} %pad_maximum_fusion.6), channel_id=1, source_target_pairs={{0,160},{32,192},{64,224},{1,161},{33,193},{65,225},{2,162},{34,19... | collective-permute-start | bytes 198152 | tf_op jit(solution)/shard_map/ppermute | solution.py:35
  30.4 1.7 %collective-permute-start.6 = (f32[1,129,128]{2,1,0:T(8,128)S(1)}, f32[1,129,128]{2,1,0:T(8,128)S(1)}, u32[]{:S(2)}, u32[]{:S(2)}) collective-permute-start(f32[1,129,128]{2,1,0:T(8,128)S(1)} %pad_maximum_fusion.6), channel_id=1, source_target_pairs={{0,128},{32,160},{64,192},{96,224},{1,129},{33,161},{65,193},{97,2... | collective-permute-start | bytes 198152 | tf_op jit(solution)/shard_map/ppermute | solution.py:35
  32.1 1.7 %collective-permute-start.5 = (f32[1,129,128]{2,1,0:T(8,128)S(1)}, f32[1,129,128]{2,1,0:T(8,128)S(1)}, u32[]{:S(2)}, u32[]{:S(2)}) collective-permute-start(f32[1,129,128]{2,1,0:T(8,128)S(1)} %pad_maximum_fusion.6), channel_id=1, source_target_pairs={{0,96},{32,128},{64,160},{96,192},{128,224},{1,97},{33,129},{65,16... | collective-permute-start | bytes 198152 | tf_op jit(solution)/shard_map/ppermute | solution.py:35
  39.0 1.5 %convolution_bitcast_fusion.7 = f32[4,128,4,128]{1,3,2,0:T(8,128)} fusion(bf16[4,4,128,128]{3,2,1,0:T(8,128)(2,1)S(1)} %fusion.11, bf16[4,128,4,128]{3,2,1,0:T(4,128)(2,1)S(1)} %reshape.476), kind=kOutput, calls=%fused_computation.20 | convolution fusion | flops 67108864 | bytes 2097152 | tf_op jit(solution)/shard_map/nhij,njhd->nihd/dot_general | solution.py:159
  41.2 1.4 %collective-permute-done.11 = f32[128,128]{1,0:T(8,128)S(1)} collective-permute-done((f32[128,128]{1,0:T(8,128)S(1)}, f32[128,128]{1,0:T(8,128)S(1)}, u32[]{:S(2)}, u32[]{:S(2)}) %collective-permute-start.11) | collective-permute-done | bytes 65568 | tf_op jit(solution)/shard_map/ppermute | solution.py:74
  45.0 1.9 %multiply_reduce_fusion.6 = (f32[4,128]{1,0:T(4,128)S(1)}, f32[4,128]{1,0:T(4,128)S(1)}, f32[4,128,4,128]{1,3,2,0:T(8,128)S(1)}) fusion(f32[4,128,4,128]{1,3,2,0:T(8,128)S(1)} %copy.114, f32[4,128,4,128]{1,3,2,0:T(8,128)} %convolution_bitcast_fusion.7, bf16[4,128,4,128]{1,3,2,0:T(8,128)(2,1)S(1)} %copy.125, f32[1,4,128,128]{3,2,1,0:T(8,128)S(1)} %bitcast.205, ...), kind=kOutput, calls=%fused_computation.39 | convolution fusion | flops 70253568 | bytes 4993088 | tf_op jit(solution)/shard_map/nihd,nhde->nihe/dot_general | solution.py:176
  47.6 4.5 %all-to-all-start = ((f32[8,2,4,128]{3,2,1,0:T(4,128)}), f32[8,2,4,128]{3,2,1,0:T(4,128)S(1)}, u32[]{:S(2)}, u32[]{:S(2)}) async-start(f32[8,2,4,128]{3,2,1,0:T(4,128)} %broadcast_in_dim.17), calls=%async_computation | async-start | bytes 65536 | tf_op jit(solution)/shard_map/all_to_all | solution.py:122
  52.0 5.4 %all-to-all-done = f32[8,2,4,128]{3,2,1,0:T(4,128)S(1)} async-done(((f32[8,2,4,128]{3,2,1,0:T(4,128)}), f32[8,2,4,128]{3,2,1,0:T(4,128)S(1)}, u32[]{:S(2)}, u32[]{:S(2)}) %all-to-all-start) | async-done | bytes 32800 | tf_op jit(solution)/shard_map/all_to_all | solution.py:122
  60.1 1.7 %multiply_reduce_fusion = (f32[4,128,128]{2,1,0:T(8,128)S(1)}, f32[4,128,128]{2,1,0:T(8,128)}, f32[4,128,128]{2,1,0:T(8,128)}, f32[4,128,128]{2,1,0:T(8,128)}, f32[4,128,128]{2,1,0:T(8,128)}) fusion(f32[4,4]{1,0:T(4,128)S(1)} %get-tuple-element.23, f32[4,4]{1,0:T(4,128)S(1)} %get-tuple-element.78, f32[4,4]{1,0:T(4,128)S(1)} %get-tuple-element.79, ...), kind=kOutput, calls=%fused_computation.31 | convolution fusion | flops 70189056 | bytes 2367808 | tf_op jit(solution)/shard_map/nihd,nihe->nhde/dot_general | solution.py:210
  61.9 2.2 %collective-permute-start.15 = (f32[129,128]{1,0:T(8,128)S(1)}, f32[129,128]{1,0:T(8,128)S(1)}, u32[]{:S(2)}, u32[]{:S(2)}) collective-permute-start(f32[129,128]{1,0:T(8,128)S(1)} %get-tuple-element.48), channel_id=1, source_target_pairs={{0,24},{8,0},{16,8},{24,16},{1,25},{9,1},{17,9},{25,17},{2,26},{10... | collective-permute-start | bytes 198152 | tf_op jit(solution)/shard_map/ppermute | solution.py:74
  67.0 2.9 %collective-permute-done.14 = f32[129,128]{1,0:T(8,128)S(1)} collective-permute-done((f32[129,128]{1,0:T(8,128)S(1)}, f32[129,128]{1,0:T(8,128)S(1)}, u32[]{:S(2)}, u32[]{:S(2)}) %collective-permute-start.14) | collective-permute-done | bytes 66080 | tf_op jit(solution)/shard_map/ppermute | solution.py:74
  75.3 6.0 %collective-permute-start.16 = (f32[1,129,128]{2,1,0:T(8,128)S(1)}, f32[1,129,128]{2,1,0:T(8,128)S(1)}, u32[]{:S(2)}, u32[]{:S(2)}) collective-permute-start(f32[1,129,128]{2,1,0:T(8,128)S(1)} %pad_maximum_fusion.7), channel_id=1, source_target_pairs={{32,0},{64,32},{96,64},{128,96},{160,128},{192,160},{224,192},{33,... | collective-permute-start | bytes 198152 | tf_op jit(solution)/shard_map/ppermute | solution.py:55
  81.3 1.5 %convolution_bitcast_fusion.3 = f32[4,128,4,128]{3,1,2,0:T(8,128)} fusion(bf16[4,4,128,128]{3,2,1,0:T(8,128)(2,1)S(1)} %fusion.12, bf16[4,128,4,128]{1,3,2,0:T(8,128)(2,1)S(1)} %copy.125), kind=kOutput, calls=%fused_computation.11 | convolution fusion | flops 67108864 | bytes 2097152 | tf_op jit(solution)/shard_map/nhij,nihd->njhd/dot_general | solution.py:201
  83.5 4.2 %collective-permute-done.19 = f32[1,129,128]{2,1,0:T(8,128)S(1)} collective-permute-done((f32[1,129,128]{2,1,0:T(8,128)S(1)}, f32[1,129,128]{2,1,0:T(8,128)S(1)}, u32[]{:S(2)}, u32[]{:S(2)}) %collective-permute-start.19) | collective-permute-done | bytes 66080 | tf_op jit(solution)/shard_map/ppermute | solution.py:55
  90.3 6.7 %collective-permute-done.20 = f32[1,129,128]{2,1,0:T(8,128)S(1)} collective-permute-done((f32[1,129,128]{2,1,0:T(8,128)S(1)}, f32[1,129,128]{2,1,0:T(8,128)S(1)}, u32[]{:S(2)}, u32[]{:S(2)}) %collective-permute-start.20) | collective-permute-done | bytes 66080 | tf_op jit(solution)/shard_map/ppermute | solution.py:55
  96.9 3.1 %collective-permute-done.21 = f32[1,129,128]{2,1,0:T(8,128)S(1)} collective-permute-done((f32[1,129,128]{2,1,0:T(8,128)S(1)}, f32[1,129,128]{2,1,0:T(8,128)S(1)}, u32[]{:S(2)}, u32[]{:S(2)}) %collective-permute-start.21) | collective-permute-done | bytes 66080 | tf_op jit(solution)/shard_map/ppermute | solution.py:55
  102.7 1.5 %convolution_bitcast_fusion.1 = f32[4,128,4,128]{3,1,2,0:T(8,128)} fusion(bf16[4,128,4,128]{1,3,2,0:T(8,128)(2,1)S(1)} %multiply_convert_fusion.1, bf16[4,4,128,128]{3,2,1,0:T(8,128)(2,1)S(1)} %copy-done.6), kind=kOutput, calls=%fused_computation.7 | convolution fusion | flops 67108864 | bytes 2097152 | tf_op jit(solution)/shard_map/nhij,nihe->njhe/dot_general | solution.py:204
  105.4 2.0 %collective-permute-done.24 = f32[128,128]{1,0:T(8,128)S(1)} collective-permute-done((f32[128,128]{1,0:T(8,128)S(1)}, f32[128,128]{1,0:T(8,128)S(1)}, u32[]{:S(2)}, u32[]{:S(2)}) %collective-permute-start.24) | collective-permute-done | bytes 65568 | tf_op jit(solution)/shard_map/ppermute | solution.py:74
  110.0 1.7 %fusion.9 = bf16[4,128,4,128]{3,1,2,0:T(8,128)(2,1)S(1)} fusion(f32[4,128,4,128]{3,1,2,0:T(8,128)S(1)} %copy-done.7, f32[4,128,4]{1,2,0:T(4,128)S(1)} %copy.108, bf16[4,128,4,128]{3,2,1,0:T(4,128)(2,1)S(1)} %copy-done.4, f32[1,4,128,128]{3,2,1,0:T(8,128)S(1)} %bitcast.233, f32[1,4,128,128]{3,2,1,0:T(8,128)} %bitcast.235, f32[1,4,128,128]{3,2,1,0:T(8,128)} %bitcast.237, ...), kind=kOutput, calls=%fused_computation.23 | convolution fusion | flops 69468160 | bytes 3416128 | tf_op jit(solution)/shard_map/njhe,nhde->njhd/dot_general | solution.py:224
  (166 shorter events, 42.0 us)
Async XLA Ops:
  6.8 5.2 %collective-permute-start.2 = (f32[129,128]{1,0:T(8,128)S(1)}, f32[129,128]{1,0:T(8,128)S(1)}, u32[]{:S(2)}, u32[]{:S(2)}) collective-permute-start(f32[129,128]{1,0:T(8,128)S(1)} %get-tuple-element.52), channel_id=1, source_target_pairs={{0,24},{8,0},{16,8},{24,16},{1,25},{9,1},{17,9},{25,17},{2,26},{10... | collective-permute-start | bytes 198152 | tf_op jit(solution)/shard_map/ppermute | solution.py:74
  9.7 5.9 %collective-permute-start.1 = (f32[129,128]{1,0:T(8,128)S(1)}, f32[129,128]{1,0:T(8,128)S(1)}, u32[]{:S(2)}, u32[]{:S(2)}) collective-permute-start(f32[129,128]{1,0:T(8,128)S(1)} %get-tuple-element.50), channel_id=1, source_target_pairs={{0,16},{8,24},{16,0},{24,8},{1,17},{9,25},{17,1},{25,9},{2,18},{10... | collective-permute-start | bytes 198152 | tf_op jit(solution)/shard_map/ppermute | solution.py:74
  10.5 5.8 %collective-permute-start = (f32[129,128]{1,0:T(8,128)S(1)}, f32[129,128]{1,0:T(8,128)S(1)}, u32[]{:S(2)}, u32[]{:S(2)}) collective-permute-start(f32[129,128]{1,0:T(8,128)S(1)} %get-tuple-element.51), channel_id=1, source_target_pairs={{0,8},{8,16},{16,24},{24,0},{1,9},{9,17},{17,25},{25,1},{2,10},{10... | collective-permute-start | bytes 198152 | tf_op jit(solution)/shard_map/ppermute | solution.py:74
  17.1 15.1 %collective-permute-start.3 = (f32[1,129,128]{2,1,0:T(8,128)S(1)}, f32[1,129,128]{2,1,0:T(8,128)S(1)}, u32[]{:S(2)}, u32[]{:S(2)}) collective-permute-start(f32[1,129,128]{2,1,0:T(8,128)S(1)} %pad_maximum_fusion.6), channel_id=1, source_target_pairs={{0,32},{32,64},{64,96},{96,128},{128,160},{160,192},{192,224},{1,3... | collective-permute-start | bytes 198152 | tf_op jit(solution)/shard_map/ppermute | solution.py:35
  20.9 13.5 %collective-permute-start.4 = (f32[1,129,128]{2,1,0:T(8,128)S(1)}, f32[1,129,128]{2,1,0:T(8,128)S(1)}, u32[]{:S(2)}, u32[]{:S(2)}) collective-permute-start(f32[1,129,128]{2,1,0:T(8,128)S(1)} %pad_maximum_fusion.6), channel_id=1, source_target_pairs={{0,64},{32,96},{64,128},{96,160},{128,192},{160,224},{1,65},{33,97... | collective-permute-start | bytes 198152 | tf_op jit(solution)/shard_map/ppermute | solution.py:35
  27.3 7.8 %collective-permute-start.8 = (f32[1,129,128]{2,1,0:T(8,128)S(1)}, f32[1,129,128]{2,1,0:T(8,128)S(1)}, u32[]{:S(2)}, u32[]{:S(2)}) collective-permute-start(f32[1,129,128]{2,1,0:T(8,128)S(1)} %pad_maximum_fusion.6), channel_id=1, source_target_pairs={{0,192},{32,224},{1,193},{33,225},{2,194},{34,226},{3,195},{35,227... | collective-permute-start | bytes 198152 | tf_op jit(solution)/shard_map/ppermute | solution.py:35
  28.6 6.5 %collective-permute-start.7 = (f32[1,129,128]{2,1,0:T(8,128)S(1)}, f32[1,129,128]{2,1,0:T(8,128)S(1)}, u32[]{:S(2)}, u32[]{:S(2)}) collective-permute-start(f32[1,129,128]{2,1,0:T(8,128)S(1)} %pad_maximum_fusion.6), channel_id=1, source_target_pairs={{0,160},{32,192},{64,224},{1,161},{33,193},{65,225},{2,162},{34,19... | collective-permute-start | bytes 198152 | tf_op jit(solution)/shard_map/ppermute | solution.py:35
  36.3 5.0 %collective-permute-start.12 = (f32[128,128]{1,0:T(8,128)S(1)}, f32[128,128]{1,0:T(8,128)S(1)}, u32[]{:S(2)}, u32[]{:S(2)}) collective-permute-start(f32[128,128]{1,0:T(8,128)S(1)} %get-tuple-element.58), channel_id=1, source_target_pairs={{0,24},{8,0},{16,8},{24,16},{1,25},{9,1},{17,9},{25,17},{2,26},{10... | collective-permute-start | bytes 196616 | tf_op jit(solution)/shard_map/ppermute | solution.py:74
  36.9 5.8 %collective-permute-start.11 = (f32[128,128]{1,0:T(8,128)S(1)}, f32[128,128]{1,0:T(8,128)S(1)}, u32[]{:S(2)}, u32[]{:S(2)}) collective-permute-start(f32[128,128]{1,0:T(8,128)S(1)} %get-tuple-element.59), channel_id=1, source_target_pairs={{0,16},{8,24},{16,0},{24,8},{1,17},{9,25},{17,1},{25,9},{2,18},{10... | collective-permute-start | bytes 196616 | tf_op jit(solution)/shard_map/ppermute | solution.py:74
  37.8 5.6 %collective-permute-start.10 = (f32[128,128]{1,0:T(8,128)S(1)}, f32[128,128]{1,0:T(8,128)S(1)}, u32[]{:S(2)}, u32[]{:S(2)}) collective-permute-start(f32[128,128]{1,0:T(8,128)S(1)} %get-tuple-element.60), channel_id=1, source_target_pairs={{0,8},{8,16},{16,24},{24,0},{1,9},{9,17},{17,25},{25,1},{2,10},{10... | collective-permute-start | bytes 196616 | tf_op jit(solution)/shard_map/ppermute | solution.py:74
  47.6 9.9 %all-to-all-start = ((f32[8,2,4,128]{3,2,1,0:T(4,128)}), f32[8,2,4,128]{3,2,1,0:T(4,128)S(1)}, u32[]{:S(2)}, u32[]{:S(2)}) async-start(f32[8,2,4,128]{3,2,1,0:T(4,128)} %broadcast_in_dim.17), calls=%async_computation | async-start | bytes 65536 | tf_op jit(solution)/shard_map/all_to_all | solution.py:122
  61.9 5.1 %collective-permute-start.15 = (f32[129,128]{1,0:T(8,128)S(1)}, f32[129,128]{1,0:T(8,128)S(1)}, u32[]{:S(2)}, u32[]{:S(2)}) collective-permute-start(f32[129,128]{1,0:T(8,128)S(1)} %get-tuple-element.48), channel_id=1, source_target_pairs={{0,24},{8,0},{16,8},{24,16},{1,25},{9,1},{17,9},{25,17},{2,26},{10... | collective-permute-start | bytes 198152 | tf_op jit(solution)/shard_map/ppermute | solution.py:74
  64.0 5.8 %collective-permute-start.14 = (f32[129,128]{1,0:T(8,128)S(1)}, f32[129,128]{1,0:T(8,128)S(1)}, u32[]{:S(2)}, u32[]{:S(2)}) collective-permute-start(f32[129,128]{1,0:T(8,128)S(1)} %get-tuple-element.47), channel_id=1, source_target_pairs={{0,16},{8,24},{16,0},{24,8},{1,17},{9,25},{17,1},{25,9},{2,18},{10... | collective-permute-start | bytes 198152 | tf_op jit(solution)/shard_map/ppermute | solution.py:74
  64.9 5.7 %collective-permute-start.13 = (f32[129,128]{1,0:T(8,128)S(1)}, f32[129,128]{1,0:T(8,128)S(1)}, u32[]{:S(2)}, u32[]{:S(2)}) collective-permute-start(f32[129,128]{1,0:T(8,128)S(1)} %get-tuple-element.46), channel_id=1, source_target_pairs={{0,8},{8,16},{16,24},{24,0},{1,9},{9,17},{17,25},{25,1},{2,10},{10... | collective-permute-start | bytes 198152 | tf_op jit(solution)/shard_map/ppermute | solution.py:74
  71.4 16.2 %collective-permute-start.19 = (f32[1,129,128]{2,1,0:T(8,128)S(1)}, f32[1,129,128]{2,1,0:T(8,128)S(1)}, u32[]{:S(2)}, u32[]{:S(2)}) collective-permute-start(f32[1,129,128]{2,1,0:T(8,128)S(1)} %pad_maximum_fusion.7), channel_id=1, source_target_pairs={{128,0},{160,32},{192,64},{224,96},{129,1},{161,33},{193,65},{225,... | collective-permute-start | bytes 198152 | tf_op jit(solution)/shard_map/ppermute | solution.py:55
  72.7 16.2 %collective-permute-start.18 = (f32[1,129,128]{2,1,0:T(8,128)S(1)}, f32[1,129,128]{2,1,0:T(8,128)S(1)}, u32[]{:S(2)}, u32[]{:S(2)}) collective-permute-start(f32[1,129,128]{2,1,0:T(8,128)S(1)} %pad_maximum_fusion.7), channel_id=1, source_target_pairs={{96,0},{128,32},{160,64},{192,96},{224,128},{97,1},{129,33},{161,6... | collective-permute-start | bytes 198152 | tf_op jit(solution)/shard_map/ppermute | solution.py:55
  74.0 16.2 %collective-permute-start.17 = (f32[1,129,128]{2,1,0:T(8,128)S(1)}, f32[1,129,128]{2,1,0:T(8,128)S(1)}, u32[]{:S(2)}, u32[]{:S(2)}) collective-permute-start(f32[1,129,128]{2,1,0:T(8,128)S(1)} %pad_maximum_fusion.7), channel_id=1, source_target_pairs={{64,0},{96,32},{128,64},{160,96},{192,128},{224,160},{65,1},{97,33... | collective-permute-start | bytes 198152 | tf_op jit(solution)/shard_map/ppermute | solution.py:55
  75.3 15.0 %collective-permute-start.16 = (f32[1,129,128]{2,1,0:T(8,128)S(1)}, f32[1,129,128]{2,1,0:T(8,128)S(1)}, u32[]{:S(2)}, u32[]{:S(2)}) collective-permute-start(f32[1,129,128]{2,1,0:T(8,128)S(1)} %pad_maximum_fusion.7), channel_id=1, source_target_pairs={{32,0},{64,32},{96,64},{128,96},{160,128},{192,160},{224,192},{33,... | collective-permute-start | bytes 198152 | tf_op jit(solution)/shard_map/ppermute | solution.py:55
  82.8 17.2 %collective-permute-start.22 = (f32[1,129,128]{2,1,0:T(8,128)S(1)}, f32[1,129,128]{2,1,0:T(8,128)S(1)}, u32[]{:S(2)}, u32[]{:S(2)}) collective-permute-start(f32[1,129,128]{2,1,0:T(8,128)S(1)} %pad_maximum_fusion.7), channel_id=1, source_target_pairs={{224,0},{225,1},{226,2},{227,3},{228,4},{229,5},{230,6},{231,7},{2... | collective-permute-start | bytes 198152 | tf_op jit(solution)/shard_map/ppermute | solution.py:55
  87.6 9.3 %collective-permute-start.20 = (f32[1,129,128]{2,1,0:T(8,128)S(1)}, f32[1,129,128]{2,1,0:T(8,128)S(1)}, u32[]{:S(2)}, u32[]{:S(2)}) collective-permute-start(f32[1,129,128]{2,1,0:T(8,128)S(1)} %pad_maximum_fusion.7), channel_id=1, source_target_pairs={{160,0},{192,32},{224,64},{161,1},{193,33},{225,65},{162,2},{194,3... | collective-permute-start | bytes 198152 | tf_op jit(solution)/shard_map/ppermute | solution.py:55
  88.9 11.1 %collective-permute-start.21 = (f32[1,129,128]{2,1,0:T(8,128)S(1)}, f32[1,129,128]{2,1,0:T(8,128)S(1)}, u32[]{:S(2)}, u32[]{:S(2)}) collective-permute-start(f32[1,129,128]{2,1,0:T(8,128)S(1)} %pad_maximum_fusion.7), channel_id=1, source_target_pairs={{192,0},{224,32},{193,1},{225,33},{194,2},{226,34},{195,3},{227,35... | collective-permute-start | bytes 198152 | tf_op jit(solution)/shard_map/ppermute | solution.py:55
  100.2 5.2 %collective-permute-start.25 = (f32[128,128]{1,0:T(8,128)S(1)}, f32[128,128]{1,0:T(8,128)S(1)}, u32[]{:S(2)}, u32[]{:S(2)}) collective-permute-start(f32[128,128]{1,0:T(8,128)S(1)} %get-tuple-element.54), channel_id=1, source_target_pairs={{0,24},{8,0},{16,8},{24,16},{1,25},{9,1},{17,9},{25,17},{2,26},{10... | collective-permute-start | bytes 196616 | tf_op jit(solution)/shard_map/ppermute | solution.py:74
  100.9 6.5 %collective-permute-start.24 = (f32[128,128]{1,0:T(8,128)S(1)}, f32[128,128]{1,0:T(8,128)S(1)}, u32[]{:S(2)}, u32[]{:S(2)}) collective-permute-start(f32[128,128]{1,0:T(8,128)S(1)} %get-tuple-element.55), channel_id=1, source_target_pairs={{0,16},{8,24},{16,0},{24,8},{1,17},{9,25},{17,1},{25,9},{2,18},{10... | collective-permute-start | bytes 196616 | tf_op jit(solution)/shard_map/ppermute | solution.py:74
  101.7 6.0 %collective-permute-start.23 = (f32[128,128]{1,0:T(8,128)S(1)}, f32[128,128]{1,0:T(8,128)}, u32[]{:S(2)}, u32[]{:S(2)}) collective-permute-start(f32[128,128]{1,0:T(8,128)S(1)} %get-tuple-element.56), channel_id=1, source_target_pairs={{0,8},{8,16},{16,24},{24,0},{1,9},{9,17},{17,25},{25,1},{2,10},{10... | collective-permute-start | bytes 196616 | tf_op jit(solution)/shard_map/ppermute | solution.py:74
  (29 other events, 130.6 us)

commit v8 on v6

--- a/solution.py
+++ b/solution.py
@@ -70,15 +70,7 @@
 
 
 def exchange(payload, axis, ranks):
-    me = lax.axis_index(axis)
-    got = [lax.dynamic_index_in_dim(payload, me, 0, keepdims=False)]
-    for shift in range(1, ranks):
-        send = lax.dynamic_index_in_dim(payload, (me + shift) % ranks, 0, keepdims=False)
-        pairs = [(i, (i + shift) % ranks) for i in range(ranks)]
-        got.append(lax.ppermute(send, axis, pairs))
-    stacked = jnp.stack(got)
-    order = (me - jnp.arange(ranks)) % ranks
-    return jnp.take(stacked, order, axis=0)
+    return lax.all_to_all(payload, axis, 0, 0, tiled=True)
 
 
 def lane_rows(shard_total, width):

time: 112 us -> 131 us (1.17)
  waiting for transfers between devices: 33.5 us -> 42.6 us
  other arithmetic: 2.45 us -> 8.57 us
  starting transfers between devices: 42.6 us -> 44.9 us
    all_to_all x0 -> x4, waiting for transfers between devices: none -> 22 us  [exchange(): return lax.all_to_all(payload, axis, 0, 0, tiled=True)]
    all_to_all x0 -> x4, starting transfers between devices: none -> 14.5 us  [exchange(): return lax.all_to_all(payload, axis, 0, 0, tiled=True)]
    ppermute x12 -> x0, starting transfers between devices: 13.1 us -> none  [exchange(): got.append(lax.ppermute(send, axis, pairs))]
    ppermute x12 -> x0, waiting for transfers between devices: 12.1 us -> none  [exchange(): got.append(lax.ppermute(send, axis, pairs))]
    gather x4 -> x0, local copies, waits for them, and re-layouts: 2.27 us -> none  [exchange(): return jnp.take(stacked, order, axis=0)]
    concatenate x6, other arithmetic: 0.08 us -> 2.1 us  [pack(): return jnp.concatenate([state, total_row], axis=1)]
    exp x1, local copies, waits for them, and re-layouts: 0.11 us -> 1.7 us  [shards(): jnp.exp(inside_block_mask)[..., None] * inter_out]
    unnamed x47 -> x89, local copies, waits for them, and re-layouts: 7.87 us -> 9.01 us
  transfers between devices with their start and end apart: 21 -> 13, of which waited for: 16 -> 11; matrix products, arithmetic and copies ran while one was open for 10% -> 11% of each run, Pallas kernels for 0% -> 0%
where the time goes in v8:
time: 131 us; the launch traced here: 130 us
  starting transfers between devices  44.9 us (34%)
  waiting for transfers between devices  42.6 us (33%)
  matrix products  17.6 us (13%)
  local copies, waits for them, and re-layouts  14.9 us (11%)
  other arithmetic  8.57 us (7%)
    all_to_all x4, waiting for transfers between devices, exchange(): return lax.all_to_all(payload, axis, 0, 0, tiled=True)  22 us
    ppermute x4, starting transfers between devices, forward_scan(): lax.ppermute(payload, axis, [(i, i + s) for i in range(ranks - s)])  19.8 us
    all_to_all x4, starting transfers between devices, exchange(): return lax.all_to_all(payload, axis, 0, 0, tiled=True)  14.5 us
    ppermute x4, waiting for transfers between devices, backward_scan(): lax.ppermute(payload, axis, [(i + s, i) for i in range(ranks - s)])  11.7 us
    unnamed x89, local copies, waits for them, and re-layouts  9.01 us
    ppermute x4, starting transfers between devices, backward_scan(): lax.ppermute(payload, axis, [(i + s, i) for i in range(ranks - s)])  5.92 us
    all_to_all x1, waiting for transfers between devices, head_sum(): gathered = lax.all_to_all(copies, 'head', 0, 0, tiled=True)  5.43 us
    all_to_all x1, starting transfers between devices, head_sum(): gathered = lax.all_to_all(copies, 'head', 0, 0, tiled=True)  4.6 us
  transfers between devices with their start and end apart: 13, of which 11 were waited for; matrix products, arithmetic and copies ran while one was open for 11% of the time, Pallas kernels for 0%

profile of v8, /device:TPU:32, one launch (start us, length us, event | category | flops | bytes accessed | tf_op | source)
XLA Modules:
  0.0 129.9 jit_solution(134107741483033868)
XLA Ops:
  5.5 2.0 %multiply_reduce_fusion.7 = (f32[4,128,128]{2,1,0:T(8,128)S(1)}, f32[4,128,128]{2,1,0:T(8,128)}, f32[4,128,128]{2,1,0:T(8,128)}, f32[4,128,128]{2,1,0:T(8,128)}, f32[4,128,128]{2,1,0:T(8,128)}) fusion(f32[4,4]{1,0:T(4,128)S(1)} %subtract_exponential_fusion.1, f32[4,4]{1,0:T(4,128)S(1)} %get-tuple-element.66, f32[4,4]{1,0:T(4,128)S(1)} %get-tuple-element.67, ...), kind=kOutput, calls=%fused_computation.36 | convolution fusion | flops 70189056 | bytes 2367808 | tf_op jit(solution)/shard_map/njhd,njhe->nhde/dot_general | solution.py:160
  8.3 4.3 %all-to-all-start = ((f32[4,129,128]{2,1,0:T(8,128)}), f32[4,129,128]{2,1,0:T(8,128)S(1)}, u32[]{:S(2)}, u32[]{:S(2)}) async-start(f32[4,129,128]{2,1,0:T(8,128)} %pad_maximum_fusion.1), calls=%async_computation | async-start | bytes 557056 | tf_op jit(solution)/shard_map/all_to_all | solution.py:73
  13.1 6.3 %all-to-all-done = f32[4,129,128]{2,1,0:T(8,128)S(1)} async-done(((f32[4,129,128]{2,1,0:T(8,128)}), f32[4,129,128]{2,1,0:T(8,128)S(1)}, u32[]{:S(2)}, u32[]{:S(2)}) %all-to-all-start) | async-done | bytes 264224 | tf_op jit(solution)/shard_map/all_to_all | solution.py:73
  20.6 3.8 %collective-permute-start = (f32[1,129,128]{2,1,0:T(8,128)S(1)}, f32[1,129,128]{2,1,0:T(8,128)S(1)}, u32[]{:S(2)}, u32[]{:S(2)}) collective-permute-start(f32[1,129,128]{2,1,0:T(8,128)S(1)} %pad_maximum_fusion.4), channel_id=1, source_target_pairs={{0,32},{32,64},{64,96},{96,128},{128,160},{160,192},{192,224},{1,3... | collective-permute-start | bytes 198152 | tf_op jit(solution)/shard_map/ppermute | solution.py:39
  24.4 6.4 %collective-permute-start.1 = (f32[1,129,128]{2,1,0:T(8,128)S(1)}, f32[1,129,128]{2,1,0:T(8,128)S(1)}, u32[]{:S(2)}, u32[]{:S(2)}) collective-permute-start(f32[1,129,128]{2,1,0:T(8,128)S(1)} %pad_maximum_fusion.4), channel_id=1, source_target_pairs={{0,64},{32,96},{64,128},{96,160},{128,192},{160,224},{1,65},{33,97... | collective-permute-start | bytes 198152 | tf_op jit(solution)/shard_map/ppermute | solution.py:39
  30.9 1.9 %collective-permute-done.1 = f32[1,129,128]{2,1,0:T(8,128)S(1)} collective-permute-done((f32[1,129,128]{2,1,0:T(8,128)S(1)}, f32[1,129,128]{2,1,0:T(8,128)S(1)}, u32[]{:S(2)}, u32[]{:S(2)}) %collective-permute-start.1) | collective-permute-done | bytes 66080 | tf_op jit(solution)/shard_map/ppermute | solution.py:39
  34.0 8.3 %collective-permute-start.2 = (f32[1,129,128]{2,1,0:T(8,128)}, f32[1,129,128]{2,1,0:T(8,128)}, u32[]{:S(2)}, u32[]{:S(2)}) collective-permute-start(f32[1,129,128]{2,1,0:T(8,128)} %pad_maximum_fusion.5), channel_id=1, source_target_pairs={{0,96},{32,128},{64,160},{96,192},{128,224},{1,97},{33,129},{65,16... | collective-permute-start | bytes 198152 | tf_op jit(solution)/shard_map/ppermute | solution.py:39
  44.4 1.7 %copy.106 = f32[4,128,4]{1,2,0:T(4,128)} copy(f32[4,128,4]{2,1,0:T(8,128)} %get-tuple-element.46) | data formatting | bytes 16384 | tf_op jit(solution)/shard_map/exp | solution.py:175
  52.6 3.4 %all-to-all-start.1 = ((f32[4,128,128]{2,1,0:T(8,128)}), f32[4,128,128]{2,1,0:T(8,128)S(1)}, u32[]{:S(2)}, u32[]{:S(2)}) async-start(f32[4,128,128]{2,1,0:T(8,128)} %pad_maximum_fusion.2), calls=%async_computation.1 | async-start | bytes 524288 | tf_op jit(solution)/shard_map/all_to_all | solution.py:73
  57.5 5.1 %all-to-all-done.1 = f32[4,128,128]{2,1,0:T(8,128)S(1)} async-done(((f32[4,128,128]{2,1,0:T(8,128)}), f32[4,128,128]{2,1,0:T(8,128)S(1)}, u32[]{:S(2)}, u32[]{:S(2)}) %all-to-all-start.1) | async-done | bytes 262176 | tf_op jit(solution)/shard_map/all_to_all | solution.py:73
  63.3 2.1 %multiply_reduce_fusion.6 = (f32[4,128]{1,0:T(4,128)S(1)}, f32[4,128]{1,0:T(4,128)S(1)}, f32[4,128,4,128]{1,3,2,0:T(8,128)S(1)}) fusion(f32[4,128,4,128]{1,3,2,0:T(8,128)S(1)} %copy.114, f32[4,128,4,128]{1,3,2,0:T(8,128)} %convolution_bitcast_fusion.7, bf16[4,128,4,128]{1,3,2,0:T(8,128)(2,1)S(1)} %copy.125, f32[1,4,128,128]{3,2,1,0:T(8,128)} %bitcast.165, ...), kind=kOutput, calls=%fused_computation.35 | convolution fusion | flops 70253568 | bytes 4993088 | tf_op jit(solution)/shard_map/nihd,nhde->nihe/dot_general | solution.py:172
  66.1 4.6 %all-to-all-start.2 = ((f32[8,2,4,128]{3,2,1,0:T(4,128)}), f32[8,2,4,128]{3,2,1,0:T(4,128)S(1)}, u32[]{:S(2)}, u32[]{:S(2)}) async-start(f32[8,2,4,128]{3,2,1,0:T(4,128)} %broadcast_in_dim.5), calls=%async_computation.2 | async-start | bytes 65536 | tf_op jit(solution)/shard_map/all_to_all | solution.py:118
  70.7 5.4 %all-to-all-done.2 = f32[8,2,4,128]{3,2,1,0:T(4,128)S(1)} async-done(((f32[8,2,4,128]{3,2,1,0:T(4,128)}), f32[8,2,4,128]{3,2,1,0:T(4,128)S(1)}, u32[]{:S(2)}, u32[]{:S(2)}) %all-to-all-start.2) | async-done | bytes 32800 | tf_op jit(solution)/shard_map/all_to_all | solution.py:118
  80.2 3.4 %all-to-all-start.3 = ((f32[4,129,128]{2,1,0:T(8,128)}), f32[4,129,128]{2,1,0:T(8,128)S(1)}, u32[]{:S(2)}, u32[]{:S(2)}) async-start(f32[4,129,128]{2,1,0:T(8,128)} %pad_maximum_fusion), calls=%async_computation.3 | async-start | bytes 557056 | tf_op jit(solution)/shard_map/all_to_all | solution.py:73
  85.2 5.5 %all-to-all-done.3 = f32[4,129,128]{2,1,0:T(8,128)S(1)} async-done(((f32[4,129,128]{2,1,0:T(8,128)}), f32[4,129,128]{2,1,0:T(8,128)S(1)}, u32[]{:S(2)}, u32[]{:S(2)}) %all-to-all-start.3) | async-done | bytes 264224 | tf_op jit(solution)/shard_map/all_to_all | solution.py:73
  90.8 2.1 %collective-permute-start.4 = (f32[1,129,128]{2,1,0:T(8,128)S(1)}, f32[1,129,128]{2,1,0:T(8,128)S(1)}, u32[]{:S(2)}, u32[]{:S(2)}) collective-permute-start(f32[1,129,128]{2,1,0:T(8,128)S(1)} %pad_maximum_fusion.6), channel_id=1, source_target_pairs={{32,0},{64,32},{96,64},{128,96},{160,128},{192,160},{224,192},{33,... | collective-permute-start | bytes 198152 | tf_op jit(solution)/shard_map/ppermute | solution.py:59
  94.2 1.8 %fusion.8 = bf16[4,128,4,128]{1,3,2,0:T(8,128)(2,1)S(1)} fusion(f32[4,128,4,128]{1,3,2,0:T(8,128)} %convolution_bitcast_fusion.5, bf16[4,128,4,128]{1,3,2,0:T(8,128)(2,1)S(1)} %multiply_convert_fusion.1, f32[4,128,4]{1,2,0:T(4,128)S(1)} %copy-done.20, f32[1,4,128,128]{3,2,1,0:T(8,128)S(1)} %bitcast.166, f32[1,4,128,128]{3,2,1,0:T(8,128)S(1)} %bitcast.168, ...), kind=kOutput, calls=%fused_computation.18 | convolution fusion | flops 69468160 | bytes 3416128 | tf_op jit(solution)/shard_map/nihe,nhde->nihd/dot_general | solution.py:194
  96.0 2.2 %collective-permute-done.4 = f32[1,129,128]{2,1,0:T(8,128)S(1)} collective-permute-done((f32[1,129,128]{2,1,0:T(8,128)S(1)}, f32[1,129,128]{2,1,0:T(8,128)S(1)}, u32[]{:S(2)}, u32[]{:S(2)}) %collective-permute-start.4) | collective-permute-done | bytes 66080 | tf_op jit(solution)/shard_map/ppermute | solution.py:59
  98.2 2.5 %collective-permute-done.5 = f32[1,129,128]{2,1,0:T(8,128)S(1)} collective-permute-done((f32[1,129,128]{2,1,0:T(8,128)S(1)}, f32[1,129,128]{2,1,0:T(8,128)S(1)}, u32[]{:S(2)}, u32[]{:S(2)}) %collective-permute-start.5) | collective-permute-done | bytes 66080 | tf_op jit(solution)/shard_map/ppermute | solution.py:59
  106.0 4.0 %collective-permute-done.6 = f32[1,129,128]{2,1,0:T(8,128)S(1)} collective-permute-done((f32[1,129,128]{2,1,0:T(8,128)S(1)}, f32[1,129,128]{2,1,0:T(8,128)S(1)}, u32[]{:S(2)}, u32[]{:S(2)}) %collective-permute-start.6) | collective-permute-done | bytes 66080 | tf_op jit(solution)/shard_map/ppermute | solution.py:59
  110.0 3.1 %collective-permute-done.7 = f32[1,129,128]{2,1,0:T(8,128)S(1)} collective-permute-done((f32[1,129,128]{2,1,0:T(8,128)S(1)}, f32[1,129,128]{2,1,0:T(8,128)S(1)}, u32[]{:S(2)}, u32[]{:S(2)}) %collective-permute-start.7) | collective-permute-done | bytes 66080 | tf_op jit(solution)/shard_map/ppermute | solution.py:59
  113.8 3.4 %all-to-all-start.4 = ((f32[4,128,128]{2,1,0:T(8,128)}), f32[4,128,128]{2,1,0:T(8,128)S(1)}, u32[]{:S(2)}, u32[]{:S(2)}) async-start(f32[4,128,128]{2,1,0:T(8,128)} %pad_maximum_fusion.3), calls=%async_computation.4 | async-start | bytes 524288 | tf_op jit(solution)/shard_map/all_to_all | solution.py:73
  118.8 5.1 %all-to-all-done.4 = f32[4,128,128]{2,1,0:T(8,128)S(1)} async-done(((f32[4,128,128]{2,1,0:T(8,128)}), f32[4,128,128]{2,1,0:T(8,128)S(1)}, u32[]{:S(2)}, u32[]{:S(2)}) %all-to-all-start.4) | async-done | bytes 262176 | tf_op jit(solution)/shard_map/all_to_all | solution.py:73
  124.6 1.8 %fusion.9 = bf16[4,128,4,128]{3,1,2,0:T(8,128)(2,1)S(1)} fusion(f32[4,128,4,128]{3,1,2,0:T(8,128)S(1)} %copy-done.7, f32[4,128,4]{1,2,0:T(4,128)S(1)} %copy-done.27, bf16[4,128,4,128]{3,2,1,0:T(4,128)(2,1)S(1)} %copy-done.4, f32[1,4,128,128]{3,2,1,0:T(8,128)} %bitcast.182, f32[1,4,128,128]{3,2,1,0:T(8,128)} %bitcast.184, f32[1,4,128,128]{3,2,1,0:T(8,128)} %bitcast.186, ...), kind=kOutput, calls=%fused_computation.19 | convolution fusion | flops 69468160 | bytes 3416128 | tf_op jit(solution)/shard_map/njhe,nhde->njhd/dot_general | solution.py:220
  (159 shorter events, 38.5 us)
Async XLA Ops:
  3.9 38.5 %copy-start = (bf16[4,128,4,128]{3,2,1,0:T(4,128)(2,1)}, bf16[4,128,4,128]{3,2,1,0:T(4,128)(2,1)S(1)}, u32[]{:S(2)}) copy-start(bf16[4,128,4,128]{3,2,1,0:T(4,128)(2,1)S(1)} %reshape.472) | copy-start | bytes 1572868
  4.0 52.0 %copy-start.2 = (bf16[4,128,4,128]{3,2,1,0:T(4,128)(2,1)}, bf16[4,128,4,128]{3,2,1,0:T(4,128)(2,1)S(1)}, u32[]{:S(2)}) copy-start(bf16[4,128,4,128]{3,2,1,0:T(4,128)(2,1)S(1)} %reshape.474) | copy-start | bytes 1572868
  7.6 5.0 %copy-start.12 = (bf16[512,512]{1,0:T(8,128)(2,1)S(1)}, bf16[512,512]{1,0:T(8,128)(2,1)}, u32[]{:S(2)}) copy-start(bf16[512,512]{1,0:T(8,128)(2,1)} %param.5) | copy-start | bytes 1572868
  8.3 11.1 %all-to-all-start = ((f32[4,129,128]{2,1,0:T(8,128)}), f32[4,129,128]{2,1,0:T(8,128)S(1)}, u32[]{:S(2)}, u32[]{:S(2)}) async-start(f32[4,129,128]{2,1,0:T(8,128)} %pad_maximum_fusion.1), calls=%async_computation | async-start | bytes 557056 | tf_op jit(solution)/shard_map/all_to_all | solution.py:73
  13.1 29.2 %copy-start.28 = (f32[4,4,128]{2,1,0:T(4,128)}, f32[4,4,128]{2,1,0:T(4,128)S(1)}, u32[]{:S(2)}) copy-start(f32[4,4,128]{2,1,0:T(4,128)S(1)} %copy.103) | copy-start | bytes 24580
  20.6 10.3 %collective-permute-start = (f32[1,129,128]{2,1,0:T(8,128)S(1)}, f32[1,129,128]{2,1,0:T(8,128)S(1)}, u32[]{:S(2)}, u32[]{:S(2)}) collective-permute-start(f32[1,129,128]{2,1,0:T(8,128)S(1)} %pad_maximum_fusion.4), channel_id=1, source_target_pairs={{0,32},{32,64},{64,96},{96,128},{128,160},{160,192},{192,224},{1,3... | collective-permute-start | bytes 198152 | tf_op jit(solution)/shard_map/ppermute | solution.py:39
  24.4 8.3 %collective-permute-start.1 = (f32[1,129,128]{2,1,0:T(8,128)S(1)}, f32[1,129,128]{2,1,0:T(8,128)S(1)}, u32[]{:S(2)}, u32[]{:S(2)}) collective-permute-start(f32[1,129,128]{2,1,0:T(8,128)S(1)} %pad_maximum_fusion.4), channel_id=1, source_target_pairs={{0,64},{32,96},{64,128},{96,160},{128,192},{160,224},{1,65},{33,97... | collective-permute-start | bytes 198152 | tf_op jit(solution)/shard_map/ppermute | solution.py:39
  34.0 9.7 %copy-start.9 = (bf16[512,512]{1,0:T(8,128)(2,1)S(1)}, bf16[512,512]{1,0:T(8,128)(2,1)}, u32[]{:S(2)}) copy-start(bf16[512,512]{1,0:T(8,128)(2,1)} %param.8) | copy-start | bytes 1572868
  34.0 13.4 %collective-permute-start.2 = (f32[1,129,128]{2,1,0:T(8,128)}, f32[1,129,128]{2,1,0:T(8,128)}, u32[]{:S(2)}, u32[]{:S(2)}) collective-permute-start(f32[1,129,128]{2,1,0:T(8,128)} %pad_maximum_fusion.5), channel_id=1, source_target_pairs={{0,96},{32,128},{64,160},{96,192},{128,224},{1,97},{33,129},{65,16... | collective-permute-start | bytes 198152 | tf_op jit(solution)/shard_map/ppermute | solution.py:39
  46.1 3.5 %collective-permute-start.3 = (f32[1,129,128]{2,1,0:T(8,128)}, f32[1,129,128]{2,1,0:T(8,128)S(1)}, u32[]{:S(2)}, u32[]{:S(2)}) collective-permute-start(f32[1,129,128]{2,1,0:T(8,128)} %pad_maximum_fusion.5), channel_id=1, source_target_pairs={{0,192},{32,224},{1,193},{33,225},{2,194},{34,226},{3,195},{35,227... | collective-permute-start | bytes 198152 | tf_op jit(solution)/shard_map/ppermute | solution.py:39
  51.9 4.2 %copy-start.5 = (bf16[4,4,128,128]{3,2,1,0:T(8,128)(2,1)S(1)}, bf16[4,4,128,128]{3,2,1,0:T(8,128)(2,1)}, u32[]{:S(2)}) copy-start(bf16[4,4,128,128]{3,2,1,0:T(8,128)(2,1)} %fusion.11) | copy-start | bytes 1572868
  52.6 10.1 %all-to-all-start.1 = ((f32[4,128,128]{2,1,0:T(8,128)}), f32[4,128,128]{2,1,0:T(8,128)S(1)}, u32[]{:S(2)}, u32[]{:S(2)}) async-start(f32[4,128,128]{2,1,0:T(8,128)} %pad_maximum_fusion.2), calls=%async_computation.1 | async-start | bytes 524288 | tf_op jit(solution)/shard_map/all_to_all | solution.py:73
  66.1 4.6 %copy-start.21 = (f32[4,4,4]{2,1,0:T(4,128)S(1)}, f32[4,4,4]{2,1,0:T(4,128)}, u32[]{:S(2)}) copy-start(f32[4,4,4]{2,1,0:T(4,128)} %get-tuple-element.69) | copy-start | bytes 772
  66.1 10.0 %all-to-all-start.2 = ((f32[8,2,4,128]{3,2,1,0:T(4,128)}), f32[8,2,4,128]{3,2,1,0:T(4,128)S(1)}, u32[]{:S(2)}, u32[]{:S(2)}) async-start(f32[8,2,4,128]{3,2,1,0:T(4,128)} %broadcast_in_dim.5), calls=%async_computation.2 | async-start | bytes 65536 | tf_op jit(solution)/shard_map/all_to_all | solution.py:118
  79.5 4.2 %copy-start.1 = (bf16[4,128,4,128]{3,2,1,0:T(4,128)(2,1)S(1)}, bf16[4,128,4,128]{3,2,1,0:T(4,128)(2,1)}, u32[]{:S(2)}) copy-start(bf16[4,128,4,128]{3,2,1,0:T(4,128)(2,1)} %copy-done) | copy-start | bytes 1572868
  80.2 10.5 %all-to-all-start.3 = ((f32[4,129,128]{2,1,0:T(8,128)}), f32[4,129,128]{2,1,0:T(8,128)S(1)}, u32[]{:S(2)}, u32[]{:S(2)}) async-start(f32[4,129,128]{2,1,0:T(8,128)} %pad_maximum_fusion), calls=%async_computation.3 | async-start | bytes 557056 | tf_op jit(solution)/shard_map/all_to_all | solution.py:73
  90.8 7.4 %collective-permute-start.4 = (f32[1,129,128]{2,1,0:T(8,128)S(1)}, f32[1,129,128]{2,1,0:T(8,128)S(1)}, u32[]{:S(2)}, u32[]{:S(2)}) collective-permute-start(f32[1,129,128]{2,1,0:T(8,128)S(1)} %pad_maximum_fusion.6), channel_id=1, source_target_pairs={{32,0},{64,32},{96,64},{128,96},{160,128},{192,160},{224,192},{33,... | collective-permute-start | bytes 198152 | tf_op jit(solution)/shard_map/ppermute | solution.py:59
  92.9 7.8 %collective-permute-start.5 = (f32[1,129,128]{2,1,0:T(8,128)S(1)}, f32[1,129,128]{2,1,0:T(8,128)S(1)}, u32[]{:S(2)}, u32[]{:S(2)}) collective-permute-start(f32[1,129,128]{2,1,0:T(8,128)S(1)} %pad_maximum_fusion.6), channel_id=1, source_target_pairs={{64,0},{96,32},{128,64},{160,96},{192,128},{224,160},{65,1},{97,33... | collective-permute-start | bytes 198152 | tf_op jit(solution)/shard_map/ppermute | solution.py:59
  100.8 9.2 %collective-permute-start.6 = (f32[1,129,128]{2,1,0:T(8,128)S(1)}, f32[1,129,128]{2,1,0:T(8,128)S(1)}, u32[]{:S(2)}, u32[]{:S(2)}) collective-permute-start(f32[1,129,128]{2,1,0:T(8,128)S(1)} %pad_maximum_fusion.7), channel_id=1, source_target_pairs={{96,0},{128,32},{160,64},{192,96},{224,128},{97,1},{129,33},{161,6... | collective-permute-start | bytes 198152 | tf_op jit(solution)/shard_map/ppermute | solution.py:59
  104.7 8.3 %collective-permute-start.7 = (f32[1,129,128]{2,1,0:T(8,128)S(1)}, f32[1,129,128]{2,1,0:T(8,128)S(1)}, u32[]{:S(2)}, u32[]{:S(2)}) collective-permute-start(f32[1,129,128]{2,1,0:T(8,128)S(1)} %pad_maximum_fusion.7), channel_id=1, source_target_pairs={{192,0},{224,32},{193,1},{225,33},{194,2},{226,34},{195,3},{227,35... | collective-permute-start | bytes 198152 | tf_op jit(solution)/shard_map/ppermute | solution.py:59
  113.8 10.1 %all-to-all-start.4 = ((f32[4,128,128]{2,1,0:T(8,128)}), f32[4,128,128]{2,1,0:T(8,128)S(1)}, u32[]{:S(2)}, u32[]{:S(2)}) async-start(f32[4,128,128]{2,1,0:T(8,128)} %pad_maximum_fusion.3), calls=%async_computation.4 | async-start | bytes 524288 | tf_op jit(solution)/shard_map/all_to_all | solution.py:73
  117.3 6.6 %copy-start.4 = (bf16[4,128,4,128]{3,2,1,0:T(4,128)(2,1)S(1)}, bf16[4,128,4,128]{3,2,1,0:T(4,128)(2,1)}, u32[]{:S(2)}) copy-start(bf16[4,128,4,128]{3,2,1,0:T(4,128)(2,1)} %copy-done.2) | copy-start | bytes 1572868
  117.3 6.6 %copy-start.7 = (f32[4,128,4,128]{3,1,2,0:T(8,128)S(1)}, f32[4,128,4,128]{3,1,2,0:T(8,128)}, u32[]{:S(2)}) copy-start(f32[4,128,4,128]{3,1,2,0:T(8,128)} %convolution_bitcast_fusion.3) | copy-start | bytes 3145732
  118.8 5.1 %copy-start.27 = (f32[4,128,4]{1,2,0:T(4,128)S(1)}, f32[4,128,4]{1,2,0:T(4,128)}, u32[]{:S(2)}) copy-start(f32[4,128,4]{1,2,0:T(4,128)} %copy-done.26) | copy-start | bytes 24580
  (32 other events, 48.4 us)

commit v9 on v6

--- a/solution.py
+++ b/solution.py
@@ -24,7 +24,8 @@
 def radix_shifts(ranks):
     rounds, width = [], 1
     while width < ranks:
-        rounds.append([s for s in (width, 2 * width) if s < ranks])
+        shifts = [s for s in (width, 2 * width) if s < ranks]
+        rounds.append(sorted(shifts, key=lambda s: -min(s, ranks - s)))
         width *= 3
     return rounds
 
@@ -35,10 +36,11 @@
     rounds = radix_shifts(ranks)
     for step, shifts in enumerate(rounds):
         payload = pack(win_a, win_b)
-        got = [
-            unpack(lax.ppermute(payload, axis, [(i, i + s) for i in range(ranks - s)]))
+        sent = {
+            s: unpack(lax.ppermute(payload, axis, [(i, i + s) for i in range(ranks - s)]))
             for s in shifts
-        ]
+        }
+        got = [sent[s] for s in sorted(shifts)]
         last = step == len(rounds) - 1
         for got_a, got_b in got:
             excl_b = jnp.exp(excl_a) * got_b + excl_b
@@ -55,10 +57,11 @@
     rounds = radix_shifts(ranks)
     for step, shifts in enumerate(rounds):
         payload = pack(win_a, win_c)
-        got = [
-            unpack(lax.ppermute(payload, axis, [(i + s, i) for i in range(ranks - s)]))
+        sent = {
+            s: unpack(lax.ppermute(payload, axis, [(i + s, i) for i in range(ranks - s)]))
             for s in shifts
-        ]
+        }
+        got = [sent[s] for s in sorted(shifts)]
         last = step == len(rounds) - 1
         for got_a, got_c in got:
             excl_c = excl_c + jnp.exp(excl_a) * got_c
@@ -72,10 +75,12 @@
 def exchange(payload, axis, ranks):
     me = lax.axis_index(axis)
     got = [lax.dynamic_index_in_dim(payload, me, 0, keepdims=False)]
-    for shift in range(1, ranks):
+    received = {}
+    for shift in sorted(range(1, ranks), key=lambda s: -min(s, ranks - s)):
         send = lax.dynamic_index_in_dim(payload, (me + shift) % ranks, 0, keepdims=False)
         pairs = [(i, (i + shift) % ranks) for i in range(ranks)]
-        got.append(lax.ppermute(send, axis, pairs))
+        received[shift] = lax.ppermute(send, axis, pairs)
+    got += [received[shift] for shift in range(1, ranks)]
     stacked = jnp.stack(got)
     order = (me - jnp.arange(ranks)) % ranks
     return jnp.take(stacked, order, axis=0)
@@ -225,16 +230,21 @@
         + jnp.exp(shard_total[None, :] - before - totals)[:, :, None, None] * later_state[None]
     )
     back_b = back_states.astype(jnp.bfloat16)
-    key_grad = key_intra + to_end[..., None] * jnp.einsum(
-        "njhe,nhde->njhd", value_block_rows, back_b, preferred_element_type=jnp.float32
-    )
-    value_grad = value_within_block + to_end[..., None] * jnp.einsum(
-        "njhd,nhde->njhe", key_blocks, back_b, preferred_element_type=jnp.float32
-    )
+    key_heads, value_heads = [], []
+    for h in range(heads_dev):
+        back_h = back_b[:, h]
+        key_h = key_intra[:, :, h] + to_end[:, :, h, None] * jnp.einsum(
+            "nje,nde->njd", value_block_rows[:, :, h], back_h, preferred_element_type=jnp.float32
+        )
+        value_h = value_within_block[:, :, h] + to_end[:, :, h, None] * jnp.einsum(
+            "njd,nde->nje", key_blocks[:, :, h], back_h, preferred_element_type=jnp.float32
+        )
+        key_heads.append(key_h.reshape(tok_rows, head_size).astype(jnp.bfloat16))
+        value_heads.append(value_h.reshape(tok_rows, head_size).astype(jnp.bfloat16))
     return (
         query_gradient.reshape(tok_rows, row_width).astype(jnp.bfloat16),
-        key_grad.reshape(tok_rows, row_width).astype(jnp.bfloat16),
-        value_grad.reshape(tok_rows, row_width).astype(jnp.bfloat16),
+        jnp.concatenate(key_heads, axis=1),
+        jnp.concatenate(value_heads, axis=1),
     )
 
 

time: 112 us -> 123 us (1.098)
  local copies, waits for them, and re-layouts: 14.5 us -> 27.8 us
  waiting for transfers between devices: 33.5 us -> 28.4 us
  other arithmetic: 2.45 us -> 6.92 us
    slice x0 -> x3, local copies, waits for them, and re-layouts: none -> 4.74 us  [the longest x1 1.85 us: shards(): value_block_rows[:, :, h]]
    unnamed x47 -> x89, local copies, waits for them, and re-layouts: 7.87 us -> 11.9 us
    ppermute x12, waiting for transfers between devices: 12.1 us -> 9.1 us  [exchange(): received[shift] = lax.ppermute(send, axis, pairs)]
    convert_element_type x2, local copies, waits for them, and re-layouts: 0.66 us -> 2.84 us  [shards(): grad_f32 = grad_blocks.astype(jnp.float32)]
    concatenate x0 -> x2, other arithmetic: none -> 1.72 us  [the longest x1 0.87 us: shards(): jnp.concatenate(value_heads, axis=1)]
    dynamic_slice x2, local copies, waits for them, and re-layouts: 0.06 us -> 1.32 us  [exchange(): got = [lax.dynamic_index_in_dim(payload, me, 0, keepdims=False)]]
  transfers between devices with their start and end apart: 21 -> 21, of which waited for: 16 -> 15; matrix products, arithmetic and copies ran while one was open for 10% -> 15% of each run, Pallas kernels for 0% -> 0%
where the time goes in v9:
time: 123 us; the launch traced here: 122 us
  starting transfers between devices  42.3 us (34%)
  waiting for transfers between devices  28.4 us (23%)
  local copies, waits for them, and re-layouts  27.8 us (23%)
  matrix products  15.4 us (13%)
  other arithmetic  6.92 us (6%)
  between operations  1.53 us (1%)
    ppermute x4, starting transfers between devices, forward_scan(): lax.ppermute(payload, axis, [(i, i + s) for i in range(ranks - s)])  19.1 us
    ppermute x12, starting transfers between devices, exchange(): received[shift] = lax.ppermute(send, axis, pairs)  12.8 us
    unnamed x89, local copies, waits for them, and re-layouts  11.9 us
    ppermute x4, waiting for transfers between devices, backward_scan(): lax.ppermute(payload, axis, [(i + s, i) for i in range(ranks - s)])  11.8 us
    ppermute x12, waiting for transfers between devices, exchange(): received[shift] = lax.ppermute(send, axis, pairs)  9.1 us
    ppermute x4, starting transfers between devices, backward_scan(): lax.ppermute(payload, axis, [(i + s, i) for i in range(ranks - s)])  5.92 us
    all_to_all x1, starting transfers between devices, head_sum(): gathered = lax.all_to_all(copies, 'head', 0, 0, tiled=True)  4.47 us
    all_to_all x1, waiting for transfers between devices, head_sum(): gathered = lax.all_to_all(copies, 'head', 0, 0, tiled=True)  4.36 us
  transfers between devices with their start and end apart: 21, of which 15 were waited for; matrix products, arithmetic and copies ran while one was open for 15% of the time, Pallas kernels for 0%

profile of v9, /device:TPU:32, one launch (start us, length us, event | category | flops | bytes accessed | tf_op | source)
XLA Modules:
  0.0 122.3 jit_solution(14235633684426226454)
XLA Ops:
  5.4 1.6 %multiply_reduce_fusion.7 = (f32[4,128,128]{2,1,0:T(8,128)S(1)}, f32[4,128,128]{2,1,0:T(8,128)}, f32[4,128,128]{2,1,0:T(8,128)}, f32[4,128,128]{2,1,0:T(8,128)}, f32[4,128,128]{2,1,0:T(8,128)}) fusion(f32[4,4]{1,0:T(4,128)S(1)} %subtract_exponential_fusion.1, f32[4,4]{1,0:T(4,128)S(1)} %get-tuple-element.96, f32[4,4]{1,0:T(4,128)S(1)} %get-tuple-element.97, ...), kind=kOutput, calls=%fused_computation.64 | convolution fusion | flops 69402624 | bytes 2359616 | tf_op jit(solution)/shard_map/njhd,njhe->nhde/dot_general | solution.py:173
  7.6 2.8 %collective-permute-start.2 = (f32[129,128]{1,0:T(8,128)S(1)}, f32[129,128]{1,0:T(8,128)S(1)}, u32[]{:S(2)}, u32[]{:S(2)}) collective-permute-start(f32[129,128]{1,0:T(8,128)S(1)} %get-tuple-element.64), channel_id=1, source_target_pairs={{0,24},{8,0},{16,8},{24,16},{1,25},{9,1},{17,9},{25,17},{2,26},{10... | collective-permute-start | bytes 198152 | tf_op jit(solution)/shard_map/ppermute | solution.py:82
  12.1 1.8 %fusion.81 = (bf16[4,128,1,128]{3,2,1,0:T(2,128)(2,1)}, bf16[4,128,1,128]{3,2,1,0:T(2,128)(2,1)}, bf16[4,128,1,128]{3,2,1,0:T(2,128)(2,1)}, bf16[4,128,1,128]{3,2,1,0:T(2,128)(2,1)}) fusion(bf16[4,128,4,128]{3,2,1,0:T(4,128)(2,1)S(1)} %reshape.496), kind=kLoop, calls=%fused_computation.258 | loop fusion | bytes 1048576 | tf_op jit(solution)/shard_map/slice | solution.py:237
  14.0 1.8 %fusion.80 = (bf16[4,128,1,128]{3,2,1,0:T(2,128)(2,1)}, bf16[4,128,1,128]{3,2,1,0:T(2,128)(2,1)}, bf16[4,128,1,128]{3,2,1,0:T(2,128)(2,1)}, bf16[4,128,1,128]{3,2,1,0:T(2,128)(2,1)}) fusion(bf16[4,128,4,128]{3,2,1,0:T(4,128)(2,1)S(1)} %reshape.494), kind=kLoop, calls=%fused_computation.257 | loop fusion | bytes 1048576 | tf_op jit(solution)/shard_map/slice | solution.py:240
  17.8 3.8 %collective-permute-start.3 = (f32[1,129,128]{2,1,0:T(8,128)S(1)}, f32[1,129,128]{2,1,0:T(8,128)S(1)}, u32[]{:S(2)}, u32[]{:S(2)}) collective-permute-start(f32[1,129,128]{2,1,0:T(8,128)S(1)} %pad_maximum_fusion.8), channel_id=1, source_target_pairs={{0,32},{32,64},{64,96},{96,128},{128,160},{160,192},{192,224},{1,3... | collective-permute-start | bytes 198152 | tf_op jit(solution)/shard_map/ppermute | solution.py:40
  21.7 6.4 %collective-permute-start.4 = (f32[1,129,128]{2,1,0:T(8,128)S(1)}, f32[1,129,128]{2,1,0:T(8,128)S(1)}, u32[]{:S(2)}, u32[]{:S(2)}) collective-permute-start(f32[1,129,128]{2,1,0:T(8,128)S(1)} %pad_maximum_fusion.8), channel_id=1, source_target_pairs={{0,64},{32,96},{64,128},{96,160},{128,192},{160,224},{1,65},{33,97... | collective-permute-start | bytes 198152 | tf_op jit(solution)/shard_map/ppermute | solution.py:40
  30.0 7.6 %collective-permute-start.5 = (f32[1,129,128]{2,1,0:T(8,128)S(1)}, f32[1,129,128]{2,1,0:T(8,128)S(1)}, u32[]{:S(2)}, u32[]{:S(2)}) collective-permute-start(f32[1,129,128]{2,1,0:T(8,128)S(1)} %pad_maximum_fusion.9), channel_id=1, source_target_pairs={{0,96},{32,128},{64,160},{96,192},{128,224},{1,97},{33,129},{65,16... | collective-permute-start | bytes 198152 | tf_op jit(solution)/shard_map/ppermute | solution.py:40
  40.4 1.9 %collective-permute-done.6 = f32[1,129,128]{2,1,0:T(8,128)S(1)} collective-permute-done((f32[1,129,128]{2,1,0:T(8,128)S(1)}, f32[1,129,128]{2,1,0:T(8,128)S(1)}, u32[]{:S(2)}, u32[]{:S(2)}) %collective-permute-start.6) | collective-permute-done | bytes 66080 | tf_op jit(solution)/shard_map/ppermute | solution.py:40
  43.1 1.7 %collective-permute-start.9 = (f32[128,128]{1,0:T(8,128)}, f32[128,128]{1,0:T(8,128)S(1)}, u32[]{:S(2)}, u32[]{:S(2)}) collective-permute-start(f32[128,128]{1,0:T(8,128)} %get-tuple-element.70), channel_id=1, source_target_pairs={{0,24},{8,0},{16,8},{24,16},{1,25},{9,1},{17,9},{25,17},{2,26},{10... | collective-permute-start | bytes 196616 | tf_op jit(solution)/shard_map/ppermute | solution.py:82
  44.8 1.5 %collective-permute-start.8 = (f32[128,128]{1,0:T(8,128)S(1)}, f32[128,128]{1,0:T(8,128)S(1)}, u32[]{:S(2)}, u32[]{:S(2)}) collective-permute-start(f32[128,128]{1,0:T(8,128)S(1)} %get-tuple-element.71), channel_id=1, source_target_pairs={{0,16},{8,24},{16,0},{24,8},{1,17},{9,25},{17,1},{25,9},{2,18},{10... | collective-permute-start | bytes 196616 | tf_op jit(solution)/shard_map/ppermute | solution.py:82
  48.2 1.5 %copy.123 = f32[4,128,4,128]{1,3,2,0:T(8,128)S(1)} copy(f32[4,128,4,128]{3,2,1,0:T(4,128)} %reshape.497) | data formatting | bytes 2097152 | tf_op jit(solution)/shard_map/convert_element_type | solution.py:189
  54.5 2.9 %multiply_reduce_fusion.6 = (f32[4,128]{1,0:T(4,128)S(1)}, f32[4,128]{1,0:T(4,128)S(1)}, f32[4,128,4,128]{1,3,2,0:T(8,128)}) fusion(f32[4,128,4,128]{1,3,2,0:T(8,128)S(1)} %copy.123, f32[4,128,4,128]{1,3,2,0:T(8,128)} %convolution_bitcast_fusion.5, bf16[4,128,4,128]{1,3,2,0:T(8,128)(2,1)S(1)} %copy.135, f32[1,4,128,128]{3,2,1,0:T(8,128)S(1)} %bitcast.315, ...), kind=kOutput, calls=%fused_computation.63 | convolution fusion | flops 70253568 | bytes 4993088 | tf_op jit(solution)/shard_map/nihd,nhde->nihe/dot_general | solution.py:185
  58.1 4.5 %all-to-all-start = ((f32[8,2,4,128]{3,2,1,0:T(4,128)}), f32[8,2,4,128]{3,2,1,0:T(4,128)S(1)}, u32[]{:S(2)}, u32[]{:S(2)}) async-start(f32[8,2,4,128]{3,2,1,0:T(4,128)} %broadcast_in_dim.17), calls=%async_computation | async-start | bytes 65536 | tf_op jit(solution)/shard_map/all_to_all | solution.py:131
  63.6 4.4 %all-to-all-done = f32[8,2,4,128]{3,2,1,0:T(4,128)S(1)} async-done(((f32[8,2,4,128]{3,2,1,0:T(4,128)}), f32[8,2,4,128]{3,2,1,0:T(4,128)S(1)}, u32[]{:S(2)}, u32[]{:S(2)}) %all-to-all-start) | async-done | bytes 32800 | tf_op jit(solution)/shard_map/all_to_all | solution.py:131
  70.8 1.7 %multiply_reduce_fusion = (f32[4,128,128]{2,1,0:T(8,128)S(1)}, f32[4,128,128]{2,1,0:T(8,128)}, f32[4,128,128]{2,1,0:T(8,128)}, f32[4,128,128]{2,1,0:T(8,128)}, f32[4,128,128]{2,1,0:T(8,128)}) fusion(f32[4,4]{1,0:T(4,128)S(1)} %copy-done.35, f32[4,4]{1,0:T(4,128)S(1)} %copy-done.41, f32[4,4]{1,0:T(4,128)S(1)} %copy-done.42, f32[4,4]{1,0:T(4,128)S(1)} %copy-done.43, ...), kind=kOutput, calls=%fused_computation.55 | convolution fusion | flops 70189056 | bytes 2367808 | tf_op jit(solution)/shard_map/nihd,nihe->nhde/dot_general | solution.py:219
  72.5 2.0 %collective-permute-start.12 = (f32[129,128]{1,0:T(8,128)S(1)}, f32[129,128]{1,0:T(8,128)S(1)}, u32[]{:S(2)}, u32[]{:S(2)}) collective-permute-start(f32[129,128]{1,0:T(8,128)S(1)} %get-tuple-element.60), channel_id=1, source_target_pairs={{0,24},{8,0},{16,8},{24,16},{1,25},{9,1},{17,9},{25,17},{2,26},{10... | collective-permute-start | bytes 198152 | tf_op jit(solution)/shard_map/ppermute | solution.py:82
  77.3 2.9 %collective-permute-done.11 = f32[129,128]{1,0:T(8,128)S(1)} collective-permute-done((f32[129,128]{1,0:T(8,128)S(1)}, f32[129,128]{1,0:T(8,128)S(1)}, u32[]{:S(2)}, u32[]{:S(2)}) %collective-permute-start.11) | collective-permute-done | bytes 66080 | tf_op jit(solution)/shard_map/ppermute | solution.py:82
  82.0 2.1 %collective-permute-start.13 = (f32[1,129,128]{2,1,0:T(8,128)S(1)}, f32[1,129,128]{2,1,0:T(8,128)S(1)}, u32[]{:S(2)}, u32[]{:S(2)}) collective-permute-start(f32[1,129,128]{2,1,0:T(8,128)S(1)} %pad_maximum_fusion.10), channel_id=1, source_target_pairs={{32,0},{64,32},{96,64},{128,96},{160,128},{192,160},{224,192},{33,... | collective-permute-start | bytes 198152 | tf_op jit(solution)/shard_map/ppermute | solution.py:61
  85.4 2.5 %fusion.4 = bf16[4,128,4,128]{1,3,2,0:T(8,128)(2,1)} fusion(f32[4,128,4,128]{1,3,2,0:T(8,128)} %convolution_bitcast_fusion.3, bf16[4,128,4,128]{1,3,2,0:T(8,128)(2,1)S(1)} %multiply_convert_fusion.1, f32[4,128,4]{1,2,0:T(4,128)S(1)} %copy.117, f32[1,4,128,128]{3,2,1,0:T(8,128)S(1)} %bitcast.316, f32[1,4,128,128]{3,2,1,0:T(8,128)S(1)} %bitcast.318, ...), kind=kOutput, calls=%fused_computation.16 | convolution fusion | flops 69468160 | bytes 3416128 | tf_op jit(solution)/shard_map/nihe,nhde->nihd/dot_general | solution.py:207
  87.8 1.6 %collective-permute-done.13 = f32[1,129,128]{2,1,0:T(8,128)S(1)} collective-permute-done((f32[1,129,128]{2,1,0:T(8,128)S(1)}, f32[1,129,128]{2,1,0:T(8,128)S(1)}, u32[]{:S(2)}, u32[]{:S(2)}) %collective-permute-start.13) | collective-permute-done | bytes 66080 | tf_op jit(solution)/shard_map/ppermute | solution.py:61
  89.4 2.5 %collective-permute-done.14 = f32[1,129,128]{2,1,0:T(8,128)S(1)} collective-permute-done((f32[1,129,128]{2,1,0:T(8,128)S(1)}, f32[1,129,128]{2,1,0:T(8,128)S(1)}, u32[]{:S(2)}, u32[]{:S(2)}) %collective-permute-start.14) | collective-permute-done | bytes 66080 | tf_op jit(solution)/shard_map/ppermute | solution.py:61
  95.0 6.1 %collective-permute-done.15 = f32[1,129,128]{2,1,0:T(8,128)S(1)} collective-permute-done((f32[1,129,128]{2,1,0:T(8,128)S(1)}, f32[1,129,128]{2,1,0:T(8,128)S(1)}, u32[]{:S(2)}, u32[]{:S(2)}) %collective-permute-start.15) | collective-permute-done | bytes 66080 | tf_op jit(solution)/shard_map/ppermute | solution.py:61
  101.2 1.6 %collective-permute-done.16 = f32[1,129,128]{2,1,0:T(8,128)S(1)} collective-permute-done((f32[1,129,128]{2,1,0:T(8,128)S(1)}, f32[1,129,128]{2,1,0:T(8,128)S(1)}, u32[]{:S(2)}, u32[]{:S(2)}) %collective-permute-start.16) | collective-permute-done | bytes 66080 | tf_op jit(solution)/shard_map/ppermute | solution.py:61
  108.3 1.8 %collective-permute-done.18 = f32[128,128]{1,0:T(8,128)S(1)} collective-permute-done((f32[128,128]{1,0:T(8,128)}, f32[128,128]{1,0:T(8,128)S(1)}, u32[]{:S(2)}, u32[]{:S(2)}) %collective-permute-start.18) | collective-permute-done | bytes 65568 | tf_op jit(solution)/shard_map/ppermute | solution.py:82
  (202 shorter events, 51.9 us)
Async XLA Ops:
  7.6 8.7 %collective-permute-start.2 = (f32[129,128]{1,0:T(8,128)S(1)}, f32[129,128]{1,0:T(8,128)S(1)}, u32[]{:S(2)}, u32[]{:S(2)}) collective-permute-start(f32[129,128]{1,0:T(8,128)S(1)} %get-tuple-element.64), channel_id=1, source_target_pairs={{0,24},{8,0},{16,8},{24,16},{1,25},{9,1},{17,9},{25,17},{2,26},{10... | collective-permute-start | bytes 198152 | tf_op jit(solution)/shard_map/ppermute | solution.py:82
  10.4 6.0 %collective-permute-start.1 = (f32[129,128]{1,0:T(8,128)S(1)}, f32[129,128]{1,0:T(8,128)S(1)}, u32[]{:S(2)}, u32[]{:S(2)}) collective-permute-start(f32[129,128]{1,0:T(8,128)S(1)} %get-tuple-element.62), channel_id=1, source_target_pairs={{0,16},{8,24},{16,0},{24,8},{1,17},{9,25},{17,1},{25,9},{2,18},{10... | collective-permute-start | bytes 198152 | tf_op jit(solution)/shard_map/ppermute | solution.py:82
  11.2 5.8 %collective-permute-start = (f32[129,128]{1,0:T(8,128)S(1)}, f32[129,128]{1,0:T(8,128)S(1)}, u32[]{:S(2)}, u32[]{:S(2)}) collective-permute-start(f32[129,128]{1,0:T(8,128)S(1)} %get-tuple-element.63), channel_id=1, source_target_pairs={{0,8},{8,16},{16,24},{24,0},{1,9},{9,17},{17,25},{25,1},{2,10},{10... | collective-permute-start | bytes 198152 | tf_op jit(solution)/shard_map/ppermute | solution.py:82
  16.3 11.7 %copy-start.36 = (f32[4,4,128]{2,1,0:T(4,128)}, f32[4,4,128]{2,1,0:T(4,128)S(1)}, u32[]{:S(2)}) copy-start(f32[4,4,128]{2,1,0:T(4,128)S(1)} %copy.114) | copy-start | bytes 24580
  16.3 36.5 %copy-start.31 = (s32[1024]{0:T(1024)}, s32[1024]{0:T(1024)S(1)}, u32[]{:S(2)}) copy-start(s32[1024]{0:T(1024)S(1)} %pad_clamp_fusion) | copy-start | bytes 12292
  16.4 37.1 %copy-start.32 = (pred[4]{0:T(512)(128)(4,1)}, pred[4]{0:T(512)(128)(4,1)S(1)}, u32[]{:S(2)}) copy-start(pred[4]{0:T(512)(128)(4,1)S(1)} %compare_and_fusion) | copy-start | bytes 16
  17.8 10.9 %collective-permute-start.3 = (f32[1,129,128]{2,1,0:T(8,128)S(1)}, f32[1,129,128]{2,1,0:T(8,128)S(1)}, u32[]{:S(2)}, u32[]{:S(2)}) collective-permute-start(f32[1,129,128]{2,1,0:T(8,128)S(1)} %pad_maximum_fusion.8), channel_id=1, source_target_pairs={{0,32},{32,64},{64,96},{96,128},{128,160},{160,192},{192,224},{1,3... | collective-permute-start | bytes 198152 | tf_op jit(solution)/shard_map/ppermute | solution.py:40
  21.7 8.3 %collective-permute-start.4 = (f32[1,129,128]{2,1,0:T(8,128)S(1)}, f32[1,129,128]{2,1,0:T(8,128)S(1)}, u32[]{:S(2)}, u32[]{:S(2)}) collective-permute-start(f32[1,129,128]{2,1,0:T(8,128)S(1)} %pad_maximum_fusion.8), channel_id=1, source_target_pairs={{0,64},{32,96},{64,128},{96,160},{128,192},{160,224},{1,65},{33,97... | collective-permute-start | bytes 198152 | tf_op jit(solution)/shard_map/ppermute | solution.py:40
  30.0 10.4 %collective-permute-start.5 = (f32[1,129,128]{2,1,0:T(8,128)S(1)}, f32[1,129,128]{2,1,0:T(8,128)S(1)}, u32[]{:S(2)}, u32[]{:S(2)}) collective-permute-start(f32[1,129,128]{2,1,0:T(8,128)S(1)} %pad_maximum_fusion.9), channel_id=1, source_target_pairs={{0,96},{32,128},{64,160},{96,192},{128,224},{1,97},{33,129},{65,16... | collective-permute-start | bytes 198152 | tf_op jit(solution)/shard_map/ppermute | solution.py:40
  39.1 3.2 %collective-permute-start.6 = (f32[1,129,128]{2,1,0:T(8,128)S(1)}, f32[1,129,128]{2,1,0:T(8,128)S(1)}, u32[]{:S(2)}, u32[]{:S(2)}) collective-permute-start(f32[1,129,128]{2,1,0:T(8,128)S(1)} %pad_maximum_fusion.9), channel_id=1, source_target_pairs={{0,192},{32,224},{1,193},{33,225},{2,194},{34,226},{3,195},{35,227... | collective-permute-start | bytes 198152 | tf_op jit(solution)/shard_map/ppermute | solution.py:40
  43.1 6.8 %collective-permute-start.9 = (f32[128,128]{1,0:T(8,128)}, f32[128,128]{1,0:T(8,128)S(1)}, u32[]{:S(2)}, u32[]{:S(2)}) collective-permute-start(f32[128,128]{1,0:T(8,128)} %get-tuple-element.70), channel_id=1, source_target_pairs={{0,24},{8,0},{16,8},{24,16},{1,25},{9,1},{17,9},{25,17},{2,26},{10... | collective-permute-start | bytes 196616 | tf_op jit(solution)/shard_map/ppermute | solution.py:82
  44.8 5.8 %collective-permute-start.8 = (f32[128,128]{1,0:T(8,128)S(1)}, f32[128,128]{1,0:T(8,128)S(1)}, u32[]{:S(2)}, u32[]{:S(2)}) collective-permute-start(f32[128,128]{1,0:T(8,128)S(1)} %get-tuple-element.71), channel_id=1, source_target_pairs={{0,16},{8,24},{16,0},{24,8},{1,17},{9,25},{17,1},{25,9},{2,18},{10... | collective-permute-start | bytes 196616 | tf_op jit(solution)/shard_map/ppermute | solution.py:82
  46.3 5.6 %collective-permute-start.7 = (f32[128,128]{1,0:T(8,128)S(1)}, f32[128,128]{1,0:T(8,128)}, u32[]{:S(2)}, u32[]{:S(2)}) collective-permute-start(f32[128,128]{1,0:T(8,128)S(1)} %get-tuple-element.72), channel_id=1, source_target_pairs={{0,8},{8,16},{16,24},{24,0},{1,9},{9,17},{17,25},{25,1},{2,10},{10... | collective-permute-start | bytes 196616 | tf_op jit(solution)/shard_map/ppermute | solution.py:82
  58.1 9.9 %all-to-all-start = ((f32[8,2,4,128]{3,2,1,0:T(4,128)}), f32[8,2,4,128]{3,2,1,0:T(4,128)S(1)}, u32[]{:S(2)}, u32[]{:S(2)}) async-start(f32[8,2,4,128]{3,2,1,0:T(4,128)} %broadcast_in_dim.17), calls=%async_computation | async-start | bytes 65536 | tf_op jit(solution)/shard_map/all_to_all | solution.py:131
  72.5 4.9 %collective-permute-start.12 = (f32[129,128]{1,0:T(8,128)S(1)}, f32[129,128]{1,0:T(8,128)S(1)}, u32[]{:S(2)}, u32[]{:S(2)}) collective-permute-start(f32[129,128]{1,0:T(8,128)S(1)} %get-tuple-element.60), channel_id=1, source_target_pairs={{0,24},{8,0},{16,8},{24,16},{1,25},{9,1},{17,9},{25,17},{2,26},{10... | collective-permute-start | bytes 198152 | tf_op jit(solution)/shard_map/ppermute | solution.py:82
  74.4 5.8 %collective-permute-start.11 = (f32[129,128]{1,0:T(8,128)S(1)}, f32[129,128]{1,0:T(8,128)S(1)}, u32[]{:S(2)}, u32[]{:S(2)}) collective-permute-start(f32[129,128]{1,0:T(8,128)S(1)} %get-tuple-element.59), channel_id=1, source_target_pairs={{0,16},{8,24},{16,0},{24,8},{1,17},{9,25},{17,1},{25,9},{2,18},{10... | collective-permute-start | bytes 198152 | tf_op jit(solution)/shard_map/ppermute | solution.py:82
  75.2 5.8 %collective-permute-start.10 = (f32[129,128]{1,0:T(8,128)S(1)}, f32[129,128]{1,0:T(8,128)S(1)}, u32[]{:S(2)}, u32[]{:S(2)}) collective-permute-start(f32[129,128]{1,0:T(8,128)S(1)} %get-tuple-element.58), channel_id=1, source_target_pairs={{0,8},{8,16},{16,24},{24,0},{1,9},{9,17},{17,25},{25,1},{2,10},{10... | collective-permute-start | bytes 198152 | tf_op jit(solution)/shard_map/ppermute | solution.py:82
  82.0 7.4 %collective-permute-start.13 = (f32[1,129,128]{2,1,0:T(8,128)S(1)}, f32[1,129,128]{2,1,0:T(8,128)S(1)}, u32[]{:S(2)}, u32[]{:S(2)}) collective-permute-start(f32[1,129,128]{2,1,0:T(8,128)S(1)} %pad_maximum_fusion.10), channel_id=1, source_target_pairs={{32,0},{64,32},{96,64},{128,96},{160,128},{192,160},{224,192},{33,... | collective-permute-start | bytes 198152 | tf_op jit(solution)/shard_map/ppermute | solution.py:61
  84.0 7.8 %collective-permute-start.14 = (f32[1,129,128]{2,1,0:T(8,128)S(1)}, f32[1,129,128]{2,1,0:T(8,128)S(1)}, u32[]{:S(2)}, u32[]{:S(2)}) collective-permute-start(f32[1,129,128]{2,1,0:T(8,128)S(1)} %pad_maximum_fusion.10), channel_id=1, source_target_pairs={{64,0},{96,32},{128,64},{160,96},{192,128},{224,160},{65,1},{97,33... | collective-permute-start | bytes 198152 | tf_op jit(solution)/shard_map/ppermute | solution.py:61
  91.9 9.2 %collective-permute-start.15 = (f32[1,129,128]{2,1,0:T(8,128)S(1)}, f32[1,129,128]{2,1,0:T(8,128)S(1)}, u32[]{:S(2)}, u32[]{:S(2)}) collective-permute-start(f32[1,129,128]{2,1,0:T(8,128)S(1)} %pad_maximum_fusion.11), channel_id=1, source_target_pairs={{96,0},{128,32},{160,64},{192,96},{224,128},{97,1},{129,33},{161,6... | collective-permute-start | bytes 198152 | tf_op jit(solution)/shard_map/ppermute | solution.py:61
  93.7 9.1 %collective-permute-start.16 = (f32[1,129,128]{2,1,0:T(8,128)S(1)}, f32[1,129,128]{2,1,0:T(8,128)S(1)}, u32[]{:S(2)}, u32[]{:S(2)}) collective-permute-start(f32[1,129,128]{2,1,0:T(8,128)S(1)} %pad_maximum_fusion.11), channel_id=1, source_target_pairs={{192,0},{224,32},{193,1},{225,33},{194,2},{226,34},{195,3},{227,35... | collective-permute-start | bytes 198152 | tf_op jit(solution)/shard_map/ppermute | solution.py:61
  103.6 4.8 %collective-permute-start.19 = (f32[128,128]{1,0:T(8,128)}, f32[128,128]{1,0:T(8,128)S(1)}, u32[]{:S(2)}, u32[]{:S(2)}) collective-permute-start(f32[128,128]{1,0:T(8,128)} %get-tuple-element.66), channel_id=1, source_target_pairs={{0,24},{8,0},{16,8},{24,16},{1,25},{9,1},{17,9},{25,17},{2,26},{10... | collective-permute-start | bytes 196616 | tf_op jit(solution)/shard_map/ppermute | solution.py:82
  104.1 6.0 %collective-permute-start.18 = (f32[128,128]{1,0:T(8,128)}, f32[128,128]{1,0:T(8,128)S(1)}, u32[]{:S(2)}, u32[]{:S(2)}) collective-permute-start(f32[128,128]{1,0:T(8,128)} %get-tuple-element.67), channel_id=1, source_target_pairs={{0,16},{8,24},{16,0},{24,8},{1,17},{9,25},{17,1},{25,9},{2,18},{10... | collective-permute-start | bytes 196616 | tf_op jit(solution)/shard_map/ppermute | solution.py:82
  104.1 6.7 %collective-permute-start.17 = (f32[128,128]{1,0:T(8,128)S(1)}, f32[128,128]{1,0:T(8,128)S(1)}, u32[]{:S(2)}, u32[]{:S(2)}) collective-permute-start(f32[128,128]{1,0:T(8,128)S(1)} %get-tuple-element.68), channel_id=1, source_target_pairs={{0,8},{8,16},{16,24},{24,0},{1,9},{9,17},{17,25},{25,1},{2,10},{10... | collective-permute-start | bytes 196616 | tf_op jit(solution)/shard_map/ppermute | solution.py:82
  (41 other events, 68.8 us)

commit v10 on v6

--- a/solution.py
+++ b/solution.py
@@ -76,9 +76,9 @@
         send = lax.dynamic_index_in_dim(payload, (me + shift) % ranks, 0, keepdims=False)
         pairs = [(i, (i + shift) % ranks) for i in range(ranks)]
         got.append(lax.ppermute(send, axis, pairs))
-    stacked = jnp.stack(got)
-    order = (me - jnp.arange(ranks)) % ranks
-    return jnp.take(stacked, order, axis=0)
+    turned = jnp.stack([got[(-k) % ranks] for k in range(ranks)])
+    doubled = jnp.concatenate([turned, turned], axis=0)
+    return lax.dynamic_slice_in_dim(doubled, ranks - me, ranks, axis=0)
 
 
 def lane_rows(shard_total, width):

time: 112 us -> 125 us (1.12)
  local copies, waits for them, and re-layouts: 14.5 us -> 22 us
  other arithmetic: 2.45 us -> 7.75 us
  waiting for transfers between devices: 33.5 us -> 37.8 us
  matrix products: 16.5 us -> 12.8 us
    unnamed x47 -> x81, local copies, waits for them, and re-layouts: 7.87 us -> 14 us
    ppermute x12, waiting for transfers between devices: 12.1 us -> 16.9 us  [exchange(): got.append(lax.ppermute(send, axis, pairs))]
    gather x4 -> x0, local copies, waits for them, and re-layouts: 2.27 us -> none  [exchange(): return jnp.take(stacked, order, axis=0)]
    add x2, other arithmetic: 0.06 us -> 1.74 us  [incoming_states(): jnp.exp(row_a[pos]) * before_row + row_b[pos]]
    exp x0 -> x2, other arithmetic: none -> 1.38 us  [incoming_states(): jnp.exp(row_a[pos]) * before_row + row_b[pos]]
    concatenate x0 -> x4, local copies, waits for them, and re-layouts: none -> 1.28 us  [exchange(): doubled = jnp.concatenate([turned, turned], axis=0)]
  transfers between devices with their start and end apart: 21 -> 21, of which waited for: 16 -> 16; matrix products, arithmetic and copies ran while one was open for 10% -> 9% of each run, Pallas kernels for 0% -> 0%
where the time goes in v10:
time: 125 us; the launch traced here: 124 us
  starting transfers between devices  41.9 us (34%)
  waiting for transfers between devices  37.8 us (30%)
  local copies, waits for them, and re-layouts  22 us (18%)
  matrix products  12.8 us (10%)
  other arithmetic  7.75 us (6%)
  between operations  1.35 us (1%)
    ppermute x4, starting transfers between devices, forward_scan(): lax.ppermute(payload, axis, [(i, i + s) for i in range(ranks - s)])  19.1 us
    ppermute x12, waiting for transfers between devices, exchange(): got.append(lax.ppermute(send, axis, pairs))  16.9 us
    unnamed x81, local copies, waits for them, and re-layouts  14 us
    ppermute x12, starting transfers between devices, exchange(): got.append(lax.ppermute(send, axis, pairs))  12.4 us
    ppermute x4, waiting for transfers between devices, backward_scan(): lax.ppermute(payload, axis, [(i + s, i) for i in range(ranks - s)])  12.2 us
    ppermute x4, starting transfers between devices, backward_scan(): lax.ppermute(payload, axis, [(i + s, i) for i in range(ranks - s)])  5.8 us
    all_to_all x1, waiting for transfers between devices, head_sum(): gathered = lax.all_to_all(copies, 'head', 0, 0, tiled=True)  4.86 us
    all_to_all x1, starting transfers between devices, head_sum(): gathered = lax.all_to_all(copies, 'head', 0, 0, tiled=True)  4.6 us
  transfers between devices with their start and end apart: 21, of which 16 were waited for; matrix products, arithmetic and copies ran while one was open for 9% of the time, Pallas kernels for 0%

profile of v10, /device:TPU:32, one launch (start us, length us, event | category | flops | bytes accessed | tf_op | source)
XLA Modules:
  0.0 123.5 jit_solution(12437726003811217171)
XLA Ops:
  4.1 2.0 %multiply_reduce_fusion.7 = (f32[4,128,128]{2,1,0:T(8,128)S(1)}, f32[4,128,128]{2,1,0:T(8,128)}, f32[4,128,128]{2,1,0:T(8,128)}, f32[4,128,128]{2,1,0:T(8,128)}, f32[4,128,128]{2,1,0:T(8,128)}) fusion(f32[4,4]{1,0:T(4,128)S(1)} %subtract_exponential_fusion.1, f32[4,4]{1,0:T(4,128)S(1)} %get-tuple-element.82, f32[4,4]{1,0:T(4,128)S(1)} %get-tuple-element.83, ...), kind=kOutput, calls=%fused_computation.36 | convolution fusion | flops 70189056 | bytes 2367808 | tf_op jit(solution)/shard_map/njhd,njhe->nhde/dot_general | solution.py:168
  6.8 2.8 %collective-permute-start = (f32[129,128]{1,0:T(8,128)}, f32[129,128]{1,0:T(8,128)S(1)}, u32[]{:S(2)}, u32[]{:S(2)}) collective-permute-start(f32[129,128]{1,0:T(8,128)} %get-tuple-element.50), channel_id=1, source_target_pairs={{0,24},{8,0},{16,8},{24,16},{1,25},{9,1},{17,9},{25,17},{2,26},{10... | collective-permute-start | bytes 198152 | tf_op jit(solution)/shard_map/ppermute | solution.py:78
  13.5 2.0 %collective-permute-done.1 = f32[129,128]{1,0:T(8,128)S(1)} collective-permute-done((f32[129,128]{1,0:T(8,128)S(1)}, f32[129,128]{1,0:T(8,128)S(1)}, u32[]{:S(2)}, u32[]{:S(2)}) %collective-permute-start.1) | collective-permute-done | bytes 66080 | tf_op jit(solution)/shard_map/ppermute | solution.py:78
  23.1 3.8 %collective-permute-start.3 = (f32[1,129,128]{2,1,0:T(8,128)S(1)}, f32[1,129,128]{2,1,0:T(8,128)S(1)}, u32[]{:S(2)}, u32[]{:S(2)}) collective-permute-start(f32[1,129,128]{2,1,0:T(8,128)S(1)} %pad_maximum_fusion.2), channel_id=1, source_target_pairs={{0,32},{32,64},{64,96},{96,128},{128,160},{160,192},{192,224},{1,3... | collective-permute-start | bytes 198152 | tf_op jit(solution)/shard_map/ppermute | solution.py:39
  26.9 6.4 %collective-permute-start.4 = (f32[1,129,128]{2,1,0:T(8,128)S(1)}, f32[1,129,128]{2,1,0:T(8,128)S(1)}, u32[]{:S(2)}, u32[]{:S(2)}) collective-permute-start(f32[1,129,128]{2,1,0:T(8,128)S(1)} %pad_maximum_fusion.2), channel_id=1, source_target_pairs={{0,64},{32,96},{64,128},{96,160},{128,192},{160,224},{1,65},{33,97... | collective-permute-start | bytes 198152 | tf_op jit(solution)/shard_map/ppermute | solution.py:39
  33.4 1.9 %collective-permute-done.4 = f32[1,129,128]{2,1,0:T(8,128)S(1)} collective-permute-done((f32[1,129,128]{2,1,0:T(8,128)S(1)}, f32[1,129,128]{2,1,0:T(8,128)S(1)}, u32[]{:S(2)}, u32[]{:S(2)}) %collective-permute-start.4) | collective-permute-done | bytes 66080 | tf_op jit(solution)/shard_map/ppermute | solution.py:39
  35.3 7.6 %collective-permute-start.5 = (f32[1,129,128]{2,1,0:T(8,128)S(1)}, f32[1,129,128]{2,1,0:T(8,128)S(1)}, u32[]{:S(2)}, u32[]{:S(2)}) collective-permute-start(f32[1,129,128]{2,1,0:T(8,128)S(1)} %pad_maximum_fusion.3), channel_id=1, source_target_pairs={{0,96},{32,128},{64,160},{96,192},{128,224},{1,97},{33,129},{65,16... | collective-permute-start | bytes 198152 | tf_op jit(solution)/shard_map/ppermute | solution.py:39
  44.9 1.9 %collective-permute-done.6 = f32[1,129,128]{2,1,0:T(8,128)S(1)} collective-permute-done((f32[1,129,128]{2,1,0:T(8,128)S(1)}, f32[1,129,128]{2,1,0:T(8,128)S(1)}, u32[]{:S(2)}, u32[]{:S(2)}) %collective-permute-start.6) | collective-permute-done | bytes 66080 | tf_op jit(solution)/shard_map/ppermute | solution.py:39
  49.2 1.5 %collective-permute-start.7 = (f32[128,128]{1,0:T(8,128)}, f32[128,128]{1,0:T(8,128)S(1)}, u32[]{:S(2)}, u32[]{:S(2)}) collective-permute-start(f32[128,128]{1,0:T(8,128)} %get-tuple-element.58), channel_id=1, source_target_pairs={{0,24},{8,0},{16,8},{24,16},{1,25},{9,1},{17,9},{25,17},{2,26},{10... | collective-permute-start | bytes 196616 | tf_op jit(solution)/shard_map/ppermute | solution.py:78
  50.7 1.5 %convolution_bitcast_fusion.7 = f32[4,128,4,128]{1,3,2,0:T(8,128)} fusion(bf16[4,4,128,128]{3,2,1,0:T(8,128)(2,1)S(1)} %fusion.11, bf16[4,128,4,128]{3,2,1,0:T(4,128)(2,1)S(1)} %reshape.474), kind=kOutput, calls=%fused_computation.16 | convolution fusion | flops 67108864 | bytes 2097152 | tf_op jit(solution)/shard_map/nhij,njhd->nihd/dot_general | solution.py:163
  54.9 4.3 %collective-permute-done.8 = f32[128,128]{1,0:T(8,128)S(1)} collective-permute-done((f32[128,128]{1,0:T(8,128)}, f32[128,128]{1,0:T(8,128)S(1)}, u32[]{:S(2)}, u32[]{:S(2)}) %collective-permute-start.8) | collective-permute-done | bytes 65568 | tf_op jit(solution)/shard_map/ppermute | solution.py:78
  64.0 1.7 %multiply_reduce_fusion.6 = (f32[4,128]{1,0:T(4,128)S(1)}, f32[4,128]{1,0:T(4,128)S(1)}, f32[4,128,4,128]{1,3,2,0:T(8,128)S(1)}) fusion(f32[4,128,4,128]{1,3,2,0:T(8,128)S(1)} %copy.114, f32[4,128,4,128]{1,3,2,0:T(8,128)S(1)} %copy-done, bf16[4,128,4,128]{1,3,2,0:T(8,128)(2,1)S(1)} %copy.125, f32[1,4,128,128]{3,2,1,0:T(8,128)S(1)} %bitcast.225, ...), kind=kOutput, calls=%fused_computation.35 | convolution fusion | flops 70253568 | bytes 4993088 | tf_op jit(solution)/shard_map/nihd,nhde->nihe/dot_general | solution.py:180
  66.4 4.6 %all-to-all-start = ((f32[8,2,4,128]{3,2,1,0:T(4,128)}), f32[8,2,4,128]{3,2,1,0:T(4,128)S(1)}, u32[]{:S(2)}, u32[]{:S(2)}) async-start(f32[8,2,4,128]{3,2,1,0:T(4,128)} %broadcast_in_dim.5), calls=%async_computation | async-start | bytes 65536 | tf_op jit(solution)/shard_map/all_to_all | solution.py:126
  71.6 4.9 %all-to-all-done = f32[8,2,4,128]{3,2,1,0:T(4,128)S(1)} async-done(((f32[8,2,4,128]{3,2,1,0:T(4,128)}), f32[8,2,4,128]{3,2,1,0:T(4,128)S(1)}, u32[]{:S(2)}, u32[]{:S(2)}) %all-to-all-start) | async-done | bytes 32800 | tf_op jit(solution)/shard_map/all_to_all | solution.py:126
  78.4 1.6 %multiply_reduce_fusion = (f32[4,128,128]{2,1,0:T(8,128)S(1)}, f32[4,128,128]{2,1,0:T(8,128)S(1)}, f32[4,128,128]{2,1,0:T(8,128)}, f32[4,128,128]{2,1,0:T(8,128)}, f32[4,128,128]{2,1,0:T(8,128)}) fusion(f32[4,4]{1,0:T(4,128)S(1)} %get-tuple-element.25, f32[4,4]{1,0:T(4,128)S(1)} %get-tuple-element.78, f32[4,4]{1,0:T(4,128)S(1)} %get-tuple-element.79, ...), kind=kOutput, calls=%fused_computation.27 | convolution fusion | flops 70189056 | bytes 2367808 | tf_op jit(solution)/shard_map/nihd,nihe->nhde/dot_general | solution.py:214
  81.1 1.5 %collective-permute-start.11 = (f32[129,128]{1,0:T(8,128)S(1)}, f32[129,128]{1,0:T(8,128)S(1)}, u32[]{:S(2)}, u32[]{:S(2)}) collective-permute-start(f32[129,128]{1,0:T(8,128)S(1)} %get-tuple-element.46), channel_id=1, source_target_pairs={{0,16},{8,24},{16,0},{24,8},{1,17},{9,25},{17,1},{25,9},{2,18},{10... | collective-permute-start | bytes 198152 | tf_op jit(solution)/shard_map/ppermute | solution.py:78
  84.7 3.0 %collective-permute-done.11 = f32[129,128]{1,0:T(8,128)S(1)} collective-permute-done((f32[129,128]{1,0:T(8,128)S(1)}, f32[129,128]{1,0:T(8,128)S(1)}, u32[]{:S(2)}, u32[]{:S(2)}) %collective-permute-start.11) | collective-permute-done | bytes 66080 | tf_op jit(solution)/shard_map/ppermute | solution.py:78
  88.5 1.9 %collective-permute-start.13 = (f32[1,129,128]{2,1,0:T(8,128)S(1)}, f32[1,129,128]{2,1,0:T(8,128)S(1)}, u32[]{:S(2)}, u32[]{:S(2)}) collective-permute-start(f32[1,129,128]{2,1,0:T(8,128)S(1)} %pad_maximum_fusion.4), channel_id=1, source_target_pairs={{32,0},{64,32},{96,64},{128,96},{160,128},{192,160},{224,192},{33,... | collective-permute-start | bytes 198152 | tf_op jit(solution)/shard_map/ppermute | solution.py:59
  91.8 1.5 %convolution_bitcast_fusion.1 = f32[4,128,4,128]{3,1,2,0:T(8,128)} fusion(bf16[4,128,4,128]{1,3,2,0:T(8,128)(2,1)S(1)} %multiply_convert_fusion.1, bf16[4,4,128,128]{3,2,1,0:T(8,128)(2,1)S(1)} %copy-done.4), kind=kOutput, calls=%fused_computation.3 | convolution fusion | flops 67108864 | bytes 2097152 | tf_op jit(solution)/shard_map/nhij,nihe->njhe/dot_general | solution.py:208
  93.2 2.5 %collective-permute-done.13 = f32[1,129,128]{2,1,0:T(8,128)S(1)} collective-permute-done((f32[1,129,128]{2,1,0:T(8,128)S(1)}, f32[1,129,128]{2,1,0:T(8,128)S(1)}, u32[]{:S(2)}, u32[]{:S(2)}) %collective-permute-start.13) | collective-permute-done | bytes 66080 | tf_op jit(solution)/shard_map/ppermute | solution.py:59
  95.8 2.5 %collective-permute-done.14 = f32[1,129,128]{2,1,0:T(8,128)S(1)} collective-permute-done((f32[1,129,128]{2,1,0:T(8,128)S(1)}, f32[1,129,128]{2,1,0:T(8,128)S(1)}, u32[]{:S(2)}, u32[]{:S(2)}) %collective-permute-start.14) | collective-permute-done | bytes 66080 | tf_op jit(solution)/shard_map/ppermute | solution.py:59
  101.0 6.9 %collective-permute-done.15 = f32[1,129,128]{2,1,0:T(8,128)S(1)} collective-permute-done((f32[1,129,128]{2,1,0:T(8,128)S(1)}, f32[1,129,128]{2,1,0:T(8,128)S(1)}, u32[]{:S(2)}, u32[]{:S(2)}) %collective-permute-start.15) | collective-permute-done | bytes 66080 | tf_op jit(solution)/shard_map/ppermute | solution.py:59
  109.6 1.5 %convolution_bitcast_fusion.3 = f32[4,128,4,128]{3,1,2,0:T(8,128)} fusion(bf16[4,4,128,128]{3,2,1,0:T(8,128)(2,1)S(1)} %fusion.12, bf16[4,128,4,128]{1,3,2,0:T(8,128)(2,1)S(1)} %copy.125), kind=kOutput, calls=%fused_computation.7 | convolution fusion | flops 67108864 | bytes 2097152 | tf_op jit(solution)/shard_map/nhij,nihd->njhd/dot_general | solution.py:205
  113.3 4.8 %collective-permute-done.18 = f32[128,128]{1,0:T(8,128)S(1)} collective-permute-done((f32[128,128]{1,0:T(8,128)S(1)}, f32[128,128]{1,0:T(8,128)S(1)}, u32[]{:S(2)}, u32[]{:S(2)}) %collective-permute-start.18) | collective-permute-done | bytes 65568 | tf_op jit(solution)/shard_map/ppermute | solution.py:78
  (182 shorter events, 47.7 us)
Async XLA Ops:
  3.9 39.0 %copy-start.1 = (bf16[4,128,4,128]{3,2,1,0:T(4,128)(2,1)}, bf16[4,128,4,128]{3,2,1,0:T(4,128)(2,1)S(1)}, u32[]{:S(2)}) copy-start(bf16[4,128,4,128]{3,2,1,0:T(4,128)(2,1)S(1)} %reshape.472) | copy-start | bytes 1572868
  6.8 6.0 %collective-permute-start = (f32[129,128]{1,0:T(8,128)}, f32[129,128]{1,0:T(8,128)S(1)}, u32[]{:S(2)}, u32[]{:S(2)}) collective-permute-start(f32[129,128]{1,0:T(8,128)} %get-tuple-element.50), channel_id=1, source_target_pairs={{0,24},{8,0},{16,8},{24,16},{1,25},{9,1},{17,9},{25,17},{2,26},{10... | collective-permute-start | bytes 198152 | tf_op jit(solution)/shard_map/ppermute | solution.py:78
  9.6 5.9 %collective-permute-start.1 = (f32[129,128]{1,0:T(8,128)S(1)}, f32[129,128]{1,0:T(8,128)S(1)}, u32[]{:S(2)}, u32[]{:S(2)}) collective-permute-start(f32[129,128]{1,0:T(8,128)S(1)} %get-tuple-element.49), channel_id=1, source_target_pairs={{0,16},{8,24},{16,0},{24,8},{1,17},{9,25},{17,1},{25,9},{2,18},{10... | collective-permute-start | bytes 198152 | tf_op jit(solution)/shard_map/ppermute | solution.py:78
  10.4 5.8 %collective-permute-start.2 = (f32[129,128]{1,0:T(8,128)S(1)}, f32[129,128]{1,0:T(8,128)S(1)}, u32[]{:S(2)}, u32[]{:S(2)}) collective-permute-start(f32[129,128]{1,0:T(8,128)S(1)} %get-tuple-element.47), channel_id=1, source_target_pairs={{0,8},{8,16},{16,24},{24,0},{1,9},{9,17},{17,25},{25,1},{2,10},{10... | collective-permute-start | bytes 198152 | tf_op jit(solution)/shard_map/ppermute | solution.py:78
  11.4 31.6 %copy-start.20 = (f32[4,4,128]{2,1,0:T(4,128)}, f32[4,4,128]{2,1,0:T(4,128)S(1)}, u32[]{:S(2)}) copy-start(f32[4,4,128]{2,1,0:T(4,128)S(1)} %copy.103) | copy-start | bytes 24580
  23.1 10.3 %collective-permute-start.3 = (f32[1,129,128]{2,1,0:T(8,128)S(1)}, f32[1,129,128]{2,1,0:T(8,128)S(1)}, u32[]{:S(2)}, u32[]{:S(2)}) collective-permute-start(f32[1,129,128]{2,1,0:T(8,128)S(1)} %pad_maximum_fusion.2), channel_id=1, source_target_pairs={{0,32},{32,64},{64,96},{96,128},{128,160},{160,192},{192,224},{1,3... | collective-permute-start | bytes 198152 | tf_op jit(solution)/shard_map/ppermute | solution.py:39
  26.9 8.3 %collective-permute-start.4 = (f32[1,129,128]{2,1,0:T(8,128)S(1)}, f32[1,129,128]{2,1,0:T(8,128)S(1)}, u32[]{:S(2)}, u32[]{:S(2)}) collective-permute-start(f32[1,129,128]{2,1,0:T(8,128)S(1)} %pad_maximum_fusion.2), channel_id=1, source_target_pairs={{0,64},{32,96},{64,128},{96,160},{128,192},{160,224},{1,65},{33,97... | collective-permute-start | bytes 198152 | tf_op jit(solution)/shard_map/ppermute | solution.py:39
  35.3 9.5 %collective-permute-start.5 = (f32[1,129,128]{2,1,0:T(8,128)S(1)}, f32[1,129,128]{2,1,0:T(8,128)S(1)}, u32[]{:S(2)}, u32[]{:S(2)}) collective-permute-start(f32[1,129,128]{2,1,0:T(8,128)S(1)} %pad_maximum_fusion.3), channel_id=1, source_target_pairs={{0,96},{32,128},{64,160},{96,192},{128,224},{1,97},{33,129},{65,16... | collective-permute-start | bytes 198152 | tf_op jit(solution)/shard_map/ppermute | solution.py:39
  43.5 3.2 %collective-permute-start.6 = (f32[1,129,128]{2,1,0:T(8,128)S(1)}, f32[1,129,128]{2,1,0:T(8,128)S(1)}, u32[]{:S(2)}, u32[]{:S(2)}) collective-permute-start(f32[1,129,128]{2,1,0:T(8,128)S(1)} %pad_maximum_fusion.3), channel_id=1, source_target_pairs={{0,192},{32,224},{1,193},{33,225},{2,194},{34,226},{3,195},{35,227... | collective-permute-start | bytes 198152 | tf_op jit(solution)/shard_map/ppermute | solution.py:39
  49.2 5.0 %collective-permute-start.7 = (f32[128,128]{1,0:T(8,128)}, f32[128,128]{1,0:T(8,128)S(1)}, u32[]{:S(2)}, u32[]{:S(2)}) collective-permute-start(f32[128,128]{1,0:T(8,128)} %get-tuple-element.58), channel_id=1, source_target_pairs={{0,24},{8,0},{16,8},{24,16},{1,25},{9,1},{17,9},{25,17},{2,26},{10... | collective-permute-start | bytes 196616 | tf_op jit(solution)/shard_map/ppermute | solution.py:78
  53.0 11.0 %copy-start = (f32[4,128,4,128]{1,3,2,0:T(8,128)S(1)}, f32[4,128,4,128]{1,3,2,0:T(8,128)}, u32[]{:S(2)}) copy-start(f32[4,128,4,128]{1,3,2,0:T(8,128)} %convolution_bitcast_fusion.7) | copy-start | bytes 3145732
  53.0 6.2 %collective-permute-start.8 = (f32[128,128]{1,0:T(8,128)}, f32[128,128]{1,0:T(8,128)S(1)}, u32[]{:S(2)}, u32[]{:S(2)}) collective-permute-start(f32[128,128]{1,0:T(8,128)} %get-tuple-element.57), channel_id=1, source_target_pairs={{0,16},{8,24},{16,0},{24,8},{1,17},{9,25},{17,1},{25,9},{2,18},{10... | collective-permute-start | bytes 196616 | tf_op jit(solution)/shard_map/ppermute | solution.py:78
  53.1 6.7 %collective-permute-start.9 = (f32[128,128]{1,0:T(8,128)}, f32[128,128]{1,0:T(8,128)S(1)}, u32[]{:S(2)}, u32[]{:S(2)}) collective-permute-start(f32[128,128]{1,0:T(8,128)} %get-tuple-element.55), channel_id=1, source_target_pairs={{0,8},{8,16},{16,24},{24,0},{1,9},{9,17},{17,25},{25,1},{2,10},{10... | collective-permute-start | bytes 196616 | tf_op jit(solution)/shard_map/ppermute | solution.py:78
  66.4 10.0 %all-to-all-start = ((f32[8,2,4,128]{3,2,1,0:T(4,128)}), f32[8,2,4,128]{3,2,1,0:T(4,128)S(1)}, u32[]{:S(2)}, u32[]{:S(2)}) async-start(f32[8,2,4,128]{3,2,1,0:T(4,128)} %broadcast_in_dim.5), calls=%async_computation | async-start | bytes 65536 | tf_op jit(solution)/shard_map/all_to_all | solution.py:126
  80.0 4.7 %collective-permute-start.10 = (f32[129,128]{1,0:T(8,128)S(1)}, f32[129,128]{1,0:T(8,128)S(1)}, u32[]{:S(2)}, u32[]{:S(2)}) collective-permute-start(f32[129,128]{1,0:T(8,128)S(1)} %get-tuple-element.45), channel_id=1, source_target_pairs={{0,24},{8,0},{16,8},{24,16},{1,25},{9,1},{17,9},{25,17},{2,26},{10... | collective-permute-start | bytes 198152 | tf_op jit(solution)/shard_map/ppermute | solution.py:78
  81.1 6.6 %collective-permute-start.11 = (f32[129,128]{1,0:T(8,128)S(1)}, f32[129,128]{1,0:T(8,128)S(1)}, u32[]{:S(2)}, u32[]{:S(2)}) collective-permute-start(f32[129,128]{1,0:T(8,128)S(1)} %get-tuple-element.46), channel_id=1, source_target_pairs={{0,16},{8,24},{16,0},{24,8},{1,17},{9,25},{17,1},{25,9},{2,18},{10... | collective-permute-start | bytes 198152 | tf_op jit(solution)/shard_map/ppermute | solution.py:78
  82.6 5.7 %collective-permute-start.12 = (f32[129,128]{1,0:T(8,128)S(1)}, f32[129,128]{1,0:T(8,128)S(1)}, u32[]{:S(2)}, u32[]{:S(2)}) collective-permute-start(f32[129,128]{1,0:T(8,128)S(1)} %get-tuple-element.43), channel_id=1, source_target_pairs={{0,8},{8,16},{16,24},{24,0},{1,9},{9,17},{17,25},{25,1},{2,10},{10... | collective-permute-start | bytes 198152 | tf_op jit(solution)/shard_map/ppermute | solution.py:78
  88.5 7.3 %collective-permute-start.13 = (f32[1,129,128]{2,1,0:T(8,128)S(1)}, f32[1,129,128]{2,1,0:T(8,128)S(1)}, u32[]{:S(2)}, u32[]{:S(2)}) collective-permute-start(f32[1,129,128]{2,1,0:T(8,128)S(1)} %pad_maximum_fusion.4), channel_id=1, source_target_pairs={{32,0},{64,32},{96,64},{128,96},{160,128},{192,160},{224,192},{33,... | collective-permute-start | bytes 198152 | tf_op jit(solution)/shard_map/ppermute | solution.py:59
  90.5 7.8 %collective-permute-start.14 = (f32[1,129,128]{2,1,0:T(8,128)S(1)}, f32[1,129,128]{2,1,0:T(8,128)S(1)}, u32[]{:S(2)}, u32[]{:S(2)}) collective-permute-start(f32[1,129,128]{2,1,0:T(8,128)S(1)} %pad_maximum_fusion.4), channel_id=1, source_target_pairs={{64,0},{96,32},{128,64},{160,96},{192,128},{224,160},{65,1},{97,33... | collective-permute-start | bytes 198152 | tf_op jit(solution)/shard_map/ppermute | solution.py:59
  98.3 9.5 %collective-permute-start.15 = (f32[1,129,128]{2,1,0:T(8,128)S(1)}, f32[1,129,128]{2,1,0:T(8,128)S(1)}, u32[]{:S(2)}, u32[]{:S(2)}) collective-permute-start(f32[1,129,128]{2,1,0:T(8,128)S(1)} %pad_maximum_fusion.5), channel_id=1, source_target_pairs={{96,0},{128,32},{160,64},{192,96},{224,128},{97,1},{129,33},{161,6... | collective-permute-start | bytes 198152 | tf_op jit(solution)/shard_map/ppermute | solution.py:59
  99.7 8.5 %collective-permute-start.16 = (f32[1,129,128]{2,1,0:T(8,128)S(1)}, f32[1,129,128]{2,1,0:T(8,128)S(1)}, u32[]{:S(2)}, u32[]{:S(2)}) collective-permute-start(f32[1,129,128]{2,1,0:T(8,128)S(1)} %pad_maximum_fusion.5), channel_id=1, source_target_pairs={{192,0},{224,32},{193,1},{225,33},{194,2},{226,34},{195,3},{227,35... | collective-permute-start | bytes 198152 | tf_op jit(solution)/shard_map/ppermute | solution.py:59
  108.3 5.1 %collective-permute-start.17 = (f32[128,128]{1,0:T(8,128)S(1)}, f32[128,128]{1,0:T(8,128)S(1)}, u32[]{:S(2)}, u32[]{:S(2)}) collective-permute-start(f32[128,128]{1,0:T(8,128)S(1)} %get-tuple-element.54), channel_id=1, source_target_pairs={{0,24},{8,0},{16,8},{24,16},{1,25},{9,1},{17,9},{25,17},{2,26},{10... | collective-permute-start | bytes 196616 | tf_op jit(solution)/shard_map/ppermute | solution.py:78
  112.3 5.8 %collective-permute-start.18 = (f32[128,128]{1,0:T(8,128)S(1)}, f32[128,128]{1,0:T(8,128)S(1)}, u32[]{:S(2)}, u32[]{:S(2)}) collective-permute-start(f32[128,128]{1,0:T(8,128)S(1)} %get-tuple-element.53), channel_id=1, source_target_pairs={{0,16},{8,24},{16,0},{24,8},{1,17},{9,25},{17,1},{25,9},{2,18},{10... | collective-permute-start | bytes 196616 | tf_op jit(solution)/shard_map/ppermute | solution.py:78
  112.8 6.0 %collective-permute-start.19 = (f32[128,128]{1,0:T(8,128)S(1)}, f32[128,128]{1,0:T(8,128)S(1)}, u32[]{:S(2)}, u32[]{:S(2)}) collective-permute-start(f32[128,128]{1,0:T(8,128)S(1)} %get-tuple-element.51), channel_id=1, source_target_pairs={{0,8},{8,16},{16,24},{24,0},{1,9},{9,17},{17,25},{25,1},{2,10},{10... | collective-permute-start | bytes 196616 | tf_op jit(solution)/shard_map/ppermute | solution.py:78
  (25 other events, 51.0 us)

commit v11 on v10

--- a/solution.py
+++ b/solution.py
@@ -76,9 +76,14 @@
         send = lax.dynamic_index_in_dim(payload, (me + shift) % ranks, 0, keepdims=False)
         pairs = [(i, (i + shift) % ranks) for i in range(ranks)]
         got.append(lax.ppermute(send, axis, pairs))
-    turned = jnp.stack([got[(-k) % ranks] for k in range(ranks)])
-    doubled = jnp.concatenate([turned, turned], axis=0)
-    return lax.dynamic_slice_in_dim(doubled, ranks - me, ranks, axis=0)
+    outs = []
+    for j in range(ranks):
+        source = (me - j) % ranks
+        pick = got[0]
+        for shift in range(1, ranks):
+            pick = jnp.where(source == shift, got[shift], pick)
+        outs.append(pick)
+    return jnp.stack(outs)
 
 
 def lane_rows(shard_total, width):

time: 125 us -> 110 us (0.88)
  local copies, waits for them, and re-layouts: 22 us -> 12.3 us
  other arithmetic: 7.75 us -> 2.29 us
  waiting for transfers between devices: 37.8 us -> 35.1 us
  matrix products: 12.8 us -> 14.9 us
    unnamed x81 -> x51, local copies, waits for them, and re-layouts: 14 us -> 7.27 us
    ppermute x12, waiting for transfers between devices: 16.9 us -> 13.3 us  [exchange(): got.append(lax.ppermute(send, axis, pairs))]
    add x2, other arithmetic: 1.74 us -> 0.06 us  [incoming_states(): jnp.exp(row_a[pos]) * before_row + row_b[pos]]
    exp x3 -> x0, other arithmetic: 1.4 us -> none  [the longest x2 1.38 us: incoming_states(): jnp.exp(row_a[pos]) * before_row + row_b[pos]]
    concatenate x4 -> x0, local copies, waits for them, and re-layouts: 1.28 us -> none  [exchange(): doubled = jnp.concatenate([turned, turned], axis=0)]
  transfers between devices with their start and end apart: 21 -> 21, of which waited for: 16 -> 17; matrix products, arithmetic and copies ran while one was open for 9% -> 9% of each run, Pallas kernels for 0% -> 0%
where the time goes in v11:
time: 110 us; the launch traced here: 108 us
  starting transfers between devices  42.5 us (39%)
  waiting for transfers between devices  35.1 us (32%)
  matrix products  14.9 us (14%)
  local copies, waits for them, and re-layouts  12.3 us (11%)
  other arithmetic  2.29 us (2%)
  between operations  1.29 us (1%)
    ppermute x4, starting transfers between devices, forward_scan(): lax.ppermute(payload, axis, [(i, i + s) for i in range(ranks - s)])  19.1 us
    ppermute x12, waiting for transfers between devices, exchange(): got.append(lax.ppermute(send, axis, pairs))  13.3 us
    ppermute x12, starting transfers between devices, exchange(): got.append(lax.ppermute(send, axis, pairs))  13 us
    ppermute x4, waiting for transfers between devices, backward_scan(): lax.ppermute(payload, axis, [(i + s, i) for i in range(ranks - s)])  12.5 us
    unnamed x51, local copies, waits for them, and re-layouts  7.27 us
    ppermute x4, starting transfers between devices, backward_scan(): lax.ppermute(payload, axis, [(i + s, i) for i in range(ranks - s)])  5.92 us
    all_to_all x1, waiting for transfers between devices, head_sum(): gathered = lax.all_to_all(copies, 'head', 0, 0, tiled=True)  5.44 us
    all_to_all x1, starting transfers between devices, head_sum(): gathered = lax.all_to_all(copies, 'head', 0, 0, tiled=True)  4.47 us
  transfers between devices with their start and end apart: 21, of which 17 were waited for; matrix products, arithmetic and copies ran while one was open for 9% of the time, Pallas kernels for 0%

profile of v11, /device:TPU:32, one launch (start us, length us, event | category | flops | bytes accessed | tf_op | source)
XLA Modules:
  0.0 108.3 jit_solution(7879074608824258662)
XLA Ops:
  4.2 2.0 %multiply_reduce_fusion.7 = (f32[4,128,128]{2,1,0:T(8,128)S(1)}, f32[4,128,128]{2,1,0:T(8,128)}, f32[4,128,128]{2,1,0:T(8,128)}, f32[4,128,128]{2,1,0:T(8,128)}, f32[4,128,128]{2,1,0:T(8,128)}) fusion(f32[4,4]{1,0:T(4,128)S(1)} %subtract_exponential_fusion.1, f32[4,4]{1,0:T(4,128)S(1)} %get-tuple-element.90, f32[4,4]{1,0:T(4,128)S(1)} %get-tuple-element.91, ...), kind=kOutput, calls=%fused_computation.36 | convolution fusion | flops 70189056 | bytes 2367808 | tf_op jit(solution)/shard_map/njhd,njhe->nhde/dot_general | solution.py:173
  6.3 2.8 %collective-permute-start = (f32[129,128]{1,0:T(8,128)S(1)}, f32[129,128]{1,0:T(8,128)S(1)}, u32[]{:S(2)}, u32[]{:S(2)}) collective-permute-start(f32[129,128]{1,0:T(8,128)S(1)} %get-tuple-element.47), channel_id=1, source_target_pairs={{0,24},{8,0},{16,8},{24,16},{1,25},{9,1},{17,9},{25,17},{2,26},{10... | collective-permute-start | bytes 198152 | tf_op jit(solution)/shard_map/ppermute | solution.py:78
  11.5 3.6 %collective-permute-done.1 = f32[129,128]{1,0:T(8,128)S(1)} collective-permute-done((f32[129,128]{1,0:T(8,128)S(1)}, f32[129,128]{1,0:T(8,128)S(1)}, u32[]{:S(2)}, u32[]{:S(2)}) %collective-permute-start.1) | collective-permute-done | bytes 66080 | tf_op jit(solution)/shard_map/ppermute | solution.py:78
  15.9 3.8 %collective-permute-start.3 = (f32[1,129,128]{2,1,0:T(8,128)S(1)}, f32[1,129,128]{2,1,0:T(8,128)S(1)}, u32[]{:S(2)}, u32[]{:S(2)}) collective-permute-start(f32[1,129,128]{2,1,0:T(8,128)S(1)} %pad_maximum_fusion.4), channel_id=1, source_target_pairs={{0,32},{32,64},{64,96},{96,128},{128,160},{160,192},{192,224},{1,3... | collective-permute-start | bytes 198152 | tf_op jit(solution)/shard_map/ppermute | solution.py:39
  19.8 6.4 %collective-permute-start.4 = (f32[1,129,128]{2,1,0:T(8,128)S(1)}, f32[1,129,128]{2,1,0:T(8,128)S(1)}, u32[]{:S(2)}, u32[]{:S(2)}) collective-permute-start(f32[1,129,128]{2,1,0:T(8,128)S(1)} %pad_maximum_fusion.4), channel_id=1, source_target_pairs={{0,64},{32,96},{64,128},{96,160},{128,192},{160,224},{1,65},{33,97... | collective-permute-start | bytes 198152 | tf_op jit(solution)/shard_map/ppermute | solution.py:39
  26.2 1.9 %collective-permute-done.4 = f32[1,129,128]{2,1,0:T(8,128)S(1)} collective-permute-done((f32[1,129,128]{2,1,0:T(8,128)S(1)}, f32[1,129,128]{2,1,0:T(8,128)S(1)}, u32[]{:S(2)}, u32[]{:S(2)}) %collective-permute-start.4) | collective-permute-done | bytes 66080 | tf_op jit(solution)/shard_map/ppermute | solution.py:39
  28.1 7.6 %collective-permute-start.5 = (f32[1,129,128]{2,1,0:T(8,128)S(1)}, f32[1,129,128]{2,1,0:T(8,128)S(1)}, u32[]{:S(2)}, u32[]{:S(2)}) collective-permute-start(f32[1,129,128]{2,1,0:T(8,128)S(1)} %pad_maximum_fusion.5), channel_id=1, source_target_pairs={{0,96},{32,128},{64,160},{96,192},{128,224},{1,97},{33,129},{65,16... | collective-permute-start | bytes 198152 | tf_op jit(solution)/shard_map/ppermute | solution.py:39
  37.7 1.9 %collective-permute-done.6 = f32[1,129,128]{2,1,0:T(8,128)S(1)} collective-permute-done((f32[1,129,128]{2,1,0:T(8,128)S(1)}, f32[1,129,128]{2,1,0:T(8,128)S(1)}, u32[]{:S(2)}, u32[]{:S(2)}) %collective-permute-start.6) | collective-permute-done | bytes 66080 | tf_op jit(solution)/shard_map/ppermute | solution.py:39
  43.7 1.5 %convolution_bitcast_fusion.7 = f32[4,128,4,128]{1,3,2,0:T(8,128)} fusion(bf16[4,4,128,128]{3,2,1,0:T(8,128)(2,1)S(1)} %fusion.11, bf16[4,128,4,128]{3,2,1,0:T(4,128)(2,1)S(1)} %reshape.474), kind=kOutput, calls=%fused_computation.16 | convolution fusion | flops 67108864 | bytes 2097152 | tf_op jit(solution)/shard_map/nhij,njhd->nihd/dot_general | solution.py:168
  46.0 1.7 %collective-permute-done.8 = f32[128,128]{1,0:T(8,128)} collective-permute-done((f32[128,128]{1,0:T(8,128)}, f32[128,128]{1,0:T(8,128)}, u32[]{:S(2)}, u32[]{:S(2)}) %collective-permute-start.8) | collective-permute-done | bytes 65568 | tf_op jit(solution)/shard_map/ppermute | solution.py:78
  49.4 1.8 %multiply_reduce_fusion.6 = (f32[4,128]{1,0:T(4,128)S(1)}, f32[4,128]{1,0:T(4,128)S(1)}, f32[4,128,4,128]{1,3,2,0:T(8,128)S(1)}) fusion(f32[4,128,4,128]{1,3,2,0:T(8,128)S(1)} %copy.114, f32[4,128,4,128]{1,3,2,0:T(8,128)S(1)} %copy-done, bf16[4,128,4,128]{1,3,2,0:T(8,128)(2,1)S(1)} %copy.125, f32[1,4,128,128]{3,2,1,0:T(8,128)} %bitcast.299, ...), kind=kOutput, calls=%fused_computation.35 | convolution fusion | flops 70253568 | bytes 4993088 | tf_op jit(solution)/shard_map/nihd,nhde->nihe/dot_general | solution.py:185
  51.8 4.5 %all-to-all-start = ((f32[8,2,4,128]{3,2,1,0:T(4,128)}), f32[8,2,4,128]{3,2,1,0:T(4,128)S(1)}, u32[]{:S(2)}, u32[]{:S(2)}) async-start(f32[8,2,4,128]{3,2,1,0:T(4,128)} %broadcast_in_dim.5), calls=%async_computation | async-start | bytes 65536 | tf_op jit(solution)/shard_map/all_to_all | solution.py:131
  56.2 5.4 %all-to-all-done = f32[8,2,4,128]{3,2,1,0:T(4,128)S(1)} async-done(((f32[8,2,4,128]{3,2,1,0:T(4,128)}), f32[8,2,4,128]{3,2,1,0:T(4,128)S(1)}, u32[]{:S(2)}, u32[]{:S(2)}) %all-to-all-start) | async-done | bytes 32800 | tf_op jit(solution)/shard_map/all_to_all | solution.py:131
  63.4 1.7 %multiply_reduce_fusion = (f32[4,128,128]{2,1,0:T(8,128)S(1)}, f32[4,128,128]{2,1,0:T(8,128)}, f32[4,128,128]{2,1,0:T(8,128)}, f32[4,128,128]{2,1,0:T(8,128)}, f32[4,128,128]{2,1,0:T(8,128)}) fusion(f32[4,4]{1,0:T(4,128)S(1)} %get-tuple-element.21, f32[4,4]{1,0:T(4,128)S(1)} %get-tuple-element.86, f32[4,4]{1,0:T(4,128)S(1)} %get-tuple-element.87, ...), kind=kOutput, calls=%fused_computation.27 | convolution fusion | flops 70189056 | bytes 2367808 | tf_op jit(solution)/shard_map/nihd,nihe->nhde/dot_general | solution.py:219
  65.1 2.0 %collective-permute-start.10 = (f32[129,128]{1,0:T(8,128)S(1)}, f32[129,128]{1,0:T(8,128)S(1)}, u32[]{:S(2)}, u32[]{:S(2)}) collective-permute-start(f32[129,128]{1,0:T(8,128)S(1)} %get-tuple-element.45), channel_id=1, source_target_pairs={{0,24},{8,0},{16,8},{24,16},{1,25},{9,1},{17,9},{25,17},{2,26},{10... | collective-permute-start | bytes 198152 | tf_op jit(solution)/shard_map/ppermute | solution.py:78
  70.0 2.9 %collective-permute-done.11 = f32[129,128]{1,0:T(8,128)S(1)} collective-permute-done((f32[129,128]{1,0:T(8,128)S(1)}, f32[129,128]{1,0:T(8,128)S(1)}, u32[]{:S(2)}, u32[]{:S(2)}) %collective-permute-start.11) | collective-permute-done | bytes 66080 | tf_op jit(solution)/shard_map/ppermute | solution.py:78
  73.8 2.1 %collective-permute-start.13 = (f32[1,129,128]{2,1,0:T(8,128)S(1)}, f32[1,129,128]{2,1,0:T(8,128)S(1)}, u32[]{:S(2)}, u32[]{:S(2)}) collective-permute-start(f32[1,129,128]{2,1,0:T(8,128)S(1)} %pad_maximum_fusion.6), channel_id=1, source_target_pairs={{32,0},{64,32},{96,64},{128,96},{160,128},{192,160},{224,192},{33,... | collective-permute-start | bytes 198152 | tf_op jit(solution)/shard_map/ppermute | solution.py:59
  78.4 2.9 %collective-permute-done.13 = f32[1,129,128]{2,1,0:T(8,128)S(1)} collective-permute-done((f32[1,129,128]{2,1,0:T(8,128)S(1)}, f32[1,129,128]{2,1,0:T(8,128)S(1)}, u32[]{:S(2)}, u32[]{:S(2)}) %collective-permute-start.13) | collective-permute-done | bytes 66080 | tf_op jit(solution)/shard_map/ppermute | solution.py:59
  81.3 2.5 %collective-permute-done.14 = f32[1,129,128]{2,1,0:T(8,128)S(1)} collective-permute-done((f32[1,129,128]{2,1,0:T(8,128)S(1)}, f32[1,129,128]{2,1,0:T(8,128)S(1)}, u32[]{:S(2)}, u32[]{:S(2)}) %collective-permute-start.14) | collective-permute-done | bytes 66080 | tf_op jit(solution)/shard_map/ppermute | solution.py:59
  85.1 1.5 %convolution_bitcast_fusion.3 = f32[4,128,4,128]{3,1,2,0:T(8,128)} fusion(bf16[4,4,128,128]{3,2,1,0:T(8,128)(2,1)S(1)} %fusion.12, bf16[4,128,4,128]{1,3,2,0:T(8,128)(2,1)S(1)} %copy.125), kind=kOutput, calls=%fused_computation.7 | convolution fusion | flops 67108864 | bytes 2097152 | tf_op jit(solution)/shard_map/nhij,nihd->njhd/dot_general | solution.py:210
  87.9 5.8 %collective-permute-done.15 = f32[1,129,128]{2,1,0:T(8,128)S(1)} collective-permute-done((f32[1,129,128]{2,1,0:T(8,128)S(1)}, f32[1,129,128]{2,1,0:T(8,128)S(1)}, u32[]{:S(2)}, u32[]{:S(2)}) %collective-permute-start.15) | collective-permute-done | bytes 66080 | tf_op jit(solution)/shard_map/ppermute | solution.py:59
  93.7 1.4 %collective-permute-done.16 = f32[1,129,128]{2,1,0:T(8,128)S(1)} collective-permute-done((f32[1,129,128]{2,1,0:T(8,128)S(1)}, f32[1,129,128]{2,1,0:T(8,128)S(1)}, u32[]{:S(2)}, u32[]{:S(2)}) %collective-permute-start.16) | collective-permute-done | bytes 66080 | tf_op jit(solution)/shard_map/ppermute | solution.py:59
  97.9 1.5 %convolution_bitcast_fusion.1 = f32[4,128,4,128]{3,1,2,0:T(8,128)} fusion(bf16[4,128,4,128]{1,3,2,0:T(8,128)(2,1)S(1)} %multiply_convert_fusion.1, bf16[4,4,128,128]{3,2,1,0:T(8,128)(2,1)S(1)} %copy-done.5), kind=kOutput, calls=%fused_computation.3 | convolution fusion | flops 67108864 | bytes 2097152 | tf_op jit(solution)/shard_map/nhij,nihe->njhe/dot_general | solution.py:213
  103.4 1.6 %fusion.9 = bf16[4,128,4,128]{3,1,2,0:T(8,128)(2,1)S(1)} fusion(f32[4,128,4,128]{3,1,2,0:T(8,128)S(1)} %copy-done.7, f32[4,128,4]{1,2,0:T(4,128)S(1)} %copy.108, bf16[4,128,4,128]{3,2,1,0:T(4,128)(2,1)S(1)} %copy-done.3, f32[1,4,128,128]{3,2,1,0:T(8,128)S(1)} %bitcast.316, f32[1,4,128,128]{3,2,1,0:T(8,128)S(1)} %bitcast.318, ...), kind=kOutput, calls=%fused_computation.19 | convolution fusion | flops 69468160 | bytes 3416128 | tf_op jit(solution)/shard_map/njhe,nhde->njhd/dot_general | solution.py:233
  (147 shorter events, 36.5 us)
Async XLA Ops:
  4.0 39.7 %copy-start.1 = (bf16[4,128,4,128]{3,2,1,0:T(4,128)(2,1)}, bf16[4,128,4,128]{3,2,1,0:T(4,128)(2,1)S(1)}, u32[]{:S(2)}) copy-start(bf16[4,128,4,128]{3,2,1,0:T(4,128)(2,1)S(1)} %reshape.474) | copy-start | bytes 1572868
  6.3 5.2 %collective-permute-start = (f32[129,128]{1,0:T(8,128)S(1)}, f32[129,128]{1,0:T(8,128)S(1)}, u32[]{:S(2)}, u32[]{:S(2)}) collective-permute-start(f32[129,128]{1,0:T(8,128)S(1)} %get-tuple-element.47), channel_id=1, source_target_pairs={{0,24},{8,0},{16,8},{24,16},{1,25},{9,1},{17,9},{25,17},{2,26},{10... | collective-permute-start | bytes 198152 | tf_op jit(solution)/shard_map/ppermute | solution.py:78
  9.1 5.9 %collective-permute-start.1 = (f32[129,128]{1,0:T(8,128)S(1)}, f32[129,128]{1,0:T(8,128)S(1)}, u32[]{:S(2)}, u32[]{:S(2)}) collective-permute-start(f32[129,128]{1,0:T(8,128)S(1)} %get-tuple-element.48), channel_id=1, source_target_pairs={{0,16},{8,24},{16,0},{24,8},{1,17},{9,25},{17,1},{25,9},{2,18},{10... | collective-permute-start | bytes 198152 | tf_op jit(solution)/shard_map/ppermute | solution.py:78
  9.9 5.8 %collective-permute-start.2 = (f32[129,128]{1,0:T(8,128)S(1)}, f32[129,128]{1,0:T(8,128)S(1)}, u32[]{:S(2)}, u32[]{:S(2)}) collective-permute-start(f32[129,128]{1,0:T(8,128)S(1)} %get-tuple-element.46), channel_id=1, source_target_pairs={{0,8},{8,16},{16,24},{24,0},{1,9},{9,17},{17,25},{25,1},{2,10},{10... | collective-permute-start | bytes 198152 | tf_op jit(solution)/shard_map/ppermute | solution.py:78
  15.9 10.3 %collective-permute-start.3 = (f32[1,129,128]{2,1,0:T(8,128)S(1)}, f32[1,129,128]{2,1,0:T(8,128)S(1)}, u32[]{:S(2)}, u32[]{:S(2)}) collective-permute-start(f32[1,129,128]{2,1,0:T(8,128)S(1)} %pad_maximum_fusion.4), channel_id=1, source_target_pairs={{0,32},{32,64},{64,96},{96,128},{128,160},{160,192},{192,224},{1,3... | collective-permute-start | bytes 198152 | tf_op jit(solution)/shard_map/ppermute | solution.py:39
  19.8 8.3 %collective-permute-start.4 = (f32[1,129,128]{2,1,0:T(8,128)S(1)}, f32[1,129,128]{2,1,0:T(8,128)S(1)}, u32[]{:S(2)}, u32[]{:S(2)}) collective-permute-start(f32[1,129,128]{2,1,0:T(8,128)S(1)} %pad_maximum_fusion.4), channel_id=1, source_target_pairs={{0,64},{32,96},{64,128},{96,160},{128,192},{160,224},{1,65},{33,97... | collective-permute-start | bytes 198152 | tf_op jit(solution)/shard_map/ppermute | solution.py:39
  26.2 9.5 %copy-start.18 = (f32[128,128]{1,0:T(8,128)}, f32[128,128]{1,0:T(8,128)S(1)}, u32[]{:S(2)}) copy-start(f32[128,128]{1,0:T(8,128)S(1)} %fusion.71) | copy-start | bytes 196612
  28.1 9.5 %collective-permute-start.5 = (f32[1,129,128]{2,1,0:T(8,128)S(1)}, f32[1,129,128]{2,1,0:T(8,128)S(1)}, u32[]{:S(2)}, u32[]{:S(2)}) collective-permute-start(f32[1,129,128]{2,1,0:T(8,128)S(1)} %pad_maximum_fusion.5), channel_id=1, source_target_pairs={{0,96},{32,128},{64,160},{96,192},{128,224},{1,97},{33,129},{65,16... | collective-permute-start | bytes 198152 | tf_op jit(solution)/shard_map/ppermute | solution.py:39
  36.3 7.3 %copy-start.4 = (bf16[4,4,128,128]{3,2,1,0:T(8,128)(2,1)}, bf16[4,4,128,128]{3,2,1,0:T(8,128)(2,1)S(1)}, u32[]{:S(2)}) copy-start(bf16[4,4,128,128]{3,2,1,0:T(8,128)(2,1)S(1)} %fusion.11) | copy-start | bytes 1572868
  36.3 3.2 %collective-permute-start.6 = (f32[1,129,128]{2,1,0:T(8,128)S(1)}, f32[1,129,128]{2,1,0:T(8,128)S(1)}, u32[]{:S(2)}, u32[]{:S(2)}) collective-permute-start(f32[1,129,128]{2,1,0:T(8,128)S(1)} %pad_maximum_fusion.5), channel_id=1, source_target_pairs={{0,192},{32,224},{1,193},{33,225},{2,194},{34,226},{3,195},{35,227... | collective-permute-start | bytes 198152 | tf_op jit(solution)/shard_map/ppermute | solution.py:39
  41.0 5.0 %collective-permute-start.7 = (f32[128,128]{1,0:T(8,128)}, f32[128,128]{1,0:T(8,128)S(1)}, u32[]{:S(2)}, u32[]{:S(2)}) collective-permute-start(f32[128,128]{1,0:T(8,128)} %get-tuple-element.54), channel_id=1, source_target_pairs={{0,24},{8,0},{16,8},{24,16},{1,25},{9,1},{17,9},{25,17},{2,26},{10... | collective-permute-start | bytes 196616 | tf_op jit(solution)/shard_map/ppermute | solution.py:78
  41.6 6.1 %collective-permute-start.8 = (f32[128,128]{1,0:T(8,128)}, f32[128,128]{1,0:T(8,128)}, u32[]{:S(2)}, u32[]{:S(2)}) collective-permute-start(f32[128,128]{1,0:T(8,128)} %get-tuple-element.53), channel_id=1, source_target_pairs={{0,16},{8,24},{16,0},{24,8},{1,17},{9,25},{17,1},{25,9},{2,18},{10... | collective-permute-start | bytes 196616 | tf_op jit(solution)/shard_map/ppermute | solution.py:78
  42.5 5.9 %collective-permute-start.9 = (f32[128,128]{1,0:T(8,128)}, f32[128,128]{1,0:T(8,128)}, u32[]{:S(2)}, u32[]{:S(2)}) collective-permute-start(f32[128,128]{1,0:T(8,128)} %get-tuple-element.52), channel_id=1, source_target_pairs={{0,8},{8,16},{16,24},{24,0},{1,9},{9,17},{17,25},{25,1},{2,10},{10... | collective-permute-start | bytes 196616 | tf_op jit(solution)/shard_map/ppermute | solution.py:78
  51.8 9.9 %all-to-all-start = ((f32[8,2,4,128]{3,2,1,0:T(4,128)}), f32[8,2,4,128]{3,2,1,0:T(4,128)S(1)}, u32[]{:S(2)}, u32[]{:S(2)}) async-start(f32[8,2,4,128]{3,2,1,0:T(4,128)} %broadcast_in_dim.5), calls=%async_computation | async-start | bytes 65536 | tf_op jit(solution)/shard_map/all_to_all | solution.py:131
  65.1 5.0 %collective-permute-start.10 = (f32[129,128]{1,0:T(8,128)S(1)}, f32[129,128]{1,0:T(8,128)S(1)}, u32[]{:S(2)}, u32[]{:S(2)}) collective-permute-start(f32[129,128]{1,0:T(8,128)S(1)} %get-tuple-element.45), channel_id=1, source_target_pairs={{0,24},{8,0},{16,8},{24,16},{1,25},{9,1},{17,9},{25,17},{2,26},{10... | collective-permute-start | bytes 198152 | tf_op jit(solution)/shard_map/ppermute | solution.py:78
  67.1 5.8 %collective-permute-start.11 = (f32[129,128]{1,0:T(8,128)S(1)}, f32[129,128]{1,0:T(8,128)S(1)}, u32[]{:S(2)}, u32[]{:S(2)}) collective-permute-start(f32[129,128]{1,0:T(8,128)S(1)} %get-tuple-element.44), channel_id=1, source_target_pairs={{0,16},{8,24},{16,0},{24,8},{1,17},{9,25},{17,1},{25,9},{2,18},{10... | collective-permute-start | bytes 198152 | tf_op jit(solution)/shard_map/ppermute | solution.py:78
  68.0 5.7 %collective-permute-start.12 = (f32[129,128]{1,0:T(8,128)S(1)}, f32[129,128]{1,0:T(8,128)S(1)}, u32[]{:S(2)}, u32[]{:S(2)}) collective-permute-start(f32[129,128]{1,0:T(8,128)S(1)} %get-tuple-element.43), channel_id=1, source_target_pairs={{0,8},{8,16},{16,24},{24,0},{1,9},{9,17},{17,25},{25,1},{2,10},{10... | collective-permute-start | bytes 198152 | tf_op jit(solution)/shard_map/ppermute | solution.py:78
  73.8 7.4 %collective-permute-start.13 = (f32[1,129,128]{2,1,0:T(8,128)S(1)}, f32[1,129,128]{2,1,0:T(8,128)S(1)}, u32[]{:S(2)}, u32[]{:S(2)}) collective-permute-start(f32[1,129,128]{2,1,0:T(8,128)S(1)} %pad_maximum_fusion.6), channel_id=1, source_target_pairs={{32,0},{64,32},{96,64},{128,96},{160,128},{192,160},{224,192},{33,... | collective-permute-start | bytes 198152 | tf_op jit(solution)/shard_map/ppermute | solution.py:59
  75.9 7.8 %collective-permute-start.14 = (f32[1,129,128]{2,1,0:T(8,128)S(1)}, f32[1,129,128]{2,1,0:T(8,128)S(1)}, u32[]{:S(2)}, u32[]{:S(2)}) collective-permute-start(f32[1,129,128]{2,1,0:T(8,128)S(1)} %pad_maximum_fusion.6), channel_id=1, source_target_pairs={{64,0},{96,32},{128,64},{160,96},{192,128},{224,160},{65,1},{97,33... | collective-permute-start | bytes 198152 | tf_op jit(solution)/shard_map/ppermute | solution.py:59
  83.8 9.9 %collective-permute-start.15 = (f32[1,129,128]{2,1,0:T(8,128)S(1)}, f32[1,129,128]{2,1,0:T(8,128)S(1)}, u32[]{:S(2)}, u32[]{:S(2)}) collective-permute-start(f32[1,129,128]{2,1,0:T(8,128)S(1)} %pad_maximum_fusion.7), channel_id=1, source_target_pairs={{96,0},{128,32},{160,64},{192,96},{224,128},{97,1},{129,33},{161,6... | collective-permute-start | bytes 198152 | tf_op jit(solution)/shard_map/ppermute | solution.py:59
  86.6 8.5 %collective-permute-start.16 = (f32[1,129,128]{2,1,0:T(8,128)S(1)}, f32[1,129,128]{2,1,0:T(8,128)S(1)}, u32[]{:S(2)}, u32[]{:S(2)}) collective-permute-start(f32[1,129,128]{2,1,0:T(8,128)S(1)} %pad_maximum_fusion.7), channel_id=1, source_target_pairs={{192,0},{224,32},{193,1},{225,33},{194,2},{226,34},{195,3},{227,35... | collective-permute-start | bytes 198152 | tf_op jit(solution)/shard_map/ppermute | solution.py:59
  95.2 5.5 %collective-permute-start.17 = (f32[128,128]{1,0:T(8,128)S(1)}, f32[128,128]{1,0:T(8,128)S(1)}, u32[]{:S(2)}, u32[]{:S(2)}) collective-permute-start(f32[128,128]{1,0:T(8,128)S(1)} %get-tuple-element.51), channel_id=1, source_target_pairs={{0,24},{8,0},{16,8},{24,16},{1,25},{9,1},{17,9},{25,17},{2,26},{10... | collective-permute-start | bytes 196616 | tf_op jit(solution)/shard_map/ppermute | solution.py:78
  95.8 5.8 %collective-permute-start.18 = (f32[128,128]{1,0:T(8,128)S(1)}, f32[128,128]{1,0:T(8,128)S(1)}, u32[]{:S(2)}, u32[]{:S(2)}) collective-permute-start(f32[128,128]{1,0:T(8,128)S(1)} %get-tuple-element.50), channel_id=1, source_target_pairs={{0,16},{8,24},{16,0},{24,8},{1,17},{9,25},{17,1},{25,9},{2,18},{10... | collective-permute-start | bytes 196616 | tf_op jit(solution)/shard_map/ppermute | solution.py:78
  96.7 5.6 %collective-permute-start.19 = (f32[128,128]{1,0:T(8,128)S(1)}, f32[128,128]{1,0:T(8,128)S(1)}, u32[]{:S(2)}, u32[]{:S(2)}) collective-permute-start(f32[128,128]{1,0:T(8,128)S(1)} %get-tuple-element.49), channel_id=1, source_target_pairs={{0,8},{8,16},{16,24},{24,0},{1,9},{9,17},{17,25},{25,1},{2,10},{10... | collective-permute-start | bytes 196616 | tf_op jit(solution)/shard_map/ppermute | solution.py:78
  (21 other events, 44.9 us)

commit v12 on v11

--- a/solution.py
+++ b/solution.py
@@ -71,9 +71,15 @@
 
 def exchange(payload, axis, ranks):
     me = lax.axis_index(axis)
-    got = [lax.dynamic_index_in_dim(payload, me, 0, keepdims=False)]
+    def entry(index):
+        pick = payload[0]
+        for k in range(1, ranks):
+            pick = jnp.where(index == k, payload[k], pick)
+        return pick
+
+    got = [entry(me)]
     for shift in range(1, ranks):
-        send = lax.dynamic_index_in_dim(payload, (me + shift) % ranks, 0, keepdims=False)
+        send = entry((me + shift) % ranks)
         pairs = [(i, (i + shift) % ranks) for i in range(ranks)]
         got.append(lax.ppermute(send, axis, pairs))
     outs = []

time: 110 us -> 112 us (1.018)
  other arithmetic: 2.29 us -> 5.63 us
  matrix products: 14.9 us -> 12.8 us
  starting transfers between devices: 42.5 us -> 43.7 us
    ppermute x12, waiting for transfers between devices: 13.3 us -> 11.4 us  [exchange(): got.append(lax.ppermute(send, axis, pairs))]
    select_n x0 -> x8, other arithmetic: none -> 1.57 us  [entry(): pick = jnp.where(index == k, payload[k], pick)]
    exp x1, local copies, waits for them, and re-layouts: 0.11 us -> 1.66 us  [shards(): jnp.exp(inside_block_mask)[..., None] * inter_out]
    unnamed x51 -> x93, local copies, waits for them, and re-layouts: 7.27 us -> 6.61 us
  transfers between devices with their start and end apart: 21 -> 21, of which waited for: 17 -> 15; matrix products, arithmetic and copies ran while one was open for 9% -> 9% of each run, Pallas kernels for 0% -> 0%
where the time goes in v12:
time: 112 us; the launch traced here: 110 us
  starting transfers between devices  43.7 us (39%)
  waiting for transfers between devices  34 us (30%)
  matrix products  12.8 us (11%)
  local copies, waits for them, and re-layouts  12.5 us (11%)
  other arithmetic  5.63 us (5%)
  between operations  1.48 us (1%)
    ppermute x4, starting transfers between devices, forward_scan(): lax.ppermute(payload, axis, [(i, i + s) for i in range(ranks - s)])  19.1 us
    ppermute x12, starting transfers between devices, exchange(): got.append(lax.ppermute(send, axis, pairs))  14 us
    ppermute x4, waiting for transfers between devices, backward_scan(): lax.ppermute(payload, axis, [(i + s, i) for i in range(ranks - s)])  13.4 us
    ppermute x12, waiting for transfers between devices, exchange(): got.append(lax.ppermute(send, axis, pairs))  11.4 us
    unnamed x93, local copies, waits for them, and re-layouts  6.61 us
    ppermute x4, starting transfers between devices, backward_scan(): lax.ppermute(payload, axis, [(i + s, i) for i in range(ranks - s)])  6.05 us
    all_to_all x1, waiting for transfers between devices, head_sum(): gathered = lax.all_to_all(copies, 'head', 0, 0, tiled=True)  5.43 us
    all_to_all x1, starting transfers between devices, head_sum(): gathered = lax.all_to_all(copies, 'head', 0, 0, tiled=True)  4.6 us
  transfers between devices with their start and end apart: 21, of which 15 were waited for; matrix products, arithmetic and copies ran while one was open for 9% of the time, Pallas kernels for 0%

profile of v12, /device:TPU:32, one launch (start us, length us, event | category | flops | bytes accessed | tf_op | source)
XLA Modules:
  0.0 110.2 jit_solution(13948543119615902485)
XLA Ops:
  5.5 2.0 %multiply_reduce_fusion.7 = (f32[4,128,128]{2,1,0:T(8,128)S(1)}, f32[4,128,128]{2,1,0:T(8,128)}, f32[4,128,128]{2,1,0:T(8,128)}, f32[4,128,128]{2,1,0:T(8,128)}, f32[4,128,128]{2,1,0:T(8,128)}) fusion(f32[4,4]{1,0:T(4,128)S(1)} %subtract_exponential_fusion.1, f32[4,4]{1,0:T(4,128)S(1)} %get-tuple-element.88, f32[4,4]{1,0:T(4,128)S(1)} %get-tuple-element.89, ...), kind=kOutput, calls=%fused_computation.36 | convolution fusion | flops 70189056 | bytes 2367808 | tf_op jit(solution)/shard_map/njhd,njhe->nhde/dot_general | solution.py:179
  7.6 2.8 %collective-permute-start = (f32[129,128]{1,0:T(8,128)S(1)}, f32[129,128]{1,0:T(8,128)S(1)}, u32[]{:S(2)}, u32[]{:S(2)}) collective-permute-start(f32[129,128]{1,0:T(8,128)S(1)} %get-tuple-element.40), channel_id=1, source_target_pairs={{0,24},{8,0},{16,8},{24,16},{1,25},{9,1},{17,9},{25,17},{2,26},{10... | collective-permute-start | bytes 198152 | tf_op jit(solution)/shard_map/ppermute | solution.py:84
  12.7 3.6 %collective-permute-done.1 = f32[129,128]{1,0:T(8,128)S(1)} collective-permute-done((f32[129,128]{1,0:T(8,128)S(1)}, f32[129,128]{1,0:T(8,128)S(1)}, u32[]{:S(2)}, u32[]{:S(2)}) %collective-permute-start.1) | collective-permute-done | bytes 66080 | tf_op jit(solution)/shard_map/ppermute | solution.py:84
  17.3 3.8 %collective-permute-start.3 = (f32[1,129,128]{2,1,0:T(8,128)S(1)}, f32[1,129,128]{2,1,0:T(8,128)S(1)}, u32[]{:S(2)}, u32[]{:S(2)}) collective-permute-start(f32[1,129,128]{2,1,0:T(8,128)S(1)} %pad_maximum_fusion.4), channel_id=1, source_target_pairs={{0,32},{32,64},{64,96},{96,128},{128,160},{160,192},{192,224},{1,3... | collective-permute-start | bytes 198152 | tf_op jit(solution)/shard_map/ppermute | solution.py:39
  21.1 6.4 %collective-permute-start.4 = (f32[1,129,128]{2,1,0:T(8,128)S(1)}, f32[1,129,128]{2,1,0:T(8,128)S(1)}, u32[]{:S(2)}, u32[]{:S(2)}) collective-permute-start(f32[1,129,128]{2,1,0:T(8,128)S(1)} %pad_maximum_fusion.4), channel_id=1, source_target_pairs={{0,64},{32,96},{64,128},{96,160},{128,192},{160,224},{1,65},{33,97... | collective-permute-start | bytes 198152 | tf_op jit(solution)/shard_map/ppermute | solution.py:39
  27.5 1.9 %collective-permute-done.4 = f32[1,129,128]{2,1,0:T(8,128)S(1)} collective-permute-done((f32[1,129,128]{2,1,0:T(8,128)S(1)}, f32[1,129,128]{2,1,0:T(8,128)S(1)}, u32[]{:S(2)}, u32[]{:S(2)}) %collective-permute-start.4) | collective-permute-done | bytes 66080 | tf_op jit(solution)/shard_map/ppermute | solution.py:39
  29.5 7.6 %collective-permute-start.5 = (f32[1,129,128]{2,1,0:T(8,128)S(1)}, f32[1,129,128]{2,1,0:T(8,128)S(1)}, u32[]{:S(2)}, u32[]{:S(2)}) collective-permute-start(f32[1,129,128]{2,1,0:T(8,128)S(1)} %pad_maximum_fusion.5), channel_id=1, source_target_pairs={{0,96},{32,128},{64,160},{96,192},{128,224},{1,97},{33,129},{65,16... | collective-permute-start | bytes 198152 | tf_op jit(solution)/shard_map/ppermute | solution.py:39
  39.0 1.9 %collective-permute-done.6 = f32[1,129,128]{2,1,0:T(8,128)S(1)} collective-permute-done((f32[1,129,128]{2,1,0:T(8,128)S(1)}, f32[1,129,128]{2,1,0:T(8,128)S(1)}, u32[]{:S(2)}, u32[]{:S(2)}) %collective-permute-start.6) | collective-permute-done | bytes 66080 | tf_op jit(solution)/shard_map/ppermute | solution.py:39
  47.2 1.7 %copy.106 = f32[4,128,4]{1,2,0:T(4,128)} copy(f32[4,128,4]{2,1,0:T(8,128)} %get-tuple-element.60) | data formatting | bytes 16384 | tf_op jit(solution)/shard_map/exp | solution.py:194
  51.7 1.6 %multiply_reduce_fusion.6 = (f32[4,128]{1,0:T(4,128)S(1)}, f32[4,128]{1,0:T(4,128)S(1)}, f32[4,128,4,128]{1,3,2,0:T(8,128)S(1)}) fusion(f32[4,128,4,128]{1,3,2,0:T(8,128)S(1)} %copy.114, f32[4,128,4,128]{1,3,2,0:T(8,128)S(1)} %copy-done, bf16[4,128,4,128]{1,3,2,0:T(8,128)(2,1)S(1)} %copy.125, f32[1,4,128,128]{3,2,1,0:T(8,128)S(1)} %bitcast.343, ...), kind=kOutput, calls=%fused_computation.35 | convolution fusion | flops 70253568 | bytes 4993088 | tf_op jit(solution)/shard_map/nihd,nhde->nihe/dot_general | solution.py:191
  53.9 4.6 %all-to-all-start = ((f32[8,2,4,128]{3,2,1,0:T(4,128)}), f32[8,2,4,128]{3,2,1,0:T(4,128)S(1)}, u32[]{:S(2)}, u32[]{:S(2)}) async-start(f32[8,2,4,128]{3,2,1,0:T(4,128)} %broadcast_in_dim.5), calls=%async_computation | async-start | bytes 65536 | tf_op jit(solution)/shard_map/all_to_all | solution.py:137
  58.6 5.4 %all-to-all-done = f32[8,2,4,128]{3,2,1,0:T(4,128)S(1)} async-done(((f32[8,2,4,128]{3,2,1,0:T(4,128)}), f32[8,2,4,128]{3,2,1,0:T(4,128)S(1)}, u32[]{:S(2)}, u32[]{:S(2)}) %all-to-all-start) | async-done | bytes 32800 | tf_op jit(solution)/shard_map/all_to_all | solution.py:137
  65.7 1.6 %multiply_reduce_fusion = (f32[4,128,128]{2,1,0:T(8,128)S(1)}, f32[4,128,128]{2,1,0:T(8,128)}, f32[4,128,128]{2,1,0:T(8,128)}, f32[4,128,128]{2,1,0:T(8,128)}, f32[4,128,128]{2,1,0:T(8,128)}) fusion(f32[4,4]{1,0:T(4,128)S(1)} %copy-done.34, f32[4,4]{1,0:T(4,128)S(1)} %get-tuple-element.84, f32[4,4]{1,0:T(4,128)S(1)} %get-tuple-element.85, ...), kind=kOutput, calls=%fused_computation.27 | convolution fusion | flops 70189056 | bytes 2367808 | tf_op jit(solution)/shard_map/nihd,nihe->nhde/dot_general | solution.py:225
  67.4 2.0 %collective-permute-start.10 = (f32[129,128]{1,0:T(8,128)S(1)}, f32[129,128]{1,0:T(8,128)S(1)}, u32[]{:S(2)}, u32[]{:S(2)}) collective-permute-start(f32[129,128]{1,0:T(8,128)S(1)} %get-tuple-element.38), channel_id=1, source_target_pairs={{0,24},{8,0},{16,8},{24,16},{1,25},{9,1},{17,9},{25,17},{2,26},{10... | collective-permute-start | bytes 198152 | tf_op jit(solution)/shard_map/ppermute | solution.py:84
  69.4 1.7 %collective-permute-start.11 = (f32[129,128]{1,0:T(8,128)S(1)}, f32[129,128]{1,0:T(8,128)S(1)}, u32[]{:S(2)}, u32[]{:S(2)}) collective-permute-start(f32[129,128]{1,0:T(8,128)S(1)} %get-tuple-element.37), channel_id=1, source_target_pairs={{0,16},{8,24},{16,0},{24,8},{1,17},{9,25},{17,1},{25,9},{2,18},{10... | collective-permute-start | bytes 198152 | tf_op jit(solution)/shard_map/ppermute | solution.py:84
  72.3 3.1 %collective-permute-done.11 = f32[129,128]{1,0:T(8,128)S(1)} collective-permute-done((f32[129,128]{1,0:T(8,128)S(1)}, f32[129,128]{1,0:T(8,128)S(1)}, u32[]{:S(2)}, u32[]{:S(2)}) %collective-permute-start.11) | collective-permute-done | bytes 66080 | tf_op jit(solution)/shard_map/ppermute | solution.py:84
  76.8 2.1 %collective-permute-start.13 = (f32[1,129,128]{2,1,0:T(8,128)S(1)}, f32[1,129,128]{2,1,0:T(8,128)S(1)}, u32[]{:S(2)}, u32[]{:S(2)}) collective-permute-start(f32[1,129,128]{2,1,0:T(8,128)S(1)} %pad_maximum_fusion.6), channel_id=1, source_target_pairs={{32,0},{64,32},{96,64},{128,96},{160,128},{192,160},{224,192},{33,... | collective-permute-start | bytes 198152 | tf_op jit(solution)/shard_map/ppermute | solution.py:59
  80.6 3.8 %collective-permute-done.13 = f32[1,129,128]{2,1,0:T(8,128)S(1)} collective-permute-done((f32[1,129,128]{2,1,0:T(8,128)S(1)}, f32[1,129,128]{2,1,0:T(8,128)S(1)}, u32[]{:S(2)}, u32[]{:S(2)}) %collective-permute-start.13) | collective-permute-done | bytes 66080 | tf_op jit(solution)/shard_map/ppermute | solution.py:59
  84.4 2.3 %collective-permute-done.14 = f32[1,129,128]{2,1,0:T(8,128)S(1)} collective-permute-done((f32[1,129,128]{2,1,0:T(8,128)S(1)}, f32[1,129,128]{2,1,0:T(8,128)S(1)}, u32[]{:S(2)}, u32[]{:S(2)}) %collective-permute-start.14) | collective-permute-done | bytes 66080 | tf_op jit(solution)/shard_map/ppermute | solution.py:59
  88.1 1.5 %convolution_bitcast_fusion.3 = f32[4,128,4,128]{3,1,2,0:T(8,128)} fusion(bf16[4,4,128,128]{3,2,1,0:T(8,128)(2,1)S(1)} %fusion.12, bf16[4,128,4,128]{1,3,2,0:T(8,128)(2,1)S(1)} %copy.125), kind=kOutput, calls=%fused_computation.7 | convolution fusion | flops 67108864 | bytes 2097152 | tf_op jit(solution)/shard_map/nhij,nihd->njhd/dot_general | solution.py:216
  91.0 5.5 %collective-permute-done.15 = f32[1,129,128]{2,1,0:T(8,128)S(1)} collective-permute-done((f32[1,129,128]{2,1,0:T(8,128)S(1)}, f32[1,129,128]{2,1,0:T(8,128)S(1)}, u32[]{:S(2)}, u32[]{:S(2)}) %collective-permute-start.15) | collective-permute-done | bytes 66080 | tf_op jit(solution)/shard_map/ppermute | solution.py:59
  96.5 1.7 %collective-permute-done.16 = f32[1,129,128]{2,1,0:T(8,128)S(1)} collective-permute-done((f32[1,129,128]{2,1,0:T(8,128)S(1)}, f32[1,129,128]{2,1,0:T(8,128)S(1)}, u32[]{:S(2)}, u32[]{:S(2)}) %collective-permute-start.16) | collective-permute-done | bytes 66080 | tf_op jit(solution)/shard_map/ppermute | solution.py:59
  98.4 1.5 %collective-permute-start.18 = (f32[128,128]{1,0:T(8,128)S(1)}, f32[128,128]{1,0:T(8,128)S(1)}, u32[]{:S(2)}, u32[]{:S(2)}) collective-permute-start(f32[128,128]{1,0:T(8,128)S(1)} %get-tuple-element.47), channel_id=1, source_target_pairs={{0,16},{8,24},{16,0},{24,8},{1,17},{9,25},{17,1},{25,9},{2,18},{10... | collective-permute-start | bytes 196616 | tf_op jit(solution)/shard_map/ppermute | solution.py:84
  100.8 1.5 %convolution_bitcast_fusion.1 = f32[4,128,4,128]{3,1,2,0:T(8,128)} fusion(bf16[4,128,4,128]{1,3,2,0:T(8,128)(2,1)S(1)} %multiply_convert_fusion.1, bf16[4,4,128,128]{3,2,1,0:T(8,128)(2,1)S(1)} %copy-done.5), kind=kOutput, calls=%fused_computation.3 | convolution fusion | flops 67108864 | bytes 2097152 | tf_op jit(solution)/shard_map/nhij,nihe->njhe/dot_general | solution.py:219
  (189 shorter events, 37.1 us)
Async XLA Ops:
  4.0 41.0 %copy-start.1 = (bf16[4,128,4,128]{3,2,1,0:T(4,128)(2,1)}, bf16[4,128,4,128]{3,2,1,0:T(4,128)(2,1)S(1)}, u32[]{:S(2)}) copy-start(bf16[4,128,4,128]{3,2,1,0:T(4,128)(2,1)S(1)} %reshape.420) | copy-start | bytes 1572868
  7.6 5.2 %collective-permute-start = (f32[129,128]{1,0:T(8,128)S(1)}, f32[129,128]{1,0:T(8,128)S(1)}, u32[]{:S(2)}, u32[]{:S(2)}) collective-permute-start(f32[129,128]{1,0:T(8,128)S(1)} %get-tuple-element.40), channel_id=1, source_target_pairs={{0,24},{8,0},{16,8},{24,16},{1,25},{9,1},{17,9},{25,17},{2,26},{10... | collective-permute-start | bytes 198152 | tf_op jit(solution)/shard_map/ppermute | solution.py:84
  10.4 5.9 %collective-permute-start.1 = (f32[129,128]{1,0:T(8,128)S(1)}, f32[129,128]{1,0:T(8,128)S(1)}, u32[]{:S(2)}, u32[]{:S(2)}) collective-permute-start(f32[129,128]{1,0:T(8,128)S(1)} %get-tuple-element.39), channel_id=1, source_target_pairs={{0,16},{8,24},{16,0},{24,8},{1,17},{9,25},{17,1},{25,9},{2,18},{10... | collective-permute-start | bytes 198152 | tf_op jit(solution)/shard_map/ppermute | solution.py:84
  11.2 5.8 %collective-permute-start.2 = (f32[129,128]{1,0:T(8,128)S(1)}, f32[129,128]{1,0:T(8,128)S(1)}, u32[]{:S(2)}, u32[]{:S(2)}) collective-permute-start(f32[129,128]{1,0:T(8,128)S(1)} %get-tuple-element.35), channel_id=1, source_target_pairs={{0,8},{8,16},{16,24},{24,0},{1,9},{9,17},{17,25},{25,1},{2,10},{10... | collective-permute-start | bytes 198152 | tf_op jit(solution)/shard_map/ppermute | solution.py:84
  17.1 24.5 %copy-start.26 = (f32[128]{0:T(128)}, f32[128]{0:T(128)S(1)}, u32[]{:S(2)}) copy-start(f32[128]{0:T(128)S(1)} %broadcast_multiply_fusion.1) | copy-start | bytes 1540
  17.2 24.4 %copy-start.22 = (f32[128]{0:T(128)}, f32[128]{0:T(128)S(1)}, u32[]{:S(2)}) copy-start(f32[128]{0:T(128)S(1)} %get-tuple-element.81) | copy-start | bytes 1540
  17.3 10.3 %collective-permute-start.3 = (f32[1,129,128]{2,1,0:T(8,128)S(1)}, f32[1,129,128]{2,1,0:T(8,128)S(1)}, u32[]{:S(2)}, u32[]{:S(2)}) collective-permute-start(f32[1,129,128]{2,1,0:T(8,128)S(1)} %pad_maximum_fusion.4), channel_id=1, source_target_pairs={{0,32},{32,64},{64,96},{96,128},{128,160},{160,192},{192,224},{1,3... | collective-permute-start | bytes 198152 | tf_op jit(solution)/shard_map/ppermute | solution.py:39
  21.1 8.3 %collective-permute-start.4 = (f32[1,129,128]{2,1,0:T(8,128)S(1)}, f32[1,129,128]{2,1,0:T(8,128)S(1)}, u32[]{:S(2)}, u32[]{:S(2)}) collective-permute-start(f32[1,129,128]{2,1,0:T(8,128)S(1)} %pad_maximum_fusion.4), channel_id=1, source_target_pairs={{0,64},{32,96},{64,128},{96,160},{128,192},{160,224},{1,65},{33,97... | collective-permute-start | bytes 198152 | tf_op jit(solution)/shard_map/ppermute | solution.py:39
  29.5 9.5 %collective-permute-start.5 = (f32[1,129,128]{2,1,0:T(8,128)S(1)}, f32[1,129,128]{2,1,0:T(8,128)S(1)}, u32[]{:S(2)}, u32[]{:S(2)}) collective-permute-start(f32[1,129,128]{2,1,0:T(8,128)S(1)} %pad_maximum_fusion.5), channel_id=1, source_target_pairs={{0,96},{32,128},{64,160},{96,192},{128,224},{1,97},{33,129},{65,16... | collective-permute-start | bytes 198152 | tf_op jit(solution)/shard_map/ppermute | solution.py:39
  37.7 3.2 %collective-permute-start.6 = (f32[1,129,128]{2,1,0:T(8,128)S(1)}, f32[1,129,128]{2,1,0:T(8,128)S(1)}, u32[]{:S(2)}, u32[]{:S(2)}) collective-permute-start(f32[1,129,128]{2,1,0:T(8,128)S(1)} %pad_maximum_fusion.5), channel_id=1, source_target_pairs={{0,192},{32,224},{1,193},{33,225},{2,194},{34,226},{3,195},{35,227... | collective-permute-start | bytes 198152 | tf_op jit(solution)/shard_map/ppermute | solution.py:39
  42.3 6.5 %collective-permute-start.7 = (f32[128,128]{1,0:T(8,128)}, f32[128,128]{1,0:T(8,128)S(1)}, u32[]{:S(2)}, u32[]{:S(2)}) collective-permute-start(f32[128,128]{1,0:T(8,128)} %get-tuple-element.50), channel_id=1, source_target_pairs={{0,24},{8,0},{16,8},{24,16},{1,25},{9,1},{17,9},{25,17},{2,26},{10... | collective-permute-start | bytes 196616 | tf_op jit(solution)/shard_map/ppermute | solution.py:84
  42.9 6.0 %collective-permute-start.8 = (f32[128,128]{1,0:T(8,128)}, f32[128,128]{1,0:T(8,128)S(1)}, u32[]{:S(2)}, u32[]{:S(2)}) collective-permute-start(f32[128,128]{1,0:T(8,128)} %get-tuple-element.49), channel_id=1, source_target_pairs={{0,16},{8,24},{16,0},{24,8},{1,17},{9,25},{17,1},{25,9},{2,18},{10... | collective-permute-start | bytes 196616 | tf_op jit(solution)/shard_map/ppermute | solution.py:84
  43.7 5.9 %collective-permute-start.9 = (f32[128,128]{1,0:T(8,128)}, f32[128,128]{1,0:T(8,128)}, u32[]{:S(2)}, u32[]{:S(2)}) collective-permute-start(f32[128,128]{1,0:T(8,128)} %get-tuple-element.29), channel_id=1, source_target_pairs={{0,8},{8,16},{16,24},{24,0},{1,9},{9,17},{17,25},{25,1},{2,10},{10... | collective-permute-start | bytes 196616 | tf_op jit(solution)/shard_map/ppermute | solution.py:84
  53.9 10.0 %all-to-all-start = ((f32[8,2,4,128]{3,2,1,0:T(4,128)}), f32[8,2,4,128]{3,2,1,0:T(4,128)S(1)}, u32[]{:S(2)}, u32[]{:S(2)}) async-start(f32[8,2,4,128]{3,2,1,0:T(4,128)} %broadcast_in_dim.5), calls=%async_computation | async-start | bytes 65536 | tf_op jit(solution)/shard_map/all_to_all | solution.py:137
  67.4 4.9 %collective-permute-start.10 = (f32[129,128]{1,0:T(8,128)S(1)}, f32[129,128]{1,0:T(8,128)S(1)}, u32[]{:S(2)}, u32[]{:S(2)}) collective-permute-start(f32[129,128]{1,0:T(8,128)S(1)} %get-tuple-element.38), channel_id=1, source_target_pairs={{0,24},{8,0},{16,8},{24,16},{1,25},{9,1},{17,9},{25,17},{2,26},{10... | collective-permute-start | bytes 198152 | tf_op jit(solution)/shard_map/ppermute | solution.py:84
  69.4 5.9 %collective-permute-start.11 = (f32[129,128]{1,0:T(8,128)S(1)}, f32[129,128]{1,0:T(8,128)S(1)}, u32[]{:S(2)}, u32[]{:S(2)}) collective-permute-start(f32[129,128]{1,0:T(8,128)S(1)} %get-tuple-element.37), channel_id=1, source_target_pairs={{0,16},{8,24},{16,0},{24,8},{1,17},{9,25},{17,1},{25,9},{2,18},{10... | collective-permute-start | bytes 198152 | tf_op jit(solution)/shard_map/ppermute | solution.py:84
  71.1 5.5 %collective-permute-start.12 = (f32[129,128]{1,0:T(8,128)S(1)}, f32[129,128]{1,0:T(8,128)S(1)}, u32[]{:S(2)}, u32[]{:S(2)}) collective-permute-start(f32[129,128]{1,0:T(8,128)S(1)} %get-tuple-element.23), channel_id=1, source_target_pairs={{0,8},{8,16},{16,24},{24,0},{1,9},{9,17},{17,25},{25,1},{2,10},{10... | collective-permute-start | bytes 198152 | tf_op jit(solution)/shard_map/ppermute | solution.py:84
  76.8 7.6 %collective-permute-start.13 = (f32[1,129,128]{2,1,0:T(8,128)S(1)}, f32[1,129,128]{2,1,0:T(8,128)S(1)}, u32[]{:S(2)}, u32[]{:S(2)}) collective-permute-start(f32[1,129,128]{2,1,0:T(8,128)S(1)} %pad_maximum_fusion.6), channel_id=1, source_target_pairs={{32,0},{64,32},{96,64},{128,96},{160,128},{192,160},{224,192},{33,... | collective-permute-start | bytes 198152 | tf_op jit(solution)/shard_map/ppermute | solution.py:59
  78.9 7.8 %collective-permute-start.14 = (f32[1,129,128]{2,1,0:T(8,128)S(1)}, f32[1,129,128]{2,1,0:T(8,128)S(1)}, u32[]{:S(2)}, u32[]{:S(2)}) collective-permute-start(f32[1,129,128]{2,1,0:T(8,128)S(1)} %pad_maximum_fusion.6), channel_id=1, source_target_pairs={{64,0},{96,32},{128,64},{160,96},{192,128},{224,160},{65,1},{97,33... | collective-permute-start | bytes 198152 | tf_op jit(solution)/shard_map/ppermute | solution.py:59
  86.8 9.7 %collective-permute-start.15 = (f32[1,129,128]{2,1,0:T(8,128)S(1)}, f32[1,129,128]{2,1,0:T(8,128)S(1)}, u32[]{:S(2)}, u32[]{:S(2)}) collective-permute-start(f32[1,129,128]{2,1,0:T(8,128)S(1)} %pad_maximum_fusion.7), channel_id=1, source_target_pairs={{96,0},{128,32},{160,64},{192,96},{224,128},{97,1},{129,33},{161,6... | collective-permute-start | bytes 198152 | tf_op jit(solution)/shard_map/ppermute | solution.py:59
  89.6 8.7 %collective-permute-start.16 = (f32[1,129,128]{2,1,0:T(8,128)S(1)}, f32[1,129,128]{2,1,0:T(8,128)S(1)}, u32[]{:S(2)}, u32[]{:S(2)}) collective-permute-start(f32[1,129,128]{2,1,0:T(8,128)S(1)} %pad_maximum_fusion.7), channel_id=1, source_target_pairs={{192,0},{224,32},{193,1},{225,33},{194,2},{226,34},{195,3},{227,35... | collective-permute-start | bytes 198152 | tf_op jit(solution)/shard_map/ppermute | solution.py:59
  98.3 5.2 %collective-permute-start.17 = (f32[128,128]{1,0:T(8,128)S(1)}, f32[128,128]{1,0:T(8,128)S(1)}, u32[]{:S(2)}, u32[]{:S(2)}) collective-permute-start(f32[128,128]{1,0:T(8,128)S(1)} %get-tuple-element.48), channel_id=1, source_target_pairs={{0,24},{8,0},{16,8},{24,16},{1,25},{9,1},{17,9},{25,17},{2,26},{10... | collective-permute-start | bytes 196616 | tf_op jit(solution)/shard_map/ppermute | solution.py:84
  98.4 5.9 %collective-permute-start.18 = (f32[128,128]{1,0:T(8,128)S(1)}, f32[128,128]{1,0:T(8,128)S(1)}, u32[]{:S(2)}, u32[]{:S(2)}) collective-permute-start(f32[128,128]{1,0:T(8,128)S(1)} %get-tuple-element.47), channel_id=1, source_target_pairs={{0,16},{8,24},{16,0},{24,8},{1,17},{9,25},{17,1},{25,9},{2,18},{10... | collective-permute-start | bytes 196616 | tf_op jit(solution)/shard_map/ppermute | solution.py:84
  100.0 5.5 %collective-permute-start.19 = (f32[128,128]{1,0:T(8,128)S(1)}, f32[128,128]{1,0:T(8,128)S(1)}, u32[]{:S(2)}, u32[]{:S(2)}) collective-permute-start(f32[128,128]{1,0:T(8,128)S(1)} %get-tuple-element.17), channel_id=1, source_target_pairs={{0,8},{8,16},{16,24},{24,0},{1,9},{9,17},{17,25},{25,1},{2,10},{10... | collective-permute-start | bytes 196616 | tf_op jit(solution)/shard_map/ppermute | solution.py:84
  (42 other events, 223.4 us)

commit v13 on v11

--- a/solution.py
+++ b/solution.py
@@ -26,6 +26,14 @@
     while width < ranks:
         rounds.append([s for s in (width, 2 * width) if s < ranks])
         width *= 3
+    return rounds
+
+
+def doubling_shifts(ranks):
+    rounds, width = [], 1
+    while width < ranks:
+        rounds.append([width])
+        width *= 2
     return rounds
 
 
@@ -52,7 +60,7 @@
 def backward_scan(total, state, axis, ranks):
     win_a, win_c = total, state
     excl_a, excl_c = jnp.zeros_like(total), jnp.zeros_like(state)
-    rounds = radix_shifts(ranks)
+    rounds = doubling_shifts(ranks)
     for step, shifts in enumerate(rounds):
         payload = pack(win_a, win_c)
         got = [

time: 110 us -> 109 us (level)
  waiting for transfers between devices: 35.1 us -> 38.3 us
  starting transfers between devices: 42.5 us -> 40.9 us
    ppermute x4 -> x3, waiting for transfers between devices: 12.5 us -> 15.6 us  [backward_scan(): lax.ppermute(payload, axis, [(i + s, i) for i in range(ranks - s)])]
    ppermute x4 -> x3, starting transfers between devices: 5.92 us -> 4.5 us  [backward_scan(): lax.ppermute(payload, axis, [(i + s, i) for i in range(ranks - s)])]
    unnamed x51 -> x49, local copies, waits for them, and re-layouts: 7.27 us -> 6.27 us
  transfers between devices with their start and end apart: 21 -> 20, of which waited for: 17 -> 16; matrix products, arithmetic and copies ran while one was open for 9% -> 9% of each run, Pallas kernels for 0% -> 0%
where the time goes in v13:
time: 109 us; the launch traced here: 108 us
  starting transfers between devices  40.9 us (38%)
  waiting for transfers between devices  38.3 us (35%)
  matrix products  13.8 us (13%)
  local copies, waits for them, and re-layouts  11.3 us (10%)
  other arithmetic  2.3 us (2%)
  between operations  1.25 us (1%)
    ppermute x4, starting transfers between devices, forward_scan(): lax.ppermute(payload, axis, [(i, i + s) for i in range(ranks - s)])  19.1 us
    ppermute x3, waiting for transfers between devices, backward_scan(): lax.ppermute(payload, axis, [(i + s, i) for i in range(ranks - s)])  15.6 us
    ppermute x12, waiting for transfers between devices, exchange(): got.append(lax.ppermute(send, axis, pairs))  13.4 us
    ppermute x12, starting transfers between devices, exchange(): got.append(lax.ppermute(send, axis, pairs))  12.9 us
    unnamed x49, local copies, waits for them, and re-layouts  6.27 us
    all_to_all x1, waiting for transfers between devices, head_sum(): gathered = lax.all_to_all(copies, 'head', 0, 0, tiled=True)  5.44 us
    ppermute x3, starting transfers between devices, backward_scan(): lax.ppermute(payload, axis, [(i + s, i) for i in range(ranks - s)])  4.5 us
    all_to_all x1, starting transfers between devices, head_sum(): gathered = lax.all_to_all(copies, 'head', 0, 0, tiled=True)  4.47 us
  transfers between devices with their start and end apart: 20, of which 16 were waited for; matrix products, arithmetic and copies ran while one was open for 9% of the time, Pallas kernels for 0%

profile of v13, /device:TPU:32, one launch (start us, length us, event | category | flops | bytes accessed | tf_op | source)
XLA Modules:
  0.0 107.9 jit_solution(15163594272890123427)
XLA Ops:
  4.2 2.0 %multiply_reduce_fusion.7 = (f32[4,128,128]{2,1,0:T(8,128)S(1)}, f32[4,128,128]{2,1,0:T(8,128)}, f32[4,128,128]{2,1,0:T(8,128)}, f32[4,128,128]{2,1,0:T(8,128)}, f32[4,128,128]{2,1,0:T(8,128)}) fusion(f32[4,4]{1,0:T(4,128)S(1)} %subtract_exponential_fusion.1, f32[4,4]{1,0:T(4,128)S(1)} %get-tuple-element.90, f32[4,4]{1,0:T(4,128)S(1)} %get-tuple-element.91, ...), kind=kOutput, calls=%fused_computation.36 | convolution fusion | flops 70189056 | bytes 2367808 | tf_op jit(solution)/shard_map/njhd,njhe->nhde/dot_general | solution.py:181
  6.3 2.8 %collective-permute-start = (f32[129,128]{1,0:T(8,128)S(1)}, f32[129,128]{1,0:T(8,128)S(1)}, u32[]{:S(2)}, u32[]{:S(2)}) collective-permute-start(f32[129,128]{1,0:T(8,128)S(1)} %get-tuple-element.49), channel_id=1, source_target_pairs={{0,24},{8,0},{16,8},{24,16},{1,25},{9,1},{17,9},{25,17},{2,26},{10... | collective-permute-start | bytes 198152 | tf_op jit(solution)/shard_map/ppermute | solution.py:86
  11.4 3.6 %collective-permute-done.1 = f32[129,128]{1,0:T(8,128)S(1)} collective-permute-done((f32[129,128]{1,0:T(8,128)S(1)}, f32[129,128]{1,0:T(8,128)S(1)}, u32[]{:S(2)}, u32[]{:S(2)}) %collective-permute-start.1) | collective-permute-done | bytes 66080 | tf_op jit(solution)/shard_map/ppermute | solution.py:86
  15.9 3.8 %collective-permute-start.3 = (f32[1,129,128]{2,1,0:T(8,128)S(1)}, f32[1,129,128]{2,1,0:T(8,128)S(1)}, u32[]{:S(2)}, u32[]{:S(2)}) collective-permute-start(f32[1,129,128]{2,1,0:T(8,128)S(1)} %pad_maximum_fusion.4), channel_id=1, source_target_pairs={{0,32},{32,64},{64,96},{96,128},{128,160},{160,192},{192,224},{1,3... | collective-permute-start | bytes 198152 | tf_op jit(solution)/shard_map/ppermute | solution.py:47
  19.7 6.4 %collective-permute-start.4 = (f32[1,129,128]{2,1,0:T(8,128)S(1)}, f32[1,129,128]{2,1,0:T(8,128)S(1)}, u32[]{:S(2)}, u32[]{:S(2)}) collective-permute-start(f32[1,129,128]{2,1,0:T(8,128)S(1)} %pad_maximum_fusion.4), channel_id=1, source_target_pairs={{0,64},{32,96},{64,128},{96,160},{128,192},{160,224},{1,65},{33,97... | collective-permute-start | bytes 198152 | tf_op jit(solution)/shard_map/ppermute | solution.py:47
  26.2 1.9 %collective-permute-done.4 = f32[1,129,128]{2,1,0:T(8,128)S(1)} collective-permute-done((f32[1,129,128]{2,1,0:T(8,128)S(1)}, f32[1,129,128]{2,1,0:T(8,128)S(1)}, u32[]{:S(2)}, u32[]{:S(2)}) %collective-permute-start.4) | collective-permute-done | bytes 66080 | tf_op jit(solution)/shard_map/ppermute | solution.py:47
  28.1 7.6 %collective-permute-start.5 = (f32[1,129,128]{2,1,0:T(8,128)S(1)}, f32[1,129,128]{2,1,0:T(8,128)S(1)}, u32[]{:S(2)}, u32[]{:S(2)}) collective-permute-start(f32[1,129,128]{2,1,0:T(8,128)S(1)} %pad_maximum_fusion.5), channel_id=1, source_target_pairs={{0,96},{32,128},{64,160},{96,192},{128,224},{1,97},{33,129},{65,16... | collective-permute-start | bytes 198152 | tf_op jit(solution)/shard_map/ppermute | solution.py:47
  36.3 1.3 %collective-permute-start.6 = (f32[1,129,128]{2,1,0:T(8,128)S(1)}, f32[1,129,128]{2,1,0:T(8,128)S(1)}, u32[]{:S(2)}, u32[]{:S(2)}) collective-permute-start(f32[1,129,128]{2,1,0:T(8,128)S(1)} %pad_maximum_fusion.5), channel_id=1, source_target_pairs={{0,192},{32,224},{1,193},{33,225},{2,194},{34,226},{3,195},{35,227... | collective-permute-start | bytes 198152 | tf_op jit(solution)/shard_map/ppermute | solution.py:47
  37.7 1.9 %collective-permute-done.6 = f32[1,129,128]{2,1,0:T(8,128)S(1)} collective-permute-done((f32[1,129,128]{2,1,0:T(8,128)S(1)}, f32[1,129,128]{2,1,0:T(8,128)S(1)}, u32[]{:S(2)}, u32[]{:S(2)}) %collective-permute-start.6) | collective-permute-done | bytes 66080 | tf_op jit(solution)/shard_map/ppermute | solution.py:47
  43.7 1.5 %convolution_bitcast_fusion.7 = f32[4,128,4,128]{1,3,2,0:T(8,128)} fusion(bf16[4,4,128,128]{3,2,1,0:T(8,128)(2,1)S(1)} %fusion.11, bf16[4,128,4,128]{3,2,1,0:T(4,128)(2,1)S(1)} %reshape.472), kind=kOutput, calls=%fused_computation.16 | convolution fusion | flops 67108864 | bytes 2097152 | tf_op jit(solution)/shard_map/nhij,njhd->nihd/dot_general | solution.py:176
  46.0 1.7 %collective-permute-done.8 = f32[128,128]{1,0:T(8,128)} collective-permute-done((f32[128,128]{1,0:T(8,128)}, f32[128,128]{1,0:T(8,128)}, u32[]{:S(2)}, u32[]{:S(2)}) %collective-permute-start.8) | collective-permute-done | bytes 65568 | tf_op jit(solution)/shard_map/ppermute | solution.py:86
  49.4 1.8 %multiply_reduce_fusion.6 = (f32[4,128]{1,0:T(4,128)S(1)}, f32[4,128]{1,0:T(4,128)S(1)}, f32[4,128,4,128]{1,3,2,0:T(8,128)S(1)}) fusion(f32[4,128,4,128]{1,3,2,0:T(8,128)S(1)} %copy.114, f32[4,128,4,128]{1,3,2,0:T(8,128)S(1)} %copy-done, bf16[4,128,4,128]{1,3,2,0:T(8,128)(2,1)S(1)} %copy.125, f32[1,4,128,128]{3,2,1,0:T(8,128)} %bitcast.297, ...), kind=kOutput, calls=%fused_computation.35 | convolution fusion | flops 70253568 | bytes 4993088 | tf_op jit(solution)/shard_map/nihd,nhde->nihe/dot_general | solution.py:193
  51.8 4.5 %all-to-all-start = ((f32[8,2,4,128]{3,2,1,0:T(4,128)}), f32[8,2,4,128]{3,2,1,0:T(4,128)S(1)}, u32[]{:S(2)}, u32[]{:S(2)}) async-start(f32[8,2,4,128]{3,2,1,0:T(4,128)} %broadcast_in_dim.5), calls=%async_computation | async-start | bytes 65536 | tf_op jit(solution)/shard_map/all_to_all | solution.py:139
  56.2 5.4 %all-to-all-done = f32[8,2,4,128]{3,2,1,0:T(4,128)S(1)} async-done(((f32[8,2,4,128]{3,2,1,0:T(4,128)}), f32[8,2,4,128]{3,2,1,0:T(4,128)S(1)}, u32[]{:S(2)}, u32[]{:S(2)}) %all-to-all-start) | async-done | bytes 32800 | tf_op jit(solution)/shard_map/all_to_all | solution.py:139
  61.9 1.7 %multiply_reduce_fusion = (f32[4,128,128]{2,1,0:T(8,128)S(1)}, f32[4,128,128]{2,1,0:T(8,128)}, f32[4,128,128]{2,1,0:T(8,128)}, f32[4,128,128]{2,1,0:T(8,128)}, f32[4,128,128]{2,1,0:T(8,128)}) fusion(f32[4,4]{1,0:T(4,128)S(1)} %get-tuple-element.23, f32[4,4]{1,0:T(4,128)S(1)} %get-tuple-element.86, f32[4,4]{1,0:T(4,128)S(1)} %get-tuple-element.87, ...), kind=kOutput, calls=%fused_computation.27 | convolution fusion | flops 70189056 | bytes 2367808 | tf_op jit(solution)/shard_map/nihd,nihe->nhde/dot_general | solution.py:227
  63.6 2.0 %collective-permute-start.10 = (f32[129,128]{1,0:T(8,128)S(1)}, f32[129,128]{1,0:T(8,128)S(1)}, u32[]{:S(2)}, u32[]{:S(2)}) collective-permute-start(f32[129,128]{1,0:T(8,128)S(1)} %get-tuple-element.47), channel_id=1, source_target_pairs={{0,24},{8,0},{16,8},{24,16},{1,25},{9,1},{17,9},{25,17},{2,26},{10... | collective-permute-start | bytes 198152 | tf_op jit(solution)/shard_map/ppermute | solution.py:86
  67.2 1.3 %collective-permute-done.10 = f32[129,128]{1,0:T(8,128)S(1)} collective-permute-done((f32[129,128]{1,0:T(8,128)S(1)}, f32[129,128]{1,0:T(8,128)S(1)}, u32[]{:S(2)}, u32[]{:S(2)}) %collective-permute-start.10) | collective-permute-done | bytes 66080 | tf_op jit(solution)/shard_map/ppermute | solution.py:86
  68.6 2.9 %collective-permute-done.11 = f32[129,128]{1,0:T(8,128)S(1)} collective-permute-done((f32[129,128]{1,0:T(8,128)S(1)}, f32[129,128]{1,0:T(8,128)S(1)}, u32[]{:S(2)}, u32[]{:S(2)}) %collective-permute-start.11) | collective-permute-done | bytes 66080 | tf_op jit(solution)/shard_map/ppermute | solution.py:86
  72.4 1.9 %collective-permute-start.13 = (f32[1,129,128]{2,1,0:T(8,128)S(1)}, f32[1,129,128]{2,1,0:T(8,128)S(1)}, u32[]{:S(2)}, u32[]{:S(2)}) collective-permute-start(f32[1,129,128]{2,1,0:T(8,128)S(1)} %pad_maximum_fusion.6), channel_id=1, source_target_pairs={{32,0},{64,32},{96,64},{128,96},{160,128},{192,160},{224,192},{33,... | collective-permute-start | bytes 198152 | tf_op jit(solution)/shard_map/ppermute | solution.py:67
  74.9 3.7 %collective-permute-done.13 = f32[1,129,128]{2,1,0:T(8,128)S(1)} collective-permute-done((f32[1,129,128]{2,1,0:T(8,128)S(1)}, f32[1,129,128]{2,1,0:T(8,128)S(1)}, u32[]{:S(2)}, u32[]{:S(2)}) %collective-permute-start.13) | collective-permute-done | bytes 66080 | tf_op jit(solution)/shard_map/ppermute | solution.py:67
  81.1 4.6 %collective-permute-done.14 = f32[1,129,128]{2,1,0:T(8,128)S(1)} collective-permute-done((f32[1,129,128]{2,1,0:T(8,128)S(1)}, f32[1,129,128]{2,1,0:T(8,128)S(1)}, u32[]{:S(2)}, u32[]{:S(2)}) %collective-permute-start.14) | collective-permute-done | bytes 66080 | tf_op jit(solution)/shard_map/ppermute | solution.py:67
  87.1 1.5 %convolution_bitcast_fusion.3 = f32[4,128,4,128]{3,1,2,0:T(8,128)} fusion(bf16[4,4,128,128]{3,2,1,0:T(8,128)(2,1)S(1)} %fusion.12, bf16[4,128,4,128]{1,3,2,0:T(8,128)(2,1)S(1)} %copy.125), kind=kOutput, calls=%fused_computation.7 | convolution fusion | flops 67108864 | bytes 2097152 | tf_op jit(solution)/shard_map/nhij,nihd->njhd/dot_general | solution.py:218
  88.6 7.3 %collective-permute-done.15 = f32[1,129,128]{2,1,0:T(8,128)S(1)} collective-permute-done((f32[1,129,128]{2,1,0:T(8,128)S(1)}, f32[1,129,128]{2,1,0:T(8,128)S(1)}, u32[]{:S(2)}, u32[]{:S(2)}) %collective-permute-start.15) | collective-permute-done | bytes 66080 | tf_op jit(solution)/shard_map/ppermute | solution.py:67
  98.8 1.5 %convolution_bitcast_fusion.1 = f32[4,128,4,128]{3,1,2,0:T(8,128)} fusion(bf16[4,128,4,128]{1,3,2,0:T(8,128)(2,1)S(1)} %multiply_convert_fusion.1, bf16[4,4,128,128]{3,2,1,0:T(8,128)(2,1)S(1)} %copy-done.4), kind=kOutput, calls=%fused_computation.3 | convolution fusion | flops 67108864 | bytes 2097152 | tf_op jit(solution)/shard_map/nhij,nihe->njhe/dot_general | solution.py:221
  (145 shorter events, 32.0 us)
Async XLA Ops:
  4.0 39.7 %copy-start.1 = (bf16[4,128,4,128]{3,2,1,0:T(4,128)(2,1)}, bf16[4,128,4,128]{3,2,1,0:T(4,128)(2,1)S(1)}, u32[]{:S(2)}) copy-start(bf16[4,128,4,128]{3,2,1,0:T(4,128)(2,1)S(1)} %reshape.472) | copy-start | bytes 1572868
  6.3 5.2 %collective-permute-start = (f32[129,128]{1,0:T(8,128)S(1)}, f32[129,128]{1,0:T(8,128)S(1)}, u32[]{:S(2)}, u32[]{:S(2)}) collective-permute-start(f32[129,128]{1,0:T(8,128)S(1)} %get-tuple-element.49), channel_id=1, source_target_pairs={{0,24},{8,0},{16,8},{24,16},{1,25},{9,1},{17,9},{25,17},{2,26},{10... | collective-permute-start | bytes 198152 | tf_op jit(solution)/shard_map/ppermute | solution.py:86
  9.1 5.9 %collective-permute-start.1 = (f32[129,128]{1,0:T(8,128)S(1)}, f32[129,128]{1,0:T(8,128)S(1)}, u32[]{:S(2)}, u32[]{:S(2)}) collective-permute-start(f32[129,128]{1,0:T(8,128)S(1)} %get-tuple-element.50), channel_id=1, source_target_pairs={{0,16},{8,24},{16,0},{24,8},{1,17},{9,25},{17,1},{25,9},{2,18},{10... | collective-permute-start | bytes 198152 | tf_op jit(solution)/shard_map/ppermute | solution.py:86
  9.9 5.8 %collective-permute-start.2 = (f32[129,128]{1,0:T(8,128)S(1)}, f32[129,128]{1,0:T(8,128)S(1)}, u32[]{:S(2)}, u32[]{:S(2)}) collective-permute-start(f32[129,128]{1,0:T(8,128)S(1)} %get-tuple-element.48), channel_id=1, source_target_pairs={{0,8},{8,16},{16,24},{24,0},{1,9},{9,17},{17,25},{25,1},{2,10},{10... | collective-permute-start | bytes 198152 | tf_op jit(solution)/shard_map/ppermute | solution.py:86
  15.9 10.3 %collective-permute-start.3 = (f32[1,129,128]{2,1,0:T(8,128)S(1)}, f32[1,129,128]{2,1,0:T(8,128)S(1)}, u32[]{:S(2)}, u32[]{:S(2)}) collective-permute-start(f32[1,129,128]{2,1,0:T(8,128)S(1)} %pad_maximum_fusion.4), channel_id=1, source_target_pairs={{0,32},{32,64},{64,96},{96,128},{128,160},{160,192},{192,224},{1,3... | collective-permute-start | bytes 198152 | tf_op jit(solution)/shard_map/ppermute | solution.py:47
  19.7 8.3 %collective-permute-start.4 = (f32[1,129,128]{2,1,0:T(8,128)S(1)}, f32[1,129,128]{2,1,0:T(8,128)S(1)}, u32[]{:S(2)}, u32[]{:S(2)}) collective-permute-start(f32[1,129,128]{2,1,0:T(8,128)S(1)} %pad_maximum_fusion.4), channel_id=1, source_target_pairs={{0,64},{32,96},{64,128},{96,160},{128,192},{160,224},{1,65},{33,97... | collective-permute-start | bytes 198152 | tf_op jit(solution)/shard_map/ppermute | solution.py:47
  26.2 9.5 %copy-start.17 = (f32[128,128]{1,0:T(8,128)}, f32[128,128]{1,0:T(8,128)S(1)}, u32[]{:S(2)}) copy-start(f32[128,128]{1,0:T(8,128)S(1)} %fusion.70) | copy-start | bytes 196612
  28.1 9.5 %collective-permute-start.5 = (f32[1,129,128]{2,1,0:T(8,128)S(1)}, f32[1,129,128]{2,1,0:T(8,128)S(1)}, u32[]{:S(2)}, u32[]{:S(2)}) collective-permute-start(f32[1,129,128]{2,1,0:T(8,128)S(1)} %pad_maximum_fusion.5), channel_id=1, source_target_pairs={{0,96},{32,128},{64,160},{96,192},{128,224},{1,97},{33,129},{65,16... | collective-permute-start | bytes 198152 | tf_op jit(solution)/shard_map/ppermute | solution.py:47
  36.3 7.4 %copy-start.3 = (bf16[4,4,128,128]{3,2,1,0:T(8,128)(2,1)}, bf16[4,4,128,128]{3,2,1,0:T(8,128)(2,1)S(1)}, u32[]{:S(2)}) copy-start(bf16[4,4,128,128]{3,2,1,0:T(8,128)(2,1)S(1)} %fusion.11) | copy-start | bytes 1572868
  36.3 3.2 %collective-permute-start.6 = (f32[1,129,128]{2,1,0:T(8,128)S(1)}, f32[1,129,128]{2,1,0:T(8,128)S(1)}, u32[]{:S(2)}, u32[]{:S(2)}) collective-permute-start(f32[1,129,128]{2,1,0:T(8,128)S(1)} %pad_maximum_fusion.5), channel_id=1, source_target_pairs={{0,192},{32,224},{1,193},{33,225},{2,194},{34,226},{3,195},{35,227... | collective-permute-start | bytes 198152 | tf_op jit(solution)/shard_map/ppermute | solution.py:47
  41.0 5.0 %collective-permute-start.7 = (f32[128,128]{1,0:T(8,128)}, f32[128,128]{1,0:T(8,128)S(1)}, u32[]{:S(2)}, u32[]{:S(2)}) collective-permute-start(f32[128,128]{1,0:T(8,128)} %get-tuple-element.56), channel_id=1, source_target_pairs={{0,24},{8,0},{16,8},{24,16},{1,25},{9,1},{17,9},{25,17},{2,26},{10... | collective-permute-start | bytes 196616 | tf_op jit(solution)/shard_map/ppermute | solution.py:86
  41.6 6.1 %collective-permute-start.8 = (f32[128,128]{1,0:T(8,128)}, f32[128,128]{1,0:T(8,128)}, u32[]{:S(2)}, u32[]{:S(2)}) collective-permute-start(f32[128,128]{1,0:T(8,128)} %get-tuple-element.55), channel_id=1, source_target_pairs={{0,16},{8,24},{16,0},{24,8},{1,17},{9,25},{17,1},{25,9},{2,18},{10... | collective-permute-start | bytes 196616 | tf_op jit(solution)/shard_map/ppermute | solution.py:86
  42.5 5.9 %collective-permute-start.9 = (f32[128,128]{1,0:T(8,128)}, f32[128,128]{1,0:T(8,128)}, u32[]{:S(2)}, u32[]{:S(2)}) collective-permute-start(f32[128,128]{1,0:T(8,128)} %get-tuple-element.54), channel_id=1, source_target_pairs={{0,8},{8,16},{16,24},{24,0},{1,9},{9,17},{17,25},{25,1},{2,10},{10... | collective-permute-start | bytes 196616 | tf_op jit(solution)/shard_map/ppermute | solution.py:86
  51.8 9.9 %all-to-all-start = ((f32[8,2,4,128]{3,2,1,0:T(4,128)}), f32[8,2,4,128]{3,2,1,0:T(4,128)S(1)}, u32[]{:S(2)}, u32[]{:S(2)}) async-start(f32[8,2,4,128]{3,2,1,0:T(4,128)} %broadcast_in_dim.5), calls=%async_computation | async-start | bytes 65536 | tf_op jit(solution)/shard_map/all_to_all | solution.py:139
  63.6 4.9 %collective-permute-start.10 = (f32[129,128]{1,0:T(8,128)S(1)}, f32[129,128]{1,0:T(8,128)S(1)}, u32[]{:S(2)}, u32[]{:S(2)}) collective-permute-start(f32[129,128]{1,0:T(8,128)S(1)} %get-tuple-element.47), channel_id=1, source_target_pairs={{0,24},{8,0},{16,8},{24,16},{1,25},{9,1},{17,9},{25,17},{2,26},{10... | collective-permute-start | bytes 198152 | tf_op jit(solution)/shard_map/ppermute | solution.py:86
  65.6 5.8 %collective-permute-start.11 = (f32[129,128]{1,0:T(8,128)S(1)}, f32[129,128]{1,0:T(8,128)S(1)}, u32[]{:S(2)}, u32[]{:S(2)}) collective-permute-start(f32[129,128]{1,0:T(8,128)S(1)} %get-tuple-element.46), channel_id=1, source_target_pairs={{0,16},{8,24},{16,0},{24,8},{1,17},{9,25},{17,1},{25,9},{2,18},{10... | collective-permute-start | bytes 198152 | tf_op jit(solution)/shard_map/ppermute | solution.py:86
  66.5 5.7 %collective-permute-start.12 = (f32[129,128]{1,0:T(8,128)S(1)}, f32[129,128]{1,0:T(8,128)S(1)}, u32[]{:S(2)}, u32[]{:S(2)}) collective-permute-start(f32[129,128]{1,0:T(8,128)S(1)} %get-tuple-element.45), channel_id=1, source_target_pairs={{0,8},{8,16},{16,24},{24,0},{1,9},{9,17},{17,25},{25,1},{2,10},{10... | collective-permute-start | bytes 198152 | tf_op jit(solution)/shard_map/ppermute | solution.py:86
  72.4 6.2 %collective-permute-start.13 = (f32[1,129,128]{2,1,0:T(8,128)S(1)}, f32[1,129,128]{2,1,0:T(8,128)S(1)}, u32[]{:S(2)}, u32[]{:S(2)}) collective-permute-start(f32[1,129,128]{2,1,0:T(8,128)S(1)} %pad_maximum_fusion.6), channel_id=1, source_target_pairs={{32,0},{64,32},{96,64},{128,96},{160,128},{192,160},{224,192},{33,... | collective-permute-start | bytes 198152 | tf_op jit(solution)/shard_map/ppermute | solution.py:67
  74.3 5.6 %copy-start.14 = (f32[4,128,128]{2,1,0:T(8,128)S(1)}, f32[4,128,128]{2,1,0:T(8,128)}, u32[]{:S(2)}) copy-start(f32[4,128,128]{2,1,0:T(8,128)} %get-tuple-element.12) | copy-start | bytes 786436
  78.6 7.1 %collective-permute-start.14 = (f32[1,129,128]{2,1,0:T(8,128)S(1)}, f32[1,129,128]{2,1,0:T(8,128)S(1)}, u32[]{:S(2)}, u32[]{:S(2)}) collective-permute-start(f32[1,129,128]{2,1,0:T(8,128)S(1)} %pad_maximum_fusion.7), channel_id=1, source_target_pairs={{64,0},{96,32},{128,64},{160,96},{192,128},{224,160},{65,1},{97,33... | collective-permute-start | bytes 198152 | tf_op jit(solution)/shard_map/ppermute | solution.py:67
  85.8 10.1 %collective-permute-start.15 = (f32[1,129,128]{2,1,0:T(8,128)S(1)}, f32[1,129,128]{2,1,0:T(8,128)S(1)}, u32[]{:S(2)}, u32[]{:S(2)}) collective-permute-start(f32[1,129,128]{2,1,0:T(8,128)S(1)} %pad_maximum_fusion.8), channel_id=1, source_target_pairs={{128,0},{160,32},{192,64},{224,96},{129,1},{161,33},{193,65},{225,... | collective-permute-start | bytes 198152 | tf_op jit(solution)/shard_map/ppermute | solution.py:67
  96.0 5.5 %collective-permute-start.16 = (f32[128,128]{1,0:T(8,128)S(1)}, f32[128,128]{1,0:T(8,128)S(1)}, u32[]{:S(2)}, u32[]{:S(2)}) collective-permute-start(f32[128,128]{1,0:T(8,128)S(1)} %get-tuple-element.53), channel_id=1, source_target_pairs={{0,24},{8,0},{16,8},{24,16},{1,25},{9,1},{17,9},{25,17},{2,26},{10... | collective-permute-start | bytes 196616 | tf_op jit(solution)/shard_map/ppermute | solution.py:86
  96.6 5.8 %collective-permute-start.17 = (f32[128,128]{1,0:T(8,128)S(1)}, f32[128,128]{1,0:T(8,128)S(1)}, u32[]{:S(2)}, u32[]{:S(2)}) collective-permute-start(f32[128,128]{1,0:T(8,128)S(1)} %get-tuple-element.52), channel_id=1, source_target_pairs={{0,16},{8,24},{16,0},{24,8},{1,17},{9,25},{17,1},{25,9},{2,18},{10... | collective-permute-start | bytes 196616 | tf_op jit(solution)/shard_map/ppermute | solution.py:86
  97.6 5.6 %collective-permute-start.18 = (f32[128,128]{1,0:T(8,128)S(1)}, f32[128,128]{1,0:T(8,128)S(1)}, u32[]{:S(2)}, u32[]{:S(2)}) collective-permute-start(f32[128,128]{1,0:T(8,128)S(1)} %get-tuple-element.51), channel_id=1, source_target_pairs={{0,8},{8,16},{16,24},{24,0},{1,9},{9,17},{17,25},{25,1},{2,10},{10... | collective-permute-start | bytes 196616 | tf_op jit(solution)/shard_map/ppermute | solution.py:86
  (19 other events, 51.2 us)

commit v14 on v13

--- a/solution.py
+++ b/solution.py
@@ -40,7 +40,7 @@
 def forward_scan(total, state, axis, ranks):
     win_a, win_b = total, state
     excl_a, excl_b = jnp.zeros_like(total), jnp.zeros_like(state)
-    rounds = radix_shifts(ranks)
+    rounds = doubling_shifts(ranks)
     for step, shifts in enumerate(rounds):
         payload = pack(win_a, win_b)
         got = [

time: 109 us -> 118 us (1.083)
  waiting for transfers between devices: 38.3 us -> 41.3 us
  local copies, waits for them, and re-layouts: 11.3 us -> 13.9 us
  other arithmetic: 2.3 us -> 4.62 us
  starting transfers between devices: 40.9 us -> 42.2 us
    unnamed x49 -> x79, local copies, waits for them, and re-layouts: 6.27 us -> 8.84 us
    ppermute x4 -> x3, waiting for transfers between devices: 3.78 us -> 5.87 us  [forward_scan(): lax.ppermute(payload, axis, [(i, i + s) for i in range(ranks - s)])]
    ppermute x3, starting transfers between devices: 4.5 us -> 6.04 us  [backward_scan(): lax.ppermute(payload, axis, [(i + s, i) for i in range(ranks - s)])]
    ppermute x4 -> x3, starting transfers between devices: 19.1 us -> 18.4 us  [forward_scan(): lax.ppermute(payload, axis, [(i, i + s) for i in range(ranks - s)])]
  transfers between devices with their start and end apart: 20 -> 19, of which waited for: 16 -> 17; matrix products, arithmetic and copies ran while one was open for 9% -> 8% of each run, Pallas kernels for 0% -> 0%
where the time goes in v14:
time: 118 us; the launch traced here: 117 us
  starting transfers between devices  42.2 us (36%)
  waiting for transfers between devices  41.3 us (35%)
  local copies, waits for them, and re-layouts  13.9 us (12%)
  matrix products  13.7 us (12%)
  other arithmetic  4.62 us (4%)
  between operations  1.35 us (1%)
    ppermute x3, starting transfers between devices, forward_scan(): lax.ppermute(payload, axis, [(i, i + s) for i in range(ranks - s)])  18.4 us
    ppermute x3, waiting for transfers between devices, backward_scan(): lax.ppermute(payload, axis, [(i + s, i) for i in range(ranks - s)])  16.1 us
    ppermute x12, waiting for transfers between devices, exchange(): got.append(lax.ppermute(send, axis, pairs))  13.9 us
    ppermute x12, starting transfers between devices, exchange(): got.append(lax.ppermute(send, axis, pairs))  13.1 us
    unnamed x79, local copies, waits for them, and re-layouts  8.84 us
    ppermute x3, starting transfers between devices, backward_scan(): lax.ppermute(payload, axis, [(i + s, i) for i in range(ranks - s)])  6.04 us
    ppermute x3, waiting for transfers between devices, forward_scan(): lax.ppermute(payload, axis, [(i, i + s) for i in range(ranks - s)])  5.87 us
    all_to_all x1, waiting for transfers between devices, head_sum(): gathered = lax.all_to_all(copies, 'head', 0, 0, tiled=True)  5.43 us
  transfers between devices with their start and end apart: 19, of which 17 were waited for; matrix products, arithmetic and copies ran while one was open for 8% of the time, Pallas kernels for 0%

profile of v14, /device:TPU:32, one launch (start us, length us, event | category | flops | bytes accessed | tf_op | source)
XLA Modules:
  0.0 117.0 jit_solution(17812951656318225404)
XLA Ops:
  5.4 1.9 %multiply_reduce_fusion.7 = (f32[4,128,128]{2,1,0:T(8,128)S(1)}, f32[4,128,128]{2,1,0:T(8,128)}, f32[4,128,128]{2,1,0:T(8,128)}, f32[4,128,128]{2,1,0:T(8,128)}, f32[4,128,128]{2,1,0:T(8,128)}) fusion(f32[4,4]{1,0:T(4,128)S(1)} %subtract_exponential_fusion.1, f32[4,4]{1,0:T(4,128)S(1)} %get-tuple-element.90, f32[4,4]{1,0:T(4,128)S(1)} %get-tuple-element.91, ...), kind=kOutput, calls=%fused_computation.36 | convolution fusion | flops 70189056 | bytes 2367808 | tf_op jit(solution)/shard_map/njhd,njhe->nhde/dot_general | solution.py:181
  7.5 2.8 %collective-permute-start = (f32[129,128]{1,0:T(8,128)S(1)}, f32[129,128]{1,0:T(8,128)S(1)}, u32[]{:S(2)}, u32[]{:S(2)}) collective-permute-start(f32[129,128]{1,0:T(8,128)S(1)} %get-tuple-element.51), channel_id=1, source_target_pairs={{0,24},{8,0},{16,8},{24,16},{1,25},{9,1},{17,9},{25,17},{2,26},{10... | collective-permute-start | bytes 198152 | tf_op jit(solution)/shard_map/ppermute | solution.py:86
  12.6 3.6 %collective-permute-done.1 = f32[129,128]{1,0:T(8,128)S(1)} collective-permute-done((f32[129,128]{1,0:T(8,128)S(1)}, f32[129,128]{1,0:T(8,128)S(1)}, u32[]{:S(2)}, u32[]{:S(2)}) %collective-permute-start.1) | collective-permute-done | bytes 66080 | tf_op jit(solution)/shard_map/ppermute | solution.py:86
  18.3 3.8 %collective-permute-start.3 = (f32[1,129,128]{2,1,0:T(8,128)}, f32[1,129,128]{2,1,0:T(8,128)S(1)}, u32[]{:S(2)}, u32[]{:S(2)}) collective-permute-start(f32[1,129,128]{2,1,0:T(8,128)} %pad_maximum_fusion.4), channel_id=1, source_target_pairs={{0,32},{32,64},{64,96},{96,128},{128,160},{160,192},{192,224},{1,3... | collective-permute-start | bytes 198152 | tf_op jit(solution)/shard_map/ppermute | solution.py:47
  22.7 2.0 %collective-permute-done.3 = f32[1,129,128]{2,1,0:T(8,128)S(1)} collective-permute-done((f32[1,129,128]{2,1,0:T(8,128)}, f32[1,129,128]{2,1,0:T(8,128)S(1)}, u32[]{:S(2)}, u32[]{:S(2)}) %collective-permute-start.3) | collective-permute-done | bytes 66080 | tf_op jit(solution)/shard_map/ppermute | solution.py:47
  25.3 6.0 %collective-permute-start.4 = (f32[1,129,128]{2,1,0:T(8,128)S(1)}, f32[1,129,128]{2,1,0:T(8,128)S(1)}, u32[]{:S(2)}, u32[]{:S(2)}) collective-permute-start(f32[1,129,128]{2,1,0:T(8,128)S(1)} %pad_maximum_fusion.5), channel_id=1, source_target_pairs={{0,64},{32,96},{64,128},{96,160},{128,192},{160,224},{1,65},{33,97... | collective-permute-start | bytes 198152 | tf_op jit(solution)/shard_map/ppermute | solution.py:47
  31.4 1.9 %collective-permute-done.4 = f32[1,129,128]{2,1,0:T(8,128)S(1)} collective-permute-done((f32[1,129,128]{2,1,0:T(8,128)S(1)}, f32[1,129,128]{2,1,0:T(8,128)S(1)}, u32[]{:S(2)}, u32[]{:S(2)}) %collective-permute-start.4) | collective-permute-done | bytes 66080 | tf_op jit(solution)/shard_map/ppermute | solution.py:47
  33.4 8.5 %collective-permute-start.5 = (f32[1,129,128]{2,1,0:T(8,128)S(1)}, f32[1,129,128]{2,1,0:T(8,128)S(1)}, u32[]{:S(2)}, u32[]{:S(2)}) collective-permute-start(f32[1,129,128]{2,1,0:T(8,128)S(1)} %pad_maximum_fusion.6), channel_id=1, source_target_pairs={{0,128},{32,160},{64,192},{96,224},{1,129},{33,161},{65,193},{97,2... | collective-permute-start | bytes 198152 | tf_op jit(solution)/shard_map/ppermute | solution.py:47
  42.5 2.0 %collective-permute-done.5 = f32[1,129,128]{2,1,0:T(8,128)S(1)} collective-permute-done((f32[1,129,128]{2,1,0:T(8,128)S(1)}, f32[1,129,128]{2,1,0:T(8,128)S(1)}, u32[]{:S(2)}, u32[]{:S(2)}) %collective-permute-start.5) | collective-permute-done | bytes 66080 | tf_op jit(solution)/shard_map/ppermute | solution.py:47
  49.9 1.5 %convolution_bitcast_fusion.7 = f32[4,128,4,128]{1,3,2,0:T(8,128)} fusion(bf16[4,4,128,128]{3,2,1,0:T(8,128)(2,1)S(1)} %fusion.11, bf16[4,128,4,128]{3,2,1,0:T(4,128)(2,1)S(1)} %reshape.470), kind=kOutput, calls=%fused_computation.16 | convolution fusion | flops 67108864 | bytes 2097152 | tf_op jit(solution)/shard_map/nhij,njhd->nihd/dot_general | solution.py:176
  52.2 1.6 %collective-permute-done.7 = f32[128,128]{1,0:T(8,128)S(1)} collective-permute-done((f32[128,128]{1,0:T(8,128)}, f32[128,128]{1,0:T(8,128)S(1)}, u32[]{:S(2)}, u32[]{:S(2)}) %collective-permute-start.7) | collective-permute-done | bytes 65568 | tf_op jit(solution)/shard_map/ppermute | solution.py:86
  56.2 1.8 %multiply_reduce_fusion.6 = (f32[4,128]{1,0:T(4,128)S(1)}, f32[4,128]{1,0:T(4,128)S(1)}, f32[4,128,4,128]{1,3,2,0:T(8,128)S(1)}) fusion(f32[4,128,4,128]{1,3,2,0:T(8,128)S(1)} %copy.114, f32[4,128,4,128]{1,3,2,0:T(8,128)S(1)} %copy-done, bf16[4,128,4,128]{1,3,2,0:T(8,128)(2,1)S(1)} %copy.125, f32[1,4,128,128]{3,2,1,0:T(8,128)} %bitcast.295, ...), kind=kOutput, calls=%fused_computation.35 | convolution fusion | flops 70253568 | bytes 4993088 | tf_op jit(solution)/shard_map/nihd,nhde->nihe/dot_general | solution.py:193
  58.6 4.6 %all-to-all-start = ((f32[8,2,4,128]{3,2,1,0:T(4,128)}), f32[8,2,4,128]{3,2,1,0:T(4,128)S(1)}, u32[]{:S(2)}, u32[]{:S(2)}) async-start(f32[8,2,4,128]{3,2,1,0:T(4,128)} %broadcast_in_dim.5), calls=%async_computation | async-start | bytes 65536 | tf_op jit(solution)/shard_map/all_to_all | solution.py:139
  63.2 5.4 %all-to-all-done = f32[8,2,4,128]{3,2,1,0:T(4,128)S(1)} async-done(((f32[8,2,4,128]{3,2,1,0:T(4,128)}), f32[8,2,4,128]{3,2,1,0:T(4,128)S(1)}, u32[]{:S(2)}, u32[]{:S(2)}) %all-to-all-start) | async-done | bytes 32800 | tf_op jit(solution)/shard_map/all_to_all | solution.py:139
  68.9 1.7 %multiply_reduce_fusion = (f32[4,128,128]{2,1,0:T(8,128)S(1)}, f32[4,128,128]{2,1,0:T(8,128)}, f32[4,128,128]{2,1,0:T(8,128)}, f32[4,128,128]{2,1,0:T(8,128)}, f32[4,128,128]{2,1,0:T(8,128)}) fusion(f32[4,4]{1,0:T(4,128)S(1)} %copy-done.20, f32[4,4]{1,0:T(4,128)S(1)} %get-tuple-element.86, f32[4,4]{1,0:T(4,128)S(1)} %get-tuple-element.87, ...), kind=kOutput, calls=%fused_computation.27 | convolution fusion | flops 70189056 | bytes 2367808 | tf_op jit(solution)/shard_map/nihd,nihe->nhde/dot_general | solution.py:227
  70.6 2.0 %collective-permute-start.9 = (f32[129,128]{1,0:T(8,128)S(1)}, f32[129,128]{1,0:T(8,128)S(1)}, u32[]{:S(2)}, u32[]{:S(2)}) collective-permute-start(f32[129,128]{1,0:T(8,128)S(1)} %get-tuple-element.49), channel_id=1, source_target_pairs={{0,24},{8,0},{16,8},{24,16},{1,25},{9,1},{17,9},{25,17},{2,26},{10... | collective-permute-start | bytes 198152 | tf_op jit(solution)/shard_map/ppermute | solution.py:86
  74.2 1.3 %collective-permute-done.9 = f32[129,128]{1,0:T(8,128)S(1)} collective-permute-done((f32[129,128]{1,0:T(8,128)S(1)}, f32[129,128]{1,0:T(8,128)S(1)}, u32[]{:S(2)}, u32[]{:S(2)}) %collective-permute-start.9) | collective-permute-done | bytes 66080 | tf_op jit(solution)/shard_map/ppermute | solution.py:86
  75.5 2.9 %collective-permute-done.10 = f32[129,128]{1,0:T(8,128)S(1)} collective-permute-done((f32[129,128]{1,0:T(8,128)S(1)}, f32[129,128]{1,0:T(8,128)S(1)}, u32[]{:S(2)}, u32[]{:S(2)}) %collective-permute-start.10) | collective-permute-done | bytes 66080 | tf_op jit(solution)/shard_map/ppermute | solution.py:86
  79.3 3.5 %collective-permute-start.12 = (f32[1,129,128]{2,1,0:T(8,128)S(1)}, f32[1,129,128]{2,1,0:T(8,128)S(1)}, u32[]{:S(2)}, u32[]{:S(2)}) collective-permute-start(f32[1,129,128]{2,1,0:T(8,128)S(1)} %pad_maximum_fusion.7), channel_id=1, source_target_pairs={{32,0},{64,32},{96,64},{128,96},{160,128},{192,160},{224,192},{33,... | collective-permute-start | bytes 198152 | tf_op jit(solution)/shard_map/ppermute | solution.py:67
  83.3 2.2 %collective-permute-done.12 = f32[1,129,128]{2,1,0:T(8,128)S(1)} collective-permute-done((f32[1,129,128]{2,1,0:T(8,128)S(1)}, f32[1,129,128]{2,1,0:T(8,128)S(1)}, u32[]{:S(2)}, u32[]{:S(2)}) %collective-permute-start.12) | collective-permute-done | bytes 66080 | tf_op jit(solution)/shard_map/ppermute | solution.py:67
  88.1 6.6 %collective-permute-done.13 = f32[1,129,128]{2,1,0:T(8,128)S(1)} collective-permute-done((f32[1,129,128]{2,1,0:T(8,128)S(1)}, f32[1,129,128]{2,1,0:T(8,128)S(1)}, u32[]{:S(2)}, u32[]{:S(2)}) %collective-permute-start.13) | collective-permute-done | bytes 66080 | tf_op jit(solution)/shard_map/ppermute | solution.py:67
  96.0 1.5 %convolution_bitcast_fusion.3 = f32[4,128,4,128]{3,1,2,0:T(8,128)} fusion(bf16[4,4,128,128]{3,2,1,0:T(8,128)(2,1)S(1)} %fusion.12, bf16[4,128,4,128]{1,3,2,0:T(8,128)(2,1)S(1)} %copy.125), kind=kOutput, calls=%fused_computation.7 | convolution fusion | flops 67108864 | bytes 2097152 | tf_op jit(solution)/shard_map/nhij,nihd->njhd/dot_general | solution.py:218
  97.5 7.4 %collective-permute-done.14 = f32[1,129,128]{2,1,0:T(8,128)S(1)} collective-permute-done((f32[1,129,128]{2,1,0:T(8,128)S(1)}, f32[1,129,128]{2,1,0:T(8,128)S(1)}, u32[]{:S(2)}, u32[]{:S(2)}) %collective-permute-start.14) | collective-permute-done | bytes 66080 | tf_op jit(solution)/shard_map/ppermute | solution.py:67
  108.0 1.5 %convolution_bitcast_fusion.1 = f32[4,128,4,128]{3,1,2,0:T(8,128)} fusion(bf16[4,128,4,128]{1,3,2,0:T(8,128)(2,1)S(1)} %multiply_convert_fusion.1, bf16[4,4,128,128]{3,2,1,0:T(8,128)(2,1)S(1)} %copy-done.4), kind=kOutput, calls=%fused_computation.3 | convolution fusion | flops 67108864 | bytes 2097152 | tf_op jit(solution)/shard_map/nhij,nihe->njhe/dot_general | solution.py:221
  (175 shorter events, 37.6 us)
Async XLA Ops:
  4.0 45.9 %copy-start.1 = (bf16[4,128,4,128]{3,2,1,0:T(4,128)(2,1)}, bf16[4,128,4,128]{3,2,1,0:T(4,128)(2,1)S(1)}, u32[]{:S(2)}) copy-start(bf16[4,128,4,128]{3,2,1,0:T(4,128)(2,1)S(1)} %reshape.470) | copy-start | bytes 1572868
  7.5 5.2 %collective-permute-start = (f32[129,128]{1,0:T(8,128)S(1)}, f32[129,128]{1,0:T(8,128)S(1)}, u32[]{:S(2)}, u32[]{:S(2)}) collective-permute-start(f32[129,128]{1,0:T(8,128)S(1)} %get-tuple-element.51), channel_id=1, source_target_pairs={{0,24},{8,0},{16,8},{24,16},{1,25},{9,1},{17,9},{25,17},{2,26},{10... | collective-permute-start | bytes 198152 | tf_op jit(solution)/shard_map/ppermute | solution.py:86
  10.3 5.9 %collective-permute-start.1 = (f32[129,128]{1,0:T(8,128)S(1)}, f32[129,128]{1,0:T(8,128)S(1)}, u32[]{:S(2)}, u32[]{:S(2)}) collective-permute-start(f32[129,128]{1,0:T(8,128)S(1)} %get-tuple-element.52), channel_id=1, source_target_pairs={{0,16},{8,24},{16,0},{24,8},{1,17},{9,25},{17,1},{25,9},{2,18},{10... | collective-permute-start | bytes 198152 | tf_op jit(solution)/shard_map/ppermute | solution.py:86
  11.1 5.8 %collective-permute-start.2 = (f32[129,128]{1,0:T(8,128)S(1)}, f32[129,128]{1,0:T(8,128)S(1)}, u32[]{:S(2)}, u32[]{:S(2)}) collective-permute-start(f32[129,128]{1,0:T(8,128)S(1)} %get-tuple-element.50), channel_id=1, source_target_pairs={{0,8},{8,16},{16,24},{24,0},{1,9},{9,17},{17,25},{25,1},{2,10},{10... | collective-permute-start | bytes 198152 | tf_op jit(solution)/shard_map/ppermute | solution.py:86
  17.0 5.1 %copy-start.11 = (bf16[512,512]{1,0:T(8,128)(2,1)S(1)}, bf16[512,512]{1,0:T(8,128)(2,1)}, u32[]{:S(2)}) copy-start(bf16[512,512]{1,0:T(8,128)(2,1)} %param.5) | copy-start | bytes 1572868
  18.3 6.4 %collective-permute-start.3 = (f32[1,129,128]{2,1,0:T(8,128)}, f32[1,129,128]{2,1,0:T(8,128)S(1)}, u32[]{:S(2)}, u32[]{:S(2)}) collective-permute-start(f32[1,129,128]{2,1,0:T(8,128)} %pad_maximum_fusion.4), channel_id=1, source_target_pairs={{0,32},{32,64},{64,96},{96,128},{128,160},{160,192},{192,224},{1,3... | collective-permute-start | bytes 198152 | tf_op jit(solution)/shard_map/ppermute | solution.py:47
  22.7 19.2 %copy-start.24 = (f32[4,4,128]{2,1,0:T(4,128)}, f32[4,4,128]{2,1,0:T(4,128)S(1)}, u32[]{:S(2)}) copy-start(f32[4,4,128]{2,1,0:T(4,128)S(1)} %copy.103) | copy-start | bytes 24580
  25.3 8.0 %collective-permute-start.4 = (f32[1,129,128]{2,1,0:T(8,128)S(1)}, f32[1,129,128]{2,1,0:T(8,128)S(1)}, u32[]{:S(2)}, u32[]{:S(2)}) collective-permute-start(f32[1,129,128]{2,1,0:T(8,128)S(1)} %pad_maximum_fusion.5), channel_id=1, source_target_pairs={{0,64},{32,96},{64,128},{96,160},{128,192},{160,224},{1,65},{33,97... | collective-permute-start | bytes 198152 | tf_op jit(solution)/shard_map/ppermute | solution.py:47
  31.4 10.5 %copy-start.17 = (f32[128,128]{1,0:T(8,128)}, f32[128,128]{1,0:T(8,128)S(1)}, u32[]{:S(2)}) copy-start(f32[128,128]{1,0:T(8,128)S(1)} %fusion.69) | copy-start | bytes 196612
  33.4 11.1 %collective-permute-start.5 = (f32[1,129,128]{2,1,0:T(8,128)S(1)}, f32[1,129,128]{2,1,0:T(8,128)S(1)}, u32[]{:S(2)}, u32[]{:S(2)}) collective-permute-start(f32[1,129,128]{2,1,0:T(8,128)S(1)} %pad_maximum_fusion.6), channel_id=1, source_target_pairs={{0,128},{32,160},{64,192},{96,224},{1,129},{33,161},{65,193},{97,2... | collective-permute-start | bytes 198152 | tf_op jit(solution)/shard_map/ppermute | solution.py:47
  42.5 7.4 %copy-start.3 = (bf16[4,4,128,128]{3,2,1,0:T(8,128)(2,1)}, bf16[4,4,128,128]{3,2,1,0:T(8,128)(2,1)S(1)}, u32[]{:S(2)}) copy-start(bf16[4,4,128,128]{3,2,1,0:T(8,128)(2,1)S(1)} %fusion.11) | copy-start | bytes 1572868
  47.3 4.9 %collective-permute-start.6 = (f32[128,128]{1,0:T(8,128)}, f32[128,128]{1,0:T(8,128)S(1)}, u32[]{:S(2)}, u32[]{:S(2)}) collective-permute-start(f32[128,128]{1,0:T(8,128)} %get-tuple-element.58), channel_id=1, source_target_pairs={{0,24},{8,0},{16,8},{24,16},{1,25},{9,1},{17,9},{25,17},{2,26},{10... | collective-permute-start | bytes 196616 | tf_op jit(solution)/shard_map/ppermute | solution.py:86
  47.8 6.0 %collective-permute-start.7 = (f32[128,128]{1,0:T(8,128)}, f32[128,128]{1,0:T(8,128)S(1)}, u32[]{:S(2)}, u32[]{:S(2)}) collective-permute-start(f32[128,128]{1,0:T(8,128)} %get-tuple-element.57), channel_id=1, source_target_pairs={{0,16},{8,24},{16,0},{24,8},{1,17},{9,25},{17,1},{25,9},{2,18},{10... | collective-permute-start | bytes 196616 | tf_op jit(solution)/shard_map/ppermute | solution.py:86
  48.7 5.9 %collective-permute-start.8 = (f32[128,128]{1,0:T(8,128)}, f32[128,128]{1,0:T(8,128)}, u32[]{:S(2)}, u32[]{:S(2)}) collective-permute-start(f32[128,128]{1,0:T(8,128)} %get-tuple-element.56), channel_id=1, source_target_pairs={{0,8},{8,16},{16,24},{24,0},{1,9},{9,17},{17,25},{25,1},{2,10},{10... | collective-permute-start | bytes 196616 | tf_op jit(solution)/shard_map/ppermute | solution.py:86
  58.6 10.0 %all-to-all-start = ((f32[8,2,4,128]{3,2,1,0:T(4,128)}), f32[8,2,4,128]{3,2,1,0:T(4,128)S(1)}, u32[]{:S(2)}, u32[]{:S(2)}) async-start(f32[8,2,4,128]{3,2,1,0:T(4,128)} %broadcast_in_dim.5), calls=%async_computation | async-start | bytes 65536 | tf_op jit(solution)/shard_map/all_to_all | solution.py:139
  70.6 4.9 %collective-permute-start.9 = (f32[129,128]{1,0:T(8,128)S(1)}, f32[129,128]{1,0:T(8,128)S(1)}, u32[]{:S(2)}, u32[]{:S(2)}) collective-permute-start(f32[129,128]{1,0:T(8,128)S(1)} %get-tuple-element.49), channel_id=1, source_target_pairs={{0,24},{8,0},{16,8},{24,16},{1,25},{9,1},{17,9},{25,17},{2,26},{10... | collective-permute-start | bytes 198152 | tf_op jit(solution)/shard_map/ppermute | solution.py:86
  72.6 5.8 %collective-permute-start.10 = (f32[129,128]{1,0:T(8,128)S(1)}, f32[129,128]{1,0:T(8,128)S(1)}, u32[]{:S(2)}, u32[]{:S(2)}) collective-permute-start(f32[129,128]{1,0:T(8,128)S(1)} %get-tuple-element.48), channel_id=1, source_target_pairs={{0,16},{8,24},{16,0},{24,8},{1,17},{9,25},{17,1},{25,9},{2,18},{10... | collective-permute-start | bytes 198152 | tf_op jit(solution)/shard_map/ppermute | solution.py:86
  73.4 5.8 %collective-permute-start.11 = (f32[129,128]{1,0:T(8,128)S(1)}, f32[129,128]{1,0:T(8,128)S(1)}, u32[]{:S(2)}, u32[]{:S(2)}) collective-permute-start(f32[129,128]{1,0:T(8,128)S(1)} %get-tuple-element.47), channel_id=1, source_target_pairs={{0,8},{8,16},{16,24},{24,0},{1,9},{9,17},{17,25},{25,1},{2,10},{10... | collective-permute-start | bytes 198152 | tf_op jit(solution)/shard_map/ppermute | solution.py:86
  79.3 6.2 %collective-permute-start.12 = (f32[1,129,128]{2,1,0:T(8,128)S(1)}, f32[1,129,128]{2,1,0:T(8,128)S(1)}, u32[]{:S(2)}, u32[]{:S(2)}) collective-permute-start(f32[1,129,128]{2,1,0:T(8,128)S(1)} %pad_maximum_fusion.7), channel_id=1, source_target_pairs={{32,0},{64,32},{96,64},{128,96},{160,128},{192,160},{224,192},{33,... | collective-permute-start | bytes 198152 | tf_op jit(solution)/shard_map/ppermute | solution.py:67
  85.6 9.1 %collective-permute-start.13 = (f32[1,129,128]{2,1,0:T(8,128)S(1)}, f32[1,129,128]{2,1,0:T(8,128)S(1)}, u32[]{:S(2)}, u32[]{:S(2)}) collective-permute-start(f32[1,129,128]{2,1,0:T(8,128)S(1)} %pad_maximum_fusion.8), channel_id=1, source_target_pairs={{64,0},{96,32},{128,64},{160,96},{192,128},{224,160},{65,1},{97,33... | collective-permute-start | bytes 198152 | tf_op jit(solution)/shard_map/ppermute | solution.py:67
  94.7 10.2 %collective-permute-start.14 = (f32[1,129,128]{2,1,0:T(8,128)S(1)}, f32[1,129,128]{2,1,0:T(8,128)S(1)}, u32[]{:S(2)}, u32[]{:S(2)}) collective-permute-start(f32[1,129,128]{2,1,0:T(8,128)S(1)} %pad_maximum_fusion.9), channel_id=1, source_target_pairs={{128,0},{160,32},{192,64},{224,96},{129,1},{161,33},{193,65},{225,... | collective-permute-start | bytes 198152 | tf_op jit(solution)/shard_map/ppermute | solution.py:67
  105.0 5.7 %collective-permute-start.15 = (f32[128,128]{1,0:T(8,128)S(1)}, f32[128,128]{1,0:T(8,128)S(1)}, u32[]{:S(2)}, u32[]{:S(2)}) collective-permute-start(f32[128,128]{1,0:T(8,128)S(1)} %get-tuple-element.55), channel_id=1, source_target_pairs={{0,24},{8,0},{16,8},{24,16},{1,25},{9,1},{17,9},{25,17},{2,26},{10... | collective-permute-start | bytes 196616 | tf_op jit(solution)/shard_map/ppermute | solution.py:86
  105.6 5.8 %collective-permute-start.16 = (f32[128,128]{1,0:T(8,128)S(1)}, f32[128,128]{1,0:T(8,128)S(1)}, u32[]{:S(2)}, u32[]{:S(2)}) collective-permute-start(f32[128,128]{1,0:T(8,128)S(1)} %get-tuple-element.54), channel_id=1, source_target_pairs={{0,16},{8,24},{16,0},{24,8},{1,17},{9,25},{17,1},{25,9},{2,18},{10... | collective-permute-start | bytes 196616 | tf_op jit(solution)/shard_map/ppermute | solution.py:86
  106.7 5.5 %collective-permute-start.17 = (f32[128,128]{1,0:T(8,128)S(1)}, f32[128,128]{1,0:T(8,128)S(1)}, u32[]{:S(2)}, u32[]{:S(2)}) collective-permute-start(f32[128,128]{1,0:T(8,128)S(1)} %get-tuple-element.53), channel_id=1, source_target_pairs={{0,8},{8,16},{16,24},{24,0},{1,9},{9,17},{17,25},{25,1},{2,10},{10... | collective-permute-start | bytes 196616 | tf_op jit(solution)/shard_map/ppermute | solution.py:86
  (33 other events, 64.7 us)
